TPU v7x, 32 devices: a whole 2x2x4 slice. The times are simulated.
32 devices in a mesh: wide: 8 (over z, x), narrow: 4 (over y, core).
Axes of the slice: x: 2, y: 2, z: 4, core: 2. Of those that a mesh axis runs over, the one named last changes fastest.
Arguments:
- start_block: float32 [4096, 256], P(('wide', 'narrow'))
- jacobian: float32 [4096, 5, 4096], P(('wide', 'narrow')), may hold values from -0.3125 to 0.3125
- counts: int32 [32], P(('wide', 'narrow')), may hold values from 2 to 128, as said below
- columns: int32 [4096, 5], P(('wide', 'narrow')), may hold values from 0 to 255, as said below
- send_list: int32 [32, 4, 32], P(('wide', 'narrow')), may hold values from 0 to 127, as said below
Outputs:
- correction: float32 [4096, 256], P(('wide', 'narrow'))
- residual: float32 [4096, 256], P(('wide', 'narrow'))
Inputs may be any that keep to these rules, and one draw needn't show every extreme that they name: `counts`: one device has exactly 128 live elements in every draw; the loads are uneven. columns[e, 0] is the element's own slot; a value below 128 in columns[e, 1:] is below the device's count, a larger one is a ghost slot of one of the four neighbour directions. `send_list`: every entry is below the count of the device that lends it; lists may repeat elements.
All inputs are finite; a program needn't handle non-finite values.
Results may differ from a plain program's by a relative error of at most 0.0003.
Values sent between devices are 32-bit elements; how exact they have to be, the bound alone decides.
No kernel may reach another device: no remote copies, remote signals or barrier semaphores. Data moves between devices by JAX's collectives and lax.ppermute only.
A program may use at most 128 MiB of HBM per device.

v0:
```python
import jax
import jax.numpy as jnp
from jax import lax
from jax.sharding import PartitionSpec as P

BLK = 64
VECS = 4
NB = 5
E_DEV = 128


DIAG_SHIFT = 1.5


def padded(cells, sides, width):
    for axis, dim in sides:
        count = lax.axis_size(axis)
        ends = count - 1
        head = lax.slice_in_dim(cells, 0, width, axis=dim)
        tail = lax.slice_in_dim(cells, cells.shape[dim] - width, cells.shape[dim], axis=dim)
        cells = jnp.concatenate(
            [
                lax.ppermute(tail, axis, [(i, (i + 1) % count) for i in range(ends)]),
                cells,
                lax.ppermute(head, axis, [((i + 1) % count, i) for i in range(ends)]),
            ],
            axis=dim,
        )
    return cells


def combine(values, mixing):
    shaped = values.reshape(values.shape[0], VECS, BLK)
    return jnp.einsum("eci,cd->edi", shaped, mixing, precision=lax.Precision.HIGHEST).reshape(
        values.shape[0], VECS * BLK
    )


def inner_block(left_side, right_side):
    left_shaped = left_side.reshape(left_side.shape[0], VECS, BLK)
    right_shaped = right_side.reshape(right_side.shape[0], VECS, BLK)
    return jnp.einsum("eci,edi->cd", left_shaped, right_shaped, precision=lax.Precision.HIGHEST)


def per_device(start_block, jacobian, counts, columns, send_list):
    living = (lax.iota(jnp.int32, E_DEV) < counts[0])[:, None]
    anchor = jnp.where(living, start_block, jnp.float32(0.0))
    lend_rows = send_list[0]

    def ghosts(values):
        outgoing = values[lend_rows]
        wide_in = padded(jnp.stack([outgoing[1], outgoing[0]]), (("wide", 0),), 1)
        narrow_in = padded(jnp.stack([outgoing[3], outgoing[2]]), (("narrow", 0),), 1)
        return jnp.concatenate([wide_in[0], wide_in[3], narrow_in[0], narrow_in[3]], 0)

    def contract(source, row_count):
        matrices = jacobian.reshape(row_count, NB, BLK, BLK)
        picked = source[columns].reshape(row_count, NB, VECS, BLK)
        summed = jnp.einsum("ekij,ekcj->eci", matrices, picked, precision=lax.Precision.HIGHEST)
        return summed.reshape(row_count, VECS * BLK)

    def product(source):
        return contract(source, E_DEV)

    def operate(values):
        ghost_rows = ghosts(values)
        summed = product(jnp.concatenate([values, ghost_rows], 0))
        return jnp.where(living, DIAG_SHIFT * values + summed, jnp.float32(0.0))

    first_image = operate(anchor)
    cross_first = inner_block(first_image, anchor)
    self_first = inner_block(first_image, first_image)
    early_sums = lax.psum((cross_first, self_first), ("wide", "narrow"))
    second_image = operate(first_image)
    cross_second = inner_block(second_image, anchor)
    mixed_terms = inner_block(second_image, first_image)
    self_second = inner_block(second_image, second_image)
    late_sums = lax.psum((cross_second, mixed_terms, self_second), ("wide", "narrow"))
    gram_parts = (early_sums[0], early_sums[1], late_sums[0], late_sums[1], late_sums[2])
    normal_matrix = jnp.concatenate(
        [
            jnp.concatenate([gram_parts[1], gram_parts[3].T], 1),
            jnp.concatenate([gram_parts[3], gram_parts[4]], 1),
        ],
        0,
    )
    right_terms = jnp.concatenate([gram_parts[0], gram_parts[2]], 0)
    factor = jnp.linalg.cholesky(normal_matrix)
    coefficients = jax.scipy.linalg.cho_solve((factor, True), right_terms)
    correction = combine(anchor, coefficients[:VECS]) + combine(first_image, coefficients[VECS:])
    residual = anchor - (
        combine(first_image, coefficients[:VECS]) + combine(second_image, coefficients[VECS:])
    )
    return (correction, residual)


def solution(mesh):
    placed = (
        P(("wide", "narrow"), None),
        P(("wide", "narrow"), None, None),
        P(("wide", "narrow")),
        P(("wide", "narrow"), None),
        P(("wide", "narrow"), None, None),
    )
    return jax.shard_map(
        per_device,
        mesh=mesh,
        in_specs=placed,
        out_specs=(P(("wide", "narrow"), None), P(("wide", "narrow"), None)),
        check_vma=False,
    )
```

profile of v0, /device:TPU:0, one launch (start us, length us, event | category | flops | bytes accessed | tf_op | source)
XLA Modules:
  0.0 167.4 jit_solution(5175704882577219557)
XLA Ops:
  1.3 0.7 compare_select_fusion.1
  2.1 1.0 constant_dynamic-update-slice_fusion
  3.1 0.8 gather_fusion
  3.8 4.8 %collective-permute-start = (f32[1,32,256]{2,1,0:T(8,128)S(1)}, f32[1,32,256]{2,1,0:T(8,128)S(1)}, u32[]{:S(2)}, u32[]{:S(2)}) collective-permute-start(f32[1,32,256]{2,1,0:T(8,128)S(1)} %get-tuple-element.20), channel_id=1, source_target_pairs={{0,4},{4,8},{8,12},{12,16},{16,20},{20,24},{24,28},{1,5},{5,9},{9,... | collective-permute-start | bytes 98312 | tf_op jit(solution)/shard_map/ppermute | solution.py:23
  8.7 1.3 collective-permute-start.1
  10.0 1.5 collective-permute-start.2
  11.5 1.3 collective-permute-start.3
  12.8 0.7 compare_select_fusion
  13.5 0.1 copy.24
  13.6 0.2 reshape.109
  13.9 11.2 %copy.25 = f32[128,5,4096]{0,2,1:T(8,128)} copy(f32[128,5,4096]{2,0,1:T(8,128)} %param.6) | data formatting | bytes 20971520 | tf_op args[1]
  25.1 19.8 %copy.26 = f32[128,5,64,64]{3,2,1,0:T(8,128)} copy(f32[128,5,64,64]{0,3,2,1:T(8,128)} %bitcast.95) | data formatting | bytes 20971520 | tf_op jit(solution)/shard_map/reshape | solution.py:57
  45.0 2.2 %gather_fusion.1 = f32[640,256]{1,0:T(8,128)S(1)} fusion(f32[256,256]{1,0:T(8,128)S(1)} %bitcast_dynamic-update-slice_fusion.4, s32[1024]{0:T(1024)S(1)} %pad_clamp_fusion), kind=kCustom, calls=%fused_computation.1 | custom fusion | bytes 1313280 | tf_op jit(solution)/shard_map/gather | solution.py:58
  47.3 0.6 reshape.91
  47.8 23.3 %convolution_bitcast_fusion.1 = f32[128,4,64]{2,1,0:T(4,128)S(1)} fusion(f32[128,5,4,64]{3,2,1,0:T(4,128)S(1)} %reshape.91, f32[128,5,64,64]{3,2,1,0:T(8,128)} %copy.26), kind=kOutput, calls=%fused_computation.5 | convolution fusion | flops 125829120 | bytes 11272192 | tf_op jit(solution)/shard_map/ekij,ekcj->eci/dot_general | solution.py:59
  71.1 0.1 copy.27
  71.2 0.1 copy.28
  71.4 0.1 constant_dynamic-update-slice_fusion.1
  71.4 0.8 gather_fusion.2
  72.3 4.4 %collective-permute-start.4 = (f32[1,32,256]{2,1,0:T(8,128)S(1)}, f32[1,32,256]{2,1,0:T(8,128)S(1)}, u32[]{:S(2)}, u32[]{:S(2)}) collective-permute-start(f32[1,32,256]{2,1,0:T(8,128)S(1)} %get-tuple-element.16), channel_id=1, source_target_pairs={{0,4},{4,8},{8,12},{12,16},{16,20},{20,24},{24,28},{1,5},{5,9},{9,... | collective-permute-start | bytes 98312 | tf_op jit(solution)/shard_map/ppermute | solution.py:23
  76.7 0.7 convolution_bitcast_fusion.3
  77.5 0.7 convolution_bitcast_fusion.6
  78.2 1.3 collective-permute-start.5
  79.5 4.5 %collective-permute-start.6 = (f32[1,32,256]{2,1,0:T(8,128)S(1)}, f32[1,32,256]{2,1,0:T(8,128)S(1)}, u32[]{:S(2)}, u32[]{:S(2)}) collective-permute-start(f32[1,32,256]{2,1,0:T(8,128)S(1)} %get-tuple-element.14), channel_id=1, source_target_pairs={{0,1},{1,2},{2,3},{4,5},{5,6},{6,7},{8,9},{9,10},{10,11},{12,13},{... | collective-permute-start | bytes 98312 | tf_op jit(solution)/shard_map/ppermute | solution.py:23
  84.0 1.5 collective-permute-start.7
  85.5 3.1 %collective-permute-done.7 = f32[1,32,256]{2,1,0:T(8,128)S(1)} collective-permute-done((f32[1,32,256]{2,1,0:T(8,128)S(1)}, f32[1,32,256]{2,1,0:T(8,128)S(1)}, u32[]{:S(2)}, u32[]{:S(2)}) %collective-permute-start.7) | collective-permute-done | bytes 32800 | tf_op jit(solution)/shard_map/ppermute | solution.py:25
  88.6 2.2 %gather_fusion.3 = f32[640,256]{1,0:T(8,128)S(1)} fusion(f32[256,256]{1,0:T(8,128)S(1)} %bitcast_dynamic-update-slice_fusion, s32[1024]{0:T(1024)S(1)} %pad_clamp_fusion), kind=kCustom, calls=%fused_computation.3 | custom fusion | bytes 1313280 | tf_op jit(solution)/shard_map/gather | solution.py:58
  90.8 0.6 reshape.95
  91.4 23.3 %convolution_bitcast_fusion = f32[128,4,64]{2,1,0:T(4,128)S(1)} fusion(f32[128,5,4,64]{3,2,1,0:T(4,128)S(1)} %reshape.95, f32[128,5,64,64]{3,2,1,0:T(8,128)} %copy.26), kind=kOutput, calls=%fused_computation.4 | convolution fusion | flops 125829120 | bytes 11272192 | tf_op jit(solution)/shard_map/ekij,ekcj->eci/dot_general | solution.py:59
  114.7 0.1 copy.33
  114.8 0.1 copy.34
  115.1 0.7 convolution_bitcast_fusion.5
  115.8 0.8 convolution_bitcast_fusion.2
  116.6 0.7 convolution_bitcast_fusion.4
  117.3 43.4 %all-reduce = (f32[4,4]{1,0:T(4,128)S(1)}, f32[4,4]{1,0:T(4,128)S(1)}, f32[4,4]{0,1:T(4,128)S(1)}, f32[4,4]{0,1:T(4,128)S(1)}, f32[4,4]{1,0:T(4,128)S(1)}) all-reduce(f32[4,4]{1,0:T(4,128)S(1)} %convolution_bitcast_fusion.2, f32[4,4]{1,0:T(4,128)S(1)} %convolution_bitcast_fusion.3, ...), channel_id=1, replica_groups=mesh['wide'=8,'narrow'=4] {'wide','narrow'}, use_global_device_ids=true, to_apply=%region_6.7 | all-reduce | flops 80 | bytes 640 | tf_op jit(solution)/shard_map/psum | solution.py:78
  161.1 0.7 cholesky.16
  161.8 0.6 compare_reduce_fusion
  162.5 0.6 fusion.16
  163.1 0.6 custom-call.10
  163.7 0.2 fusion.17
  163.9 0.2 fusion.22
  164.1 0.4 fusion.10
  164.6 0.4 fusion.4
  165.0 0.4 fusion
  165.4 0.1 copy.52
  165.5 0.7 sub.3
  166.2 0.4 fusion.1
  166.6 0.8 copy.53
  (33 shorter events, 1.0 us)
Async XLA Ops:
  3.8 41.1 %collective-permute-start = (f32[1,32,256]{2,1,0:T(8,128)S(1)}, f32[1,32,256]{2,1,0:T(8,128)S(1)}, u32[]{:S(2)}, u32[]{:S(2)}) collective-permute-start(f32[1,32,256]{2,1,0:T(8,128)S(1)} %get-tuple-element.20), channel_id=1, source_target_pairs={{0,4},{4,8},{8,12},{12,16},{16,20},{20,24},{24,28},{1,5},{5,9},{9,... | collective-permute-start | bytes 98312 | tf_op jit(solution)/shard_map/ppermute | solution.py:23
  8.7 36.3 %collective-permute-start.1 = (f32[1,32,256]{2,1,0:T(8,128)S(1)}, f32[1,32,256]{2,1,0:T(8,128)S(1)}, u32[]{:S(2)}, u32[]{:S(2)}) collective-permute-start(f32[1,32,256]{2,1,0:T(8,128)S(1)} %get-tuple-element.19), channel_id=1, source_target_pairs={{4,0},{8,4},{12,8},{16,12},{20,16},{24,20},{28,24},{5,1},{9,5},{13... | collective-permute-start | bytes 98312 | tf_op jit(solution)/shard_map/ppermute | solution.py:25
  10.0 35.0 %collective-permute-start.2 = (f32[1,32,256]{2,1,0:T(8,128)S(1)}, f32[1,32,256]{2,1,0:T(8,128)S(1)}, u32[]{:S(2)}, u32[]{:S(2)}) collective-permute-start(f32[1,32,256]{2,1,0:T(8,128)S(1)} %get-tuple-element.18), channel_id=1, source_target_pairs={{0,1},{1,2},{2,3},{4,5},{5,6},{6,7},{8,9},{9,10},{10,11},{12,13},{... | collective-permute-start | bytes 98312 | tf_op jit(solution)/shard_map/ppermute | solution.py:23
  11.5 33.6 %collective-permute-start.3 = (f32[1,32,256]{2,1,0:T(8,128)S(1)}, f32[1,32,256]{2,1,0:T(8,128)S(1)}, u32[]{:S(2)}, u32[]{:S(2)}) collective-permute-start(f32[1,32,256]{2,1,0:T(8,128)S(1)} %get-tuple-element.17), channel_id=1, source_target_pairs={{1,0},{2,1},{3,2},{5,4},{6,5},{7,6},{9,8},{10,9},{11,10},{13,12},{... | collective-permute-start | bytes 98312 | tf_op jit(solution)/shard_map/ppermute | solution.py:25
  72.3 13.1 %collective-permute-start.4 = (f32[1,32,256]{2,1,0:T(8,128)S(1)}, f32[1,32,256]{2,1,0:T(8,128)S(1)}, u32[]{:S(2)}, u32[]{:S(2)}) collective-permute-start(f32[1,32,256]{2,1,0:T(8,128)S(1)} %get-tuple-element.16), channel_id=1, source_target_pairs={{0,4},{4,8},{8,12},{12,16},{16,20},{20,24},{24,28},{1,5},{5,9},{9,... | collective-permute-start | bytes 98312 | tf_op jit(solution)/shard_map/ppermute | solution.py:23
  78.2 7.3 %collective-permute-start.5 = (f32[1,32,256]{2,1,0:T(8,128)S(1)}, f32[1,32,256]{2,1,0:T(8,128)S(1)}, u32[]{:S(2)}, u32[]{:S(2)}) collective-permute-start(f32[1,32,256]{2,1,0:T(8,128)S(1)} %get-tuple-element.15), channel_id=1, source_target_pairs={{4,0},{8,4},{12,8},{16,12},{20,16},{24,20},{28,24},{5,1},{9,5},{13... | collective-permute-start | bytes 98312 | tf_op jit(solution)/shard_map/ppermute | solution.py:25
  79.5 6.0 %collective-permute-start.6 = (f32[1,32,256]{2,1,0:T(8,128)S(1)}, f32[1,32,256]{2,1,0:T(8,128)S(1)}, u32[]{:S(2)}, u32[]{:S(2)}) collective-permute-start(f32[1,32,256]{2,1,0:T(8,128)S(1)} %get-tuple-element.14), channel_id=1, source_target_pairs={{0,1},{1,2},{2,3},{4,5},{5,6},{6,7},{8,9},{9,10},{10,11},{12,13},{... | collective-permute-start | bytes 98312 | tf_op jit(solution)/shard_map/ppermute | solution.py:23
  84.0 4.6 %collective-permute-start.7 = (f32[1,32,256]{2,1,0:T(8,128)S(1)}, f32[1,32,256]{2,1,0:T(8,128)S(1)}, u32[]{:S(2)}, u32[]{:S(2)}) collective-permute-start(f32[1,32,256]{2,1,0:T(8,128)S(1)} %get-tuple-element.13), channel_id=1, source_target_pairs={{1,0},{2,1},{3,2},{5,4},{6,5},{7,6},{9,8},{10,9},{11,10},{13,12},{... | collective-permute-start | bytes 98312 | tf_op jit(solution)/shard_map/ppermute | solution.py:25
where the time goes:
time: 168 us; the launch traced here: 167 us
  matrix products  52.3 us (31%)
  blocking collectives  43.4 us (26%)
  local copies, waits for them, and re-layouts  40.3 us (24%)
  starting transfers between devices  20.5 us (12%)
  other arithmetic  6.13 us (4%)
  waiting for transfers between devices  3.09 us (2%)
    dot_general x2, matrix products, contract(): jnp.einsum('ekij,ekcj->eci', matrices, picked, precision=lax.Precision.HI...  46.6 us
    psum x1, blocking collectives, per_device(): lax.psum((cross_second, mixed_terms, self_second), ('wide', 'narrow'))  43.4 us
    reshape x1, local copies, waits for them, and re-layouts, contract(): matrices = jacobian.reshape(row_count, NB, BLK, BLK)  19.8 us
    ppermute x4, starting transfers between devices, padded(): lax.ppermute(tail, axis, [(i, (i + 1) % count) for i in range(ends)])  15.2 us
    unnamed x8, local copies, waits for them, and re-layouts  12 us
    ppermute x4, starting transfers between devices, padded(): lax.ppermute(head, axis, [((i + 1) % count, i) for i in range(ends)])  5.35 us
    gather x2, local copies, waits for them, and re-layouts, contract(): picked = source[columns].reshape(row_count, NB, VECS, BLK)  4.41 us
    dot_general x5, matrix products, inner_block(): jnp.einsum('eci,edi->cd', left_shaped, right_shaped, precision=lax.Precis...  3.65 us
  transfers between devices with their start and end apart: 8, of which 1 were waited for; matrix products, arithmetic and copies ran while one was open for 20% of the time, Pallas kernels for 0%

commit v1 on v0

--- a/solution.py
+++ b/solution.py
@@ -1,12 +1,16 @@
 import jax
 import jax.numpy as jnp
 from jax import lax
+from jax.experimental import pallas as pl
+from jax.experimental.pallas import tpu as pltpu
 from jax.sharding import PartitionSpec as P
 
 BLK = 64
 VECS = 4
 NB = 5
 E_DEV = 128
+LANES = 128
+ROWS_PER_STEP = 32
 
 
 DIAG_SHIFT = 1.5
@@ -42,10 +46,82 @@
     return jnp.einsum("eci,edi->cd", left_shaped, right_shaped, precision=lax.Precision.HIGHEST)
 
 
+def tree_sum(values, axes):
+    for axis in axes:
+        count = lax.axis_size(axis)
+        if count & (count - 1):
+            values = lax.psum(values, axis)
+            continue
+        stride = 1
+        while stride < count:
+            values = values + lax.ppermute(values, axis, [(i, i ^ stride) for i in range(count)])
+            stride *= 2
+    return values
+
+
+def coupling_kernel(jac_ref, picked_ref, seg_ref, out_ref, parts_ref):
+    step = pl.program_id(0)
+    rows = jac_ref.shape[1]
+    tiles = jac_ref.shape[2] // LANES
+    row0 = pl.multiple_of(step * rows, rows)
+
+    def one_tile(t, carry):
+        off = pl.multiple_of(t * LANES, LANES)
+        blocks = [jac_ref[k, :, pl.ds(off, LANES)] for k in range(NB)]
+        for c in range(VECS):
+            total = blocks[0] * picked_ref[0, :, c * LANES:(c + 1) * LANES]
+            for k in range(1, NB):
+                total = total + blocks[k] * picked_ref[k, :, c * LANES:(c + 1) * LANES]
+            high = total.astype(jnp.bfloat16)
+            low = (total - high.astype(jnp.float32)).astype(jnp.bfloat16)
+            parts_ref[2 * c, pl.ds(row0, rows), pl.ds(off, LANES)] = high
+            parts_ref[2 * c + 1, pl.ds(row0, rows), pl.ds(off, LANES)] = low
+        return carry
+
+    lax.fori_loop(0, tiles, one_tile, 0)
+
+    @pl.when(step == pl.num_programs(0) - 1)
+    def _():
+        count = parts_ref.shape[1]
+        flat = parts_ref[...].reshape(2 * VECS * count, tiles * LANES)
+        sums = jnp.dot(flat, seg_ref[...], preferred_element_type=jnp.float32)
+        for c in range(VECS):
+            high = sums[(2 * c) * count:(2 * c + 1) * count]
+            low = sums[(2 * c + 1) * count:(2 * c + 2) * count]
+            out_ref[:, c * BLK:(c + 1) * BLK] = high + low
+
+
+def coupled_sum(jac_t, picked, seg):
+    blocks, count, width = jac_t.shape
+    rows = min(ROWS_PER_STEP, count)
+    return pl.pallas_call(
+        coupling_kernel,
+        out_shape=jax.ShapeDtypeStruct((count, VECS * BLK), jnp.float32),
+        grid=(count // rows,),
+        in_specs=[
+            pl.BlockSpec((blocks, rows, width), lambda b: (0, b, 0)),
+            pl.BlockSpec((blocks, rows, VECS * LANES), lambda b: (0, b, 0)),
+            pl.BlockSpec((width, BLK), lambda b: (0, 0)),
+        ],
+        out_specs=pl.BlockSpec((count, VECS * BLK), lambda b: (0, 0)),
+        scratch_shapes=[pltpu.VMEM((2 * VECS, count, width), jnp.bfloat16)],
+        compiler_params=pltpu.CompilerParams(dimension_semantics=("arbitrary",)),
+        cost_estimate=pl.CostEstimate(
+            flops=2 * blocks * count * width * VECS + 2 * 2 * VECS * count * width * BLK,
+            bytes_accessed=4 * (blocks * count * width + blocks * count * VECS * LANES + count * VECS * BLK),
+            transcendentals=0,
+        ),
+    )(jac_t, picked, seg)
+
+
 def per_device(start_block, jacobian, counts, columns, send_list):
     living = (lax.iota(jnp.int32, E_DEV) < counts[0])[:, None]
     anchor = jnp.where(living, start_block, jnp.float32(0.0))
     lend_rows = send_list[0]
+    jac_t = jnp.transpose(jacobian, (1, 0, 2))
+    lane = lax.broadcasted_iota(jnp.int32, (BLK * BLK, BLK), 0)
+    col = lax.broadcasted_iota(jnp.int32, (BLK * BLK, BLK), 1)
+    seg = (lane // BLK == col).astype(jnp.bfloat16)
 
     def ghosts(values):
         outgoing = values[lend_rows]
@@ -53,30 +129,25 @@
         narrow_in = padded(jnp.stack([outgoing[3], outgoing[2]]), (("narrow", 0),), 1)
         return jnp.concatenate([wide_in[0], wide_in[3], narrow_in[0], narrow_in[3]], 0)
 
-    def contract(source, row_count):
-        matrices = jacobian.reshape(row_count, NB, BLK, BLK)
-        picked = source[columns].reshape(row_count, NB, VECS, BLK)
-        summed = jnp.einsum("ekij,ekcj->eci", matrices, picked, precision=lax.Precision.HIGHEST)
-        return summed.reshape(row_count, VECS * BLK)
-
-    def product(source):
-        return contract(source, E_DEV)
-
     def operate(values):
         ghost_rows = ghosts(values)
-        summed = product(jnp.concatenate([values, ghost_rows], 0))
+        source = jnp.concatenate([values, ghost_rows], 0)
+        picked = source[columns].reshape(E_DEV, NB, VECS, 1, BLK)
+        picked = jnp.broadcast_to(picked, (E_DEV, NB, VECS, 2, BLK)).reshape(E_DEV, NB, VECS * LANES)
+        picked = jnp.transpose(picked, (1, 0, 2))
+        summed = coupled_sum(jac_t, picked, seg)
         return jnp.where(living, DIAG_SHIFT * values + summed, jnp.float32(0.0))
 
     first_image = operate(anchor)
-    cross_first = inner_block(first_image, anchor)
-    self_first = inner_block(first_image, first_image)
-    early_sums = lax.psum((cross_first, self_first), ("wide", "narrow"))
     second_image = operate(first_image)
-    cross_second = inner_block(second_image, anchor)
-    mixed_terms = inner_block(second_image, first_image)
-    self_second = inner_block(second_image, second_image)
-    late_sums = lax.psum((cross_second, mixed_terms, self_second), ("wide", "narrow"))
-    gram_parts = (early_sums[0], early_sums[1], late_sums[0], late_sums[1], late_sums[2])
+    blocks = (
+        inner_block(first_image, anchor),
+        inner_block(first_image, first_image),
+        inner_block(second_image, anchor),
+        inner_block(second_image, first_image),
+        inner_block(second_image, second_image),
+    )
+    gram_parts = tree_sum(jnp.stack(blocks), ("narrow", "wide"))
     normal_matrix = jnp.concatenate(
         [
             jnp.concatenate([gram_parts[1], gram_parts[3].T], 1),

time: 168 us -> 101 us (0.60)
  matrix products: 52.3 us -> 5.78 us
  blocking collectives: 43.4 us -> 0 us
  local copies, waits for them, and re-layouts: 40.3 us -> 14.3 us
  Pallas kernels: 0 us -> 22.8 us
  starting transfers between devices: 20.5 us -> 33.2 us
  waiting for transfers between devices: 3.09 us -> 10.7 us
  other arithmetic: 6.13 us -> 11.8 us
    dot_general x2 -> x0, matrix products: 46.6 us -> none  [contract(): jnp.einsum('ekij,ekcj->eci', matrices, picked, precision=lax.Precision.HI...]
    psum x1 -> x0, blocking collectives: 43.4 us -> none  [per_device(): lax.psum((cross_second, mixed_terms, self_second), ('wide', 'narrow'))]
    pallas_call x0 -> x2, Pallas kernels: none -> 22.8 us  [coupled_sum(): pl.pallas_call(coupling_kernel, out_shape=jax.ShapeDtypeStruct((count, VE...]
    reshape x5 -> x2, local copies, waits for them, and re-layouts: 21.2 us -> 2.97 us  [operate(): jnp.broadcast_to(picked, (E_DEV, NB, VECS, 2, BLK))]
    ppermute x0 -> x5, starting transfers between devices: none -> 12.6 us  [tree_sum(): lax.ppermute(values, axis, [(i, i ^ stride) for i in range(count)])]
    unnamed x8 -> x9, local copies, waits for them, and re-layouts: 12 us -> 0.8 us
    ppermute x0 -> x5, waiting for transfers between devices: none -> 9.06 us  [tree_sum(): lax.ppermute(values, axis, [(i, i ^ stride) for i in range(count)])]
    convert_element_type x0 -> x1, other arithmetic: none -> 4.7 us  [per_device(): seg = (lane // BLK == col).astype(jnp.bfloat16)]
  transfers between devices with their start and end apart: 8 -> 13, of which waited for: 1 -> 6; matrix products, arithmetic and copies ran while one was open for 20% -> 7% of each run, Pallas kernels for 0% -> 0%
where the time goes in v1:
time: 101 us; the launch traced here: 100 us
  starting transfers between devices  33.2 us (33%)
  Pallas kernels  22.8 us (23%)
  local copies, waits for them, and re-layouts  14.3 us (14%)
  other arithmetic  11.8 us (12%)
  waiting for transfers between devices  10.7 us (11%)
  matrix products  5.78 us (6%)
  between operations  1.72 us (2%)
    pallas_call x2, Pallas kernels, coupled_sum(): pl.pallas_call(coupling_kernel, out_shape=jax.ShapeDtypeStruct((count, VE...  22.8 us
    ppermute x4, starting transfers between devices, padded(): lax.ppermute(tail, axis, [(i, (i + 1) % count) for i in range(ends)])  15.2 us
    ppermute x5, starting transfers between devices, tree_sum(): lax.ppermute(values, axis, [(i, i ^ stride) for i in range(count)])  12.6 us
    ppermute x5, waiting for transfers between devices, tree_sum(): lax.ppermute(values, axis, [(i, i ^ stride) for i in range(count)])  9.06 us
    ppermute x4, starting transfers between devices, padded(): lax.ppermute(head, axis, [((i + 1) % count, i) for i in range(ends)])  5.35 us
    convert_element_type x1, other arithmetic, per_device(): seg = (lane // BLK == col).astype(jnp.bfloat16)  4.7 us
    gather x2, local copies, waits for them, and re-layouts, operate(): picked = source[columns].reshape(E_DEV, NB, VECS, 1, BLK)  4.41 us
    dot_general x5, matrix products, inner_block(): jnp.einsum('eci,edi->cd', left_shaped, right_shaped, precision=lax.Precis...  3.71 us
  transfers between devices with their start and end apart: 13, of which 6 were waited for; matrix products, arithmetic and copies ran while one was open for 7% of the time, Pallas kernels for 0%

profile of v1, /device:TPU:0, one launch (start us, length us, event | category | flops | bytes accessed | tf_op | source)
XLA Modules:
  0.0 100.3 jit_solution(14767830013046269593)
XLA Ops:
  1.3 0.7 compare_select_fusion.1
  2.1 1.0 constant_dynamic-update-slice_fusion
  3.1 0.8 gather_fusion
  3.9 4.8 %collective-permute-start = (f32[1,32,256]{2,1,0:T(8,128)S(1)}, f32[1,32,256]{2,1,0:T(8,128)S(1)}, u32[]{:S(2)}, u32[]{:S(2)}) collective-permute-start(f32[1,32,256]{2,1,0:T(8,128)S(1)} %get-tuple-element.15), channel_id=1, source_target_pairs={{0,4},{4,8},{8,12},{12,16},{16,20},{20,24},{24,28},{1,5},{5,9},{9,... | collective-permute-start | bytes 98312 | tf_op jit(solution)/shard_map/ppermute | solution.py:27
  8.7 1.3 %collective-permute-start.1 = (f32[1,32,256]{2,1,0:T(8,128)S(1)}, f32[1,32,256]{2,1,0:T(8,128)S(1)}, u32[]{:S(2)}, u32[]{:S(2)}) collective-permute-start(f32[1,32,256]{2,1,0:T(8,128)S(1)} %get-tuple-element.14), channel_id=1, source_target_pairs={{4,0},{8,4},{12,8},{16,12},{20,16},{24,20},{28,24},{5,1},{9,5},{13... | collective-permute-start | bytes 98312 | tf_op jit(solution)/shard_map/ppermute | solution.py:29
  10.0 1.5 %collective-permute-start.2 = (f32[1,32,256]{2,1,0:T(8,128)S(1)}, f32[1,32,256]{2,1,0:T(8,128)S(1)}, u32[]{:S(2)}, u32[]{:S(2)}) collective-permute-start(f32[1,32,256]{2,1,0:T(8,128)S(1)} %get-tuple-element.13), channel_id=1, source_target_pairs={{0,1},{1,2},{2,3},{4,5},{5,6},{6,7},{8,9},{9,10},{10,11},{12,13},{... | collective-permute-start | bytes 98312 | tf_op jit(solution)/shard_map/ppermute | solution.py:27
  11.5 1.3 %collective-permute-start.3 = (f32[1,32,256]{2,1,0:T(8,128)S(1)}, f32[1,32,256]{2,1,0:T(8,128)S(1)}, u32[]{:S(2)}, u32[]{:S(2)}) collective-permute-start(f32[1,32,256]{2,1,0:T(8,128)S(1)} %get-tuple-element.12), channel_id=1, source_target_pairs={{1,0},{2,1},{3,2},{5,4},{6,5},{7,6},{9,8},{10,9},{11,10},{13,12},{... | collective-permute-start | bytes 98312 | tf_op jit(solution)/shard_map/ppermute | solution.py:29
  13.2 4.7 %fusion.seg_ref = bf16[4096,64]{1,0:T(8,128)(2,1)} fusion(s32[4096]{0:T(1024)S(1)} %get-tuple-element.22, s32[4096]{0:T(1024)S(1)} %get-tuple-element.23, pred[4096]{0:T(1024)(128)(4,1)S(1)} %fusion.24), kind=kLoop, calls=%fused_computation.5 | loop fusion | flops 786432 | bytes 561152 | tf_op jit(solution)/shard_map/convert_element_type | solution.py:124
  18.0 2.2 %gather_fusion.1 = f32[640,256]{1,0:T(8,128)S(1)} fusion(f32[256,256]{1,0:T(8,128)S(1)} %bitcast_dynamic-update-slice_fusion.4, s32[1024]{0:T(1024)S(1)} %pad_clamp_fusion), kind=kCustom, calls=%fused_computation.1 | custom fusion | bytes 1313280 | tf_op jit(solution)/shard_map/gather | solution.py:135
  20.3 0.6 broadcast_in_dim.46
  20.8 1.0 %copy.30 = f32[128,5,4,64]{0,3,2,1:T(8,128)S(1)} copy(f32[128,5,4,64]{3,2,1,0:T(4,128)S(1)} %broadcast_in_dim.46) | data formatting | bytes 1310720 | tf_op jit(solution)/shard_map/broadcast_in_dim | solution.py:136
  22.0 1.5 %copy.31 = f32[128,5,512]{2,0,1:T(8,128)} copy(f32[128,5,512]{0,2,1:T(8,128)S(1)} %bitcast.118) | data formatting | bytes 2621440 | tf_op jit(solution)/shard_map/reshape | solution.py:136
  23.5 11.4 %shard_map.68 = f32[128,256]{1,0:T(8,128)} custom-call(f32[5,128,4096]{2,1,0:T(8,128)} %bitcast.114, f32[5,128,512]{2,1,0:T(8,128)} %bitcast.117, bf16[4096,64]{1,0:T(8,128)(2,1)} %fusion.seg_ref), custom_call_target="tpu_custom_call" | custom-call | flops 557842432 | bytes 11927552 | tf_op jit(solution)/shard_map/pallas_call | solution.py:97
  34.9 1.0 constant_dynamic-update-slice_fusion.1
  35.9 0.8 gather_fusion.2
  36.8 4.4 %collective-permute-start.4 = (f32[1,32,256]{2,1,0:T(8,128)S(1)}, f32[1,32,256]{2,1,0:T(8,128)S(1)}, u32[]{:S(2)}, u32[]{:S(2)}) collective-permute-start(f32[1,32,256]{2,1,0:T(8,128)S(1)} %get-tuple-element.11), channel_id=1, source_target_pairs={{0,4},{4,8},{8,12},{12,16},{16,20},{20,24},{24,28},{1,5},{5,9},{9,... | collective-permute-start | bytes 98312 | tf_op jit(solution)/shard_map/ppermute | solution.py:27
  41.2 1.3 %collective-permute-start.5 = (f32[1,32,256]{2,1,0:T(8,128)S(1)}, f32[1,32,256]{2,1,0:T(8,128)S(1)}, u32[]{:S(2)}, u32[]{:S(2)}) collective-permute-start(f32[1,32,256]{2,1,0:T(8,128)S(1)} %get-tuple-element.10), channel_id=1, source_target_pairs={{4,0},{8,4},{12,8},{16,12},{20,16},{24,20},{28,24},{5,1},{9,5},{13... | collective-permute-start | bytes 98312 | tf_op jit(solution)/shard_map/ppermute | solution.py:29
  42.5 4.5 %collective-permute-start.6 = (f32[1,32,256]{2,1,0:T(8,128)S(1)}, f32[1,32,256]{2,1,0:T(8,128)S(1)}, u32[]{:S(2)}, u32[]{:S(2)}) collective-permute-start(f32[1,32,256]{2,1,0:T(8,128)S(1)} %get-tuple-element.9), channel_id=1, source_target_pairs={{0,1},{1,2},{2,3},{4,5},{5,6},{6,7},{8,9},{9,10},{10,11},{12,13},{... | collective-permute-start | bytes 98312 | tf_op jit(solution)/shard_map/ppermute | solution.py:27
  47.0 1.5 %collective-permute-start.7 = (f32[1,32,256]{2,1,0:T(8,128)S(1)}, f32[1,32,256]{2,1,0:T(8,128)S(1)}, u32[]{:S(2)}, u32[]{:S(2)}) collective-permute-start(f32[1,32,256]{2,1,0:T(8,128)S(1)} %get-tuple-element.8), channel_id=1, source_target_pairs={{1,0},{2,1},{3,2},{5,4},{6,5},{7,6},{9,8},{10,9},{11,10},{13,12},{... | collective-permute-start | bytes 98312 | tf_op jit(solution)/shard_map/ppermute | solution.py:29
  48.5 0.7 fusion.7
  49.2 0.7 fusion.6
  50.0 1.6 %collective-permute-done.7 = f32[1,32,256]{2,1,0:T(8,128)S(1)} collective-permute-done((f32[1,32,256]{2,1,0:T(8,128)S(1)}, f32[1,32,256]{2,1,0:T(8,128)S(1)}, u32[]{:S(2)}, u32[]{:S(2)}) %collective-permute-start.7) | collective-permute-done | bytes 32800 | tf_op jit(solution)/shard_map/ppermute | solution.py:29
  51.6 2.2 %gather_fusion.3 = f32[640,256]{1,0:T(8,128)S(1)} fusion(f32[256,256]{1,0:T(8,128)S(1)} %bitcast_dynamic-update-slice_fusion, s32[1024]{0:T(1024)S(1)} %pad_clamp_fusion), kind=kCustom, calls=%fused_computation.3 | custom fusion | bytes 1313280 | tf_op jit(solution)/shard_map/gather | solution.py:135
  53.8 0.6 broadcast_in_dim.48
  54.4 1.0 %copy.38 = f32[128,5,4,64]{0,3,2,1:T(8,128)S(1)} copy(f32[128,5,4,64]{3,2,1,0:T(4,128)S(1)} %broadcast_in_dim.48) | data formatting | bytes 1310720 | tf_op jit(solution)/shard_map/broadcast_in_dim | solution.py:136
  55.6 1.5 %copy.39 = f32[128,5,512]{2,0,1:T(8,128)} copy(f32[128,5,512]{0,2,1:T(8,128)S(1)} %bitcast.119) | data formatting | bytes 2621440 | tf_op jit(solution)/shard_map/reshape | solution.py:136
  57.0 11.4 %shard_map.69 = f32[128,256]{1,0:T(8,128)} custom-call(f32[5,128,4096]{2,1,0:T(8,128)} %bitcast.115, f32[5,128,512]{2,1,0:T(8,128)} %bitcast.116, bf16[4096,64]{1,0:T(8,128)(2,1)} %fusion.seg_ref), custom_call_target="tpu_custom_call" | custom-call | flops 557842432 | bytes 11927552 | tf_op jit(solution)/shard_map/pallas_call | solution.py:97
  68.5 1.0 add_select_fusion
  69.5 0.8 fusion.5
  70.3 0.8 fusion.4
  71.1 0.7 fusion.3
  71.8 2.6 %collective-permute-start.8 = (f32[5,4,4]{2,1,0:T(4,128)S(1)}, f32[5,4,4]{2,1,0:T(4,128)S(1)}, u32[]{:S(2)}, u32[]{:S(2)}) collective-permute-start(f32[5,4,4]{2,1,0:T(4,128)S(1)} %fusion.3), channel_id=1, source_target_pairs={{0,1},{1,0},{2,3},{3,2},{4,5},{5,4},{6,7},{7,6},{8,9},{9,8},{10,11... | collective-permute-start | bytes 968 | tf_op jit(solution)/shard_map/ppermute | solution.py:57
  74.4 0.8 collective-permute-done.8
  75.7 3.3 %collective-permute-done.9 = f32[5,4,4]{2,1,0:T(4,128)S(1)} collective-permute-done((f32[5,4,4]{2,1,0:T(4,128)S(1)}, f32[5,4,4]{2,1,0:T(4,128)S(1)}, u32[]{:S(2)}, u32[]{:S(2)}) %collective-permute-start.9) | collective-permute-done | bytes 352 | tf_op jit(solution)/shard_map/ppermute | solution.py:57
  78.9 3.1 %collective-permute-start.10 = (f32[5,4,4]{2,1,0:T(4,128)S(1)}, f32[5,4,4]{2,1,0:T(4,128)S(1)}, u32[]{:S(2)}, u32[]{:S(2)}) collective-permute-start(f32[5,4,4]{2,1,0:T(4,128)S(1)} %add.76), channel_id=1, source_target_pairs={{0,4},{4,0},{8,12},{12,8},{16,20},{20,16},{24,28},{28,24},{1,5},{5... | collective-permute-start | bytes 968 | tf_op jit(solution)/shard_map/ppermute | solution.py:57
  82.0 1.6 %collective-permute-done.10 = f32[5,4,4]{2,1,0:T(4,128)S(1)} collective-permute-done((f32[5,4,4]{2,1,0:T(4,128)S(1)}, f32[5,4,4]{2,1,0:T(4,128)S(1)}, u32[]{:S(2)}, u32[]{:S(2)}) %collective-permute-start.10) | collective-permute-done | bytes 352 | tf_op jit(solution)/shard_map/ppermute | solution.py:57
  83.7 3.5 %collective-permute-start.11 = (f32[5,4,4]{2,1,0:T(4,128)S(1)}, f32[5,4,4]{2,1,0:T(4,128)S(1)}, u32[]{:S(2)}, u32[]{:S(2)}) collective-permute-start(f32[5,4,4]{2,1,0:T(4,128)S(1)} %add.77), channel_id=1, source_target_pairs={{0,8},{4,12},{8,0},{12,4},{16,24},{20,28},{24,16},{28,20},{1,9},{5... | collective-permute-start | bytes 968 | tf_op jit(solution)/shard_map/ppermute | solution.py:57
  87.2 1.6 %collective-permute-done.11 = f32[5,4,4]{2,1,0:T(4,128)S(1)} collective-permute-done((f32[5,4,4]{2,1,0:T(4,128)S(1)}, f32[5,4,4]{2,1,0:T(4,128)S(1)}, u32[]{:S(2)}, u32[]{:S(2)}) %collective-permute-start.11) | collective-permute-done | bytes 352 | tf_op jit(solution)/shard_map/ppermute | solution.py:57
  88.8 3.0 %collective-permute-start.12 = (f32[5,4,4]{2,1,0:T(4,128)S(1)}, f32[5,4,4]{2,1,0:T(4,128)S(1)}, u32[]{:S(2)}, u32[]{:S(2)}) collective-permute-start(f32[5,4,4]{2,1,0:T(4,128)S(1)} %add.78), channel_id=1, source_target_pairs={{0,16},{4,20},{8,24},{12,28},{16,0},{20,4},{24,8},{28,12},{1,17},{... | collective-permute-start | bytes 968 | tf_op jit(solution)/shard_map/ppermute | solution.py:57
  91.9 1.6 %collective-permute-done.12 = f32[5,4,4]{2,1,0:T(4,128)S(1)} collective-permute-done((f32[5,4,4]{2,1,0:T(4,128)S(1)}, f32[5,4,4]{2,1,0:T(4,128)S(1)}, u32[]{:S(2)}, u32[]{:S(2)}) %collective-permute-start.12) | collective-permute-done | bytes 352 | tf_op jit(solution)/shard_map/ppermute | solution.py:57
  94.0 0.7 cholesky.16
  94.7 0.6 compare_reduce_fusion
  95.4 0.6 fusion.25
  96.0 0.6 custom-call.10
  97.0 0.4 fusion.16
  97.9 0.4 fusion.1
  98.4 0.7 sub.13
  99.5 0.8 copy.59
  (54 shorter events, 3.3 us)
Async XLA Ops:
  0.6 12.2 %copy-start = (s32[128,5]{0,1:T(8,128)S(1)}, s32[128,5]{0,1:T(8,128)}, u32[]{:S(2)}) copy-start(s32[128,5]{0,1:T(8,128)} %param.8) | copy-start | bytes 7684
  3.9 14.1 %collective-permute-start = (f32[1,32,256]{2,1,0:T(8,128)S(1)}, f32[1,32,256]{2,1,0:T(8,128)S(1)}, u32[]{:S(2)}, u32[]{:S(2)}) collective-permute-start(f32[1,32,256]{2,1,0:T(8,128)S(1)} %get-tuple-element.15), channel_id=1, source_target_pairs={{0,4},{4,8},{8,12},{12,16},{16,20},{20,24},{24,28},{1,5},{5,9},{9,... | collective-permute-start | bytes 98312 | tf_op jit(solution)/shard_map/ppermute | solution.py:27
  8.7 9.3 %collective-permute-start.1 = (f32[1,32,256]{2,1,0:T(8,128)S(1)}, f32[1,32,256]{2,1,0:T(8,128)S(1)}, u32[]{:S(2)}, u32[]{:S(2)}) collective-permute-start(f32[1,32,256]{2,1,0:T(8,128)S(1)} %get-tuple-element.14), channel_id=1, source_target_pairs={{4,0},{8,4},{12,8},{16,12},{20,16},{24,20},{28,24},{5,1},{9,5},{13... | collective-permute-start | bytes 98312 | tf_op jit(solution)/shard_map/ppermute | solution.py:29
  10.0 8.0 %collective-permute-start.2 = (f32[1,32,256]{2,1,0:T(8,128)S(1)}, f32[1,32,256]{2,1,0:T(8,128)S(1)}, u32[]{:S(2)}, u32[]{:S(2)}) collective-permute-start(f32[1,32,256]{2,1,0:T(8,128)S(1)} %get-tuple-element.13), channel_id=1, source_target_pairs={{0,1},{1,2},{2,3},{4,5},{5,6},{6,7},{8,9},{9,10},{10,11},{12,13},{... | collective-permute-start | bytes 98312 | tf_op jit(solution)/shard_map/ppermute | solution.py:27
  11.5 6.5 %collective-permute-start.3 = (f32[1,32,256]{2,1,0:T(8,128)S(1)}, f32[1,32,256]{2,1,0:T(8,128)S(1)}, u32[]{:S(2)}, u32[]{:S(2)}) collective-permute-start(f32[1,32,256]{2,1,0:T(8,128)S(1)} %get-tuple-element.12), channel_id=1, source_target_pairs={{1,0},{2,1},{3,2},{5,4},{6,5},{7,6},{9,8},{10,9},{11,10},{13,12},{... | collective-permute-start | bytes 98312 | tf_op jit(solution)/shard_map/ppermute | solution.py:29
  36.8 13.2 %collective-permute-start.4 = (f32[1,32,256]{2,1,0:T(8,128)S(1)}, f32[1,32,256]{2,1,0:T(8,128)S(1)}, u32[]{:S(2)}, u32[]{:S(2)}) collective-permute-start(f32[1,32,256]{2,1,0:T(8,128)S(1)} %get-tuple-element.11), channel_id=1, source_target_pairs={{0,4},{4,8},{8,12},{12,16},{16,20},{20,24},{24,28},{1,5},{5,9},{9,... | collective-permute-start | bytes 98312 | tf_op jit(solution)/shard_map/ppermute | solution.py:27
  41.2 8.8 %collective-permute-start.5 = (f32[1,32,256]{2,1,0:T(8,128)S(1)}, f32[1,32,256]{2,1,0:T(8,128)S(1)}, u32[]{:S(2)}, u32[]{:S(2)}) collective-permute-start(f32[1,32,256]{2,1,0:T(8,128)S(1)} %get-tuple-element.10), channel_id=1, source_target_pairs={{4,0},{8,4},{12,8},{16,12},{20,16},{24,20},{28,24},{5,1},{9,5},{13... | collective-permute-start | bytes 98312 | tf_op jit(solution)/shard_map/ppermute | solution.py:29
  42.5 7.5 %collective-permute-start.6 = (f32[1,32,256]{2,1,0:T(8,128)S(1)}, f32[1,32,256]{2,1,0:T(8,128)S(1)}, u32[]{:S(2)}, u32[]{:S(2)}) collective-permute-start(f32[1,32,256]{2,1,0:T(8,128)S(1)} %get-tuple-element.9), channel_id=1, source_target_pairs={{0,1},{1,2},{2,3},{4,5},{5,6},{6,7},{8,9},{9,10},{10,11},{12,13},{... | collective-permute-start | bytes 98312 | tf_op jit(solution)/shard_map/ppermute | solution.py:27
  47.0 4.6 %collective-permute-start.7 = (f32[1,32,256]{2,1,0:T(8,128)S(1)}, f32[1,32,256]{2,1,0:T(8,128)S(1)}, u32[]{:S(2)}, u32[]{:S(2)}) collective-permute-start(f32[1,32,256]{2,1,0:T(8,128)S(1)} %get-tuple-element.8), channel_id=1, source_target_pairs={{1,0},{2,1},{3,2},{5,4},{6,5},{7,6},{9,8},{10,9},{11,10},{13,12},{... | collective-permute-start | bytes 98312 | tf_op jit(solution)/shard_map/ppermute | solution.py:29
  71.8 3.5 %collective-permute-start.8 = (f32[5,4,4]{2,1,0:T(4,128)S(1)}, f32[5,4,4]{2,1,0:T(4,128)S(1)}, u32[]{:S(2)}, u32[]{:S(2)}) collective-permute-start(f32[5,4,4]{2,1,0:T(4,128)S(1)} %fusion.3), channel_id=1, source_target_pairs={{0,1},{1,0},{2,3},{3,2},{4,5},{5,4},{6,7},{7,6},{8,9},{9,8},{10,11... | collective-permute-start | bytes 968 | tf_op jit(solution)/shard_map/ppermute | solution.py:57
  75.3 3.7 %collective-permute-start.9 = (f32[5,4,4]{2,1,0:T(4,128)S(1)}, f32[5,4,4]{2,1,0:T(4,128)S(1)}, u32[]{:S(2)}, u32[]{:S(2)}) collective-permute-start(f32[5,4,4]{2,1,0:T(4,128)S(1)} %add.75), channel_id=1, source_target_pairs={{0,2},{1,3},{2,0},{3,1},{4,6},{5,7},{6,4},{7,5},{8,10},{9,11},{10,... | collective-permute-start | bytes 968 | tf_op jit(solution)/shard_map/ppermute | solution.py:57
  78.9 4.7 %collective-permute-start.10 = (f32[5,4,4]{2,1,0:T(4,128)S(1)}, f32[5,4,4]{2,1,0:T(4,128)S(1)}, u32[]{:S(2)}, u32[]{:S(2)}) collective-permute-start(f32[5,4,4]{2,1,0:T(4,128)S(1)} %add.76), channel_id=1, source_target_pairs={{0,4},{4,0},{8,12},{12,8},{16,20},{20,16},{24,28},{28,24},{1,5},{5... | collective-permute-start | bytes 968 | tf_op jit(solution)/shard_map/ppermute | solution.py:57
  83.7 5.1 %collective-permute-start.11 = (f32[5,4,4]{2,1,0:T(4,128)S(1)}, f32[5,4,4]{2,1,0:T(4,128)S(1)}, u32[]{:S(2)}, u32[]{:S(2)}) collective-permute-start(f32[5,4,4]{2,1,0:T(4,128)S(1)} %add.77), channel_id=1, source_target_pairs={{0,8},{4,12},{8,0},{12,4},{16,24},{20,28},{24,16},{28,20},{1,9},{5... | collective-permute-start | bytes 968 | tf_op jit(solution)/shard_map/ppermute | solution.py:57
  88.8 4.7 %collective-permute-start.12 = (f32[5,4,4]{2,1,0:T(4,128)S(1)}, f32[5,4,4]{2,1,0:T(4,128)S(1)}, u32[]{:S(2)}, u32[]{:S(2)}) collective-permute-start(f32[5,4,4]{2,1,0:T(4,128)S(1)} %add.78), channel_id=1, source_target_pairs={{0,16},{4,20},{8,24},{12,28},{16,0},{20,4},{24,8},{28,12},{1,17},{... | collective-permute-start | bytes 968 | tf_op jit(solution)/shard_map/ppermute | solution.py:57

commit v2 on v1

--- a/solution.py
+++ b/solution.py
@@ -59,19 +59,26 @@
     return values
 
 
-def coupling_kernel(jac_ref, picked_ref, seg_ref, out_ref, parts_ref):
+def coupling_kernel(jac_ref, picked_ref, out_ref, parts_ref, doubled_ref):
     step = pl.program_id(0)
     rows = jac_ref.shape[1]
     tiles = jac_ref.shape[2] // LANES
     row0 = pl.multiple_of(step * rows, rows)
+    lane = lax.broadcasted_iota(jnp.int32, (rows, LANES), 1)
+    for k in range(NB):
+        for pair in range(VECS // 2):
+            tile = picked_ref[k, :, pair * LANES:(pair + 1) * LANES]
+            swapped = pltpu.roll(tile, BLK, 1)
+            doubled_ref[k, :, (2 * pair) * LANES:(2 * pair + 1) * LANES] = jnp.where(lane < BLK, tile, swapped)
+            doubled_ref[k, :, (2 * pair + 1) * LANES:(2 * pair + 2) * LANES] = jnp.where(lane >= BLK, tile, swapped)
 
     def one_tile(t, carry):
         off = pl.multiple_of(t * LANES, LANES)
         blocks = [jac_ref[k, :, pl.ds(off, LANES)] for k in range(NB)]
         for c in range(VECS):
-            total = blocks[0] * picked_ref[0, :, c * LANES:(c + 1) * LANES]
+            total = blocks[0] * doubled_ref[0, :, c * LANES:(c + 1) * LANES]
             for k in range(1, NB):
-                total = total + blocks[k] * picked_ref[k, :, c * LANES:(c + 1) * LANES]
+                total = total + blocks[k] * doubled_ref[k, :, c * LANES:(c + 1) * LANES]
             high = total.astype(jnp.bfloat16)
             low = (total - high.astype(jnp.float32)).astype(jnp.bfloat16)
             parts_ref[2 * c, pl.ds(row0, rows), pl.ds(off, LANES)] = high
@@ -84,14 +91,19 @@
     def _():
         count = parts_ref.shape[1]
         flat = parts_ref[...].reshape(2 * VECS * count, tiles * LANES)
-        sums = jnp.dot(flat, seg_ref[...], preferred_element_type=jnp.float32)
+        width = tiles * LANES
+        seg = (
+            lax.broadcasted_iota(jnp.int32, (width, BLK), 0) // BLK
+            == lax.broadcasted_iota(jnp.int32, (width, BLK), 1)
+        ).astype(jnp.bfloat16)
+        sums = jnp.dot(flat, seg, preferred_element_type=jnp.float32)
         for c in range(VECS):
             high = sums[(2 * c) * count:(2 * c + 1) * count]
             low = sums[(2 * c + 1) * count:(2 * c + 2) * count]
             out_ref[:, c * BLK:(c + 1) * BLK] = high + low
 
 
-def coupled_sum(jac_t, picked, seg):
+def coupled_sum(jac_t, picked):
     blocks, count, width = jac_t.shape
     rows = min(ROWS_PER_STEP, count)
     return pl.pallas_call(
@@ -100,18 +112,20 @@
         grid=(count // rows,),
         in_specs=[
             pl.BlockSpec((blocks, rows, width), lambda b: (0, b, 0)),
-            pl.BlockSpec((blocks, rows, VECS * LANES), lambda b: (0, b, 0)),
-            pl.BlockSpec((width, BLK), lambda b: (0, 0)),
+            pl.BlockSpec((blocks, rows, VECS * BLK), lambda b: (0, b, 0)),
         ],
         out_specs=pl.BlockSpec((count, VECS * BLK), lambda b: (0, 0)),
-        scratch_shapes=[pltpu.VMEM((2 * VECS, count, width), jnp.bfloat16)],
+        scratch_shapes=[
+            pltpu.VMEM((2 * VECS, count, width), jnp.bfloat16),
+            pltpu.VMEM((blocks, rows, VECS * LANES), jnp.float32),
+        ],
         compiler_params=pltpu.CompilerParams(dimension_semantics=("arbitrary",)),
         cost_estimate=pl.CostEstimate(
             flops=2 * blocks * count * width * VECS + 2 * 2 * VECS * count * width * BLK,
-            bytes_accessed=4 * (blocks * count * width + blocks * count * VECS * LANES + count * VECS * BLK),
+            bytes_accessed=4 * (blocks * count * width + blocks * count * VECS * BLK + count * VECS * BLK),
             transcendentals=0,
         ),
-    )(jac_t, picked, seg)
+    )(jac_t, picked)
 
 
 def per_device(start_block, jacobian, counts, columns, send_list):
@@ -119,9 +133,7 @@
     anchor = jnp.where(living, start_block, jnp.float32(0.0))
     lend_rows = send_list[0]
     jac_t = jnp.transpose(jacobian, (1, 0, 2))
-    lane = lax.broadcasted_iota(jnp.int32, (BLK * BLK, BLK), 0)
-    col = lax.broadcasted_iota(jnp.int32, (BLK * BLK, BLK), 1)
-    seg = (lane // BLK == col).astype(jnp.bfloat16)
+    gather_rows = jnp.transpose(columns, (1, 0))
 
     def ghosts(values):
         outgoing = values[lend_rows]
@@ -132,10 +144,8 @@
     def operate(values):
         ghost_rows = ghosts(values)
         source = jnp.concatenate([values, ghost_rows], 0)
-        picked = source[columns].reshape(E_DEV, NB, VECS, 1, BLK)
-        picked = jnp.broadcast_to(picked, (E_DEV, NB, VECS, 2, BLK)).reshape(E_DEV, NB, VECS * LANES)
-        picked = jnp.transpose(picked, (1, 0, 2))
-        summed = coupled_sum(jac_t, picked, seg)
+        picked = source[gather_rows]
+        summed = coupled_sum(jac_t, picked)
         return jnp.where(living, DIAG_SHIFT * values + summed, jnp.float32(0.0))
 
     first_image = operate(anchor)

time: 101 us -> 92.8 us (0.919)
  local copies, waits for them, and re-layouts: 14.3 us -> 8.88 us
  other arithmetic: 11.8 us -> 7.8 us
  waiting for transfers between devices: 10.7 us -> 12.1 us
    convert_element_type x1 -> x0, other arithmetic: 4.7 us -> none  [per_device(): seg = (lane // BLK == col).astype(jnp.bfloat16)]
    broadcast_in_dim x7 -> x0, local copies, waits for them, and re-layouts: 3.68 us -> none  [the longest x6 3.48 us: operate(): jnp.broadcast_to(picked, (E_DEV, NB, VECS, 2, BLK))]
    reshape x2 -> x0, local copies, waits for them, and re-layouts: 2.97 us -> none  [operate(): jnp.broadcast_to(picked, (E_DEV, NB, VECS, 2, BLK))]
    gather x2, local copies, waits for them, and re-layouts: 4.41 us -> 5.73 us  [operate(): picked = source[gather_rows]]
    ppermute x4, waiting for transfers between devices: 1.61 us -> 2.82 us  [padded(): lax.ppermute(head, axis, [((i + 1) % count, i) for i in range(ends)])]
  transfers between devices with their start and end apart: 13 -> 13, of which waited for: 6 -> 8; matrix products, arithmetic and copies ran while one was open for 7% -> 2% of each run, Pallas kernels for 0% -> 0%
where the time goes in v2:
time: 92.8 us; the launch traced here: 92.3 us
  starting transfers between devices  32.5 us (35%)
  Pallas kernels  23.7 us (26%)
  waiting for transfers between devices  12.1 us (13%)
  local copies, waits for them, and re-layouts  8.88 us (10%)
  other arithmetic  7.8 us (8%)
  matrix products  5.76 us (6%)
  between operations  1.57 us (2%)
    pallas_call x2, Pallas kernels, coupled_sum(): pl.pallas_call(coupling_kernel, out_shape=jax.ShapeDtypeStruct((count, VE...  23.7 us
    ppermute x4, starting transfers between devices, padded(): lax.ppermute(tail, axis, [(i, (i + 1) % count) for i in range(ends)])  15.1 us
    ppermute x5, starting transfers between devices, tree_sum(): lax.ppermute(values, axis, [(i, i ^ stride) for i in range(count)])  12.2 us
    ppermute x5, waiting for transfers between devices, tree_sum(): lax.ppermute(values, axis, [(i, i ^ stride) for i in range(count)])  9.22 us
    gather x2, local copies, waits for them, and re-layouts, operate(): picked = source[gather_rows]  5.73 us
    ppermute x4, starting transfers between devices, padded(): lax.ppermute(head, axis, [((i + 1) % count, i) for i in range(ends)])  5.17 us
    dot_general x5, matrix products, inner_block(): jnp.einsum('eci,edi->cd', left_shaped, right_shaped, precision=lax.Precis...  3.71 us
    ppermute x4, waiting for transfers between devices, padded(): lax.ppermute(head, axis, [((i + 1) % count, i) for i in range(ends)])  2.82 us
  transfers between devices with their start and end apart: 13, of which 8 were waited for; matrix products, arithmetic and copies ran while one was open for 2% of the time, Pallas kernels for 0%

profile of v2, /device:TPU:0, one launch (start us, length us, event | category | flops | bytes accessed | tf_op | source)
XLA Modules:
  0.0 92.3 jit_solution(10136679470287853353)
XLA Ops:
  1.3 0.7 compare_select_fusion.1
  2.1 1.0 %constant_dynamic-update-slice_fusion = (f32[256,256]{1,0:T(8,128)S(1)}, f32[128,256]{1,0:T(8,128)S(1)}) fusion(f32[128,256]{1,0:T(8,128)} %param.5, pred[128]{0:T(512)(128)(4,1)S(1)} %iota_compare_fusion.2), kind=kLoop, calls=%fused_computation.51 | loop fusion | flops 32767 | bytes 393344
  3.1 0.8 gather_fusion
  3.8 4.8 %collective-permute-start = (f32[1,32,256]{2,1,0:T(8,128)S(1)}, f32[1,32,256]{2,1,0:T(8,128)S(1)}, u32[]{:S(2)}, u32[]{:S(2)}) collective-permute-start(f32[1,32,256]{2,1,0:T(8,128)S(1)} %get-tuple-element.15), channel_id=1, source_target_pairs={{0,4},{4,8},{8,12},{12,16},{16,20},{20,24},{24,28},{1,5},{5,9},{9,... | collective-permute-start | bytes 98312 | tf_op jit(solution)/shard_map/ppermute | solution.py:27
  8.7 1.3 %collective-permute-start.1 = (f32[1,32,256]{2,1,0:T(8,128)S(1)}, f32[1,32,256]{2,1,0:T(8,128)S(1)}, u32[]{:S(2)}, u32[]{:S(2)}) collective-permute-start(f32[1,32,256]{2,1,0:T(8,128)S(1)} %get-tuple-element.14), channel_id=1, source_target_pairs={{4,0},{8,4},{12,8},{16,12},{20,16},{24,20},{28,24},{5,1},{9,5},{13... | collective-permute-start | bytes 98312 | tf_op jit(solution)/shard_map/ppermute | solution.py:29
  10.0 1.5 %collective-permute-start.2 = (f32[1,32,256]{2,1,0:T(8,128)S(1)}, f32[1,32,256]{2,1,0:T(8,128)S(1)}, u32[]{:S(2)}, u32[]{:S(2)}) collective-permute-start(f32[1,32,256]{2,1,0:T(8,128)S(1)} %get-tuple-element.13), channel_id=1, source_target_pairs={{0,1},{1,2},{2,3},{4,5},{5,6},{6,7},{8,9},{9,10},{10,11},{12,13},{... | collective-permute-start | bytes 98312 | tf_op jit(solution)/shard_map/ppermute | solution.py:27
  11.5 1.3 %collective-permute-start.3 = (f32[1,32,256]{2,1,0:T(8,128)S(1)}, f32[1,32,256]{2,1,0:T(8,128)S(1)}, u32[]{:S(2)}, u32[]{:S(2)}) collective-permute-start(f32[1,32,256]{2,1,0:T(8,128)S(1)} %get-tuple-element.12), channel_id=1, source_target_pairs={{1,0},{2,1},{3,2},{5,4},{6,5},{7,6},{9,8},{10,9},{11,10},{13,12},{... | collective-permute-start | bytes 98312 | tf_op jit(solution)/shard_map/ppermute | solution.py:29
  12.8 0.7 fusion.22
  13.6 0.9 collective-permute-done.1
  14.5 1.6 %collective-permute-done.3 = f32[1,32,256]{2,1,0:T(8,128)S(1)} collective-permute-done((f32[1,32,256]{2,1,0:T(8,128)S(1)}, f32[1,32,256]{2,1,0:T(8,128)S(1)}, u32[]{:S(2)}, u32[]{:S(2)}) %collective-permute-start.3) | collective-permute-done | bytes 32800 | tf_op jit(solution)/shard_map/ppermute | solution.py:29
  16.2 2.9 %gather_fusion.1 = f32[640,256]{1,0:T(8,128)} fusion(f32[256,256]{1,0:T(8,128)S(1)} %bitcast_dynamic-update-slice_fusion.4, s32[1024]{0:T(1024)S(1)} %pad_clamp_fusion), kind=kCustom, calls=%fused_computation.1 | custom fusion | bytes 1313280 | tf_op jit(solution)/shard_map/gather | solution.py:147
  19.0 11.8 %shard_map.68 = f32[128,256]{1,0:T(8,128)} custom-call(f32[5,128,4096]{2,1,0:T(8,128)} %bitcast.116, f32[5,128,256]{2,1,0:T(8,128)} %bitcast.128), custom_call_target="tpu_custom_call" | custom-call | flops 557842432 | bytes 11272192 | tf_op jit(solution)/shard_map/pallas_call | solution.py:109
  30.9 1.0 %constant_dynamic-update-slice_fusion.1 = (f32[256,256]{1,0:T(8,128)S(1)}, f32[128,256]{1,0:T(8,128)S(1)}) fusion(f32[128,256]{1,0:T(8,128)} %shard_map.68, f32[128,256]{1,0:T(8,128)S(1)} %get-tuple-element.7, pred[128]{0:T(512)(128)(4,1)S(1)} %iota_compare_fusion.2), kind=kLoop, calls=%fused_computation.52 | loop fusion | flops 98303 | bytes 524416
  31.9 0.8 gather_fusion.2
  32.7 4.5 %collective-permute-start.4 = (f32[1,32,256]{2,1,0:T(8,128)S(1)}, f32[1,32,256]{2,1,0:T(8,128)S(1)}, u32[]{:S(2)}, u32[]{:S(2)}) collective-permute-start(f32[1,32,256]{2,1,0:T(8,128)S(1)} %get-tuple-element.11), channel_id=1, source_target_pairs={{0,4},{4,8},{8,12},{12,16},{16,20},{20,24},{24,28},{1,5},{5,9},{9,... | collective-permute-start | bytes 98312 | tf_op jit(solution)/shard_map/ppermute | solution.py:27
  37.3 1.3 %collective-permute-start.5 = (f32[1,32,256]{2,1,0:T(8,128)S(1)}, f32[1,32,256]{2,1,0:T(8,128)S(1)}, u32[]{:S(2)}, u32[]{:S(2)}) collective-permute-start(f32[1,32,256]{2,1,0:T(8,128)S(1)} %get-tuple-element.10), channel_id=1, source_target_pairs={{4,0},{8,4},{12,8},{16,12},{20,16},{24,20},{28,24},{5,1},{9,5},{13... | collective-permute-start | bytes 98312 | tf_op jit(solution)/shard_map/ppermute | solution.py:29
  38.6 4.3 %collective-permute-start.6 = (f32[1,32,256]{2,1,0:T(8,128)S(1)}, f32[1,32,256]{2,1,0:T(8,128)S(1)}, u32[]{:S(2)}, u32[]{:S(2)}) collective-permute-start(f32[1,32,256]{2,1,0:T(8,128)S(1)} %get-tuple-element.9), channel_id=1, source_target_pairs={{0,1},{1,2},{2,3},{4,5},{5,6},{6,7},{8,9},{9,10},{10,11},{12,13},{... | collective-permute-start | bytes 98312 | tf_op jit(solution)/shard_map/ppermute | solution.py:27
  42.9 1.3 %collective-permute-start.7 = (f32[1,32,256]{2,1,0:T(8,128)S(1)}, f32[1,32,256]{2,1,0:T(8,128)S(1)}, u32[]{:S(2)}, u32[]{:S(2)}) collective-permute-start(f32[1,32,256]{2,1,0:T(8,128)S(1)} %get-tuple-element.8), channel_id=1, source_target_pairs={{1,0},{2,1},{3,2},{5,4},{6,5},{7,6},{9,8},{10,9},{11,10},{13,12},{... | collective-permute-start | bytes 98312 | tf_op jit(solution)/shard_map/ppermute | solution.py:29
  44.2 0.8 fusion.6
  44.9 0.7 fusion.5
  45.7 0.3 collective-permute-done.7
  46.0 2.9 %gather_fusion.3 = f32[640,256]{1,0:T(8,128)} fusion(f32[256,256]{1,0:T(8,128)S(1)} %bitcast_dynamic-update-slice_fusion, s32[1024]{0:T(1024)S(1)} %pad_clamp_fusion), kind=kCustom, calls=%fused_computation.3 | custom fusion | bytes 1313280 | tf_op jit(solution)/shard_map/gather | solution.py:147
  48.8 11.8 %shard_map.69 = f32[128,256]{1,0:T(8,128)} custom-call(f32[5,128,4096]{2,1,0:T(8,128)} %bitcast.117, f32[5,128,256]{2,1,0:T(8,128)} %bitcast.127), custom_call_target="tpu_custom_call" | custom-call | flops 557842432 | bytes 11272192 | tf_op jit(solution)/shard_map/pallas_call | solution.py:109
  60.7 1.0 %add_select_fusion = f32[128,256]{1,0:T(8,128)S(1)} fusion(f32[128,256]{1,0:T(8,128)} %shard_map.69, f32[128,256]{1,0:T(8,128)S(1)} %get-tuple-element.5, pred[128]{0:T(512)(128)(4,1)S(1)} %iota_compare_fusion.2), kind=kLoop, calls=%fused_computation.18 | loop fusion | flops 98304 | bytes 393344 | tf_op jit(solution)/shard_map/jit(_where)/select_n | solution.py:149
  61.8 0.8 fusion.4
  62.5 0.8 fusion.3
  63.3 0.7 fusion.2
  64.0 2.4 %collective-permute-start.8 = (f32[5,4,4]{2,1,0:T(4,128)S(1)}, f32[5,4,4]{2,1,0:T(4,128)S(1)}, u32[]{:S(2)}, u32[]{:S(2)}) collective-permute-start(f32[5,4,4]{2,1,0:T(4,128)S(1)} %fusion.2), channel_id=1, source_target_pairs={{0,1},{1,0},{2,3},{3,2},{4,5},{5,4},{6,7},{7,6},{8,9},{9,8},{10,11... | collective-permute-start | bytes 968 | tf_op jit(solution)/shard_map/ppermute | solution.py:57
  66.4 0.8 collective-permute-done.8
  67.3 0.2 collective-permute-start.9
  67.5 3.4 %collective-permute-done.9 = f32[5,4,4]{2,1,0:T(4,128)S(1)} collective-permute-done((f32[5,4,4]{2,1,0:T(4,128)S(1)}, f32[5,4,4]{2,1,0:T(4,128)S(1)}, u32[]{:S(2)}, u32[]{:S(2)}) %collective-permute-start.9) | collective-permute-done | bytes 352 | tf_op jit(solution)/shard_map/ppermute | solution.py:57
  71.0 3.1 %collective-permute-start.10 = (f32[5,4,4]{2,1,0:T(4,128)S(1)}, f32[5,4,4]{2,1,0:T(4,128)S(1)}, u32[]{:S(2)}, u32[]{:S(2)}) collective-permute-start(f32[5,4,4]{2,1,0:T(4,128)S(1)} %add.74), channel_id=1, source_target_pairs={{0,4},{4,0},{8,12},{12,8},{16,20},{20,16},{24,28},{28,24},{1,5},{5... | collective-permute-start | bytes 968 | tf_op jit(solution)/shard_map/ppermute | solution.py:57
  74.0 1.6 %collective-permute-done.10 = f32[5,4,4]{2,1,0:T(4,128)S(1)} collective-permute-done((f32[5,4,4]{2,1,0:T(4,128)S(1)}, f32[5,4,4]{2,1,0:T(4,128)S(1)}, u32[]{:S(2)}, u32[]{:S(2)}) %collective-permute-start.10) | collective-permute-done | bytes 352 | tf_op jit(solution)/shard_map/ppermute | solution.py:57
  75.7 3.5 %collective-permute-start.11 = (f32[5,4,4]{2,1,0:T(4,128)S(1)}, f32[5,4,4]{2,1,0:T(4,128)S(1)}, u32[]{:S(2)}, u32[]{:S(2)}) collective-permute-start(f32[5,4,4]{2,1,0:T(4,128)S(1)} %add.75), channel_id=1, source_target_pairs={{0,8},{4,12},{8,0},{12,4},{16,24},{20,28},{24,16},{28,20},{1,9},{5... | collective-permute-start | bytes 968 | tf_op jit(solution)/shard_map/ppermute | solution.py:57
  79.2 1.6 %collective-permute-done.11 = f32[5,4,4]{2,1,0:T(4,128)S(1)} collective-permute-done((f32[5,4,4]{2,1,0:T(4,128)S(1)}, f32[5,4,4]{2,1,0:T(4,128)S(1)}, u32[]{:S(2)}, u32[]{:S(2)}) %collective-permute-start.11) | collective-permute-done | bytes 352 | tf_op jit(solution)/shard_map/ppermute | solution.py:57
  80.8 3.0 %collective-permute-start.12 = (f32[5,4,4]{2,1,0:T(4,128)S(1)}, f32[5,4,4]{2,1,0:T(4,128)S(1)}, u32[]{:S(2)}, u32[]{:S(2)}) collective-permute-start(f32[5,4,4]{2,1,0:T(4,128)S(1)} %add.76), channel_id=1, source_target_pairs={{0,16},{4,20},{8,24},{12,28},{16,0},{20,4},{24,8},{28,12},{1,17},{... | collective-permute-start | bytes 968 | tf_op jit(solution)/shard_map/ppermute | solution.py:57
  83.9 1.6 %collective-permute-done.12 = f32[5,4,4]{2,1,0:T(4,128)S(1)} collective-permute-done((f32[5,4,4]{2,1,0:T(4,128)S(1)}, f32[5,4,4]{2,1,0:T(4,128)S(1)}, u32[]{:S(2)}, u32[]{:S(2)}) %collective-permute-start.12) | collective-permute-done | bytes 352 | tf_op jit(solution)/shard_map/ppermute | solution.py:57
  86.0 0.7 cholesky.16
  86.7 0.6 compare_reduce_fusion
  87.4 0.6 fusion.21
  88.0 0.6 custom-call.10
  88.8 0.2 fusion.28
  89.0 0.4 fusion.15
  89.5 0.4 fusion.7
  89.9 0.4 fusion
  90.4 0.7 sub.3
  91.1 0.4 fusion.1
  91.5 0.8 copy.52
  (39 shorter events, 1.3 us)
Async XLA Ops:
  3.8 9.7 %collective-permute-start = (f32[1,32,256]{2,1,0:T(8,128)S(1)}, f32[1,32,256]{2,1,0:T(8,128)S(1)}, u32[]{:S(2)}, u32[]{:S(2)}) collective-permute-start(f32[1,32,256]{2,1,0:T(8,128)S(1)} %get-tuple-element.15), channel_id=1, source_target_pairs={{0,4},{4,8},{8,12},{12,16},{16,20},{20,24},{24,28},{1,5},{5,9},{9,... | collective-permute-start | bytes 98312 | tf_op jit(solution)/shard_map/ppermute | solution.py:27
  8.7 5.8 %collective-permute-start.1 = (f32[1,32,256]{2,1,0:T(8,128)S(1)}, f32[1,32,256]{2,1,0:T(8,128)S(1)}, u32[]{:S(2)}, u32[]{:S(2)}) collective-permute-start(f32[1,32,256]{2,1,0:T(8,128)S(1)} %get-tuple-element.14), channel_id=1, source_target_pairs={{4,0},{8,4},{12,8},{16,12},{20,16},{24,20},{28,24},{5,1},{9,5},{13... | collective-permute-start | bytes 98312 | tf_op jit(solution)/shard_map/ppermute | solution.py:29
  10.0 4.5 %collective-permute-start.2 = (f32[1,32,256]{2,1,0:T(8,128)S(1)}, f32[1,32,256]{2,1,0:T(8,128)S(1)}, u32[]{:S(2)}, u32[]{:S(2)}) collective-permute-start(f32[1,32,256]{2,1,0:T(8,128)S(1)} %get-tuple-element.13), channel_id=1, source_target_pairs={{0,1},{1,2},{2,3},{4,5},{5,6},{6,7},{8,9},{9,10},{10,11},{12,13},{... | collective-permute-start | bytes 98312 | tf_op jit(solution)/shard_map/ppermute | solution.py:27
  11.5 4.7 %collective-permute-start.3 = (f32[1,32,256]{2,1,0:T(8,128)S(1)}, f32[1,32,256]{2,1,0:T(8,128)S(1)}, u32[]{:S(2)}, u32[]{:S(2)}) collective-permute-start(f32[1,32,256]{2,1,0:T(8,128)S(1)} %get-tuple-element.12), channel_id=1, source_target_pairs={{1,0},{2,1},{3,2},{5,4},{6,5},{7,6},{9,8},{10,9},{11,10},{13,12},{... | collective-permute-start | bytes 98312 | tf_op jit(solution)/shard_map/ppermute | solution.py:29
  32.7 12.9 %collective-permute-start.4 = (f32[1,32,256]{2,1,0:T(8,128)S(1)}, f32[1,32,256]{2,1,0:T(8,128)S(1)}, u32[]{:S(2)}, u32[]{:S(2)}) collective-permute-start(f32[1,32,256]{2,1,0:T(8,128)S(1)} %get-tuple-element.11), channel_id=1, source_target_pairs={{0,4},{4,8},{8,12},{12,16},{16,20},{20,24},{24,28},{1,5},{5,9},{9,... | collective-permute-start | bytes 98312 | tf_op jit(solution)/shard_map/ppermute | solution.py:27
  37.3 8.4 %collective-permute-start.5 = (f32[1,32,256]{2,1,0:T(8,128)S(1)}, f32[1,32,256]{2,1,0:T(8,128)S(1)}, u32[]{:S(2)}, u32[]{:S(2)}) collective-permute-start(f32[1,32,256]{2,1,0:T(8,128)S(1)} %get-tuple-element.10), channel_id=1, source_target_pairs={{4,0},{8,4},{12,8},{16,12},{20,16},{24,20},{28,24},{5,1},{9,5},{13... | collective-permute-start | bytes 98312 | tf_op jit(solution)/shard_map/ppermute | solution.py:29
  38.6 7.1 %collective-permute-start.6 = (f32[1,32,256]{2,1,0:T(8,128)S(1)}, f32[1,32,256]{2,1,0:T(8,128)S(1)}, u32[]{:S(2)}, u32[]{:S(2)}) collective-permute-start(f32[1,32,256]{2,1,0:T(8,128)S(1)} %get-tuple-element.9), channel_id=1, source_target_pairs={{0,1},{1,2},{2,3},{4,5},{5,6},{6,7},{8,9},{9,10},{10,11},{12,13},{... | collective-permute-start | bytes 98312 | tf_op jit(solution)/shard_map/ppermute | solution.py:27
  42.9 3.1 %collective-permute-start.7 = (f32[1,32,256]{2,1,0:T(8,128)S(1)}, f32[1,32,256]{2,1,0:T(8,128)S(1)}, u32[]{:S(2)}, u32[]{:S(2)}) collective-permute-start(f32[1,32,256]{2,1,0:T(8,128)S(1)} %get-tuple-element.8), channel_id=1, source_target_pairs={{1,0},{2,1},{3,2},{5,4},{6,5},{7,6},{9,8},{10,9},{11,10},{13,12},{... | collective-permute-start | bytes 98312 | tf_op jit(solution)/shard_map/ppermute | solution.py:29
  64.0 3.3 %collective-permute-start.8 = (f32[5,4,4]{2,1,0:T(4,128)S(1)}, f32[5,4,4]{2,1,0:T(4,128)S(1)}, u32[]{:S(2)}, u32[]{:S(2)}) collective-permute-start(f32[5,4,4]{2,1,0:T(4,128)S(1)} %fusion.2), channel_id=1, source_target_pairs={{0,1},{1,0},{2,3},{3,2},{4,5},{5,4},{6,7},{7,6},{8,9},{9,8},{10,11... | collective-permute-start | bytes 968 | tf_op jit(solution)/shard_map/ppermute | solution.py:57
  67.3 3.7 %collective-permute-start.9 = (f32[5,4,4]{2,1,0:T(4,128)S(1)}, f32[5,4,4]{2,1,0:T(4,128)S(1)}, u32[]{:S(2)}, u32[]{:S(2)}) collective-permute-start(f32[5,4,4]{2,1,0:T(4,128)S(1)} %add.73), channel_id=1, source_target_pairs={{0,2},{1,3},{2,0},{3,1},{4,6},{5,7},{6,4},{7,5},{8,10},{9,11},{10,... | collective-permute-start | bytes 968 | tf_op jit(solution)/shard_map/ppermute | solution.py:57
  71.0 4.7 %collective-permute-start.10 = (f32[5,4,4]{2,1,0:T(4,128)S(1)}, f32[5,4,4]{2,1,0:T(4,128)S(1)}, u32[]{:S(2)}, u32[]{:S(2)}) collective-permute-start(f32[5,4,4]{2,1,0:T(4,128)S(1)} %add.74), channel_id=1, source_target_pairs={{0,4},{4,0},{8,12},{12,8},{16,20},{20,16},{24,28},{28,24},{1,5},{5... | collective-permute-start | bytes 968 | tf_op jit(solution)/shard_map/ppermute | solution.py:57
  75.7 5.1 %collective-permute-start.11 = (f32[5,4,4]{2,1,0:T(4,128)S(1)}, f32[5,4,4]{2,1,0:T(4,128)S(1)}, u32[]{:S(2)}, u32[]{:S(2)}) collective-permute-start(f32[5,4,4]{2,1,0:T(4,128)S(1)} %add.75), channel_id=1, source_target_pairs={{0,8},{4,12},{8,0},{12,4},{16,24},{20,28},{24,16},{28,20},{1,9},{5... | collective-permute-start | bytes 968 | tf_op jit(solution)/shard_map/ppermute | solution.py:57
  80.8 4.7 %collective-permute-start.12 = (f32[5,4,4]{2,1,0:T(4,128)S(1)}, f32[5,4,4]{2,1,0:T(4,128)S(1)}, u32[]{:S(2)}, u32[]{:S(2)}) collective-permute-start(f32[5,4,4]{2,1,0:T(4,128)S(1)} %add.76), channel_id=1, source_target_pairs={{0,16},{4,20},{8,24},{12,28},{16,0},{20,4},{24,8},{28,12},{1,17},{... | collective-permute-start | bytes 968 | tf_op jit(solution)/shard_map/ppermute | solution.py:57

commit v3 on v2

v3 whole, which is shorter than its diff:
```python
import jax
import jax.numpy as jnp
from jax import lax
from jax.experimental import pallas as pl
from jax.experimental.pallas import tpu as pltpu
from jax.sharding import PartitionSpec as P

BLK = 64
VECS = 4
NB = 5
E_DEV = 128
LANES = 128
SUBLANES = 8
ROWS_PER_STEP = 32


DIAG_SHIFT = 1.5


def padded(cells, sides, width):
    for axis, dim in sides:
        count = lax.axis_size(axis)
        ends = count - 1
        head = lax.slice_in_dim(cells, 0, width, axis=dim)
        tail = lax.slice_in_dim(cells, cells.shape[dim] - width, cells.shape[dim], axis=dim)
        cells = jnp.concatenate(
            [
                lax.ppermute(tail, axis, [(i, (i + 1) % count) for i in range(ends)]),
                cells,
                lax.ppermute(head, axis, [((i + 1) % count, i) for i in range(ends)]),
            ],
            axis=dim,
        )
    return cells


def combine(values, mixing):
    shaped = values.reshape(values.shape[0], VECS, BLK)
    return jnp.einsum("eci,cd->edi", shaped, mixing, precision=lax.Precision.HIGHEST).reshape(
        values.shape[0], VECS * BLK
    )


def inner_block(left_side, right_side):
    left_shaped = left_side.reshape(left_side.shape[0], VECS, BLK)
    right_shaped = right_side.reshape(right_side.shape[0], VECS, BLK)
    return jnp.einsum("eci,edi->cd", left_shaped, right_shaped, precision=lax.Precision.HIGHEST)


def tree_sum(values, axes):
    for axis in axes:
        count = lax.axis_size(axis)
        if count & (count - 1):
            values = lax.psum(values, axis)
            continue
        stride = 1
        while stride < count:
            values = values + lax.ppermute(values, axis, [(i, i ^ stride) for i in range(count)])
            stride *= 2
    return values


def split_three(values):
    high = values.astype(jnp.bfloat16)
    rest = values - high.astype(jnp.float32)
    middle = rest.astype(jnp.bfloat16)
    low = (rest - middle.astype(jnp.float32)).astype(jnp.bfloat16)
    return jnp.concatenate([high, middle, low], axis=1)


def exchange_sum(values, axes):
    count = 1
    for axis in axes:
        count *= lax.axis_size(axis)
    flat = values.reshape(1, -1)
    everyone = lax.all_to_all(jnp.broadcast_to(flat, (count, flat.shape[1])), axes, 0, 0, tiled=True)
    return jnp.sum(everyone, axis=0).reshape(values.shape)


def coupling_kernel(jac_ref, own_ref, ghost_ref, cols_ref, mask_ref, out_ref, source_ref, picked_ref, z_ref, parts_ref):
    step = pl.program_id(0)
    rows = jac_ref.shape[1]
    tiles = jac_ref.shape[2] // LANES
    count = own_ref.shape[0]
    width = own_ref.shape[1]
    row0 = pl.multiple_of(step * rows, rows)

    @pl.when(step == 0)
    def _():
        source_ref[0:count] = split_three(own_ref[...])
        source_ref[count:2 * count] = split_three(ghost_ref[...])

    slots = lax.broadcasted_iota(jnp.int32, (rows, 2 * count), 1)
    for k in range(NB):
        chosen = (cols_ref[k] == slots).astype(jnp.bfloat16)
        spread = jnp.dot(chosen, source_ref[...], preferred_element_type=jnp.float32)
        picked_ref[k] = spread[:, 0:width] + spread[:, width:2 * width] + spread[:, 2 * width:3 * width]

    lane = lax.broadcasted_iota(jnp.int32, (SUBLANES, LANES), 1)
    for group in range(rows // SUBLANES):
        top = group * SUBLANES
        doubled = []
        for k in range(NB):
            per_vector = []
            for pair in range(VECS // 2):
                tile = picked_ref[k, top:top + SUBLANES, pair * LANES:(pair + 1) * LANES]
                swapped = pltpu.roll(tile, BLK, 1)
                per_vector.append(jnp.where(lane < BLK, tile, swapped))
                per_vector.append(jnp.where(lane >= BLK, tile, swapped))
            doubled.append(per_vector)

        def one_tile(t, carry):
            off = pl.multiple_of(t * LANES, LANES)
            blocks = [jac_ref[k, top:top + SUBLANES, pl.ds(off, LANES)] for k in range(NB)]
            for c in range(VECS):
                total = blocks[0] * doubled[0][c]
                for k in range(1, NB):
                    total = total + blocks[k] * doubled[k][c]
                z_ref[c, pl.ds(row0 + top, SUBLANES), pl.ds(off, LANES)] = total
            return carry

        lax.fori_loop(0, tiles, one_tile, 0)

    @pl.when(step == pl.num_programs(0) - 1)
    def _():
        full = tiles * LANES
        for c in range(VECS):
            total = z_ref[c]
            high = total.astype(jnp.bfloat16)
            parts_ref[2 * c] = high
            parts_ref[2 * c + 1] = (total - high.astype(jnp.float32)).astype(jnp.bfloat16)
        flat = parts_ref[...].reshape(2 * VECS * count, full)
        seg = (
            lax.broadcasted_iota(jnp.int32, (full, BLK), 0) // BLK
            == lax.broadcasted_iota(jnp.int32, (full, BLK), 1)
        ).astype(jnp.bfloat16)
        sums = jnp.dot(flat, seg, preferred_element_type=jnp.float32)
        coupled = jnp.concatenate(
            [sums[(2 * c) * count:(2 * c + 1) * count] + sums[(2 * c + 1) * count:(2 * c + 2) * count] for c in range(VECS)],
            axis=1,
        )
        summed = DIAG_SHIFT * own_ref[...] + coupled
        out_ref[...] = jnp.where(mask_ref[...] > 0.0, summed, jnp.float32(0.0))


def apply_operator(jac_t, own, ghost_rows, cols, mask):
    blocks, count, full = jac_t.shape
    width = own.shape[1]
    rows = min(ROWS_PER_STEP, count)
    return pl.pallas_call(
        coupling_kernel,
        out_shape=jax.ShapeDtypeStruct((count, width), jnp.float32),
        grid=(count // rows,),
        in_specs=[
            pl.BlockSpec((blocks, rows, full), lambda b: (0, b, 0)),
            pl.BlockSpec((count, width), lambda b: (0, 0)),
            pl.BlockSpec((count, width), lambda b: (0, 0)),
            pl.BlockSpec((blocks, rows, 1), lambda b: (0, b, 0)),
            pl.BlockSpec((count, 1), lambda b: (0, 0)),
        ],
        out_specs=pl.BlockSpec((count, width), lambda b: (0, 0)),
        scratch_shapes=[
            pltpu.VMEM((2 * count, 3 * width), jnp.bfloat16),
            pltpu.VMEM((blocks, rows, width), jnp.float32),
            pltpu.VMEM((VECS, count, full), jnp.float32),
            pltpu.VMEM((2 * VECS, count, full), jnp.bfloat16),
        ],
        compiler_params=pltpu.CompilerParams(dimension_semantics=("arbitrary",)),
        cost_estimate=pl.CostEstimate(
            flops=2 * blocks * count * full * VECS + 2 * 2 * VECS * count * full * BLK,
            bytes_accessed=4 * (blocks * count * full + 4 * count * width),
            transcendentals=0,
        ),
    )(jac_t, own, ghost_rows, cols, mask)


def per_device(start_block, jacobian, counts, columns, send_list):
    living = (lax.iota(jnp.int32, E_DEV) < counts[0])[:, None]
    anchor = jnp.where(living, start_block, jnp.float32(0.0))
    lend_rows = send_list[0]
    jac_t = jnp.transpose(jacobian, (1, 0, 2))
    cols = jnp.transpose(columns, (1, 0))[:, :, None]
    mask = living.astype(jnp.float32)

    def ghosts(values):
        outgoing = values[lend_rows]
        wide_in = padded(jnp.stack([outgoing[1], outgoing[0]]), (("wide", 0),), 1)
        narrow_in = padded(jnp.stack([outgoing[3], outgoing[2]]), (("narrow", 0),), 1)
        return jnp.concatenate([wide_in[0], wide_in[3], narrow_in[0], narrow_in[3]], 0)

    def operate(values):
        return apply_operator(jac_t, values, ghosts(values), cols, mask)

    first_image = operate(anchor)
    second_image = operate(first_image)
    blocks = (
        inner_block(first_image, anchor),
        inner_block(first_image, first_image),
        inner_block(second_image, anchor),
        inner_block(second_image, first_image),
        inner_block(second_image, second_image),
    )
    gram_parts = exchange_sum(jnp.stack(blocks), ("wide", "narrow"))
    normal_matrix = jnp.concatenate(
        [
            jnp.concatenate([gram_parts[1], gram_parts[3].T], 1),
            jnp.concatenate([gram_parts[3], gram_parts[4]], 1),
        ],
        0,
    )
    right_terms = jnp.concatenate([gram_parts[0], gram_parts[2]], 0)
    factor = jnp.linalg.cholesky(normal_matrix)
    coefficients = jax.scipy.linalg.cho_solve((factor, True), right_terms)
    correction = combine(anchor, coefficients[:VECS]) + combine(first_image, coefficients[VECS:])
    residual = anchor - (
        combine(first_image, coefficients[:VECS]) + combine(second_image, coefficients[VECS:])
    )
    return (correction, residual)


def solution(mesh):
    placed = (
        P(("wide", "narrow"), None),
        P(("wide", "narrow"), None, None),
        P(("wide", "narrow")),
        P(("wide", "narrow"), None),
        P(("wide", "narrow"), None, None),
    )
    return jax.shard_map(
        per_device,
        mesh=mesh,
        in_specs=placed,
        out_specs=(P(("wide", "narrow"), None), P(("wide", "narrow"), None)),
        check_vma=False,
    )
```

time: 92.8 us -> 87.3 us (0.941)
  blocking collectives: 0 us -> 16.1 us
  starting transfers between devices: 32.5 us -> 20.4 us
  waiting for transfers between devices: 12.1 us -> 1.08 us
  Pallas kernels: 23.7 us -> 26.8 us
    all_to_all x0 -> x1, blocking collectives: none -> 16.1 us  [exchange_sum(): lax.all_to_all(jnp.broadcast_to(flat, (count, flat.shape[1])), axes, 0, 0...]
    ppermute x5 -> x0, starting transfers between devices: 12.2 us -> none  [tree_sum(): lax.ppermute(values, axis, [(i, i ^ stride) for i in range(count)])]
    ppermute x5 -> x0, waiting for transfers between devices: 9.22 us -> none  [tree_sum(): lax.ppermute(values, axis, [(i, i ^ stride) for i in range(count)])]
    gather x2 -> x0, local copies, waits for them, and re-layouts: 5.73 us -> none  [operate(): picked = source[gather_rows]]
    pallas_call x2, Pallas kernels: 23.7 us -> 26.8 us  [apply_operator(): pl.pallas_call(coupling_kernel, out_shape=jax.ShapeDtypeStruct((count, wi...]
    pallas_call x0 -> x2, local copies, waits for them, and re-layouts: none -> 1.98 us  [apply_operator(): pl.pallas_call(coupling_kernel, out_shape=jax.ShapeDtypeStruct((count, wi...]
    unnamed x2 -> x0, other arithmetic: 1.97 us -> none
    ppermute x4, waiting for transfers between devices: 2.82 us -> 1.07 us  [padded(): lax.ppermute(head, axis, [((i + 1) % count, i) for i in range(ends)])]
  transfers between devices with their start and end apart: 13 -> 8, of which waited for: 8 -> 1; matrix products, arithmetic and copies ran while one was open for 2% -> 4% of each run, Pallas kernels for 0% -> 0%
where the time goes in v3:
time: 87.3 us; the launch traced here: 86.8 us
  Pallas kernels  26.8 us (31%)
  starting transfers between devices  20.4 us (23%)
  blocking collectives  16.1 us (18%)
  local copies, waits for them, and re-layouts  8.06 us (9%)
  other arithmetic  7.19 us (8%)
  matrix products  5.71 us (7%)
  between operations  1.54 us (2%)
  waiting for transfers between devices  1.08 us (1%)
    pallas_call x2, Pallas kernels, apply_operator(): pl.pallas_call(coupling_kernel, out_shape=jax.ShapeDtypeStruct((count, wi...  26.8 us
    all_to_all x1, blocking collectives, exchange_sum(): lax.all_to_all(jnp.broadcast_to(flat, (count, flat.shape[1])), axes, 0, 0...  16.1 us
    ppermute x4, starting transfers between devices, padded(): lax.ppermute(tail, axis, [(i, (i + 1) % count) for i in range(ends)])  15.2 us
    ppermute x4, starting transfers between devices, padded(): lax.ppermute(head, axis, [((i + 1) % count, i) for i in range(ends)])  5.17 us
    dot_general x5, matrix products, inner_block(): jnp.einsum('eci,edi->cd', left_shaped, right_shaped, precision=lax.Precis...  3.71 us
    gather x2, local copies, waits for them, and re-layouts, ghosts(): outgoing = values[lend_rows]  2.45 us
    pallas_call x2, local copies, waits for them, and re-layouts, apply_operator(): pl.pallas_call(coupling_kernel, out_shape=jax.ShapeDtypeStruct((count, wi...  1.98 us
  transfers between devices with their start and end apart: 8, of which 1 were waited for; matrix products, arithmetic and copies ran while one was open for 4% of the time, Pallas kernels for 0%

profile of v3, /device:TPU:0, one launch (start us, length us, event | category | flops | bytes accessed | tf_op | source)
XLA Modules:
  0.0 86.8 jit_solution(15417250786642093922)
XLA Ops:
  1.3 0.7 compare_select_fusion
  2.0 0.1 reshape.149
  2.1 1.0 %broadcast_select_fusion.own_ref = f32[128,256]{1,0:T(8,128)S(1)} fusion(f32[128,256]{1,0:T(8,128)} %param.5, pred[128]{0:T(512)(128)(4,1)S(1)} %iota_compare_fusion.3), kind=kLoop, calls=%fused_computation.33 | loop fusion | flops 32768 | bytes 262272 | tf_op jit(solution)/shard_map/jit(_where)/select_n | solution.py:179
  3.1 0.8 gather_fusion
  3.9 1.3 %collective-permute-start.3 = (f32[1,32,256]{2,1,0:T(8,128)S(1)}, f32[1,32,256]{2,1,0:T(8,128)S(1)}, u32[]{:S(2)}, u32[]{:S(2)}) collective-permute-start(f32[1,32,256]{2,1,0:T(8,128)S(1)} %get-tuple-element.15), channel_id=1, source_target_pairs={{1,0},{2,1},{3,2},{5,4},{6,5},{7,6},{9,8},{10,9},{11,10},{13,12},{... | collective-permute-start | bytes 98312 | tf_op jit(solution)/shard_map/ppermute | solution.py:30
  5.2 4.8 %collective-permute-start = (f32[1,32,256]{2,1,0:T(8,128)S(1)}, f32[1,32,256]{2,1,0:T(8,128)S(1)}, u32[]{:S(2)}, u32[]{:S(2)}) collective-permute-start(f32[1,32,256]{2,1,0:T(8,128)S(1)} %get-tuple-element.12), channel_id=1, source_target_pairs={{0,4},{4,8},{8,12},{12,16},{16,20},{20,24},{24,28},{1,5},{5,9},{9,... | collective-permute-start | bytes 98312 | tf_op jit(solution)/shard_map/ppermute | solution.py:28
  10.0 1.3 %collective-permute-start.1 = (f32[1,32,256]{2,1,0:T(8,128)S(1)}, f32[1,32,256]{2,1,0:T(8,128)S(1)}, u32[]{:S(2)}, u32[]{:S(2)}) collective-permute-start(f32[1,32,256]{2,1,0:T(8,128)S(1)} %get-tuple-element.14), channel_id=1, source_target_pairs={{4,0},{8,4},{12,8},{16,12},{20,16},{24,20},{28,24},{5,1},{9,5},{13... | collective-permute-start | bytes 98312 | tf_op jit(solution)/shard_map/ppermute | solution.py:30
  11.3 2.8 %collective-permute-start.2 = (f32[1,32,256]{2,1,0:T(8,128)S(1)}, f32[1,32,256]{2,1,0:T(8,128)S(1)}, u32[]{:S(2)}, u32[]{:S(2)}) collective-permute-start(f32[1,32,256]{2,1,0:T(8,128)S(1)} %get-tuple-element.13), channel_id=1, source_target_pairs={{0,1},{1,2},{2,3},{4,5},{5,6},{6,7},{8,9},{9,10},{10,11},{12,13},{... | collective-permute-start | bytes 98312 | tf_op jit(solution)/shard_map/ppermute | solution.py:28
  14.1 0.6 fusion.21.mask_ref
  14.7 0.1 copy.85
  14.8 1.6 %copy.83.cols_ref = s32[5,128,1]{2,1,0:T(8,128)} copy(s32[5,128,1]{1,0,2:T(8,128)} %bitcast.121) | data formatting | bytes 5120 | tf_op jit(solution)/shard_map/broadcast_in_dim | solution.py:182
  16.4 0.7 pad_maximum_fusion.ghost_ref
  17.1 13.4 %shard_map.68.own_ref = f32[128,256]{1,0:T(8,128)} custom-call(f32[5,128,4096]{2,1,0:T(8,128)} %bitcast.95, f32[128,256]{1,0:T(8,128)} %copy-done, f32[128,256]{1,0:T(8,128)} %pad_maximum_fusion.ghost_ref, s32[5,128,1]{2,1,0:T(8,128)} %copy.83.cols_ref, f32[128,1]{1,0:T(8,128)} %fusion.21.mask_ref), custom_call_target="tpu_custom_call" | custom-call | flops 557842432 | bytes 11010048 | tf_op jit(solution)/shard_map/pallas_call | solution.py:150
  30.5 1.7 %gather_fusion.1 = f32[128,256]{1,0:T(8,128)S(1)} fusion(f32[128,256]{1,0:T(8,128)} %shard_map.68.own_ref, s32[1024]{0:T(1024)S(1)} %pad_clamp_fusion), kind=kCustom, calls=%fused_computation.1 | custom fusion | bytes 262656 | tf_op jit(solution)/shard_map/gather | solution.py:186
  32.2 1.0 %copy.84 = f32[128,256]{0,1:T(8,128)S(1)} copy(f32[128,256]{1,0:T(8,128)} %shard_map.68.own_ref) | data formatting | bytes 262144 | tf_op jit(solution)/shard_map/pallas_call | solution.py:150
  33.2 4.3 %collective-permute-start.4 = (f32[1,32,256]{2,1,0:T(8,128)S(1)}, f32[1,32,256]{2,1,0:T(8,128)S(1)}, u32[]{:S(2)}, u32[]{:S(2)}) collective-permute-start(f32[1,32,256]{2,1,0:T(8,128)S(1)} %get-tuple-element.8), channel_id=1, source_target_pairs={{0,4},{4,8},{8,12},{12,16},{16,20},{20,24},{24,28},{1,5},{5,9},{9,... | collective-permute-start | bytes 98312 | tf_op jit(solution)/shard_map/ppermute | solution.py:28
  37.5 1.3 %collective-permute-start.5 = (f32[1,32,256]{2,1,0:T(8,128)S(1)}, f32[1,32,256]{2,1,0:T(8,128)S(1)}, u32[]{:S(2)}, u32[]{:S(2)}) collective-permute-start(f32[1,32,256]{2,1,0:T(8,128)S(1)} %get-tuple-element.10), channel_id=1, source_target_pairs={{4,0},{8,4},{12,8},{16,12},{20,16},{24,20},{28,24},{5,1},{9,5},{13... | collective-permute-start | bytes 98312 | tf_op jit(solution)/shard_map/ppermute | solution.py:30
  38.8 3.3 %collective-permute-start.6 = (f32[1,32,256]{2,1,0:T(8,128)S(1)}, f32[1,32,256]{2,1,0:T(8,128)S(1)}, u32[]{:S(2)}, u32[]{:S(2)}) collective-permute-start(f32[1,32,256]{2,1,0:T(8,128)S(1)} %get-tuple-element.9), channel_id=1, source_target_pairs={{0,1},{1,2},{2,3},{4,5},{5,6},{6,7},{8,9},{9,10},{10,11},{12,13},{... | collective-permute-start | bytes 98312 | tf_op jit(solution)/shard_map/ppermute | solution.py:28
  42.1 1.3 %collective-permute-start.7 = (f32[1,32,256]{2,1,0:T(8,128)S(1)}, f32[1,32,256]{2,1,0:T(8,128)S(1)}, u32[]{:S(2)}, u32[]{:S(2)}) collective-permute-start(f32[1,32,256]{2,1,0:T(8,128)S(1)} %get-tuple-element.11), channel_id=1, source_target_pairs={{1,0},{2,1},{3,2},{5,4},{6,5},{7,6},{9,8},{10,9},{11,10},{13,12},{... | collective-permute-start | bytes 98312 | tf_op jit(solution)/shard_map/ppermute | solution.py:30
  43.4 0.8 fusion.6
  44.2 0.7 fusion.5
  44.9 1.1 %collective-permute-done.7 = f32[1,32,256]{2,1,0:T(8,128)S(1)} collective-permute-done((f32[1,32,256]{2,1,0:T(8,128)S(1)}, f32[1,32,256]{2,1,0:T(8,128)S(1)}, u32[]{:S(2)}, u32[]{:S(2)}) %collective-permute-start.7) | collective-permute-done | bytes 32800 | tf_op jit(solution)/shard_map/ppermute | solution.py:30
  46.0 0.7 pad_maximum_fusion.1.ghost_ref
  46.6 13.4 %shard_map.69 = f32[128,256]{1,0:T(8,128)} custom-call(f32[5,128,4096]{2,1,0:T(8,128)} %bitcast.96, f32[128,256]{1,0:T(8,128)} %shard_map.68.own_ref, f32[128,256]{1,0:T(8,128)} %pad_maximum_fusion.1.ghost_ref, s32[5,128,1]{2,1,0:T(8,128)} %copy.83.cols_ref, f32[128,1]{1,0:T(8,128)} %fusion.21.mask_ref), custom_call_target="tpu_custom_call" | custom-call | flops 557842432 | bytes 11010048 | tf_op jit(solution)/shard_map/pallas_call | solution.py:150
  60.0 1.0 %copy.91 = f32[128,256]{0,1:T(8,128)S(1)} copy(f32[128,256]{1,0:T(8,128)} %shard_map.69) | data formatting | bytes 262144 | tf_op jit(solution)/shard_map/pallas_call | solution.py:150
  61.0 0.8 fusion.4
  61.8 0.8 fusion.3
  62.5 0.7 fusion.2
  63.3 0.1 broadcast_in_dim.30
  63.4 16.1 %all_to_all.6 = f32[32,1,80]{2,1,0:T(1,128)S(1)} all-to-all(f32[32,1,80]{2,1,0:T(1,128)S(1)} %broadcast_in_dim.31), channel_id=1, replica_groups=mesh['wide'=8,'narrow'=4] {'wide','narrow'}, dimensions={0} | all-to-all | bytes 20480 | tf_op jit(solution)/shard_map/all_to_all | solution.py:76
  79.6 0.1 squeeze.57
  79.7 0.1 copy.100
  79.8 0.1 squeeze.58
  79.9 0.1 copy.101
  80.0 0.1 copy.99
  80.3 0.7 cholesky.16
  81.1 0.6 compare_reduce_fusion
  81.7 0.6 fusion.22
  82.4 0.6 custom-call.10
  83.2 0.2 fusion.23
  83.4 0.1 fusion.28
  83.5 0.4 fusion.15
  83.9 0.4 fusion.7
  84.3 0.4 fusion
  84.8 0.1 copy.110
  84.9 0.7 fusion.42
  85.6 0.4 fusion.1
  86.1 0.8 copy.111
  (27 shorter events, 0.7 us)
Async XLA Ops:
  3.1 14.0 %copy-start = (f32[128,256]{1,0:T(8,128)}, f32[128,256]{1,0:T(8,128)S(1)}, u32[]{:S(2)}) copy-start(f32[128,256]{1,0:T(8,128)S(1)} %broadcast_select_fusion.own_ref) | copy-start | bytes 393220
  3.9 12.5 %collective-permute-start.3 = (f32[1,32,256]{2,1,0:T(8,128)S(1)}, f32[1,32,256]{2,1,0:T(8,128)S(1)}, u32[]{:S(2)}, u32[]{:S(2)}) collective-permute-start(f32[1,32,256]{2,1,0:T(8,128)S(1)} %get-tuple-element.15), channel_id=1, source_target_pairs={{1,0},{2,1},{3,2},{5,4},{6,5},{7,6},{9,8},{10,9},{11,10},{13,12},{... | collective-permute-start | bytes 98312 | tf_op jit(solution)/shard_map/ppermute | solution.py:30
  5.2 11.2 %collective-permute-start = (f32[1,32,256]{2,1,0:T(8,128)S(1)}, f32[1,32,256]{2,1,0:T(8,128)S(1)}, u32[]{:S(2)}, u32[]{:S(2)}) collective-permute-start(f32[1,32,256]{2,1,0:T(8,128)S(1)} %get-tuple-element.12), channel_id=1, source_target_pairs={{0,4},{4,8},{8,12},{12,16},{16,20},{20,24},{24,28},{1,5},{5,9},{9,... | collective-permute-start | bytes 98312 | tf_op jit(solution)/shard_map/ppermute | solution.py:28
  10.0 6.4 %collective-permute-start.1 = (f32[1,32,256]{2,1,0:T(8,128)S(1)}, f32[1,32,256]{2,1,0:T(8,128)S(1)}, u32[]{:S(2)}, u32[]{:S(2)}) collective-permute-start(f32[1,32,256]{2,1,0:T(8,128)S(1)} %get-tuple-element.14), channel_id=1, source_target_pairs={{4,0},{8,4},{12,8},{16,12},{20,16},{24,20},{28,24},{5,1},{9,5},{13... | collective-permute-start | bytes 98312 | tf_op jit(solution)/shard_map/ppermute | solution.py:30
  11.3 5.1 %collective-permute-start.2 = (f32[1,32,256]{2,1,0:T(8,128)S(1)}, f32[1,32,256]{2,1,0:T(8,128)S(1)}, u32[]{:S(2)}, u32[]{:S(2)}) collective-permute-start(f32[1,32,256]{2,1,0:T(8,128)S(1)} %get-tuple-element.13), channel_id=1, source_target_pairs={{0,1},{1,2},{2,3},{4,5},{5,6},{6,7},{8,9},{9,10},{10,11},{12,13},{... | collective-permute-start | bytes 98312 | tf_op jit(solution)/shard_map/ppermute | solution.py:28
  30.5 54.4 %copy-start.1 = (f32[128,256]{1,0:T(8,128)S(1)}, f32[128,256]{1,0:T(8,128)}, u32[]{:S(2)}) copy-start(f32[128,256]{1,0:T(8,128)} %param.5) | copy-start | bytes 393220
  33.2 11.7 %collective-permute-start.4 = (f32[1,32,256]{2,1,0:T(8,128)S(1)}, f32[1,32,256]{2,1,0:T(8,128)S(1)}, u32[]{:S(2)}, u32[]{:S(2)}) collective-permute-start(f32[1,32,256]{2,1,0:T(8,128)S(1)} %get-tuple-element.8), channel_id=1, source_target_pairs={{0,4},{4,8},{8,12},{12,16},{16,20},{20,24},{24,28},{1,5},{5,9},{9,... | collective-permute-start | bytes 98312 | tf_op jit(solution)/shard_map/ppermute | solution.py:28
  37.5 7.4 %collective-permute-start.5 = (f32[1,32,256]{2,1,0:T(8,128)S(1)}, f32[1,32,256]{2,1,0:T(8,128)S(1)}, u32[]{:S(2)}, u32[]{:S(2)}) collective-permute-start(f32[1,32,256]{2,1,0:T(8,128)S(1)} %get-tuple-element.10), channel_id=1, source_target_pairs={{4,0},{8,4},{12,8},{16,12},{20,16},{24,20},{28,24},{5,1},{9,5},{13... | collective-permute-start | bytes 98312 | tf_op jit(solution)/shard_map/ppermute | solution.py:30
  38.8 6.1 %collective-permute-start.6 = (f32[1,32,256]{2,1,0:T(8,128)S(1)}, f32[1,32,256]{2,1,0:T(8,128)S(1)}, u32[]{:S(2)}, u32[]{:S(2)}) collective-permute-start(f32[1,32,256]{2,1,0:T(8,128)S(1)} %get-tuple-element.9), channel_id=1, source_target_pairs={{0,1},{1,2},{2,3},{4,5},{5,6},{6,7},{8,9},{9,10},{10,11},{12,13},{... | collective-permute-start | bytes 98312 | tf_op jit(solution)/shard_map/ppermute | solution.py:28
  42.1 3.9 %collective-permute-start.7 = (f32[1,32,256]{2,1,0:T(8,128)S(1)}, f32[1,32,256]{2,1,0:T(8,128)S(1)}, u32[]{:S(2)}, u32[]{:S(2)}) collective-permute-start(f32[1,32,256]{2,1,0:T(8,128)S(1)} %get-tuple-element.11), channel_id=1, source_target_pairs={{1,0},{2,1},{3,2},{5,4},{6,5},{7,6},{9,8},{10,9},{11,10},{13,12},{... | collective-permute-start | bytes 98312 | tf_op jit(solution)/shard_map/ppermute | solution.py:30

commit v4 on v3

--- a/solution.py
+++ b/solution.py
@@ -11,6 +11,7 @@
 E_DEV = 128
 LANES = 128
 SUBLANES = 8
+UNROLL = 4
 ROWS_PER_STEP = 32
 
 
@@ -113,13 +114,15 @@
             off = pl.multiple_of(t * LANES, LANES)
             blocks = [jac_ref[k, top:top + SUBLANES, pl.ds(off, LANES)] for k in range(NB)]
             for c in range(VECS):
-                total = blocks[0] * doubled[0][c]
-                for k in range(1, NB):
-                    total = total + blocks[k] * doubled[k][c]
-                z_ref[c, pl.ds(row0 + top, SUBLANES), pl.ds(off, LANES)] = total
+                terms = [blocks[k] * doubled[k][c] for k in range(NB)]
+                while len(terms) > 1:
+                    terms = [terms[i] + terms[i + 1] for i in range(0, len(terms) - 1, 2)] + (
+                        [terms[-1]] if len(terms) % 2 else []
+                    )
+                z_ref[c, pl.ds(row0 + top, SUBLANES), pl.ds(off, LANES)] = terms[0]
             return carry
 
-        lax.fori_loop(0, tiles, one_tile, 0)
+        lax.fori_loop(0, tiles, one_tile, 0, unroll=UNROLL)
 
     @pl.when(step == pl.num_programs(0) - 1)
     def _():

time: 87.3 us -> 83.8 us (0.960)
  Pallas kernels: 26.8 us -> 23.2 us
    pallas_call x2, Pallas kernels: 26.8 us -> 23.2 us  [apply_operator(): pl.pallas_call(coupling_kernel, out_shape=jax.ShapeDtypeStruct((count, wi...]
  transfers between devices with their start and end apart: 8 -> 8, of which waited for: 1 -> 1; matrix products, arithmetic and copies ran while one was open for 4% -> 5% of each run, Pallas kernels for 0% -> 0%
where the time goes in v4:
time: 83.8 us; the launch traced here: 83.2 us
  Pallas kernels  23.2 us (28%)
  starting transfers between devices  20.4 us (24%)
  blocking collectives  16.1 us (19%)
  local copies, waits for them, and re-layouts  8.06 us (10%)
  other arithmetic  7.19 us (9%)
  matrix products  5.71 us (7%)
  between operations  1.54 us (2%)
  waiting for transfers between devices  1.09 us (1%)
    pallas_call x2, Pallas kernels, apply_operator(): pl.pallas_call(coupling_kernel, out_shape=jax.ShapeDtypeStruct((count, wi...  23.2 us
    all_to_all x1, blocking collectives, exchange_sum(): lax.all_to_all(jnp.broadcast_to(flat, (count, flat.shape[1])), axes, 0, 0...  16.1 us
    ppermute x4, starting transfers between devices, padded(): lax.ppermute(tail, axis, [(i, (i + 1) % count) for i in range(ends)])  15.2 us
    ppermute x4, starting transfers between devices, padded(): lax.ppermute(head, axis, [((i + 1) % count, i) for i in range(ends)])  5.17 us
    dot_general x5, matrix products, inner_block(): jnp.einsum('eci,edi->cd', left_shaped, right_shaped, precision=lax.Precis...  3.71 us
    gather x2, local copies, waits for them, and re-layouts, ghosts(): outgoing = values[lend_rows]  2.45 us
    pallas_call x2, local copies, waits for them, and re-layouts, apply_operator(): pl.pallas_call(coupling_kernel, out_shape=jax.ShapeDtypeStruct((count, wi...  1.98 us
  transfers between devices with their start and end apart: 8, of which 1 were waited for; matrix products, arithmetic and copies ran while one was open for 5% of the time, Pallas kernels for 0%

profile of v4, /device:TPU:0, one launch (start us, length us, event | category | flops | bytes accessed | tf_op | source)
XLA Modules:
  0.0 83.2 jit_solution(17982947341748618750)
XLA Ops:
  1.3 0.7 compare_select_fusion
  2.0 0.1 reshape.149
  2.1 1.0 %broadcast_select_fusion.own_ref = f32[128,256]{1,0:T(8,128)S(1)} fusion(f32[128,256]{1,0:T(8,128)} %param.5, pred[128]{0:T(512)(128)(4,1)S(1)} %iota_compare_fusion.3), kind=kLoop, calls=%fused_computation.33 | loop fusion | flops 32768 | bytes 262272 | tf_op jit(solution)/shard_map/jit(_where)/select_n | solution.py:182
  3.1 0.8 gather_fusion
  3.9 1.3 %collective-permute-start.3 = (f32[1,32,256]{2,1,0:T(8,128)S(1)}, f32[1,32,256]{2,1,0:T(8,128)S(1)}, u32[]{:S(2)}, u32[]{:S(2)}) collective-permute-start(f32[1,32,256]{2,1,0:T(8,128)S(1)} %get-tuple-element.15), channel_id=1, source_target_pairs={{1,0},{2,1},{3,2},{5,4},{6,5},{7,6},{9,8},{10,9},{11,10},{13,12},{... | collective-permute-start | bytes 98312 | tf_op jit(solution)/shard_map/ppermute | solution.py:31
  5.2 4.8 %collective-permute-start = (f32[1,32,256]{2,1,0:T(8,128)S(1)}, f32[1,32,256]{2,1,0:T(8,128)S(1)}, u32[]{:S(2)}, u32[]{:S(2)}) collective-permute-start(f32[1,32,256]{2,1,0:T(8,128)S(1)} %get-tuple-element.12), channel_id=1, source_target_pairs={{0,4},{4,8},{8,12},{12,16},{16,20},{20,24},{24,28},{1,5},{5,9},{9,... | collective-permute-start | bytes 98312 | tf_op jit(solution)/shard_map/ppermute | solution.py:29
  10.0 1.3 %collective-permute-start.1 = (f32[1,32,256]{2,1,0:T(8,128)S(1)}, f32[1,32,256]{2,1,0:T(8,128)S(1)}, u32[]{:S(2)}, u32[]{:S(2)}) collective-permute-start(f32[1,32,256]{2,1,0:T(8,128)S(1)} %get-tuple-element.14), channel_id=1, source_target_pairs={{4,0},{8,4},{12,8},{16,12},{20,16},{24,20},{28,24},{5,1},{9,5},{13... | collective-permute-start | bytes 98312 | tf_op jit(solution)/shard_map/ppermute | solution.py:31
  11.3 2.8 %collective-permute-start.2 = (f32[1,32,256]{2,1,0:T(8,128)S(1)}, f32[1,32,256]{2,1,0:T(8,128)S(1)}, u32[]{:S(2)}, u32[]{:S(2)}) collective-permute-start(f32[1,32,256]{2,1,0:T(8,128)S(1)} %get-tuple-element.13), channel_id=1, source_target_pairs={{0,1},{1,2},{2,3},{4,5},{5,6},{6,7},{8,9},{9,10},{10,11},{12,13},{... | collective-permute-start | bytes 98312 | tf_op jit(solution)/shard_map/ppermute | solution.py:29
  14.1 0.6 fusion.21.mask_ref
  14.7 0.1 copy.85
  14.8 1.6 %copy.83.cols_ref = s32[5,128,1]{2,1,0:T(8,128)} copy(s32[5,128,1]{1,0,2:T(8,128)} %bitcast.121) | data formatting | bytes 5120 | tf_op jit(solution)/shard_map/broadcast_in_dim | solution.py:185
  16.4 0.7 pad_maximum_fusion.ghost_ref
  17.1 11.6 %shard_map.68.own_ref = f32[128,256]{1,0:T(8,128)} custom-call(f32[5,128,4096]{2,1,0:T(8,128)} %bitcast.95, f32[128,256]{1,0:T(8,128)} %copy-done, f32[128,256]{1,0:T(8,128)} %pad_maximum_fusion.ghost_ref, s32[5,128,1]{2,1,0:T(8,128)} %copy.83.cols_ref, f32[128,1]{1,0:T(8,128)} %fusion.21.mask_ref), custom_call_target="tpu_custom_call" | custom-call | flops 557842432 | bytes 11010048 | tf_op jit(solution)/shard_map/pallas_call | solution.py:153
  28.7 1.7 %gather_fusion.1 = f32[128,256]{1,0:T(8,128)S(1)} fusion(f32[128,256]{1,0:T(8,128)} %shard_map.68.own_ref, s32[1024]{0:T(1024)S(1)} %pad_clamp_fusion), kind=kCustom, calls=%fused_computation.1 | custom fusion | bytes 262656 | tf_op jit(solution)/shard_map/gather | solution.py:189
  30.4 1.0 %copy.84 = f32[128,256]{0,1:T(8,128)S(1)} copy(f32[128,256]{1,0:T(8,128)} %shard_map.68.own_ref) | data formatting | bytes 262144 | tf_op jit(solution)/shard_map/pallas_call | solution.py:153
  31.4 4.3 %collective-permute-start.4 = (f32[1,32,256]{2,1,0:T(8,128)S(1)}, f32[1,32,256]{2,1,0:T(8,128)S(1)}, u32[]{:S(2)}, u32[]{:S(2)}) collective-permute-start(f32[1,32,256]{2,1,0:T(8,128)S(1)} %get-tuple-element.8), channel_id=1, source_target_pairs={{0,4},{4,8},{8,12},{12,16},{16,20},{20,24},{24,28},{1,5},{5,9},{9,... | collective-permute-start | bytes 98312 | tf_op jit(solution)/shard_map/ppermute | solution.py:29
  35.7 1.3 %collective-permute-start.5 = (f32[1,32,256]{2,1,0:T(8,128)S(1)}, f32[1,32,256]{2,1,0:T(8,128)S(1)}, u32[]{:S(2)}, u32[]{:S(2)}) collective-permute-start(f32[1,32,256]{2,1,0:T(8,128)S(1)} %get-tuple-element.10), channel_id=1, source_target_pairs={{4,0},{8,4},{12,8},{16,12},{20,16},{24,20},{28,24},{5,1},{9,5},{13... | collective-permute-start | bytes 98312 | tf_op jit(solution)/shard_map/ppermute | solution.py:31
  37.0 3.3 %collective-permute-start.6 = (f32[1,32,256]{2,1,0:T(8,128)S(1)}, f32[1,32,256]{2,1,0:T(8,128)S(1)}, u32[]{:S(2)}, u32[]{:S(2)}) collective-permute-start(f32[1,32,256]{2,1,0:T(8,128)S(1)} %get-tuple-element.9), channel_id=1, source_target_pairs={{0,1},{1,2},{2,3},{4,5},{5,6},{6,7},{8,9},{9,10},{10,11},{12,13},{... | collective-permute-start | bytes 98312 | tf_op jit(solution)/shard_map/ppermute | solution.py:29
  40.3 1.3 %collective-permute-start.7 = (f32[1,32,256]{2,1,0:T(8,128)S(1)}, f32[1,32,256]{2,1,0:T(8,128)S(1)}, u32[]{:S(2)}, u32[]{:S(2)}) collective-permute-start(f32[1,32,256]{2,1,0:T(8,128)S(1)} %get-tuple-element.11), channel_id=1, source_target_pairs={{1,0},{2,1},{3,2},{5,4},{6,5},{7,6},{9,8},{10,9},{11,10},{13,12},{... | collective-permute-start | bytes 98312 | tf_op jit(solution)/shard_map/ppermute | solution.py:31
  41.6 0.8 fusion.6
  42.4 0.7 fusion.5
  43.1 1.1 %collective-permute-done.7 = f32[1,32,256]{2,1,0:T(8,128)S(1)} collective-permute-done((f32[1,32,256]{2,1,0:T(8,128)S(1)}, f32[1,32,256]{2,1,0:T(8,128)S(1)}, u32[]{:S(2)}, u32[]{:S(2)}) %collective-permute-start.7) | collective-permute-done | bytes 32800 | tf_op jit(solution)/shard_map/ppermute | solution.py:31
  44.2 0.7 pad_maximum_fusion.1.ghost_ref
  44.8 11.6 %shard_map.69 = f32[128,256]{1,0:T(8,128)} custom-call(f32[5,128,4096]{2,1,0:T(8,128)} %bitcast.96, f32[128,256]{1,0:T(8,128)} %shard_map.68.own_ref, f32[128,256]{1,0:T(8,128)} %pad_maximum_fusion.1.ghost_ref, s32[5,128,1]{2,1,0:T(8,128)} %copy.83.cols_ref, f32[128,1]{1,0:T(8,128)} %fusion.21.mask_ref), custom_call_target="tpu_custom_call" | custom-call | flops 557842432 | bytes 11010048 | tf_op jit(solution)/shard_map/pallas_call | solution.py:153
  56.4 1.0 %copy.91 = f32[128,256]{0,1:T(8,128)S(1)} copy(f32[128,256]{1,0:T(8,128)} %shard_map.69) | data formatting | bytes 262144 | tf_op jit(solution)/shard_map/pallas_call | solution.py:153
  57.4 0.8 fusion.4
  58.2 0.8 fusion.3
  58.9 0.7 fusion.2
  59.7 0.1 broadcast_in_dim.30
  59.8 16.1 %all_to_all.6 = f32[32,1,80]{2,1,0:T(1,128)S(1)} all-to-all(f32[32,1,80]{2,1,0:T(1,128)S(1)} %broadcast_in_dim.31), channel_id=1, replica_groups=mesh['wide'=8,'narrow'=4] {'wide','narrow'}, dimensions={0} | all-to-all | bytes 20480 | tf_op jit(solution)/shard_map/all_to_all | solution.py:77
  76.0 0.1 squeeze.57
  76.1 0.1 copy.100
  76.2 0.1 squeeze.58
  76.3 0.1 copy.101
  76.4 0.1 copy.99
  76.7 0.7 cholesky.16
  77.5 0.6 compare_reduce_fusion
  78.1 0.6 fusion.22
  78.8 0.6 custom-call.10
  79.6 0.2 fusion.23
  79.7 0.1 fusion.28
  79.9 0.4 fusion.15
  80.3 0.4 fusion.7
  80.7 0.4 fusion
  81.2 0.1 copy.110
  81.3 0.7 fusion.42
  82.0 0.4 fusion.1
  82.5 0.8 copy.111
  (27 shorter events, 0.7 us)
Async XLA Ops:
  3.1 14.0 %copy-start = (f32[128,256]{1,0:T(8,128)}, f32[128,256]{1,0:T(8,128)S(1)}, u32[]{:S(2)}) copy-start(f32[128,256]{1,0:T(8,128)S(1)} %broadcast_select_fusion.own_ref) | copy-start | bytes 393220
  3.9 12.5 %collective-permute-start.3 = (f32[1,32,256]{2,1,0:T(8,128)S(1)}, f32[1,32,256]{2,1,0:T(8,128)S(1)}, u32[]{:S(2)}, u32[]{:S(2)}) collective-permute-start(f32[1,32,256]{2,1,0:T(8,128)S(1)} %get-tuple-element.15), channel_id=1, source_target_pairs={{1,0},{2,1},{3,2},{5,4},{6,5},{7,6},{9,8},{10,9},{11,10},{13,12},{... | collective-permute-start | bytes 98312 | tf_op jit(solution)/shard_map/ppermute | solution.py:31
  5.2 11.2 %collective-permute-start = (f32[1,32,256]{2,1,0:T(8,128)S(1)}, f32[1,32,256]{2,1,0:T(8,128)S(1)}, u32[]{:S(2)}, u32[]{:S(2)}) collective-permute-start(f32[1,32,256]{2,1,0:T(8,128)S(1)} %get-tuple-element.12), channel_id=1, source_target_pairs={{0,4},{4,8},{8,12},{12,16},{16,20},{20,24},{24,28},{1,5},{5,9},{9,... | collective-permute-start | bytes 98312 | tf_op jit(solution)/shard_map/ppermute | solution.py:29
  10.0 6.4 %collective-permute-start.1 = (f32[1,32,256]{2,1,0:T(8,128)S(1)}, f32[1,32,256]{2,1,0:T(8,128)S(1)}, u32[]{:S(2)}, u32[]{:S(2)}) collective-permute-start(f32[1,32,256]{2,1,0:T(8,128)S(1)} %get-tuple-element.14), channel_id=1, source_target_pairs={{4,0},{8,4},{12,8},{16,12},{20,16},{24,20},{28,24},{5,1},{9,5},{13... | collective-permute-start | bytes 98312 | tf_op jit(solution)/shard_map/ppermute | solution.py:31
  11.3 5.1 %collective-permute-start.2 = (f32[1,32,256]{2,1,0:T(8,128)S(1)}, f32[1,32,256]{2,1,0:T(8,128)S(1)}, u32[]{:S(2)}, u32[]{:S(2)}) collective-permute-start(f32[1,32,256]{2,1,0:T(8,128)S(1)} %get-tuple-element.13), channel_id=1, source_target_pairs={{0,1},{1,2},{2,3},{4,5},{5,6},{6,7},{8,9},{9,10},{10,11},{12,13},{... | collective-permute-start | bytes 98312 | tf_op jit(solution)/shard_map/ppermute | solution.py:29
  28.7 52.6 %copy-start.1 = (f32[128,256]{1,0:T(8,128)S(1)}, f32[128,256]{1,0:T(8,128)}, u32[]{:S(2)}) copy-start(f32[128,256]{1,0:T(8,128)} %param.5) | copy-start | bytes 393220
  31.4 11.7 %collective-permute-start.4 = (f32[1,32,256]{2,1,0:T(8,128)S(1)}, f32[1,32,256]{2,1,0:T(8,128)S(1)}, u32[]{:S(2)}, u32[]{:S(2)}) collective-permute-start(f32[1,32,256]{2,1,0:T(8,128)S(1)} %get-tuple-element.8), channel_id=1, source_target_pairs={{0,4},{4,8},{8,12},{12,16},{16,20},{20,24},{24,28},{1,5},{5,9},{9,... | collective-permute-start | bytes 98312 | tf_op jit(solution)/shard_map/ppermute | solution.py:29
  35.7 7.4 %collective-permute-start.5 = (f32[1,32,256]{2,1,0:T(8,128)S(1)}, f32[1,32,256]{2,1,0:T(8,128)S(1)}, u32[]{:S(2)}, u32[]{:S(2)}) collective-permute-start(f32[1,32,256]{2,1,0:T(8,128)S(1)} %get-tuple-element.10), channel_id=1, source_target_pairs={{4,0},{8,4},{12,8},{16,12},{20,16},{24,20},{28,24},{5,1},{9,5},{13... | collective-permute-start | bytes 98312 | tf_op jit(solution)/shard_map/ppermute | solution.py:31
  37.0 6.1 %collective-permute-start.6 = (f32[1,32,256]{2,1,0:T(8,128)S(1)}, f32[1,32,256]{2,1,0:T(8,128)S(1)}, u32[]{:S(2)}, u32[]{:S(2)}) collective-permute-start(f32[1,32,256]{2,1,0:T(8,128)S(1)} %get-tuple-element.9), channel_id=1, source_target_pairs={{0,1},{1,2},{2,3},{4,5},{5,6},{6,7},{8,9},{9,10},{10,11},{12,13},{... | collective-permute-start | bytes 98312 | tf_op jit(solution)/shard_map/ppermute | solution.py:29
  40.3 3.9 %collective-permute-start.7 = (f32[1,32,256]{2,1,0:T(8,128)S(1)}, f32[1,32,256]{2,1,0:T(8,128)S(1)}, u32[]{:S(2)}, u32[]{:S(2)}) collective-permute-start(f32[1,32,256]{2,1,0:T(8,128)S(1)} %get-tuple-element.11), channel_id=1, source_target_pairs={{1,0},{2,1},{3,2},{5,4},{6,5},{7,6},{9,8},{10,9},{11,10},{13,12},{... | collective-permute-start | bytes 98312 | tf_op jit(solution)/shard_map/ppermute | solution.py:31

commit v5 on v4

--- a/solution.py
+++ b/solution.py
@@ -78,22 +78,28 @@
     return jnp.sum(everyone, axis=0).reshape(values.shape)
 
 
-def coupling_kernel(jac_ref, own_ref, ghost_ref, cols_ref, mask_ref, out_ref, source_ref, picked_ref, z_ref, parts_ref):
+def coupling_kernel(
+    count_ref, lend_ref, jac_ref, own_ref, g0_ref, g1_ref, g2_ref, g3_ref, cols_ref,
+    out_ref, lent_ref, kept_ref, source_ref, picked_ref, z_ref, parts_ref,
+):
     step = pl.program_id(0)
     rows = jac_ref.shape[1]
     tiles = jac_ref.shape[2] // LANES
     count = own_ref.shape[0]
     width = own_ref.shape[1]
+    ghost = g0_ref.shape[0]
     row0 = pl.multiple_of(step * rows, rows)
 
     @pl.when(step == 0)
     def _():
-        source_ref[0:count] = split_three(own_ref[...])
-        source_ref[count:2 * count] = split_three(ghost_ref[...])
-
-    slots = lax.broadcasted_iota(jnp.int32, (rows, 2 * count), 1)
+        living = lax.broadcasted_iota(jnp.int32, (count, 1), 0) < count_ref[0]
+        source_ref[0:count] = split_three(jnp.where(living, own_ref[...], jnp.float32(0.0)))
+        for q, piece in enumerate((g0_ref, g1_ref, g2_ref, g3_ref)):
+            source_ref[count + q * ghost:count + (q + 1) * ghost] = split_three(piece[...])
+
+    slots = lax.broadcasted_iota(jnp.int32, (rows, source_ref.shape[0]), 1)
     for k in range(NB):
-        chosen = (cols_ref[k] == slots).astype(jnp.bfloat16)
+        chosen = (cols_ref[:, k:k + 1] == slots).astype(jnp.bfloat16)
         spread = jnp.dot(chosen, source_ref[...], preferred_element_type=jnp.float32)
         picked_ref[k] = spread[:, 0:width] + spread[:, width:2 * width] + spread[:, 2 * width:3 * width]
 
@@ -142,28 +148,47 @@
             [sums[(2 * c) * count:(2 * c + 1) * count] + sums[(2 * c + 1) * count:(2 * c + 2) * count] for c in range(VECS)],
             axis=1,
         )
-        summed = DIAG_SHIFT * own_ref[...] + coupled
-        out_ref[...] = jnp.where(mask_ref[...] > 0.0, summed, jnp.float32(0.0))
-
-
-def apply_operator(jac_t, own, ghost_rows, cols, mask):
+        own = own_ref[...]
+        living = lax.broadcasted_iota(jnp.int32, (count, 1), 0) < count_ref[0]
+        out_ref[...] = jnp.where(living, DIAG_SHIFT * own + coupled, jnp.float32(0.0))
+        kept_ref[...] = jnp.where(living, own, jnp.float32(0.0))
+        for q in range(lend_ref.shape[0]):
+            for j in range(lend_ref.shape[1]):
+                row = q * lend_ref.shape[1] + j
+                lent_ref[row:row + 1, :] = out_ref[pl.ds(lend_ref[q, j], 1), :]
+
+
+def apply_operator(jac_t, own, ghost_rows, columns, counts, lend_rows):
     blocks, count, full = jac_t.shape
     width = own.shape[1]
+    ghost = ghost_rows[0].shape[0]
     rows = min(ROWS_PER_STEP, count)
+    smem = pl.BlockSpec(memory_space=pltpu.SMEM)
+    whole = pl.BlockSpec((count, width), lambda b: (0, 0))
+    piece = pl.BlockSpec((ghost, width), lambda b: (0, 0))
+    lent = lend_rows.shape[0] * lend_rows.shape[1]
     return pl.pallas_call(
         coupling_kernel,
-        out_shape=jax.ShapeDtypeStruct((count, width), jnp.float32),
+        out_shape=(
+            jax.ShapeDtypeStruct((count, width), jnp.float32),
+            jax.ShapeDtypeStruct((lent, width), jnp.float32),
+            jax.ShapeDtypeStruct((count, width), jnp.float32),
+        ),
         grid=(count // rows,),
         in_specs=[
+            smem,
+            smem,
             pl.BlockSpec((blocks, rows, full), lambda b: (0, b, 0)),
-            pl.BlockSpec((count, width), lambda b: (0, 0)),
-            pl.BlockSpec((count, width), lambda b: (0, 0)),
-            pl.BlockSpec((blocks, rows, 1), lambda b: (0, b, 0)),
-            pl.BlockSpec((count, 1), lambda b: (0, 0)),
+            whole,
+            piece,
+            piece,
+            piece,
+            piece,
+            pl.BlockSpec((rows, blocks), lambda b: (b, 0)),
         ],
-        out_specs=pl.BlockSpec((count, width), lambda b: (0, 0)),
+        out_specs=(whole, pl.BlockSpec((lent, width), lambda b: (0, 0)), whole),
         scratch_shapes=[
-            pltpu.VMEM((2 * count, 3 * width), jnp.bfloat16),
+            pltpu.VMEM((count + 4 * ghost, 3 * width), jnp.bfloat16),
             pltpu.VMEM((blocks, rows, width), jnp.float32),
             pltpu.VMEM((VECS, count, full), jnp.float32),
             pltpu.VMEM((2 * VECS, count, full), jnp.bfloat16),
@@ -171,31 +196,31 @@
         compiler_params=pltpu.CompilerParams(dimension_semantics=("arbitrary",)),
         cost_estimate=pl.CostEstimate(
             flops=2 * blocks * count * full * VECS + 2 * 2 * VECS * count * full * BLK,
-            bytes_accessed=4 * (blocks * count * full + 4 * count * width),
+            bytes_accessed=4 * (blocks * count * full + 6 * count * width),
             transcendentals=0,
         ),
-    )(jac_t, own, ghost_rows, cols, mask)
+    )(counts, lend_rows, jac_t, own, *ghost_rows, columns)
 
 
 def per_device(start_block, jacobian, counts, columns, send_list):
-    living = (lax.iota(jnp.int32, E_DEV) < counts[0])[:, None]
-    anchor = jnp.where(living, start_block, jnp.float32(0.0))
     lend_rows = send_list[0]
     jac_t = jnp.transpose(jacobian, (1, 0, 2))
-    cols = jnp.transpose(columns, (1, 0))[:, :, None]
-    mask = living.astype(jnp.float32)
-
-    def ghosts(values):
-        outgoing = values[lend_rows]
-        wide_in = padded(jnp.stack([outgoing[1], outgoing[0]]), (("wide", 0),), 1)
-        narrow_in = padded(jnp.stack([outgoing[3], outgoing[2]]), (("narrow", 0),), 1)
-        return jnp.concatenate([wide_in[0], wide_in[3], narrow_in[0], narrow_in[3]], 0)
-
-    def operate(values):
-        return apply_operator(jac_t, values, ghosts(values), cols, mask)
-
-    first_image = operate(anchor)
-    second_image = operate(first_image)
+
+    def ghosts(outgoing):
+        wide, narrow = lax.axis_size("wide"), lax.axis_size("narrow")
+        return (
+            lax.ppermute(outgoing[0], "wide", [(i, i + 1) for i in range(wide - 1)]),
+            lax.ppermute(outgoing[1], "wide", [(i + 1, i) for i in range(wide - 1)]),
+            lax.ppermute(outgoing[2], "narrow", [(i, i + 1) for i in range(narrow - 1)]),
+            lax.ppermute(outgoing[3], "narrow", [(i + 1, i) for i in range(narrow - 1)]),
+        )
+
+    def operate(values, outgoing):
+        image, lent, kept = apply_operator(jac_t, values, ghosts(outgoing), columns, counts, lend_rows)
+        return image, lent.reshape(outgoing.shape), kept
+
+    first_image, first_lent, anchor = operate(start_block, start_block[lend_rows])
+    second_image, _, _ = operate(first_image, first_lent)
     blocks = (
         inner_block(first_image, anchor),
         inner_block(first_image, first_image),

time: 83.8 us -> 84.4 us (level)
  other arithmetic: 7.19 us -> 4.15 us
  local copies, waits for them, and re-layouts: 8.06 us -> 10.6 us
    unnamed x5 -> x20, local copies, waits for them, and re-layouts: 0.77 us -> 3.96 us
    broadcast_in_dim x1 -> x0, local copies, waits for them, and re-layouts: 1.58 us -> none  [per_device(): cols = jnp.transpose(columns, (1, 0))[:, :, None]]
    concatenate x2 -> x0, other arithmetic: 1.33 us -> none  [ghosts(): jnp.concatenate([wide_in[0], wide_in[3], narrow_in[0], narrow_in[3]], 0)]
    pallas_call x2 -> x3, local copies, waits for them, and re-layouts: 1.98 us -> 2.98 us  [apply_operator(): pl.pallas_call(coupling_kernel, out_shape=(jax.ShapeDtypeStruct((count, w...]
    select_n x2 -> x1, other arithmetic: 1.67 us -> 0.69 us  [per_device(): start_block[lend_rows]]
    gather x2 -> x1, local copies, waits for them, and re-layouts: 2.45 us -> 1.66 us  [per_device(): start_block[lend_rows]]
  transfers between devices with their start and end apart: 8 -> 8, of which waited for: 1 -> 1; matrix products, arithmetic and copies ran while one was open for 5% -> 6% of each run, Pallas kernels for 0% -> 0%
where the time goes in v5:
time: 84.4 us; the launch traced here: 83.8 us
  Pallas kernels  23.8 us (28%)
  starting transfers between devices  20.3 us (24%)
  blocking collectives  16.4 us (19%)
  local copies, waits for them, and re-layouts  10.6 us (13%)
  matrix products  5.72 us (7%)
  other arithmetic  4.15 us (5%)
  between operations  1.59 us (2%)
  waiting for transfers between devices  1.28 us (2%)
    pallas_call x2, Pallas kernels, apply_operator(): pl.pallas_call(coupling_kernel, out_shape=(jax.ShapeDtypeStruct((count, w...  23.8 us
    all_to_all x1, blocking collectives, exchange_sum(): lax.all_to_all(jnp.broadcast_to(flat, (count, flat.shape[1])), axes, 0, 0...  16.4 us
    ppermute x2, starting transfers between devices, ghosts(): lax.ppermute(outgoing[0], 'wide', [(i, i + 1) for i in range(wide - 1)])  9.39 us
    ppermute x2, starting transfers between devices, ghosts(): lax.ppermute(outgoing[2], 'narrow', [(i, i + 1) for i in range(narrow - 1)])  5.72 us
    unnamed x20, local copies, waits for them, and re-layouts  3.96 us
    dot_general x5, matrix products, inner_block(): jnp.einsum('eci,edi->cd', left_shaped, right_shaped, precision=lax.Precis...  3.71 us
    pallas_call x3, local copies, waits for them, and re-layouts, apply_operator(): pl.pallas_call(coupling_kernel, out_shape=(jax.ShapeDtypeStruct((count, w...  2.98 us
    ppermute x2, starting transfers between devices, ghosts(): lax.ppermute(outgoing[1], 'wide', [(i + 1, i) for i in range(wide - 1)])  2.58 us
  transfers between devices with their start and end apart: 8, of which 1 were waited for; matrix products, arithmetic and copies ran while one was open for 6% of the time, Pallas kernels for 0%

profile of v5, /device:TPU:0, one launch (start us, length us, event | category | flops | bytes accessed | tf_op | source)
XLA Modules:
  0.0 83.8 jit_solution(10391196553767171339)
XLA Ops:
  0.6 0.7 compare_select_fusion
  1.3 0.1 reshape.145
  1.4 1.7 %gather_fusion = f32[128,256]{1,0:T(8,128)S(1)} fusion(f32[128,256]{1,0:T(8,128)} %own_ref.1, s32[1024]{0:T(1024)S(1)} %pad_clamp_fusion), kind=kCustom, calls=%fused_computation | custom fusion | bytes 262656 | tf_op jit(solution)/shard_map/gather | solution.py:222
  3.1 4.8 %collective-permute-start = (f32[32,256]{1,0:T(8,128)S(1)}, f32[32,256]{1,0:T(8,128)S(1)}, u32[]{:S(2)}, u32[]{:S(2)}) collective-permute-start(f32[32,256]{1,0:T(8,128)S(1)} %get-tuple-element.23), channel_id=1, source_target_pairs={{0,4},{4,8},{8,12},{12,16},{16,20},{20,24},{24,28},{1,5},{5,9},{9,... | collective-permute-start | bytes 98312 | tf_op jit(solution)/shard_map/ppermute | solution.py:212
  7.9 1.3 %collective-permute-start.1 = (f32[32,256]{1,0:T(8,128)S(1)}, f32[32,256]{1,0:T(8,128)S(1)}, u32[]{:S(2)}, u32[]{:S(2)}) collective-permute-start(f32[32,256]{1,0:T(8,128)S(1)} %get-tuple-element.22), channel_id=1, source_target_pairs={{4,0},{8,4},{12,8},{16,12},{20,16},{24,20},{28,24},{5,1},{9,5},{13... | collective-permute-start | bytes 98312 | tf_op jit(solution)/shard_map/ppermute | solution.py:213
  9.2 1.5 %collective-permute-start.2 = (f32[32,256]{1,0:T(8,128)S(1)}, f32[32,256]{1,0:T(8,128)S(1)}, u32[]{:S(2)}, u32[]{:S(2)}) collective-permute-start(f32[32,256]{1,0:T(8,128)S(1)} %get-tuple-element.21), channel_id=1, source_target_pairs={{0,1},{1,2},{2,3},{4,5},{5,6},{6,7},{8,9},{9,10},{10,11},{12,13},{... | collective-permute-start | bytes 98312 | tf_op jit(solution)/shard_map/ppermute | solution.py:214
  10.7 1.3 %collective-permute-start.3 = (f32[32,256]{1,0:T(8,128)S(1)}, f32[32,256]{1,0:T(8,128)S(1)}, u32[]{:S(2)}, u32[]{:S(2)}) collective-permute-start(f32[32,256]{1,0:T(8,128)S(1)} %get-tuple-element.20), channel_id=1, source_target_pairs={{1,0},{2,1},{3,2},{5,4},{6,5},{7,6},{9,8},{10,9},{11,10},{13,12},{... | collective-permute-start | bytes 98312 | tf_op jit(solution)/shard_map/ppermute | solution.py:215
  12.0 1.4 %copy.85.cols_ref = s32[128,5]{1,0:T(8,128)} copy(s32[128,5]{0,1:T(8,128)} %param.8) | data formatting | bytes 5120 | tf_op args[3]
  14.1 1.3 %collective-permute-done.3.g3_ref = f32[32,256]{1,0:T(8,128)S(1)} collective-permute-done((f32[32,256]{1,0:T(8,128)S(1)}, f32[32,256]{1,0:T(8,128)S(1)}, u32[]{:S(2)}, u32[]{:S(2)}) %collective-permute-start.3) | collective-permute-done | bytes 32800 | tf_op jit(solution)/shard_map/ppermute | solution.py:215
  15.4 0.6 copy-done.8
  16.0 11.9 %shard_map.68 = (f32[128,256]{1,0:T(8,128)}, f32[128,256]{1,0:T(8,128)}, f32[128,256]{1,0:T(8,128)}) custom-call(s32[1]{0:T(128)S(6)} %copy.142.count_ref, s32[4,32]{1,0:T(4,128)} %bitcast.83, f32[5,128,4096]{2,1,0:T(8,128)} %bitcast.66, f32[128,256]{1,0:T(8,128)} %own_ref.1, f32[32,256]{1,0:T(8,128)} %copy-done.4, f32[32,256]{1,0:T(8,128)} %copy-done.5, ...), custom_call_target="tpu_custom_call" | custom-call | flops 557842432 | bytes 11272192 | tf_op jit(solution)/shard_map/pallas_call | solution.py:170
  27.9 0.9 %fusion.39 = (f32[32,256]{1,0:T(8,128)S(1)}, f32[32,256]{1,0:T(8,128)S(1)}, f32[32,256]{1,0:T(8,128)S(1)}, f32[32,256]{1,0:T(8,128)S(1)}) fusion(f32[128,256]{1,0:T(8,128)} %get-tuple-element.8), kind=kLoop, calls=%fused_computation.56 | loop fusion | bytes 262144 | tf_op jit(solution)/shard_map/slice | solution.py:215
  28.7 4.5 %collective-permute-start.4 = (f32[32,256]{1,0:T(8,128)S(1)}, f32[32,256]{1,0:T(8,128)S(1)}, u32[]{:S(2)}, u32[]{:S(2)}) collective-permute-start(f32[32,256]{1,0:T(8,128)S(1)} %get-tuple-element.19), channel_id=1, source_target_pairs={{0,4},{4,8},{8,12},{12,16},{16,20},{20,24},{24,28},{1,5},{5,9},{9,... | collective-permute-start | bytes 98312 | tf_op jit(solution)/shard_map/ppermute | solution.py:212
  33.3 1.3 %collective-permute-start.5 = (f32[32,256]{1,0:T(8,128)S(1)}, f32[32,256]{1,0:T(8,128)S(1)}, u32[]{:S(2)}, u32[]{:S(2)}) collective-permute-start(f32[32,256]{1,0:T(8,128)S(1)} %get-tuple-element.18), channel_id=1, source_target_pairs={{4,0},{8,4},{12,8},{16,12},{20,16},{24,20},{28,24},{5,1},{9,5},{13... | collective-permute-start | bytes 98312 | tf_op jit(solution)/shard_map/ppermute | solution.py:213
  34.6 4.3 %collective-permute-start.6 = (f32[32,256]{1,0:T(8,128)S(1)}, f32[32,256]{1,0:T(8,128)S(1)}, u32[]{:S(2)}, u32[]{:S(2)}) collective-permute-start(f32[32,256]{1,0:T(8,128)S(1)} %get-tuple-element.17), channel_id=1, source_target_pairs={{0,1},{1,2},{2,3},{4,5},{5,6},{6,7},{8,9},{9,10},{10,11},{12,13},{... | collective-permute-start | bytes 98312 | tf_op jit(solution)/shard_map/ppermute | solution.py:214
  38.9 1.3 %collective-permute-start.7 = (f32[32,256]{1,0:T(8,128)S(1)}, f32[32,256]{1,0:T(8,128)S(1)}, u32[]{:S(2)}, u32[]{:S(2)}) collective-permute-start(f32[32,256]{1,0:T(8,128)S(1)} %get-tuple-element.16), channel_id=1, source_target_pairs={{1,0},{2,1},{3,2},{5,4},{6,5},{7,6},{9,8},{10,9},{11,10},{13,12},{... | collective-permute-start | bytes 98312 | tf_op jit(solution)/shard_map/ppermute | solution.py:215
  40.2 1.0 %copy.86 = f32[128,256]{0,1:T(8,128)S(1)} copy(f32[128,256]{1,0:T(8,128)} %get-tuple-element.6.own_ref) | data formatting | bytes 262144 | tf_op jit(solution)/shard_map/pallas_call | solution.py:170
  41.2 1.0 %copy.87 = f32[128,256]{0,1:T(8,128)S(1)} copy(f32[128,256]{1,0:T(8,128)} %get-tuple-element.7) | data formatting | bytes 262144 | tf_op jit(solution)/shard_map/pallas_call | solution.py:170
  42.2 0.8 fusion.6
  42.9 0.7 fusion.5
  43.7 0.6 copy-done.1
  44.3 0.6 copy-done.6
  44.9 11.9 %shard_map.69 = (f32[128,256]{1,0:T(8,128)}, f32[128,256]{1,0:T(8,128)}, f32[128,256]{1,0:T(8,128)}) custom-call(s32[1]{0:T(128)S(6)} %copy.142.count_ref, s32[4,32]{1,0:T(4,128)} %bitcast.84, f32[5,128,4096]{2,1,0:T(8,128)} %bitcast.67, f32[128,256]{1,0:T(8,128)} %get-tuple-element.6.own_ref, f32[32,256]{1,0:T(8,128)} %copy-done.1, f32[32,256]{1,0:T(8,128)} %copy-done.2, ...), custom_call_target="tpu_custom_call" | custom-call | flops 557842432 | bytes 11272192 | tf_op jit(solution)/shard_map/pallas_call | solution.py:170
  56.8 1.0 %copy.93 = f32[128,256]{0,1:T(8,128)S(1)} copy(f32[128,256]{1,0:T(8,128)} %get-tuple-element.9) | data formatting | bytes 262144 | tf_op jit(solution)/shard_map/pallas_call | solution.py:170
  57.8 0.8 fusion.4
  58.5 0.8 fusion.3
  59.3 0.7 fusion.2
  60.0 0.1 broadcast_in_dim.10
  60.1 16.4 %all_to_all.6 = f32[32,1,80]{2,1,0:T(1,128)S(1)} all-to-all(f32[32,1,80]{2,1,0:T(1,128)S(1)} %broadcast_in_dim.11), channel_id=1, replica_groups=mesh['wide'=8,'narrow'=4] {'wide','narrow'}, dimensions={0} | all-to-all | bytes 20480 | tf_op jit(solution)/shard_map/all_to_all | solution.py:77
  76.7 0.1 squeeze.43
  76.7 0.1 copy.101
  76.8 0.1 squeeze.44
  76.9 0.1 copy.102
  77.0 0.1 squeeze.45
  77.1 0.1 copy.103
  77.3 0.7 cholesky.16
  78.1 0.6 compare_reduce_fusion
  78.8 0.6 fusion.21
  79.4 0.6 custom-call.10
  80.2 0.2 fusion.22
  80.4 0.1 fusion.27
  80.5 0.4 fusion.15
  81.0 0.4 fusion.7
  81.4 0.4 fusion
  81.8 0.1 copy.112
  81.9 0.7 sub.3
  82.6 0.4 fusion.1
  83.1 0.8 copy.113
  (35 shorter events, 0.6 us)
Async XLA Ops:
  3.1 11.0 %collective-permute-start = (f32[32,256]{1,0:T(8,128)S(1)}, f32[32,256]{1,0:T(8,128)S(1)}, u32[]{:S(2)}, u32[]{:S(2)}) collective-permute-start(f32[32,256]{1,0:T(8,128)S(1)} %get-tuple-element.23), channel_id=1, source_target_pairs={{0,4},{4,8},{8,12},{12,16},{16,20},{20,24},{24,28},{1,5},{5,9},{9,... | collective-permute-start | bytes 98312 | tf_op jit(solution)/shard_map/ppermute | solution.py:212
  7.9 6.2 %collective-permute-start.1 = (f32[32,256]{1,0:T(8,128)S(1)}, f32[32,256]{1,0:T(8,128)S(1)}, u32[]{:S(2)}, u32[]{:S(2)}) collective-permute-start(f32[32,256]{1,0:T(8,128)S(1)} %get-tuple-element.22), channel_id=1, source_target_pairs={{4,0},{8,4},{12,8},{16,12},{20,16},{24,20},{28,24},{5,1},{9,5},{13... | collective-permute-start | bytes 98312 | tf_op jit(solution)/shard_map/ppermute | solution.py:213
  9.2 4.9 %collective-permute-start.2 = (f32[32,256]{1,0:T(8,128)S(1)}, f32[32,256]{1,0:T(8,128)S(1)}, u32[]{:S(2)}, u32[]{:S(2)}) collective-permute-start(f32[32,256]{1,0:T(8,128)S(1)} %get-tuple-element.21), channel_id=1, source_target_pairs={{0,1},{1,2},{2,3},{4,5},{5,6},{6,7},{8,9},{9,10},{10,11},{12,13},{... | collective-permute-start | bytes 98312 | tf_op jit(solution)/shard_map/ppermute | solution.py:214
  10.7 4.7 %collective-permute-start.3 = (f32[32,256]{1,0:T(8,128)S(1)}, f32[32,256]{1,0:T(8,128)S(1)}, u32[]{:S(2)}, u32[]{:S(2)}) collective-permute-start(f32[32,256]{1,0:T(8,128)S(1)} %get-tuple-element.20), channel_id=1, source_target_pairs={{1,0},{2,1},{3,2},{5,4},{6,5},{7,6},{9,8},{10,9},{11,10},{13,12},{... | collective-permute-start | bytes 98312 | tf_op jit(solution)/shard_map/ppermute | solution.py:215
  14.1 1.3 %copy-start.4 = (f32[32,256]{1,0:T(8,128)}, f32[32,256]{1,0:T(8,128)S(1)}, u32[]{:S(2)}) copy-start(f32[32,256]{1,0:T(8,128)S(1)} %collective-permute-done.g0_ref) | copy-start | bytes 98308
  14.1 1.3 %copy-start.5 = (f32[32,256]{1,0:T(8,128)}, f32[32,256]{1,0:T(8,128)S(1)}, u32[]{:S(2)}) copy-start(f32[32,256]{1,0:T(8,128)S(1)} %collective-permute-done.1.g1_ref) | copy-start | bytes 98308
  14.1 1.3 %copy-start.7 = (f32[32,256]{1,0:T(8,128)}, f32[32,256]{1,0:T(8,128)S(1)}, u32[]{:S(2)}) copy-start(f32[32,256]{1,0:T(8,128)S(1)} %collective-permute-done.2.g2_ref) | copy-start | bytes 98308
  15.4 0.6 copy-start.8
  27.9 54.0 %copy-start = (f32[128,256]{1,0:T(8,128)S(1)}, f32[128,256]{1,0:T(8,128)}, u32[]{:S(2)}) copy-start(f32[128,256]{1,0:T(8,128)} %get-tuple-element.7) | copy-start | bytes 393220
  28.7 14.9 %collective-permute-start.4 = (f32[32,256]{1,0:T(8,128)S(1)}, f32[32,256]{1,0:T(8,128)S(1)}, u32[]{:S(2)}, u32[]{:S(2)}) collective-permute-start(f32[32,256]{1,0:T(8,128)S(1)} %get-tuple-element.19), channel_id=1, source_target_pairs={{0,4},{4,8},{8,12},{12,16},{16,20},{20,24},{24,28},{1,5},{5,9},{9,... | collective-permute-start | bytes 98312 | tf_op jit(solution)/shard_map/ppermute | solution.py:212
  33.3 10.4 %collective-permute-start.5 = (f32[32,256]{1,0:T(8,128)S(1)}, f32[32,256]{1,0:T(8,128)S(1)}, u32[]{:S(2)}, u32[]{:S(2)}) collective-permute-start(f32[32,256]{1,0:T(8,128)S(1)} %get-tuple-element.18), channel_id=1, source_target_pairs={{4,0},{8,4},{12,8},{16,12},{20,16},{24,20},{28,24},{5,1},{9,5},{13... | collective-permute-start | bytes 98312 | tf_op jit(solution)/shard_map/ppermute | solution.py:213
  34.6 9.1 %collective-permute-start.6 = (f32[32,256]{1,0:T(8,128)S(1)}, f32[32,256]{1,0:T(8,128)S(1)}, u32[]{:S(2)}, u32[]{:S(2)}) collective-permute-start(f32[32,256]{1,0:T(8,128)S(1)} %get-tuple-element.17), channel_id=1, source_target_pairs={{0,1},{1,2},{2,3},{4,5},{5,6},{6,7},{8,9},{9,10},{10,11},{12,13},{... | collective-permute-start | bytes 98312 | tf_op jit(solution)/shard_map/ppermute | solution.py:214
  38.9 4.8 %collective-permute-start.7 = (f32[32,256]{1,0:T(8,128)S(1)}, f32[32,256]{1,0:T(8,128)S(1)}, u32[]{:S(2)}, u32[]{:S(2)}) collective-permute-start(f32[32,256]{1,0:T(8,128)S(1)} %get-tuple-element.16), channel_id=1, source_target_pairs={{1,0},{2,1},{3,2},{5,4},{6,5},{7,6},{9,8},{10,9},{11,10},{13,12},{... | collective-permute-start | bytes 98312 | tf_op jit(solution)/shard_map/ppermute | solution.py:215
  43.6 0.6 copy-start.1
  43.7 0.6 copy-start.2
  43.7 0.6 copy-start.3
  44.3 0.6 copy-start.6

commit v6 on v5

--- a/solution.py
+++ b/solution.py
@@ -1,5 +1,8 @@
+import functools
+
 import jax
 import jax.numpy as jnp
+import numpy as np
 from jax import lax
 from jax.experimental import pallas as pl
 from jax.experimental.pallas import tpu as pltpu
@@ -78,10 +81,37 @@
     return jnp.sum(everyone, axis=0).reshape(values.shape)
 
 
-def coupling_kernel(
-    count_ref, lend_ref, jac_ref, own_ref, g0_ref, g1_ref, g2_ref, g3_ref, cols_ref,
-    out_ref, lent_ref, kept_ref, source_ref, picked_ref, z_ref, parts_ref,
-):
+def segment_sums(values, segments):
+    width = values.shape[1]
+    seg = (
+        lax.broadcasted_iota(jnp.int32, (width, segments), 0) // (width // segments)
+        == lax.broadcasted_iota(jnp.int32, (width, segments), 1)
+    ).astype(jnp.bfloat16)
+    parts = split_three(values)
+    return (
+        jnp.dot(parts[:, 0:width], seg, preferred_element_type=jnp.float32)
+        + jnp.dot(parts[:, width:2 * width], seg, preferred_element_type=jnp.float32)
+        + jnp.dot(parts[:, 2 * width:3 * width], seg, preferred_element_type=jnp.float32)
+    )
+
+
+def gram_rows(pairs):
+    rows = []
+    for left, right in pairs:
+        for shift in range(VECS):
+            moved = right if shift == 0 else pltpu.roll(right, shift * BLK, 1)
+            rows.append(jnp.sum(left * moved, axis=0, keepdims=True))
+    return segment_sums(jnp.concatenate(rows, axis=0), VECS)
+
+
+def coupling_kernel(with_gram, count_ref, lend_ref, jac_ref, own_ref, g0_ref, g1_ref, g2_ref, g3_ref, cols_ref, *rest):
+    if with_gram:
+        anchor_ref, rest = rest[0], rest[1:]
+    out_ref, l0_ref, l1_ref, l2_ref, l3_ref, kept_ref = rest[:6]
+    rest = rest[6:]
+    if with_gram:
+        gram_ref, rest = rest[0], rest[1:]
+    source_ref, picked_ref, z_ref, parts_ref = rest
     step = pl.program_id(0)
     rows = jac_ref.shape[1]
     tiles = jac_ref.shape[2] // LANES
@@ -96,21 +126,23 @@
         source_ref[0:count] = split_three(jnp.where(living, own_ref[...], jnp.float32(0.0)))
         for q, piece in enumerate((g0_ref, g1_ref, g2_ref, g3_ref)):
             source_ref[count + q * ghost:count + (q + 1) * ghost] = split_three(piece[...])
-
-    slots = lax.broadcasted_iota(jnp.int32, (rows, source_ref.shape[0]), 1)
-    for k in range(NB):
-        chosen = (cols_ref[:, k:k + 1] == slots).astype(jnp.bfloat16)
-        spread = jnp.dot(chosen, source_ref[...], preferred_element_type=jnp.float32)
-        picked_ref[k] = spread[:, 0:width] + spread[:, width:2 * width] + spread[:, 2 * width:3 * width]
+        slots = lax.broadcasted_iota(jnp.int32, (source_ref.shape[0], count), 0)
+        for k in range(NB):
+            chosen = (cols_ref[k:k + 1, :] == slots).astype(jnp.bfloat16)
+            spread = lax.dot_general(
+                chosen, source_ref[...], (((0,), (0,)), ((), ())), preferred_element_type=jnp.float32
+            )
+            picked_ref[k] = spread[:, 0:width] + spread[:, width:2 * width] + spread[:, 2 * width:3 * width]
 
     lane = lax.broadcasted_iota(jnp.int32, (SUBLANES, LANES), 1)
     for group in range(rows // SUBLANES):
         top = group * SUBLANES
+        first_row = pl.multiple_of(row0 + top, SUBLANES)
         doubled = []
         for k in range(NB):
             per_vector = []
             for pair in range(VECS // 2):
-                tile = picked_ref[k, top:top + SUBLANES, pair * LANES:(pair + 1) * LANES]
+                tile = picked_ref[k, pl.ds(first_row, SUBLANES), pair * LANES:(pair + 1) * LANES]
                 swapped = pltpu.roll(tile, BLK, 1)
                 per_vector.append(jnp.where(lane < BLK, tile, swapped))
                 per_vector.append(jnp.where(lane >= BLK, tile, swapped))
@@ -125,7 +157,7 @@
                     terms = [terms[i] + terms[i + 1] for i in range(0, len(terms) - 1, 2)] + (
                         [terms[-1]] if len(terms) % 2 else []
                     )
-                z_ref[c, pl.ds(row0 + top, SUBLANES), pl.ds(off, LANES)] = terms[0]
+                z_ref[c, pl.ds(first_row, SUBLANES), pl.ds(off, LANES)] = terms[0]
             return carry
 
         lax.fori_loop(0, tiles, one_tile, 0, unroll=UNROLL)
@@ -150,46 +182,53 @@
         )
         own = own_ref[...]
         living = lax.broadcasted_iota(jnp.int32, (count, 1), 0) < count_ref[0]
-        out_ref[...] = jnp.where(living, DIAG_SHIFT * own + coupled, jnp.float32(0.0))
-        kept_ref[...] = jnp.where(living, own, jnp.float32(0.0))
-        for q in range(lend_ref.shape[0]):
+        image = jnp.where(living, DIAG_SHIFT * own + coupled, jnp.float32(0.0))
+        out_ref[...] = image
+        kept = jnp.where(living, own, jnp.float32(0.0))
+        kept_ref[...] = kept
+        for q, lent_ref in enumerate((l0_ref, l1_ref, l2_ref, l3_ref)):
             for j in range(lend_ref.shape[1]):
-                row = q * lend_ref.shape[1] + j
-                lent_ref[row:row + 1, :] = out_ref[pl.ds(lend_ref[q, j], 1), :]
-
-
-def apply_operator(jac_t, own, ghost_rows, columns, counts, lend_rows):
+                lent_ref[j:j + 1, :] = out_ref[pl.ds(lend_ref[q, j], 1), :]
+        if with_gram:
+            anchor = anchor_ref[...]
+            gram_ref[...] = gram_rows(
+                ((kept, anchor), (kept, kept), (image, anchor), (image, kept), (image, image))
+            )
+
+
+def apply_operator(jac_t, own, ghost_rows, cols_t, counts, lend_rows, anchor=None):
     blocks, count, full = jac_t.shape
     width = own.shape[1]
     ghost = ghost_rows[0].shape[0]
     rows = min(ROWS_PER_STEP, count)
+    with_gram = anchor is not None
     smem = pl.BlockSpec(memory_space=pltpu.SMEM)
     whole = pl.BlockSpec((count, width), lambda b: (0, 0))
     piece = pl.BlockSpec((ghost, width), lambda b: (0, 0))
-    lent = lend_rows.shape[0] * lend_rows.shape[1]
+    lent = lend_rows.shape[1]
+    lent_spec = pl.BlockSpec((lent, width), lambda b: (0, 0))
+    in_specs = [smem, smem, pl.BlockSpec((blocks, rows, full), lambda b: (0, b, 0)), whole, piece, piece, piece, piece,
+                pl.BlockSpec((blocks, count), lambda b: (0, 0))]
+    out_shape = [jax.ShapeDtypeStruct((count, width), jnp.float32)]
+    out_shape += [jax.ShapeDtypeStruct((lent, width), jnp.float32)] * lend_rows.shape[0]
+    out_shape += [jax.ShapeDtypeStruct((count, width), jnp.float32)]
+    out_specs = [whole] + [lent_spec] * lend_rows.shape[0] + [whole]
+    args = [counts, lend_rows, jac_t, own, *ghost_rows, cols_t]
+    if with_gram:
+        in_specs.append(whole)
+        args.append(anchor)
+        gram_count = 5 * VECS
+        out_shape.append(jax.ShapeDtypeStruct((gram_count, VECS), jnp.float32))
+        out_specs.append(pl.BlockSpec((gram_count, VECS), lambda b: (0, 0)))
     return pl.pallas_call(
-        coupling_kernel,
-        out_shape=(
-            jax.ShapeDtypeStruct((count, width), jnp.float32),
-            jax.ShapeDtypeStruct((lent, width), jnp.float32),
-            jax.ShapeDtypeStruct((count, width), jnp.float32),
-        ),
+        functools.partial(coupling_kernel, with_gram),
+        out_shape=tuple(out_shape),
         grid=(count // rows,),
-        in_specs=[
-            smem,
-            smem,
-            pl.BlockSpec((blocks, rows, full), lambda b: (0, b, 0)),
-            whole,
-            piece,
-            piece,
-            piece,
-            piece,
-            pl.BlockSpec((rows, blocks), lambda b: (b, 0)),
-        ],
-        out_specs=(whole, pl.BlockSpec((lent, width), lambda b: (0, 0)), whole),
+        in_specs=in_specs,
+        out_specs=tuple(out_specs),
         scratch_shapes=[
             pltpu.VMEM((count + 4 * ghost, 3 * width), jnp.bfloat16),
-            pltpu.VMEM((blocks, rows, width), jnp.float32),
+            pltpu.VMEM((blocks, count, width), jnp.float32),
             pltpu.VMEM((VECS, count, full), jnp.float32),
             pltpu.VMEM((2 * VECS, count, full), jnp.bfloat16),
         ],
@@ -199,7 +238,7 @@
             bytes_accessed=4 * (blocks * count * full + 6 * count * width),
             transcendentals=0,
         ),
-    )(counts, lend_rows, jac_t, own, *ghost_rows, columns)
+    )(*args)
 
 
 def per_device(start_block, jacobian, counts, columns, send_list):
@@ -215,20 +254,16 @@
             lax.ppermute(outgoing[3], "narrow", [(i + 1, i) for i in range(narrow - 1)]),
         )
 
-    def operate(values, outgoing):
-        image, lent, kept = apply_operator(jac_t, values, ghosts(outgoing), columns, counts, lend_rows)
-        return image, lent.reshape(outgoing.shape), kept
-
-    first_image, first_lent, anchor = operate(start_block, start_block[lend_rows])
-    second_image, _, _ = operate(first_image, first_lent)
-    blocks = (
-        inner_block(first_image, anchor),
-        inner_block(first_image, first_image),
-        inner_block(second_image, anchor),
-        inner_block(second_image, first_image),
-        inner_block(second_image, second_image),
-    )
-    gram_parts = exchange_sum(jnp.stack(blocks), ("wide", "narrow"))
+    cols_t = jnp.transpose(columns, (1, 0))
+    first = apply_operator(jac_t, start_block, ghosts(start_block[lend_rows]), cols_t, counts, lend_rows)
+    first_image, first_lent, anchor = first[0], jnp.stack(first[1:5]), first[5]
+    second = apply_operator(jac_t, first_image, ghosts(first_lent), cols_t, counts, lend_rows, anchor)
+    second_image, raw_gram = second[0], second[6]
+    raw_gram = exchange_sum(raw_gram, ("wide", "narrow"))
+    pair = np.arange(5)[:, None, None]
+    row_c = np.arange(VECS)[None, :, None]
+    col_d = np.arange(VECS)[None, None, :]
+    gram_parts = raw_gram[pair * VECS + (row_c - col_d) % VECS, np.broadcast_to(row_c, (5, VECS, VECS))]
     normal_matrix = jnp.concatenate(
         [
             jnp.concatenate([gram_parts[1], gram_parts[3].T], 1),

time: 84.4 us -> 79.4 us (0.941)
  blocking collectives: 16.4 us -> 0 us
  waiting for transfers between devices: 1.28 us -> 10.6 us
  starting transfers between devices: 20.3 us -> 29.3 us
  matrix products: 5.72 us -> 2 us
  Pallas kernels: 23.8 us -> 22.2 us
  local copies, waits for them, and re-layouts: 10.6 us -> 9.04 us
    all_to_all x1 -> x0, blocking collectives: 16.4 us -> none  [exchange_sum(): lax.all_to_all(jnp.broadcast_to(flat, (count, flat.shape[1])), axes, 0, 0...]
    all_to_all x0 -> x1, starting transfers between devices: none -> 8.94 us  [exchange_sum(): lax.all_to_all(jnp.broadcast_to(flat, (count, flat.shape[1])), axes, 0, 0...]
    all_to_all x0 -> x1, waiting for transfers between devices: none -> 5.92 us  [exchange_sum(): lax.all_to_all(jnp.broadcast_to(flat, (count, flat.shape[1])), axes, 0, 0...]
    dot_general x5 -> x0, matrix products: 3.71 us -> none  [inner_block(): jnp.einsum('eci,edi->cd', left_shaped, right_shaped, precision=lax.Precis...]
    ppermute x2, waiting for transfers between devices: 1.27 us -> 3.59 us  [ghosts(): lax.ppermute(outgoing[3], 'narrow', [(i + 1, i) for i in range(narrow - 1)])]
    unnamed x20 -> x23, local copies, waits for them, and re-layouts: 3.96 us -> 1.99 us
    pallas_call x3, local copies, waits for them, and re-layouts: 2.98 us -> 1.17 us  [apply_operator(): pl.pallas_call(functools.partial(coupling_kernel, with_gram), out_shape=t...]
    gather x0 -> x1, local copies, waits for them, and re-layouts: none -> 1.68 us  [per_device(): raw_gram[pair * VECS + (row_c - col_d) % VECS, np.broadcast_to(row_c, (5,...]
  transfers between devices with their start and end apart: 8 -> 9, of which waited for: 1 -> 4; matrix products, arithmetic and copies ran while one was open for 6% -> 1% of each run, Pallas kernels for 0% -> 0%
where the time goes in v6:
time: 79.4 us; the launch traced here: 78.9 us
  starting transfers between devices  29.3 us (37%)
  Pallas kernels  22.2 us (28%)
  waiting for transfers between devices  10.6 us (13%)
  local copies, waits for them, and re-layouts  9.04 us (11%)
  other arithmetic  4.15 us (5%)
  matrix products  2 us (3%)
  between operations  1.59 us (2%)
    pallas_call x2, Pallas kernels, apply_operator(): pl.pallas_call(functools.partial(coupling_kernel, with_gram), out_shape=t...  22.2 us
    ppermute x2, starting transfers between devices, ghosts(): lax.ppermute(outgoing[0], 'wide', [(i, i + 1) for i in range(wide - 1)])  9.52 us
    all_to_all x1, starting transfers between devices, exchange_sum(): lax.all_to_all(jnp.broadcast_to(flat, (count, flat.shape[1])), axes, 0, 0...  8.94 us
    all_to_all x1, waiting for transfers between devices, exchange_sum(): lax.all_to_all(jnp.broadcast_to(flat, (count, flat.shape[1])), axes, 0, 0...  5.92 us
    ppermute x2, starting transfers between devices, ghosts(): lax.ppermute(outgoing[2], 'narrow', [(i, i + 1) for i in range(narrow - 1)])  5.72 us
    ppermute x2, waiting for transfers between devices, ghosts(): lax.ppermute(outgoing[3], 'narrow', [(i + 1, i) for i in range(narrow - 1)])  3.59 us
    ppermute x2, starting transfers between devices, ghosts(): lax.ppermute(outgoing[1], 'wide', [(i + 1, i) for i in range(wide - 1)])  2.58 us
    ppermute x2, starting transfers between devices, ghosts(): lax.ppermute(outgoing[3], 'narrow', [(i + 1, i) for i in range(narrow - 1)])  2.58 us
  transfers between devices with their start and end apart: 9, of which 4 were waited for; matrix products, arithmetic and copies ran while one was open for 1% of the time, Pallas kernels for 0%

profile of v6, /device:TPU:0, one launch (start us, length us, event | category | flops | bytes accessed | tf_op | source)
XLA Modules:
  0.0 78.9 jit_solution(8979414087724096023)
XLA Ops:
  0.6 0.7 compare_select_fusion
  1.3 0.1 reshape.79
  1.4 1.7 %gather_fusion = f32[128,256]{1,0:T(8,128)S(1)} fusion(f32[128,256]{1,0:T(8,128)} %own_ref.1, s32[1024]{0:T(1024)S(1)} %pad_clamp_fusion), kind=kCustom, calls=%fused_computation | custom fusion | bytes 262656 | tf_op jit(solution)/shard_map/gather | solution.py:258
  3.1 4.8 %collective-permute-start = (f32[32,256]{1,0:T(8,128)S(1)}, f32[32,256]{1,0:T(8,128)S(1)}, u32[]{:S(2)}, u32[]{:S(2)}) collective-permute-start(f32[32,256]{1,0:T(8,128)S(1)} %get-tuple-element.27), channel_id=1, source_target_pairs={{0,4},{4,8},{8,12},{12,16},{16,20},{20,24},{24,28},{1,5},{5,9},{9,... | collective-permute-start | bytes 98312 | tf_op jit(solution)/shard_map/ppermute | solution.py:251
  7.9 1.3 %collective-permute-start.1 = (f32[32,256]{1,0:T(8,128)S(1)}, f32[32,256]{1,0:T(8,128)S(1)}, u32[]{:S(2)}, u32[]{:S(2)}) collective-permute-start(f32[32,256]{1,0:T(8,128)S(1)} %get-tuple-element.26), channel_id=1, source_target_pairs={{4,0},{8,4},{12,8},{16,12},{20,16},{24,20},{28,24},{5,1},{9,5},{13... | collective-permute-start | bytes 98312 | tf_op jit(solution)/shard_map/ppermute | solution.py:252
  9.2 1.5 %collective-permute-start.2 = (f32[32,256]{1,0:T(8,128)S(1)}, f32[32,256]{1,0:T(8,128)S(1)}, u32[]{:S(2)}, u32[]{:S(2)}) collective-permute-start(f32[32,256]{1,0:T(8,128)S(1)} %get-tuple-element.25), channel_id=1, source_target_pairs={{0,1},{1,2},{2,3},{4,5},{5,6},{6,7},{8,9},{9,10},{10,11},{12,13},{... | collective-permute-start | bytes 98312 | tf_op jit(solution)/shard_map/ppermute | solution.py:253
  10.7 1.3 %collective-permute-start.3 = (f32[32,256]{1,0:T(8,128)S(1)}, f32[32,256]{1,0:T(8,128)S(1)}, u32[]{:S(2)}, u32[]{:S(2)}) collective-permute-start(f32[32,256]{1,0:T(8,128)S(1)} %get-tuple-element.24), channel_id=1, source_target_pairs={{1,0},{2,1},{3,2},{5,4},{6,5},{7,6},{9,8},{10,9},{11,10},{13,12},{... | collective-permute-start | bytes 98312 | tf_op jit(solution)/shard_map/ppermute | solution.py:254
  12.7 1.1 %collective-permute-done.1.g1_ref = f32[32,256]{1,0:T(8,128)S(1)} collective-permute-done((f32[32,256]{1,0:T(8,128)S(1)}, f32[32,256]{1,0:T(8,128)S(1)}, u32[]{:S(2)}, u32[]{:S(2)}) %collective-permute-start.1) | collective-permute-done | bytes 32800 | tf_op jit(solution)/shard_map/ppermute | solution.py:252
  13.8 1.6 %collective-permute-done.3.g3_ref = f32[32,256]{1,0:T(8,128)S(1)} collective-permute-done((f32[32,256]{1,0:T(8,128)S(1)}, f32[32,256]{1,0:T(8,128)S(1)}, u32[]{:S(2)}, u32[]{:S(2)}) %collective-permute-start.3) | collective-permute-done | bytes 32800 | tf_op jit(solution)/shard_map/ppermute | solution.py:254
  15.4 0.6 copy-done.10
  16.0 11.0 %shard_map.104 = (f32[128,256]{1,0:T(8,128)}, f32[32,256]{1,0:T(8,128)}, f32[32,256]{1,0:T(8,128)}, f32[32,256]{1,0:T(8,128)}, f32[32,256]{1,0:T(8,128)}, /*index=5*/f32[128,256]{1,0:T(8,128)}) custom-call(s32[1]{0:T(128)S(6)} %copy.78.count_ref, s32[4,32]{1,0:T(4,128)} %bitcast.52, f32[5,128,4096]{2,1,0:T(8,128)} %bitcast.42, f32[128,256]{1,0:T(8,128)} %own_ref.1, ...), custom_call_target="tpu_custom_call" | custom-call | flops 557842432 | bytes 11272192 | tf_op jit(solution)/shard_map/pallas_call | solution.py:223
  27.0 4.7 %collective-permute-start.4 = (f32[32,256]{1,0:T(8,128)}, f32[32,256]{1,0:T(8,128)S(1)}, u32[]{:S(2)}, u32[]{:S(2)}) collective-permute-start(f32[32,256]{1,0:T(8,128)} %get-tuple-element.11), channel_id=1, source_target_pairs={{0,4},{4,8},{8,12},{12,16},{16,20},{20,24},{24,28},{1,5},{5,9},{9,... | collective-permute-start | bytes 98312 | tf_op jit(solution)/shard_map/ppermute | solution.py:251
  31.7 1.3 %collective-permute-start.5 = (f32[32,256]{1,0:T(8,128)}, f32[32,256]{1,0:T(8,128)S(1)}, u32[]{:S(2)}, u32[]{:S(2)}) collective-permute-start(f32[32,256]{1,0:T(8,128)} %get-tuple-element.12), channel_id=1, source_target_pairs={{4,0},{8,4},{12,8},{16,12},{20,16},{24,20},{28,24},{5,1},{9,5},{13... | collective-permute-start | bytes 98312 | tf_op jit(solution)/shard_map/ppermute | solution.py:252
  33.0 4.3 %collective-permute-start.6 = (f32[32,256]{1,0:T(8,128)}, f32[32,256]{1,0:T(8,128)S(1)}, u32[]{:S(2)}, u32[]{:S(2)}) collective-permute-start(f32[32,256]{1,0:T(8,128)} %get-tuple-element.13), channel_id=1, source_target_pairs={{0,1},{1,2},{2,3},{4,5},{5,6},{6,7},{8,9},{9,10},{10,11},{12,13},{... | collective-permute-start | bytes 98312 | tf_op jit(solution)/shard_map/ppermute | solution.py:253
  37.3 1.3 %collective-permute-start.7 = (f32[32,256]{1,0:T(8,128)}, f32[32,256]{1,0:T(8,128)S(1)}, u32[]{:S(2)}, u32[]{:S(2)}) collective-permute-start(f32[32,256]{1,0:T(8,128)} %get-tuple-element.14), channel_id=1, source_target_pairs={{1,0},{2,1},{3,2},{5,4},{6,5},{7,6},{9,8},{10,9},{11,10},{13,12},{... | collective-permute-start | bytes 98312 | tf_op jit(solution)/shard_map/ppermute | solution.py:254
  38.6 1.9 %collective-permute-done.7.g3_ref = f32[32,256]{1,0:T(8,128)S(1)} collective-permute-done((f32[32,256]{1,0:T(8,128)}, f32[32,256]{1,0:T(8,128)S(1)}, u32[]{:S(2)}, u32[]{:S(2)}) %collective-permute-start.7) | collective-permute-done | bytes 32800 | tf_op jit(solution)/shard_map/ppermute | solution.py:254
  40.6 0.6 copy-done.9
  41.2 11.2 %shard_map.105 = (f32[128,256]{1,0:T(8,128)}, f32[32,256]{1,0:T(8,128)}, f32[32,256]{1,0:T(8,128)}, f32[32,256]{1,0:T(8,128)}, f32[32,256]{1,0:T(8,128)}, /*index=5*/f32[128,256]{1,0:T(8,128)}, f32[20,4]{1,0:T(8,128)}) custom-call(s32[1]{0:T(128)S(6)} %copy.78.count_ref, s32[4,32]{1,0:T(4,128)} %bitcast.53, f32[5,128,4096]{2,1,0:T(8,128)} %bitcast.43, ...), custom_call_target="tpu_custom_call" | custom-call | flops 557842432 | bytes 11272192 | tf_op jit(solution)/shard_map/pallas_call | solution.py:223
  52.4 0.8 %broadcast_in_dim.16 = f32[80]{0:T(128)S(1)} reshape(f32[20,4]{1,0:T(8,128)} %get-tuple-element.16) | data formatting | bytes 640 | tf_op jit(solution)/shard_map/broadcast_in_dim | solution.py:80
  53.2 0.6 broadcast_in_dim.17
  53.8 8.9 %all-to-all-start = ((f32[32,1,80]{2,1,0:T(1,128)}), f32[32,1,80]{2,1,0:T(1,128)S(1)}, u32[]{:S(2)}, u32[]{:S(2)}) async-start(f32[32,1,80]{2,1,0:T(1,128)} %broadcast_in_dim.17), calls=%async_computation | async-start | bytes 32768 | tf_op jit(solution)/shard_map/all_to_all | solution.py:80
  62.7 0.1 copy.61
  62.8 0.1 copy.59
  62.9 1.0 %copy.65 = f32[128,256]{0,1:T(8,128)S(1)} copy(f32[128,256]{1,0:T(8,128)} %get-tuple-element.17) | data formatting | bytes 262144 | tf_op jit(solution)/shard_map/pallas_call | solution.py:223
  63.9 5.9 %all-to-all-done = f32[32,1,80]{2,1,0:T(1,128)S(1)} async-done(((f32[32,1,80]{2,1,0:T(1,128)}), f32[32,1,80]{2,1,0:T(1,128)S(1)}, u32[]{:S(2)}, u32[]{:S(2)}) %all-to-all-start) | async-done | bytes 10272 | tf_op jit(solution)/shard_map/all_to_all | solution.py:80
  69.9 0.1 reshape.73
  70.0 1.7 %gather_fusion.1 = f32[80]{0:T(128)S(1)} fusion(f32[20,4]{1,0:T(8,128)S(1)} %reshape.73, s32[80]{0:T(128)S(1)} %copy-done), kind=kCustom, calls=%fused_computation.1 | custom fusion | bytes 1280 | tf_op jit(solution)/shard_map/gather | solution.py:266
  71.7 0.1 squeeze.39
  71.8 0.1 copy.54
  71.9 0.1 squeeze.40
  72.0 0.1 copy.55
  72.1 0.1 squeeze.41
  72.2 0.1 copy.56
  72.4 0.7 cholesky.16
  73.2 0.6 compare_reduce_fusion
  73.8 0.6 fusion.8
  74.5 0.6 custom-call.10
  75.1 0.1 squeeze.42
  75.2 0.1 squeeze.43
  75.3 0.2 fusion.9
  75.5 0.1 fusion.14
  75.6 0.4 fusion.5
  76.1 0.4 fusion
  76.5 0.1 copy.68
  76.6 0.7 sub.3
  77.3 0.4 fusion.3
  77.7 0.4 fusion.1
  78.1 0.8 copy.69
  (35 shorter events, 0.4 us)
Async XLA Ops:
  3.1 9.6 %collective-permute-start = (f32[32,256]{1,0:T(8,128)S(1)}, f32[32,256]{1,0:T(8,128)S(1)}, u32[]{:S(2)}, u32[]{:S(2)}) collective-permute-start(f32[32,256]{1,0:T(8,128)S(1)} %get-tuple-element.27), channel_id=1, source_target_pairs={{0,4},{4,8},{8,12},{12,16},{16,20},{20,24},{24,28},{1,5},{5,9},{9,... | collective-permute-start | bytes 98312 | tf_op jit(solution)/shard_map/ppermute | solution.py:251
  7.9 5.8 %collective-permute-start.1 = (f32[32,256]{1,0:T(8,128)S(1)}, f32[32,256]{1,0:T(8,128)S(1)}, u32[]{:S(2)}, u32[]{:S(2)}) collective-permute-start(f32[32,256]{1,0:T(8,128)S(1)} %get-tuple-element.26), channel_id=1, source_target_pairs={{4,0},{8,4},{12,8},{16,12},{20,16},{24,20},{28,24},{5,1},{9,5},{13... | collective-permute-start | bytes 98312 | tf_op jit(solution)/shard_map/ppermute | solution.py:252
  9.2 4.5 %collective-permute-start.2 = (f32[32,256]{1,0:T(8,128)S(1)}, f32[32,256]{1,0:T(8,128)S(1)}, u32[]{:S(2)}, u32[]{:S(2)}) collective-permute-start(f32[32,256]{1,0:T(8,128)S(1)} %get-tuple-element.25), channel_id=1, source_target_pairs={{0,1},{1,2},{2,3},{4,5},{5,6},{6,7},{8,9},{9,10},{10,11},{12,13},{... | collective-permute-start | bytes 98312 | tf_op jit(solution)/shard_map/ppermute | solution.py:253
  10.7 4.7 %collective-permute-start.3 = (f32[32,256]{1,0:T(8,128)S(1)}, f32[32,256]{1,0:T(8,128)S(1)}, u32[]{:S(2)}, u32[]{:S(2)}) collective-permute-start(f32[32,256]{1,0:T(8,128)S(1)} %get-tuple-element.24), channel_id=1, source_target_pairs={{1,0},{2,1},{3,2},{5,4},{6,5},{7,6},{9,8},{10,9},{11,10},{13,12},{... | collective-permute-start | bytes 98312 | tf_op jit(solution)/shard_map/ppermute | solution.py:254
  12.7 2.7 %copy-start.4 = (f32[32,256]{1,0:T(8,128)}, f32[32,256]{1,0:T(8,128)S(1)}, u32[]{:S(2)}) copy-start(f32[32,256]{1,0:T(8,128)S(1)} %collective-permute-done.g0_ref) | copy-start | bytes 98308
  13.8 1.7 %copy-start.6 = (f32[32,256]{1,0:T(8,128)}, f32[32,256]{1,0:T(8,128)S(1)}, u32[]{:S(2)}) copy-start(f32[32,256]{1,0:T(8,128)S(1)} %collective-permute-done.1.g1_ref) | copy-start | bytes 98308
  13.8 1.7 %copy-start.8 = (f32[32,256]{1,0:T(8,128)}, f32[32,256]{1,0:T(8,128)S(1)}, u32[]{:S(2)}) copy-start(f32[32,256]{1,0:T(8,128)S(1)} %collective-permute-done.2.g2_ref) | copy-start | bytes 98308
  15.4 0.6 copy-start.10
  16.0 54.0 %copy-start = (s32[80]{0:T(128)S(1)}, s32[80]{0:T(128)}, u32[]{:S(2)}) copy-start(s32[80]{0:T(128)} %constant.92) | copy-start | bytes 964
  27.0 35.7 %copy-start.2 = (f32[128,256]{1,0:T(8,128)S(1)}, f32[128,256]{1,0:T(8,128)}, u32[]{:S(2)}) copy-start(f32[128,256]{1,0:T(8,128)} %get-tuple-element.10.own_ref) | copy-start | bytes 393220
  27.0 35.8 %copy-start.1 = (f32[128,256]{1,0:T(8,128)S(1)}, f32[128,256]{1,0:T(8,128)}, u32[]{:S(2)}) copy-start(f32[128,256]{1,0:T(8,128)} %get-tuple-element.15.rest_0_) | copy-start | bytes 393220
  27.0 11.6 %collective-permute-start.4 = (f32[32,256]{1,0:T(8,128)}, f32[32,256]{1,0:T(8,128)S(1)}, u32[]{:S(2)}, u32[]{:S(2)}) collective-permute-start(f32[32,256]{1,0:T(8,128)} %get-tuple-element.11), channel_id=1, source_target_pairs={{0,4},{4,8},{8,12},{12,16},{16,20},{20,24},{24,28},{1,5},{5,9},{9,... | collective-permute-start | bytes 98312 | tf_op jit(solution)/shard_map/ppermute | solution.py:251
  31.7 6.9 %collective-permute-start.5 = (f32[32,256]{1,0:T(8,128)}, f32[32,256]{1,0:T(8,128)S(1)}, u32[]{:S(2)}, u32[]{:S(2)}) collective-permute-start(f32[32,256]{1,0:T(8,128)} %get-tuple-element.12), channel_id=1, source_target_pairs={{4,0},{8,4},{12,8},{16,12},{20,16},{24,20},{28,24},{5,1},{9,5},{13... | collective-permute-start | bytes 98312 | tf_op jit(solution)/shard_map/ppermute | solution.py:252
  33.0 5.6 %collective-permute-start.6 = (f32[32,256]{1,0:T(8,128)}, f32[32,256]{1,0:T(8,128)S(1)}, u32[]{:S(2)}, u32[]{:S(2)}) collective-permute-start(f32[32,256]{1,0:T(8,128)} %get-tuple-element.13), channel_id=1, source_target_pairs={{0,1},{1,2},{2,3},{4,5},{5,6},{6,7},{8,9},{9,10},{10,11},{12,13},{... | collective-permute-start | bytes 98312 | tf_op jit(solution)/shard_map/ppermute | solution.py:253
  37.3 3.3 %collective-permute-start.7 = (f32[32,256]{1,0:T(8,128)}, f32[32,256]{1,0:T(8,128)S(1)}, u32[]{:S(2)}, u32[]{:S(2)}) collective-permute-start(f32[32,256]{1,0:T(8,128)} %get-tuple-element.14), channel_id=1, source_target_pairs={{1,0},{2,1},{3,2},{5,4},{6,5},{7,6},{9,8},{10,9},{11,10},{13,12},{... | collective-permute-start | bytes 98312 | tf_op jit(solution)/shard_map/ppermute | solution.py:254
  38.6 2.0 %copy-start.3 = (f32[32,256]{1,0:T(8,128)}, f32[32,256]{1,0:T(8,128)S(1)}, u32[]{:S(2)}) copy-start(f32[32,256]{1,0:T(8,128)S(1)} %collective-permute-done.4.g0_ref) | copy-start | bytes 98308
  38.6 2.0 %copy-start.5 = (f32[32,256]{1,0:T(8,128)}, f32[32,256]{1,0:T(8,128)S(1)}, u32[]{:S(2)}) copy-start(f32[32,256]{1,0:T(8,128)S(1)} %collective-permute-done.5.g1_ref) | copy-start | bytes 98308
  38.6 2.0 %copy-start.7 = (f32[32,256]{1,0:T(8,128)}, f32[32,256]{1,0:T(8,128)S(1)}, u32[]{:S(2)}) copy-start(f32[32,256]{1,0:T(8,128)S(1)} %collective-permute-done.6.g2_ref) | copy-start | bytes 98308
  40.6 0.6 copy-start.9
  53.8 16.1 %all-to-all-start = ((f32[32,1,80]{2,1,0:T(1,128)}), f32[32,1,80]{2,1,0:T(1,128)S(1)}, u32[]{:S(2)}, u32[]{:S(2)}) async-start(f32[32,1,80]{2,1,0:T(1,128)} %broadcast_in_dim.17), calls=%async_computation | async-start | bytes 32768 | tf_op jit(solution)/shard_map/all_to_all | solution.py:80

commit v7 on v6

--- a/solution.py
+++ b/solution.py
@@ -191,12 +191,12 @@
                 lent_ref[j:j + 1, :] = out_ref[pl.ds(lend_ref[q, j], 1), :]
         if with_gram:
             anchor = anchor_ref[...]
-            gram_ref[...] = gram_rows(
-                ((kept, anchor), (kept, kept), (image, anchor), (image, kept), (image, image))
-            )
-
-
-def apply_operator(jac_t, own, ghost_rows, cols_t, counts, lend_rows, anchor=None):
+            partial = gram_rows(((kept, anchor), (kept, kept), (image, anchor), (image, kept), (image, image)))
+            for target in range(gram_ref.shape[0]):
+                gram_ref[target] = partial
+
+
+def apply_operator(jac_t, own, ghost_rows, cols_t, counts, lend_rows, anchor=None, peers=1):
     blocks, count, full = jac_t.shape
     width = own.shape[1]
     ghost = ghost_rows[0].shape[0]
@@ -218,8 +218,8 @@
         in_specs.append(whole)
         args.append(anchor)
         gram_count = 5 * VECS
-        out_shape.append(jax.ShapeDtypeStruct((gram_count, VECS), jnp.float32))
-        out_specs.append(pl.BlockSpec((gram_count, VECS), lambda b: (0, 0)))
+        out_shape.append(jax.ShapeDtypeStruct((peers, gram_count, VECS), jnp.float32))
+        out_specs.append(pl.BlockSpec((peers, gram_count, VECS), lambda b: (0, 0, 0)))
     return pl.pallas_call(
         functools.partial(coupling_kernel, with_gram),
         out_shape=tuple(out_shape),
@@ -257,13 +257,16 @@
     cols_t = jnp.transpose(columns, (1, 0))
     first = apply_operator(jac_t, start_block, ghosts(start_block[lend_rows]), cols_t, counts, lend_rows)
     first_image, first_lent, anchor = first[0], jnp.stack(first[1:5]), first[5]
-    second = apply_operator(jac_t, first_image, ghosts(first_lent), cols_t, counts, lend_rows, anchor)
+    peers = lax.axis_size("wide") * lax.axis_size("narrow")
+    second = apply_operator(jac_t, first_image, ghosts(first_lent), cols_t, counts, lend_rows, anchor, peers)
     second_image, raw_gram = second[0], second[6]
-    raw_gram = exchange_sum(raw_gram, ("wide", "narrow"))
-    pair = np.arange(5)[:, None, None]
+    everyone = lax.all_to_all(raw_gram, ("wide", "narrow"), 0, 0, tiled=True)
+    raw_gram = jnp.sum(everyone, axis=0).reshape(5, VECS, VECS)
+    shift = np.arange(VECS)[:, None, None]
     row_c = np.arange(VECS)[None, :, None]
     col_d = np.arange(VECS)[None, None, :]
-    gram_parts = raw_gram[pair * VECS + (row_c - col_d) % VECS, np.broadcast_to(row_c, (5, VECS, VECS))]
+    pick = jnp.asarray(((row_c - col_d) % VECS == shift).astype(np.float32))
+    gram_parts = jnp.sum(raw_gram[:, :, :, None] * pick[None], axis=1)
     normal_matrix = jnp.concatenate(
         [
             jnp.concatenate([gram_parts[1], gram_parts[3].T], 1),

time: 79.4 us -> 78.6 us (0.990)
  local copies, waits for them, and re-layouts: 9.04 us -> 7.68 us
    pallas_call x3 -> x4, local copies, waits for them, and re-layouts: 1.17 us -> 3.08 us  [apply_operator(): pl.pallas_call(functools.partial(coupling_kernel, with_gram), out_shape=t...]
    gather x1 -> x0, local copies, waits for them, and re-layouts: 1.68 us -> none  [per_device(): raw_gram[pair * VECS + (row_c - col_d) % VECS, np.broadcast_to(row_c, (5,...]
    broadcast_in_dim x2 -> x0, local copies, waits for them, and re-layouts: 1.41 us -> none  [exchange_sum(): jnp.broadcast_to(flat, (count, flat.shape[1]))]
  transfers between devices with their start and end apart: 9 -> 9, of which waited for: 4 -> 4; matrix products, arithmetic and copies ran while one was open for 1% -> 2% of each run, Pallas kernels for 0% -> 0%
where the time goes in v7:
time: 78.6 us; the launch traced here: 78 us
  starting transfers between devices  29.4 us (37%)
  Pallas kernels  22.3 us (28%)
  waiting for transfers between devices  10.9 us (14%)
  local copies, waits for them, and re-layouts  7.68 us (10%)
  other arithmetic  4.26 us (5%)
  matrix products  2 us (3%)
  between operations  1.57 us (2%)
    pallas_call x2, Pallas kernels, apply_operator(): pl.pallas_call(functools.partial(coupling_kernel, with_gram), out_shape=t...  22.3 us
    ppermute x2, starting transfers between devices, ghosts(): lax.ppermute(outgoing[0], 'wide', [(i, i + 1) for i in range(wide - 1)])  9.52 us
    all_to_all x1, starting transfers between devices, per_device(): everyone = lax.all_to_all(raw_gram, ('wide', 'narrow'), 0, 0, tiled=True)  8.94 us
    all_to_all x1, waiting for transfers between devices, per_device(): everyone = lax.all_to_all(raw_gram, ('wide', 'narrow'), 0, 0, tiled=True)  6.19 us
    ppermute x2, starting transfers between devices, ghosts(): lax.ppermute(outgoing[2], 'narrow', [(i, i + 1) for i in range(narrow - 1)])  5.72 us
    ppermute x2, waiting for transfers between devices, ghosts(): lax.ppermute(outgoing[3], 'narrow', [(i + 1, i) for i in range(narrow - 1)])  3.59 us
    pallas_call x4, local copies, waits for them, and re-layouts, apply_operator(): pl.pallas_call(functools.partial(coupling_kernel, with_gram), out_shape=t...  3.08 us
    ppermute x2, starting transfers between devices, ghosts(): lax.ppermute(outgoing[1], 'wide', [(i + 1, i) for i in range(wide - 1)])  2.58 us
  transfers between devices with their start and end apart: 9, of which 4 were waited for; matrix products, arithmetic and copies ran while one was open for 2% of the time, Pallas kernels for 0%

profile of v7, /device:TPU:0, one launch (start us, length us, event | category | flops | bytes accessed | tf_op | source)
XLA Modules:
  0.0 78.0 jit_solution(3332740714025000463)
XLA Ops:
  0.6 0.7 compare_select_fusion
  1.3 0.1 reshape.68
  1.4 1.7 %gather_fusion = f32[128,256]{1,0:T(8,128)S(1)} fusion(f32[128,256]{1,0:T(8,128)} %own_ref.1, s32[1024]{0:T(1024)S(1)} %pad_clamp_fusion), kind=kCustom, calls=%fused_computation | custom fusion | bytes 262656 | tf_op jit(solution)/shard_map/gather | solution.py:258
  3.1 4.8 %collective-permute-start = (f32[32,256]{1,0:T(8,128)S(1)}, f32[32,256]{1,0:T(8,128)S(1)}, u32[]{:S(2)}, u32[]{:S(2)}) collective-permute-start(f32[32,256]{1,0:T(8,128)S(1)} %get-tuple-element.32), channel_id=1, source_target_pairs={{0,4},{4,8},{8,12},{12,16},{16,20},{20,24},{24,28},{1,5},{5,9},{9,... | collective-permute-start | bytes 98312 | tf_op jit(solution)/shard_map/ppermute | solution.py:251
  7.9 1.3 %collective-permute-start.1 = (f32[32,256]{1,0:T(8,128)S(1)}, f32[32,256]{1,0:T(8,128)S(1)}, u32[]{:S(2)}, u32[]{:S(2)}) collective-permute-start(f32[32,256]{1,0:T(8,128)S(1)} %get-tuple-element.31), channel_id=1, source_target_pairs={{4,0},{8,4},{12,8},{16,12},{20,16},{24,20},{28,24},{5,1},{9,5},{13... | collective-permute-start | bytes 98312 | tf_op jit(solution)/shard_map/ppermute | solution.py:252
  9.2 1.5 %collective-permute-start.2 = (f32[32,256]{1,0:T(8,128)S(1)}, f32[32,256]{1,0:T(8,128)S(1)}, u32[]{:S(2)}, u32[]{:S(2)}) collective-permute-start(f32[32,256]{1,0:T(8,128)S(1)} %get-tuple-element.30), channel_id=1, source_target_pairs={{0,1},{1,2},{2,3},{4,5},{5,6},{6,7},{8,9},{9,10},{10,11},{12,13},{... | collective-permute-start | bytes 98312 | tf_op jit(solution)/shard_map/ppermute | solution.py:253
  10.7 1.3 %collective-permute-start.3 = (f32[32,256]{1,0:T(8,128)S(1)}, f32[32,256]{1,0:T(8,128)S(1)}, u32[]{:S(2)}, u32[]{:S(2)}) collective-permute-start(f32[32,256]{1,0:T(8,128)S(1)} %get-tuple-element.29), channel_id=1, source_target_pairs={{1,0},{2,1},{3,2},{5,4},{6,5},{7,6},{9,8},{10,9},{11,10},{13,12},{... | collective-permute-start | bytes 98312 | tf_op jit(solution)/shard_map/ppermute | solution.py:254
  12.7 1.1 %collective-permute-done.1.g1_ref = f32[32,256]{1,0:T(8,128)S(1)} collective-permute-done((f32[32,256]{1,0:T(8,128)S(1)}, f32[32,256]{1,0:T(8,128)S(1)}, u32[]{:S(2)}, u32[]{:S(2)}) %collective-permute-start.1) | collective-permute-done | bytes 32800 | tf_op jit(solution)/shard_map/ppermute | solution.py:252
  13.8 1.6 %collective-permute-done.3.g3_ref = f32[32,256]{1,0:T(8,128)S(1)} collective-permute-done((f32[32,256]{1,0:T(8,128)S(1)}, f32[32,256]{1,0:T(8,128)S(1)}, u32[]{:S(2)}, u32[]{:S(2)}) %collective-permute-start.3) | collective-permute-done | bytes 32800 | tf_op jit(solution)/shard_map/ppermute | solution.py:254
  15.4 0.6 copy-done.9
  16.0 11.0 %shard_map.77 = (f32[128,256]{1,0:T(8,128)}, f32[32,256]{1,0:T(8,128)}, f32[32,256]{1,0:T(8,128)}, f32[32,256]{1,0:T(8,128)}, f32[32,256]{1,0:T(8,128)}, /*index=5*/f32[128,256]{1,0:T(8,128)}) custom-call(s32[1]{0:T(128)S(6)} %copy.111.count_ref, s32[4,32]{1,0:T(4,128)} %bitcast.54, f32[5,128,4096]{2,1,0:T(8,128)} %bitcast.45, f32[128,256]{1,0:T(8,128)} %own_ref.1, ...), custom_call_target="tpu_custom_call" | custom-call | flops 557842432 | bytes 11272192 | tf_op jit(solution)/shard_map/pallas_call | solution.py:223
  27.0 4.7 %collective-permute-start.4 = (f32[32,256]{1,0:T(8,128)}, f32[32,256]{1,0:T(8,128)S(1)}, u32[]{:S(2)}, u32[]{:S(2)}) collective-permute-start(f32[32,256]{1,0:T(8,128)} %get-tuple-element.11), channel_id=1, source_target_pairs={{0,4},{4,8},{8,12},{12,16},{16,20},{20,24},{24,28},{1,5},{5,9},{9,... | collective-permute-start | bytes 98312 | tf_op jit(solution)/shard_map/ppermute | solution.py:251
  31.7 1.3 %collective-permute-start.5 = (f32[32,256]{1,0:T(8,128)}, f32[32,256]{1,0:T(8,128)S(1)}, u32[]{:S(2)}, u32[]{:S(2)}) collective-permute-start(f32[32,256]{1,0:T(8,128)} %get-tuple-element.12), channel_id=1, source_target_pairs={{4,0},{8,4},{12,8},{16,12},{20,16},{24,20},{28,24},{5,1},{9,5},{13... | collective-permute-start | bytes 98312 | tf_op jit(solution)/shard_map/ppermute | solution.py:252
  33.0 4.3 %collective-permute-start.6 = (f32[32,256]{1,0:T(8,128)}, f32[32,256]{1,0:T(8,128)S(1)}, u32[]{:S(2)}, u32[]{:S(2)}) collective-permute-start(f32[32,256]{1,0:T(8,128)} %get-tuple-element.13), channel_id=1, source_target_pairs={{0,1},{1,2},{2,3},{4,5},{5,6},{6,7},{8,9},{9,10},{10,11},{12,13},{... | collective-permute-start | bytes 98312 | tf_op jit(solution)/shard_map/ppermute | solution.py:253
  37.3 1.3 %collective-permute-start.7 = (f32[32,256]{1,0:T(8,128)}, f32[32,256]{1,0:T(8,128)S(1)}, u32[]{:S(2)}, u32[]{:S(2)}) collective-permute-start(f32[32,256]{1,0:T(8,128)} %get-tuple-element.14), channel_id=1, source_target_pairs={{1,0},{2,1},{3,2},{5,4},{6,5},{7,6},{9,8},{10,9},{11,10},{13,12},{... | collective-permute-start | bytes 98312 | tf_op jit(solution)/shard_map/ppermute | solution.py:254
  38.6 0.0 collective-permute-done.4.g0_ref
  38.6 1.9 %collective-permute-done.7.g3_ref = f32[32,256]{1,0:T(8,128)S(1)} collective-permute-done((f32[32,256]{1,0:T(8,128)}, f32[32,256]{1,0:T(8,128)S(1)}, u32[]{:S(2)}, u32[]{:S(2)}) %collective-permute-start.7) | collective-permute-done | bytes 32800 | tf_op jit(solution)/shard_map/ppermute | solution.py:254
  40.6 0.6 copy-done.8
  41.2 11.3 %shard_map.78 = (f32[128,256]{1,0:T(8,128)}, f32[32,256]{1,0:T(8,128)}, f32[32,256]{1,0:T(8,128)}, f32[32,256]{1,0:T(8,128)}, f32[32,256]{1,0:T(8,128)}, /*index=5*/f32[128,256]{1,0:T(8,128)}, f32[32,20,4]{2,1,0:T(8,128)}) custom-call(s32[1]{0:T(128)S(6)} %copy.111.count_ref, s32[4,32]{1,0:T(4,128)} %bitcast.55, f32[5,128,4096]{2,1,0:T(8,128)} %bitcast.46, ...), custom_call_target="tpu_custom_call" | custom-call | flops 557842432 | bytes 11272192 | tf_op jit(solution)/shard_map/pallas_call | solution.py:223
  52.5 1.9 %copy.76 = f32[32,20,4]{1,2,0:T(4,128)} copy(f32[32,20,4]{2,1,0:T(8,128)} %get-tuple-element.16) | data formatting | bytes 20480 | tf_op jit(solution)/shard_map/pallas_call | solution.py:223
  54.4 8.9 %all-to-all-start = ((f32[32,20,4]{1,2,0:T(4,128)}), f32[32,20,4]{1,2,0:T(4,128)S(1)}, u32[]{:S(2)}, u32[]{:S(2)}) async-start(f32[32,20,4]{1,2,0:T(4,128)} %copy.76), calls=%async_computation | async-start | bytes 131072 | tf_op jit(solution)/shard_map/all_to_all | solution.py:263
  63.4 0.1 copy.87
  63.5 0.1 copy.85
  63.6 1.0 %copy.91 = f32[128,256]{0,1:T(8,128)S(1)} copy(f32[128,256]{1,0:T(8,128)} %get-tuple-element.17) | data formatting | bytes 262144 | tf_op jit(solution)/shard_map/pallas_call | solution.py:223
  64.6 6.2 %all-to-all-done = f32[32,20,4]{1,2,0:T(4,128)S(1)} async-done(((f32[32,20,4]{1,2,0:T(4,128)}), f32[32,20,4]{1,2,0:T(4,128)S(1)}, u32[]{:S(2)}, u32[]{:S(2)}) %all-to-all-start) | async-done | bytes 10272 | tf_op jit(solution)/shard_map/all_to_all | solution.py:263
  70.8 0.1 reshape.86
  70.9 0.1 copy.79
  71.0 0.1 multiply_reduce_fusion
  71.1 0.2 fusion.27
  71.3 0.1 copy.98
  71.4 0.1 copy.99
  71.5 0.1 copy.81
  71.6 0.1 maximum_maximum_fusion
  71.7 0.1 copy.83
  71.8 0.7 cholesky.16
  72.5 0.1 select_reduce_fusion
  72.5 0.6 compare_reduce_fusion
  73.2 0.6 fusion.8
  73.8 0.6 custom-call.10
  74.5 0.2 fusion.9
  74.6 0.1 fusion.14
  74.8 0.4 fusion.5
  75.2 0.4 fusion
  75.7 0.1 copy.94
  75.8 0.7 sub.3
  76.4 0.4 fusion.3
  76.8 0.4 fusion.1
  77.3 0.8 copy.95
  (30 shorter events, 0.1 us)
Async XLA Ops:
  3.1 9.6 %collective-permute-start = (f32[32,256]{1,0:T(8,128)S(1)}, f32[32,256]{1,0:T(8,128)S(1)}, u32[]{:S(2)}, u32[]{:S(2)}) collective-permute-start(f32[32,256]{1,0:T(8,128)S(1)} %get-tuple-element.32), channel_id=1, source_target_pairs={{0,4},{4,8},{8,12},{12,16},{16,20},{20,24},{24,28},{1,5},{5,9},{9,... | collective-permute-start | bytes 98312 | tf_op jit(solution)/shard_map/ppermute | solution.py:251
  7.9 5.8 %collective-permute-start.1 = (f32[32,256]{1,0:T(8,128)S(1)}, f32[32,256]{1,0:T(8,128)S(1)}, u32[]{:S(2)}, u32[]{:S(2)}) collective-permute-start(f32[32,256]{1,0:T(8,128)S(1)} %get-tuple-element.31), channel_id=1, source_target_pairs={{4,0},{8,4},{12,8},{16,12},{20,16},{24,20},{28,24},{5,1},{9,5},{13... | collective-permute-start | bytes 98312 | tf_op jit(solution)/shard_map/ppermute | solution.py:252
  9.2 4.5 %collective-permute-start.2 = (f32[32,256]{1,0:T(8,128)S(1)}, f32[32,256]{1,0:T(8,128)S(1)}, u32[]{:S(2)}, u32[]{:S(2)}) collective-permute-start(f32[32,256]{1,0:T(8,128)S(1)} %get-tuple-element.30), channel_id=1, source_target_pairs={{0,1},{1,2},{2,3},{4,5},{5,6},{6,7},{8,9},{9,10},{10,11},{12,13},{... | collective-permute-start | bytes 98312 | tf_op jit(solution)/shard_map/ppermute | solution.py:253
  10.7 4.7 %collective-permute-start.3 = (f32[32,256]{1,0:T(8,128)S(1)}, f32[32,256]{1,0:T(8,128)S(1)}, u32[]{:S(2)}, u32[]{:S(2)}) collective-permute-start(f32[32,256]{1,0:T(8,128)S(1)} %get-tuple-element.29), channel_id=1, source_target_pairs={{1,0},{2,1},{3,2},{5,4},{6,5},{7,6},{9,8},{10,9},{11,10},{13,12},{... | collective-permute-start | bytes 98312 | tf_op jit(solution)/shard_map/ppermute | solution.py:254
  12.7 2.7 %copy-start.3 = (f32[32,256]{1,0:T(8,128)}, f32[32,256]{1,0:T(8,128)S(1)}, u32[]{:S(2)}) copy-start(f32[32,256]{1,0:T(8,128)S(1)} %collective-permute-done.g0_ref) | copy-start | bytes 98308
  13.8 1.7 %copy-start.5 = (f32[32,256]{1,0:T(8,128)}, f32[32,256]{1,0:T(8,128)S(1)}, u32[]{:S(2)}) copy-start(f32[32,256]{1,0:T(8,128)S(1)} %collective-permute-done.1.g1_ref) | copy-start | bytes 98308
  13.8 1.7 %copy-start.7 = (f32[32,256]{1,0:T(8,128)}, f32[32,256]{1,0:T(8,128)S(1)}, u32[]{:S(2)}) copy-start(f32[32,256]{1,0:T(8,128)S(1)} %collective-permute-done.2.g2_ref) | copy-start | bytes 98308
  15.4 0.6 copy-start.9
  16.0 55.0 %copy-start.10 = (f32[4,4,4]{2,1,0:T(4,128)S(1)}, f32[4,4,4]{2,1,0:T(4,128)}, u32[]{:S(2)}) copy-start(f32[4,4,4]{2,1,0:T(4,128)} %constant.56.clone) | copy-start | bytes 772
  27.0 36.4 %copy-start.1 = (f32[128,256]{1,0:T(8,128)S(1)}, f32[128,256]{1,0:T(8,128)}, u32[]{:S(2)}) copy-start(f32[128,256]{1,0:T(8,128)} %get-tuple-element.10.own_ref) | copy-start | bytes 393220
  27.0 36.5 %copy-start = (f32[128,256]{1,0:T(8,128)S(1)}, f32[128,256]{1,0:T(8,128)}, u32[]{:S(2)}) copy-start(f32[128,256]{1,0:T(8,128)} %get-tuple-element.15.rest_0_) | copy-start | bytes 393220
  27.0 11.6 %collective-permute-start.4 = (f32[32,256]{1,0:T(8,128)}, f32[32,256]{1,0:T(8,128)S(1)}, u32[]{:S(2)}, u32[]{:S(2)}) collective-permute-start(f32[32,256]{1,0:T(8,128)} %get-tuple-element.11), channel_id=1, source_target_pairs={{0,4},{4,8},{8,12},{12,16},{16,20},{20,24},{24,28},{1,5},{5,9},{9,... | collective-permute-start | bytes 98312 | tf_op jit(solution)/shard_map/ppermute | solution.py:251
  31.7 6.9 %collective-permute-start.5 = (f32[32,256]{1,0:T(8,128)}, f32[32,256]{1,0:T(8,128)S(1)}, u32[]{:S(2)}, u32[]{:S(2)}) collective-permute-start(f32[32,256]{1,0:T(8,128)} %get-tuple-element.12), channel_id=1, source_target_pairs={{4,0},{8,4},{12,8},{16,12},{20,16},{24,20},{28,24},{5,1},{9,5},{13... | collective-permute-start | bytes 98312 | tf_op jit(solution)/shard_map/ppermute | solution.py:252
  33.0 5.6 %collective-permute-start.6 = (f32[32,256]{1,0:T(8,128)}, f32[32,256]{1,0:T(8,128)S(1)}, u32[]{:S(2)}, u32[]{:S(2)}) collective-permute-start(f32[32,256]{1,0:T(8,128)} %get-tuple-element.13), channel_id=1, source_target_pairs={{0,1},{1,2},{2,3},{4,5},{5,6},{6,7},{8,9},{9,10},{10,11},{12,13},{... | collective-permute-start | bytes 98312 | tf_op jit(solution)/shard_map/ppermute | solution.py:253
  37.3 3.3 %collective-permute-start.7 = (f32[32,256]{1,0:T(8,128)}, f32[32,256]{1,0:T(8,128)S(1)}, u32[]{:S(2)}, u32[]{:S(2)}) collective-permute-start(f32[32,256]{1,0:T(8,128)} %get-tuple-element.14), channel_id=1, source_target_pairs={{1,0},{2,1},{3,2},{5,4},{6,5},{7,6},{9,8},{10,9},{11,10},{13,12},{... | collective-permute-start | bytes 98312 | tf_op jit(solution)/shard_map/ppermute | solution.py:254
  38.6 2.0 %copy-start.2 = (f32[32,256]{1,0:T(8,128)}, f32[32,256]{1,0:T(8,128)S(1)}, u32[]{:S(2)}) copy-start(f32[32,256]{1,0:T(8,128)S(1)} %collective-permute-done.4.g0_ref) | copy-start | bytes 98308
  38.6 2.0 %copy-start.4 = (f32[32,256]{1,0:T(8,128)}, f32[32,256]{1,0:T(8,128)S(1)}, u32[]{:S(2)}) copy-start(f32[32,256]{1,0:T(8,128)S(1)} %collective-permute-done.5.g1_ref) | copy-start | bytes 98308
  38.6 2.0 %copy-start.6 = (f32[32,256]{1,0:T(8,128)}, f32[32,256]{1,0:T(8,128)S(1)}, u32[]{:S(2)}) copy-start(f32[32,256]{1,0:T(8,128)S(1)} %collective-permute-done.6.g2_ref) | copy-start | bytes 98308
  40.6 0.6 copy-start.8
  54.4 16.4 %all-to-all-start = ((f32[32,20,4]{1,2,0:T(4,128)}), f32[32,20,4]{1,2,0:T(4,128)S(1)}, u32[]{:S(2)}, u32[]{:S(2)}) async-start(f32[32,20,4]{1,2,0:T(4,128)} %copy.76), calls=%async_computation | async-start | bytes 131072 | tf_op jit(solution)/shard_map/all_to_all | solution.py:263

commit v8 on v7

--- a/solution.py
+++ b/solution.py
@@ -95,13 +95,24 @@
     )
 
 
-def gram_rows(pairs):
+def gram_columns(pairs):
     rows = []
     for left, right in pairs:
         for shift in range(VECS):
             moved = right if shift == 0 else pltpu.roll(right, shift * BLK, 1)
             rows.append(jnp.sum(left * moved, axis=0, keepdims=True))
-    return segment_sums(jnp.concatenate(rows, axis=0), VECS)
+    stacked = jnp.concatenate(rows, axis=0)
+    width = stacked.shape[1]
+    seg = (
+        lax.broadcasted_iota(jnp.int32, (VECS, width), 1) // BLK
+        == lax.broadcasted_iota(jnp.int32, (VECS, width), 0)
+    ).astype(jnp.bfloat16)
+    parts = split_three(stacked)
+    dims = (((1,), (1,)), ((), ()))
+    return sum(
+        lax.dot_general(seg, parts[:, p * width:(p + 1) * width], dims, preferred_element_type=jnp.float32)
+        for p in range(3)
+    )
 
 
 def coupling_kernel(with_gram, count_ref, lend_ref, jac_ref, own_ref, g0_ref, g1_ref, g2_ref, g3_ref, cols_ref, *rest):
@@ -191,7 +202,7 @@
                 lent_ref[j:j + 1, :] = out_ref[pl.ds(lend_ref[q, j], 1), :]
         if with_gram:
             anchor = anchor_ref[...]
-            partial = gram_rows(((kept, anchor), (kept, kept), (image, anchor), (image, kept), (image, image)))
+            partial = gram_columns(((kept, anchor), (kept, kept), (image, anchor), (image, kept), (image, image)))
             for target in range(gram_ref.shape[0]):
                 gram_ref[target] = partial
 
@@ -218,8 +229,8 @@
         in_specs.append(whole)
         args.append(anchor)
         gram_count = 5 * VECS
-        out_shape.append(jax.ShapeDtypeStruct((peers, gram_count, VECS), jnp.float32))
-        out_specs.append(pl.BlockSpec((peers, gram_count, VECS), lambda b: (0, 0, 0)))
+        out_shape.append(jax.ShapeDtypeStruct((peers, VECS, gram_count), jnp.float32))
+        out_specs.append(pl.BlockSpec((peers, VECS, gram_count), lambda b: (0, 0, 0)))
     return pl.pallas_call(
         functools.partial(coupling_kernel, with_gram),
         out_shape=tuple(out_shape),
@@ -241,6 +252,41 @@
     )(*args)
 
 
+def mixing_kernel(mix_ref, anchor_ref, first_ref, second_ref, correction_ref, residual_ref):
+    width = anchor_ref.shape[1]
+    segment = lax.broadcasted_iota(jnp.int32, (1, width), 1) // BLK
+
+    def weights(row_offset, shift):
+        out = jnp.zeros((1, width), jnp.float32)
+        for d in range(VECS):
+            out = jnp.where(segment == d, mix_ref[row_offset + (d - shift) % VECS, d], out)
+        return out
+
+    def mixed(values, row_offset):
+        total = None
+        for shift in range(VECS):
+            moved = values if shift == 0 else pltpu.roll(values, shift * BLK, 1)
+            term = moved * weights(row_offset, shift)
+            total = term if total is None else total + term
+        return total
+
+    anchor = anchor_ref[...]
+    first = first_ref[...]
+    second = second_ref[...]
+    correction_ref[...] = mixed(anchor, 0) + mixed(first, VECS)
+    residual_ref[...] = anchor - (mixed(first, 0) + mixed(second, VECS))
+
+
+def mix_outputs(coefficients, anchor, first, second):
+    whole = pl.BlockSpec(memory_space=pltpu.VMEM)
+    return pl.pallas_call(
+        mixing_kernel,
+        out_shape=(jax.ShapeDtypeStruct(anchor.shape, jnp.float32),) * 2,
+        in_specs=[pl.BlockSpec(memory_space=pltpu.SMEM), whole, whole, whole],
+        out_specs=(whole, whole),
+    )(coefficients, anchor, first, second)
+
+
 def per_device(start_block, jacobian, counts, columns, send_list):
     lend_rows = send_list[0]
     jac_t = jnp.transpose(jacobian, (1, 0, 2))
@@ -261,7 +307,7 @@
     second = apply_operator(jac_t, first_image, ghosts(first_lent), cols_t, counts, lend_rows, anchor, peers)
     second_image, raw_gram = second[0], second[6]
     everyone = lax.all_to_all(raw_gram, ("wide", "narrow"), 0, 0, tiled=True)
-    raw_gram = jnp.sum(everyone, axis=0).reshape(5, VECS, VECS)
+    raw_gram = jnp.transpose(jnp.sum(everyone, axis=0), (1, 0)).reshape(5, VECS, VECS)
     shift = np.arange(VECS)[:, None, None]
     row_c = np.arange(VECS)[None, :, None]
     col_d = np.arange(VECS)[None, None, :]
@@ -277,11 +323,7 @@
     right_terms = jnp.concatenate([gram_parts[0], gram_parts[2]], 0)
     factor = jnp.linalg.cholesky(normal_matrix)
     coefficients = jax.scipy.linalg.cho_solve((factor, True), right_terms)
-    correction = combine(anchor, coefficients[:VECS]) + combine(first_image, coefficients[VECS:])
-    residual = anchor - (
-        combine(first_image, coefficients[:VECS]) + combine(second_image, coefficients[VECS:])
-    )
-    return (correction, residual)
+    return mix_outputs(coefficients, anchor, first_image, second_image)
 
 
 def solution(mesh):

time: 78.6 us -> 76.1 us (0.968)
  blocking collectives: 0 us -> 17.4 us
  starting transfers between devices: 29.4 us -> 20.2 us
  waiting for transfers between devices: 10.9 us -> 4.2 us
  local copies, waits for them, and re-layouts: 7.68 us -> 3.73 us
  Pallas kernels: 22.3 us -> 24.1 us
  matrix products: 2 us -> 0.93 us
    all_to_all x0 -> x1, blocking collectives: none -> 17.4 us  [per_device(): everyone = lax.all_to_all(raw_gram, ('wide', 'narrow'), 0, 0, tiled=True)]
    all_to_all x1 -> x0, starting transfers between devices: 8.94 us -> none  [per_device(): everyone = lax.all_to_all(raw_gram, ('wide', 'narrow'), 0, 0, tiled=True)]
    all_to_all x1 -> x0, waiting for transfers between devices: 6.19 us -> none  [per_device(): everyone = lax.all_to_all(raw_gram, ('wide', 'narrow'), 0, 0, tiled=True)]
    ppermute x2, waiting for transfers between devices: 3.59 us -> 0.19 us  [ghosts(): lax.ppermute(outgoing[3], 'narrow', [(i + 1, i) for i in range(narrow - 1)])]
    pallas_call x4 -> x0, local copies, waits for them, and re-layouts: 3.08 us -> none  [apply_operator(): pl.pallas_call(functools.partial(coupling_kernel, with_gram), out_shape=t...]
    ppermute x2, waiting for transfers between devices: 1.07 us -> 3.14 us  [ghosts(): lax.ppermute(outgoing[1], 'wide', [(i + 1, i) for i in range(wide - 1)])]
    pallas_call x0 -> x1, Pallas kernels: none -> 1.93 us  [mix_outputs(): pl.pallas_call(mixing_kernel, out_shape=(jax.ShapeDtypeStruct(anchor.shap...]
    dot_general x4 -> x0, matrix products: 1.66 us -> none  [combine(): jnp.einsum('eci,cd->edi', shaped, mixing, precision=lax.Precision.HIGHEST)]
  transfers between devices with their start and end apart: 9 -> 8, of which waited for: 4 -> 3; matrix products, arithmetic and copies ran while one was open for 2% -> 0% of each run, Pallas kernels for 0% -> 0%
where the time goes in v8:
time: 76.1 us; the launch traced here: 75.6 us
  Pallas kernels  24.1 us (32%)
  starting transfers between devices  20.2 us (27%)
  blocking collectives  17.4 us (23%)
  waiting for transfers between devices  4.2 us (6%)
  local copies, waits for them, and re-layouts  3.73 us (5%)
  other arithmetic  3.58 us (5%)
  between operations  1.46 us (2%)
  matrix products  0.93 us (1%)
    pallas_call x2, Pallas kernels, apply_operator(): pl.pallas_call(functools.partial(coupling_kernel, with_gram), out_shape=t...  22.2 us
    all_to_all x1, blocking collectives, per_device(): everyone = lax.all_to_all(raw_gram, ('wide', 'narrow'), 0, 0, tiled=True)  17.4 us
    ppermute x2, starting transfers between devices, ghosts(): lax.ppermute(outgoing[0], 'wide', [(i, i + 1) for i in range(wide - 1)])  10.4 us
    ppermute x2, starting transfers between devices, ghosts(): lax.ppermute(outgoing[2], 'narrow', [(i, i + 1) for i in range(narrow - 1)])  4.66 us
    ppermute x2, waiting for transfers between devices, ghosts(): lax.ppermute(outgoing[1], 'wide', [(i + 1, i) for i in range(wide - 1)])  3.14 us
    ppermute x2, starting transfers between devices, ghosts(): lax.ppermute(outgoing[3], 'narrow', [(i + 1, i) for i in range(narrow - 1)])  2.58 us
    ppermute x2, starting transfers between devices, ghosts(): lax.ppermute(outgoing[1], 'wide', [(i + 1, i) for i in range(wide - 1)])  2.58 us
    pallas_call x1, Pallas kernels, mix_outputs(): pl.pallas_call(mixing_kernel, out_shape=(jax.ShapeDtypeStruct(anchor.shap...  1.93 us
  transfers between devices with their start and end apart: 8, of which 3 were waited for; matrix products, arithmetic and copies ran while one was open for 0% of the time, Pallas kernels for 0%

profile of v8, /device:TPU:0, one launch (start us, length us, event | category | flops | bytes accessed | tf_op | source)
XLA Modules:
  0.0 75.6 jit_solution(7114969498945352395)
XLA Ops:
  0.6 0.7 compare_select_fusion
  1.3 0.1 reshape.49
  1.4 1.7 %gather_fusion = f32[128,256]{1,0:T(8,128)S(1)} fusion(f32[128,256]{1,0:T(8,128)} %own_ref.1, s32[1024]{0:T(1024)S(1)} %pad_clamp_fusion), kind=kCustom, calls=%fused_computation | custom fusion | bytes 262656 | tf_op jit(solution)/shard_map/gather | solution.py:304
  3.1 1.3 %collective-permute-start.3 = (f32[32,256]{1,0:T(8,128)S(1)}, f32[32,256]{1,0:T(8,128)S(1)}, u32[]{:S(2)}, u32[]{:S(2)}) collective-permute-start(f32[32,256]{1,0:T(8,128)S(1)} %get-tuple-element.21), channel_id=1, source_target_pairs={{1,0},{2,1},{3,2},{5,4},{6,5},{7,6},{9,8},{10,9},{11,10},{13,12},{... | collective-permute-start | bytes 98312 | tf_op jit(solution)/shard_map/ppermute | solution.py:300
  4.4 3.0 %collective-permute-start.2 = (f32[32,256]{1,0:T(8,128)S(1)}, f32[32,256]{1,0:T(8,128)S(1)}, u32[]{:S(2)}, u32[]{:S(2)}) collective-permute-start(f32[32,256]{1,0:T(8,128)S(1)} %get-tuple-element.22), channel_id=1, source_target_pairs={{0,1},{1,2},{2,3},{4,5},{5,6},{6,7},{8,9},{9,10},{10,11},{12,13},{... | collective-permute-start | bytes 98312 | tf_op jit(solution)/shard_map/ppermute | solution.py:299
  7.4 1.3 %collective-permute-start.1 = (f32[32,256]{1,0:T(8,128)S(1)}, f32[32,256]{1,0:T(8,128)S(1)}, u32[]{:S(2)}, u32[]{:S(2)}) collective-permute-start(f32[32,256]{1,0:T(8,128)S(1)} %get-tuple-element.23), channel_id=1, source_target_pairs={{4,0},{8,4},{12,8},{16,12},{20,16},{24,20},{28,24},{5,1},{9,5},{13... | collective-permute-start | bytes 98312 | tf_op jit(solution)/shard_map/ppermute | solution.py:298
  8.7 5.5 %collective-permute-start = (f32[32,256]{1,0:T(8,128)S(1)}, f32[32,256]{1,0:T(8,128)S(1)}, u32[]{:S(2)}, u32[]{:S(2)}) collective-permute-start(f32[32,256]{1,0:T(8,128)S(1)} %get-tuple-element.24), channel_id=1, source_target_pairs={{0,4},{4,8},{8,12},{12,16},{16,20},{20,24},{24,28},{1,5},{5,9},{9,... | collective-permute-start | bytes 98312 | tf_op jit(solution)/shard_map/ppermute | solution.py:297
  14.9 0.0 collective-permute-done.3.g3_ref
  14.9 0.0 copy-start.1
  14.9 0.0 collective-permute-done.2.g2_ref
  14.9 0.0 copy-start.3
  14.9 0.0 collective-permute-done.1.g1_ref
  14.9 0.0 copy-start.5
  14.9 0.9 %collective-permute-done.g0_ref = f32[32,256]{1,0:T(8,128)S(1)} collective-permute-done((f32[32,256]{1,0:T(8,128)S(1)}, f32[32,256]{1,0:T(8,128)S(1)}, u32[]{:S(2)}, u32[]{:S(2)}) %collective-permute-start) | collective-permute-done | bytes 32800 | tf_op jit(solution)/shard_map/ppermute | solution.py:297
  15.8 0.0 copy-done.3
  15.8 0.6 copy-done.7
  16.4 11.0 %shard_map.77 = (f32[128,256]{1,0:T(8,128)}, f32[32,256]{1,0:T(8,128)}, f32[32,256]{1,0:T(8,128)}, f32[32,256]{1,0:T(8,128)}, f32[32,256]{1,0:T(8,128)}, /*index=5*/f32[128,256]{1,0:T(8,128)}) custom-call(s32[1]{0:T(128)S(6)} %copy.39.count_ref, s32[4,32]{1,0:T(4,128)} %bitcast.30, f32[5,128,4096]{2,1,0:T(8,128)} %bitcast.27, f32[128,256]{1,0:T(8,128)} %own_ref.1, ...), custom_call_target="tpu_custom_call" | custom-call | flops 557842432 | bytes 11272192 | tf_op jit(solution)/shard_map/pallas_call | solution.py:234
  27.4 4.9 %collective-permute-start.4 = (f32[32,256]{1,0:T(8,128)}, f32[32,256]{1,0:T(8,128)S(1)}, u32[]{:S(2)}, u32[]{:S(2)}) collective-permute-start(f32[32,256]{1,0:T(8,128)} %get-tuple-element.11), channel_id=1, source_target_pairs={{0,4},{4,8},{8,12},{12,16},{16,20},{20,24},{24,28},{1,5},{5,9},{9,... | collective-permute-start | bytes 98312 | tf_op jit(solution)/shard_map/ppermute | solution.py:297
  32.3 1.3 %collective-permute-start.5 = (f32[32,256]{1,0:T(8,128)}, f32[32,256]{1,0:T(8,128)S(1)}, u32[]{:S(2)}, u32[]{:S(2)}) collective-permute-start(f32[32,256]{1,0:T(8,128)} %get-tuple-element.12), channel_id=1, source_target_pairs={{4,0},{8,4},{12,8},{16,12},{20,16},{24,20},{28,24},{5,1},{9,5},{13... | collective-permute-start | bytes 98312 | tf_op jit(solution)/shard_map/ppermute | solution.py:298
  33.6 1.6 %collective-permute-start.6 = (f32[32,256]{1,0:T(8,128)}, f32[32,256]{1,0:T(8,128)S(1)}, u32[]{:S(2)}, u32[]{:S(2)}) collective-permute-start(f32[32,256]{1,0:T(8,128)} %get-tuple-element.13), channel_id=1, source_target_pairs={{0,1},{1,2},{2,3},{4,5},{5,6},{6,7},{8,9},{9,10},{10,11},{12,13},{... | collective-permute-start | bytes 98312 | tf_op jit(solution)/shard_map/ppermute | solution.py:299
  35.2 1.3 %collective-permute-start.7 = (f32[32,256]{1,0:T(8,128)}, f32[32,256]{1,0:T(8,128)S(1)}, u32[]{:S(2)}, u32[]{:S(2)}) collective-permute-start(f32[32,256]{1,0:T(8,128)} %get-tuple-element.14), channel_id=1, source_target_pairs={{1,0},{2,1},{3,2},{5,4},{6,5},{7,6},{9,8},{10,9},{11,10},{13,12},{... | collective-permute-start | bytes 98312 | tf_op jit(solution)/shard_map/ppermute | solution.py:300
  36.5 0.0 collective-permute-done.4.g0_ref
  36.5 3.1 %collective-permute-done.5.g1_ref = f32[32,256]{1,0:T(8,128)S(1)} collective-permute-done((f32[32,256]{1,0:T(8,128)}, f32[32,256]{1,0:T(8,128)S(1)}, u32[]{:S(2)}, u32[]{:S(2)}) %collective-permute-start.5) | collective-permute-done | bytes 32800 | tf_op jit(solution)/shard_map/ppermute | solution.py:298
  39.7 0.0 collective-permute-done.6.g2_ref
  39.7 0.2 collective-permute-done.7.g3_ref
  39.9 0.4 copy-done.2
  40.3 0.0 copy-done.4
  40.3 0.2 copy-done.6
  40.5 11.2 %shard_map.78 = (f32[128,256]{1,0:T(8,128)}, f32[32,256]{1,0:T(8,128)}, f32[32,256]{1,0:T(8,128)}, f32[32,256]{1,0:T(8,128)}, f32[32,256]{1,0:T(8,128)}, /*index=5*/f32[128,256]{1,0:T(8,128)}, f32[32,4,20]{2,1,0:T(4,128)}) custom-call(s32[1]{0:T(128)S(6)} %copy.39.count_ref, s32[4,32]{1,0:T(4,128)} %bitcast.31, f32[5,128,4096]{2,1,0:T(8,128)} %bitcast.28, ...), custom_call_target="tpu_custom_call" | custom-call | flops 557842432 | bytes 11272192 | tf_op jit(solution)/shard_map/pallas_call | solution.py:234
  51.7 17.4 %all_to_all.5 = f32[32,4,20]{2,1,0:T(4,128)S(1)} all-to-all(f32[32,4,20]{2,1,0:T(4,128)} %get-tuple-element.16), channel_id=1, replica_groups=mesh['wide'=8,'narrow'=4] {'wide','narrow'}, dimensions={0} | all-to-all | bytes 20480 | tf_op jit(solution)/shard_map/all_to_all | solution.py:309
  69.1 0.1 mul.15
  69.2 0.1 copy.29
  69.3 0.0 copy-done.8
  69.3 0.1 multiply_reduce_fusion
  69.4 0.2 fusion.11
  69.5 0.1 copy.37
  69.7 0.1 copy.38
  69.8 0.1 copy.31
  69.9 0.1 maximum_maximum_fusion
  69.9 0.1 copy.33
  70.0 0.7 cholesky.16
  70.7 0.1 select_reduce_fusion
  70.8 0.6 compare_reduce_fusion
  71.4 0.6 fusion
  72.1 0.6 custom-call.10
  72.7 0.2 fusion.1
  72.9 0.7 fusion.6.mix_ref
  73.6 1.9 %shard_map.79 = (f32[128,256]{1,0:T(8,128)}, f32[128,256]{1,0:T(8,128)}) custom-call(f32[8,4]{1,0:T(8,128)} %fusion.6.mix_ref, f32[128,256]{1,0:T(8,128)} %get-tuple-element.15.rest_0_.anchor_ref, f32[128,256]{1,0:T(8,128)} %get-tuple-element.10.own_ref.first_ref, f32[128,256]{1,0:T(8,128)} %get-tuple-element.17.second_ref), custom_call_target="tpu_custom_call" | custom-call | tf_op jit(solution)/shard_map/pallas_call | solution.py:282
  (13 shorter events, 0.1 us)
Async XLA Ops:
  3.1 11.8 %collective-permute-start.3 = (f32[32,256]{1,0:T(8,128)S(1)}, f32[32,256]{1,0:T(8,128)S(1)}, u32[]{:S(2)}, u32[]{:S(2)}) collective-permute-start(f32[32,256]{1,0:T(8,128)S(1)} %get-tuple-element.21), channel_id=1, source_target_pairs={{1,0},{2,1},{3,2},{5,4},{6,5},{7,6},{9,8},{10,9},{11,10},{13,12},{... | collective-permute-start | bytes 98312 | tf_op jit(solution)/shard_map/ppermute | solution.py:300
  4.4 10.5 %collective-permute-start.2 = (f32[32,256]{1,0:T(8,128)S(1)}, f32[32,256]{1,0:T(8,128)S(1)}, u32[]{:S(2)}, u32[]{:S(2)}) collective-permute-start(f32[32,256]{1,0:T(8,128)S(1)} %get-tuple-element.22), channel_id=1, source_target_pairs={{0,1},{1,2},{2,3},{4,5},{5,6},{6,7},{8,9},{9,10},{10,11},{12,13},{... | collective-permute-start | bytes 98312 | tf_op jit(solution)/shard_map/ppermute | solution.py:299
  7.4 7.5 %collective-permute-start.1 = (f32[32,256]{1,0:T(8,128)S(1)}, f32[32,256]{1,0:T(8,128)S(1)}, u32[]{:S(2)}, u32[]{:S(2)}) collective-permute-start(f32[32,256]{1,0:T(8,128)S(1)} %get-tuple-element.23), channel_id=1, source_target_pairs={{4,0},{8,4},{12,8},{16,12},{20,16},{24,20},{28,24},{5,1},{9,5},{13... | collective-permute-start | bytes 98312 | tf_op jit(solution)/shard_map/ppermute | solution.py:298
  8.7 7.1 %collective-permute-start = (f32[32,256]{1,0:T(8,128)S(1)}, f32[32,256]{1,0:T(8,128)S(1)}, u32[]{:S(2)}, u32[]{:S(2)}) collective-permute-start(f32[32,256]{1,0:T(8,128)S(1)} %get-tuple-element.24), channel_id=1, source_target_pairs={{0,4},{4,8},{8,12},{12,16},{16,20},{20,24},{24,28},{1,5},{5,9},{9,... | collective-permute-start | bytes 98312 | tf_op jit(solution)/shard_map/ppermute | solution.py:297
  14.9 0.9 %copy-start.1 = (f32[32,256]{1,0:T(8,128)}, f32[32,256]{1,0:T(8,128)S(1)}, u32[]{:S(2)}) copy-start(f32[32,256]{1,0:T(8,128)S(1)} %collective-permute-done.3.g3_ref) | copy-start | bytes 98308
  14.9 0.9 %copy-start.3 = (f32[32,256]{1,0:T(8,128)}, f32[32,256]{1,0:T(8,128)S(1)}, u32[]{:S(2)}) copy-start(f32[32,256]{1,0:T(8,128)S(1)} %collective-permute-done.2.g2_ref) | copy-start | bytes 98308
  14.9 0.9 %copy-start.5 = (f32[32,256]{1,0:T(8,128)}, f32[32,256]{1,0:T(8,128)S(1)}, u32[]{:S(2)}) copy-start(f32[32,256]{1,0:T(8,128)S(1)} %collective-permute-done.1.g1_ref) | copy-start | bytes 98308
  15.8 0.6 copy-start.7
  16.4 52.9 %copy-start.8 = (f32[4,4,4]{2,1,0:T(4,128)S(1)}, f32[4,4,4]{2,1,0:T(4,128)}, u32[]{:S(2)}) copy-start(f32[4,4,4]{2,1,0:T(4,128)} %constant.56.clone) | copy-start | bytes 772
  27.4 9.1 %collective-permute-start.4 = (f32[32,256]{1,0:T(8,128)}, f32[32,256]{1,0:T(8,128)S(1)}, u32[]{:S(2)}, u32[]{:S(2)}) collective-permute-start(f32[32,256]{1,0:T(8,128)} %get-tuple-element.11), channel_id=1, source_target_pairs={{0,4},{4,8},{8,12},{12,16},{16,20},{20,24},{24,28},{1,5},{5,9},{9,... | collective-permute-start | bytes 98312 | tf_op jit(solution)/shard_map/ppermute | solution.py:297
  32.3 7.4 %collective-permute-start.5 = (f32[32,256]{1,0:T(8,128)}, f32[32,256]{1,0:T(8,128)S(1)}, u32[]{:S(2)}, u32[]{:S(2)}) collective-permute-start(f32[32,256]{1,0:T(8,128)} %get-tuple-element.12), channel_id=1, source_target_pairs={{4,0},{8,4},{12,8},{16,12},{20,16},{24,20},{28,24},{5,1},{9,5},{13... | collective-permute-start | bytes 98312 | tf_op jit(solution)/shard_map/ppermute | solution.py:298
  33.6 6.1 %collective-permute-start.6 = (f32[32,256]{1,0:T(8,128)}, f32[32,256]{1,0:T(8,128)S(1)}, u32[]{:S(2)}, u32[]{:S(2)}) collective-permute-start(f32[32,256]{1,0:T(8,128)} %get-tuple-element.13), channel_id=1, source_target_pairs={{0,1},{1,2},{2,3},{4,5},{5,6},{6,7},{8,9},{9,10},{10,11},{12,13},{... | collective-permute-start | bytes 98312 | tf_op jit(solution)/shard_map/ppermute | solution.py:299
  35.2 4.6 %collective-permute-start.7 = (f32[32,256]{1,0:T(8,128)}, f32[32,256]{1,0:T(8,128)S(1)}, u32[]{:S(2)}, u32[]{:S(2)}) collective-permute-start(f32[32,256]{1,0:T(8,128)} %get-tuple-element.14), channel_id=1, source_target_pairs={{1,0},{2,1},{3,2},{5,4},{6,5},{7,6},{9,8},{10,9},{11,10},{13,12},{... | collective-permute-start | bytes 98312 | tf_op jit(solution)/shard_map/ppermute | solution.py:300
  36.5 3.3 %copy-start = (f32[32,256]{1,0:T(8,128)}, f32[32,256]{1,0:T(8,128)S(1)}, u32[]{:S(2)}) copy-start(f32[32,256]{1,0:T(8,128)S(1)} %collective-permute-done.4.g0_ref) | copy-start | bytes 98308
  39.7 0.6 copy-start.2
  39.7 0.6 copy-start.4
  39.9 0.6 copy-start.6

commit v9 on v8

--- a/solution.py
+++ b/solution.py
@@ -252,6 +252,23 @@
     )(*args)
 
 
+def lending_kernel(lend_ref, values_ref, *lent_refs):
+    for q, lent_ref in enumerate(lent_refs):
+        for j in range(lend_ref.shape[1]):
+            lent_ref[j:j + 1, :] = values_ref[pl.ds(lend_ref[q, j], 1), :]
+
+
+def lent_rows_of(values, lend_rows):
+    shape = jax.ShapeDtypeStruct((lend_rows.shape[1], values.shape[1]), values.dtype)
+    whole = pl.BlockSpec(memory_space=pltpu.VMEM)
+    return pl.pallas_call(
+        lending_kernel,
+        out_shape=(shape,) * lend_rows.shape[0],
+        in_specs=[pl.BlockSpec(memory_space=pltpu.SMEM), whole],
+        out_specs=(whole,) * lend_rows.shape[0],
+    )(lend_rows, values)
+
+
 def mixing_kernel(mix_ref, anchor_ref, first_ref, second_ref, correction_ref, residual_ref):
     width = anchor_ref.shape[1]
     segment = lax.broadcasted_iota(jnp.int32, (1, width), 1) // BLK
@@ -301,7 +318,7 @@
         )
 
     cols_t = jnp.transpose(columns, (1, 0))
-    first = apply_operator(jac_t, start_block, ghosts(start_block[lend_rows]), cols_t, counts, lend_rows)
+    first = apply_operator(jac_t, start_block, ghosts(lent_rows_of(start_block, lend_rows)), cols_t, counts, lend_rows)
     first_image, first_lent, anchor = first[0], jnp.stack(first[1:5]), first[5]
     peers = lax.axis_size("wide") * lax.axis_size("narrow")
     second = apply_operator(jac_t, first_image, ghosts(first_lent), cols_t, counts, lend_rows, anchor, peers)

time: 76.1 us -> 75.2 us (0.988)
  Pallas kernels: 24.1 us -> 25.9 us
  local copies, waits for them, and re-layouts: 3.73 us -> 1.98 us
  blocking collectives: 17.4 us -> 16.5 us
    ppermute x2, waiting for transfers between devices: 0.19 us -> 3.59 us  [ghosts(): lax.ppermute(outgoing[3], 'narrow', [(i + 1, i) for i in range(narrow - 1)])]
    ppermute x2, waiting for transfers between devices: 3.14 us -> 1.28 us  [ghosts(): lax.ppermute(outgoing[1], 'wide', [(i + 1, i) for i in range(wide - 1)])]
    pallas_call x0 -> x1, Pallas kernels: none -> 1.76 us  [lent_rows_of(): pl.pallas_call(lending_kernel, out_shape=(shape,) * lend_rows.shape[0], i...]
    gather x1 -> x0, local copies, waits for them, and re-layouts: 1.66 us -> none  [per_device(): start_block[lend_rows]]
    ppermute x2, starting transfers between devices: 4.66 us -> 5.72 us  [ghosts(): lax.ppermute(outgoing[2], 'narrow', [(i, i + 1) for i in range(narrow - 1)])]
    ppermute x2, starting transfers between devices: 10.4 us -> 9.37 us  [ghosts(): lax.ppermute(outgoing[0], 'wide', [(i, i + 1) for i in range(wide - 1)])]
    all_to_all x1, blocking collectives: 17.4 us -> 16.5 us  [per_device(): everyone = lax.all_to_all(raw_gram, ('wide', 'narrow'), 0, 0, tiled=True)]
    ppermute x2, waiting for transfers between devices: 0.87 us -> 0.01 us  [ghosts(): lax.ppermute(outgoing[0], 'wide', [(i, i + 1) for i in range(wide - 1)])]
where the time goes in v9:
time: 75.2 us; the launch traced here: 74.7 us
  Pallas kernels  25.9 us (34%)
  starting transfers between devices  20.3 us (27%)
  blocking collectives  16.5 us (22%)
  waiting for transfers between devices  4.88 us (6%)
  other arithmetic  2.89 us (4%)
  local copies, waits for them, and re-layouts  1.98 us (3%)
  between operations  1.45 us (2%)
  matrix products  0.93 us (1%)
    pallas_call x2, Pallas kernels, apply_operator(): pl.pallas_call(functools.partial(coupling_kernel, with_gram), out_shape=t...  22.2 us
    all_to_all x1, blocking collectives, per_device(): everyone = lax.all_to_all(raw_gram, ('wide', 'narrow'), 0, 0, tiled=True)  16.5 us
    ppermute x2, starting transfers between devices, ghosts(): lax.ppermute(outgoing[0], 'wide', [(i, i + 1) for i in range(wide - 1)])  9.37 us
    ppermute x2, starting transfers between devices, ghosts(): lax.ppermute(outgoing[2], 'narrow', [(i, i + 1) for i in range(narrow - 1)])  5.72 us
    ppermute x2, waiting for transfers between devices, ghosts(): lax.ppermute(outgoing[3], 'narrow', [(i + 1, i) for i in range(narrow - 1)])  3.59 us
    ppermute x2, starting transfers between devices, ghosts(): lax.ppermute(outgoing[1], 'wide', [(i + 1, i) for i in range(wide - 1)])  2.58 us
    ppermute x2, starting transfers between devices, ghosts(): lax.ppermute(outgoing[3], 'narrow', [(i + 1, i) for i in range(narrow - 1)])  2.58 us
    pallas_call x1, Pallas kernels, mix_outputs(): pl.pallas_call(mixing_kernel, out_shape=(jax.ShapeDtypeStruct(anchor.shap...  1.93 us
  transfers between devices with their start and end apart: 8, of which 3 were waited for; matrix products, arithmetic and copies ran while one was open for 0% of the time, Pallas kernels for 0%

profile of v9, /device:TPU:0, one launch (start us, length us, event | category | flops | bytes accessed | tf_op | source)
XLA Modules:
  0.0 74.7 jit_solution(11905450626183888188)
XLA Ops:
  0.6 1.8 %shard_map.77 = (f32[32,256]{1,0:T(8,128)}, f32[32,256]{1,0:T(8,128)}, f32[32,256]{1,0:T(8,128)}, f32[32,256]{1,0:T(8,128)}) custom-call(s32[4,32]{1,0:T(4,128)} %bitcast.26, f32[128,256]{1,0:T(8,128)} %own_ref.1), custom_call_target="tpu_custom_call" | custom-call | tf_op jit(solution)/shard_map/pallas_call | solution.py:264
  2.4 4.8 %collective-permute-start = (f32[32,256]{1,0:T(8,128)}, f32[32,256]{1,0:T(8,128)S(1)}, u32[]{:S(2)}, u32[]{:S(2)}) collective-permute-start(f32[32,256]{1,0:T(8,128)} %get-tuple-element.14), channel_id=1, source_target_pairs={{0,4},{4,8},{8,12},{12,16},{16,20},{20,24},{24,28},{1,5},{5,9},{9,... | collective-permute-start | bytes 98312 | tf_op jit(solution)/shard_map/ppermute | solution.py:314
  7.2 1.3 %collective-permute-start.1 = (f32[32,256]{1,0:T(8,128)}, f32[32,256]{1,0:T(8,128)S(1)}, u32[]{:S(2)}, u32[]{:S(2)}) collective-permute-start(f32[32,256]{1,0:T(8,128)} %get-tuple-element.15), channel_id=1, source_target_pairs={{4,0},{8,4},{12,8},{16,12},{20,16},{24,20},{28,24},{5,1},{9,5},{13... | collective-permute-start | bytes 98312 | tf_op jit(solution)/shard_map/ppermute | solution.py:315
  8.5 1.5 %collective-permute-start.2 = (f32[32,256]{1,0:T(8,128)}, f32[32,256]{1,0:T(8,128)S(1)}, u32[]{:S(2)}, u32[]{:S(2)}) collective-permute-start(f32[32,256]{1,0:T(8,128)} %get-tuple-element.16), channel_id=1, source_target_pairs={{0,1},{1,2},{2,3},{4,5},{5,6},{6,7},{8,9},{9,10},{10,11},{12,13},{... | collective-permute-start | bytes 98312 | tf_op jit(solution)/shard_map/ppermute | solution.py:316
  10.0 1.3 %collective-permute-start.3 = (f32[32,256]{1,0:T(8,128)}, f32[32,256]{1,0:T(8,128)S(1)}, u32[]{:S(2)}, u32[]{:S(2)}) collective-permute-start(f32[32,256]{1,0:T(8,128)} %get-tuple-element.17), channel_id=1, source_target_pairs={{1,0},{2,1},{3,2},{5,4},{6,5},{7,6},{9,8},{10,9},{11,10},{13,12},{... | collective-permute-start | bytes 98312 | tf_op jit(solution)/shard_map/ppermute | solution.py:317
  11.9 0.0 collective-permute-done.g0_ref
  11.9 0.0 copy-start.1
  12.0 1.3 %collective-permute-done.1.g1_ref = f32[32,256]{1,0:T(8,128)S(1)} collective-permute-done((f32[32,256]{1,0:T(8,128)}, f32[32,256]{1,0:T(8,128)S(1)}, u32[]{:S(2)}, u32[]{:S(2)}) %collective-permute-start.1) | collective-permute-done | bytes 32800 | tf_op jit(solution)/shard_map/ppermute | solution.py:315
  13.2 0.0 collective-permute-done.2.g2_ref
  13.2 1.6 %collective-permute-done.3.g3_ref = f32[32,256]{1,0:T(8,128)S(1)} collective-permute-done((f32[32,256]{1,0:T(8,128)}, f32[32,256]{1,0:T(8,128)S(1)}, u32[]{:S(2)}, u32[]{:S(2)}) %collective-permute-start.3) | collective-permute-done | bytes 32800 | tf_op jit(solution)/shard_map/ppermute | solution.py:317
  14.9 0.0 copy-done.1
  14.9 0.0 copy-done.3
  14.9 0.0 copy-done.5
  14.9 0.6 copy-done.7
  15.5 11.0 %shard_map.78 = (f32[128,256]{1,0:T(8,128)}, f32[32,256]{1,0:T(8,128)}, f32[32,256]{1,0:T(8,128)}, f32[32,256]{1,0:T(8,128)}, f32[32,256]{1,0:T(8,128)}, /*index=5*/f32[128,256]{1,0:T(8,128)}) custom-call(s32[1]{0:T(128)S(6)} %copy.39.count_ref, s32[4,32]{1,0:T(4,128)} %bitcast.27, f32[5,128,4096]{2,1,0:T(8,128)} %bitcast.23, f32[128,256]{1,0:T(8,128)} %own_ref.1, ...), custom_call_target="tpu_custom_call" | custom-call | flops 557842432 | bytes 11272192 | tf_op jit(solution)/shard_map/pallas_call | solution.py:234
  26.5 4.5 %collective-permute-start.4 = (f32[32,256]{1,0:T(8,128)}, f32[32,256]{1,0:T(8,128)S(1)}, u32[]{:S(2)}, u32[]{:S(2)}) collective-permute-start(f32[32,256]{1,0:T(8,128)} %get-tuple-element.19), channel_id=1, source_target_pairs={{0,4},{4,8},{8,12},{12,16},{16,20},{20,24},{24,28},{1,5},{5,9},{9,... | collective-permute-start | bytes 98312 | tf_op jit(solution)/shard_map/ppermute | solution.py:314
  31.0 1.3 %collective-permute-start.5 = (f32[32,256]{1,0:T(8,128)}, f32[32,256]{1,0:T(8,128)S(1)}, u32[]{:S(2)}, u32[]{:S(2)}) collective-permute-start(f32[32,256]{1,0:T(8,128)} %get-tuple-element.20), channel_id=1, source_target_pairs={{4,0},{8,4},{12,8},{16,12},{20,16},{24,20},{28,24},{5,1},{9,5},{13... | collective-permute-start | bytes 98312 | tf_op jit(solution)/shard_map/ppermute | solution.py:315
  32.3 4.3 %collective-permute-start.6 = (f32[32,256]{1,0:T(8,128)}, f32[32,256]{1,0:T(8,128)S(1)}, u32[]{:S(2)}, u32[]{:S(2)}) collective-permute-start(f32[32,256]{1,0:T(8,128)} %get-tuple-element.21), channel_id=1, source_target_pairs={{0,1},{1,2},{2,3},{4,5},{5,6},{6,7},{8,9},{9,10},{10,11},{12,13},{... | collective-permute-start | bytes 98312 | tf_op jit(solution)/shard_map/ppermute | solution.py:316
  36.6 1.3 %collective-permute-start.7 = (f32[32,256]{1,0:T(8,128)}, f32[32,256]{1,0:T(8,128)S(1)}, u32[]{:S(2)}, u32[]{:S(2)}) collective-permute-start(f32[32,256]{1,0:T(8,128)} %get-tuple-element.22), channel_id=1, source_target_pairs={{1,0},{2,1},{3,2},{5,4},{6,5},{7,6},{9,8},{10,9},{11,10},{13,12},{... | collective-permute-start | bytes 98312 | tf_op jit(solution)/shard_map/ppermute | solution.py:317
  37.9 0.0 collective-permute-done.4.g0_ref
  37.9 0.0 copy-start
  37.9 0.0 collective-permute-done.5.g1_ref
  37.9 0.0 copy-start.2
  38.0 0.0 collective-permute-done.6.g2_ref
  38.0 0.0 copy-start.4
  38.0 1.9 %collective-permute-done.7.g3_ref = f32[32,256]{1,0:T(8,128)S(1)} collective-permute-done((f32[32,256]{1,0:T(8,128)}, f32[32,256]{1,0:T(8,128)S(1)}, u32[]{:S(2)}, u32[]{:S(2)}) %collective-permute-start.7) | collective-permute-done | bytes 32800 | tf_op jit(solution)/shard_map/ppermute | solution.py:317
  39.9 0.0 copy-done
  39.9 0.0 copy-done.2
  39.9 0.6 copy-done.6
  40.5 11.2 %shard_map.79 = (f32[128,256]{1,0:T(8,128)}, f32[32,256]{1,0:T(8,128)}, f32[32,256]{1,0:T(8,128)}, f32[32,256]{1,0:T(8,128)}, f32[32,256]{1,0:T(8,128)}, /*index=5*/f32[128,256]{1,0:T(8,128)}, f32[32,4,20]{2,1,0:T(4,128)}) custom-call(s32[1]{0:T(128)S(6)} %copy.39.count_ref, s32[4,32]{1,0:T(4,128)} %bitcast.28, f32[5,128,4096]{2,1,0:T(8,128)} %bitcast.24, ...), custom_call_target="tpu_custom_call" | custom-call | flops 557842432 | bytes 11272192 | tf_op jit(solution)/shard_map/pallas_call | solution.py:234
  51.7 16.5 %all_to_all.5 = f32[32,4,20]{2,1,0:T(4,128)S(1)} all-to-all(f32[32,4,20]{2,1,0:T(4,128)} %get-tuple-element.24), channel_id=1, replica_groups=mesh['wide'=8,'narrow'=4] {'wide','narrow'}, dimensions={0} | all-to-all | bytes 20480 | tf_op jit(solution)/shard_map/all_to_all | solution.py:326
  68.3 0.1 mul.15
  68.3 0.1 copy.29
  68.5 0.1 multiply_reduce_fusion
  68.5 0.2 fusion.10
  68.7 0.1 copy.37
  68.8 0.1 copy.38
  68.9 0.1 copy.31
  69.0 0.1 maximum_maximum_fusion
  69.1 0.1 copy.33
  69.2 0.7 cholesky.16
  69.9 0.1 select_reduce_fusion
  69.9 0.6 compare_reduce_fusion
  70.6 0.6 fusion
  71.3 0.6 custom-call.10
  71.9 0.2 fusion.1
  72.1 0.7 fusion.6.mix_ref
  72.8 1.9 %shard_map.80 = (f32[128,256]{1,0:T(8,128)}, f32[128,256]{1,0:T(8,128)}) custom-call(f32[8,4]{1,0:T(8,128)} %fusion.6.mix_ref, f32[128,256]{1,0:T(8,128)} %get-tuple-element.23.rest_0_.anchor_ref, f32[128,256]{1,0:T(8,128)} %get-tuple-element.18.own_ref.first_ref, f32[128,256]{1,0:T(8,128)} %get-tuple-element.25.second_ref), custom_call_target="tpu_custom_call" | custom-call | tf_op jit(solution)/shard_map/pallas_call | solution.py:299
  (9 shorter events, 0.1 us)
Async XLA Ops:
  2.4 9.6 %collective-permute-start = (f32[32,256]{1,0:T(8,128)}, f32[32,256]{1,0:T(8,128)S(1)}, u32[]{:S(2)}, u32[]{:S(2)}) collective-permute-start(f32[32,256]{1,0:T(8,128)} %get-tuple-element.14), channel_id=1, source_target_pairs={{0,4},{4,8},{8,12},{12,16},{16,20},{20,24},{24,28},{1,5},{5,9},{9,... | collective-permute-start | bytes 98312 | tf_op jit(solution)/shard_map/ppermute | solution.py:314
  7.2 6.0 %collective-permute-start.1 = (f32[32,256]{1,0:T(8,128)}, f32[32,256]{1,0:T(8,128)S(1)}, u32[]{:S(2)}, u32[]{:S(2)}) collective-permute-start(f32[32,256]{1,0:T(8,128)} %get-tuple-element.15), channel_id=1, source_target_pairs={{4,0},{8,4},{12,8},{16,12},{20,16},{24,20},{28,24},{5,1},{9,5},{13... | collective-permute-start | bytes 98312 | tf_op jit(solution)/shard_map/ppermute | solution.py:315
  8.5 4.7 %collective-permute-start.2 = (f32[32,256]{1,0:T(8,128)}, f32[32,256]{1,0:T(8,128)S(1)}, u32[]{:S(2)}, u32[]{:S(2)}) collective-permute-start(f32[32,256]{1,0:T(8,128)} %get-tuple-element.16), channel_id=1, source_target_pairs={{0,1},{1,2},{2,3},{4,5},{5,6},{6,7},{8,9},{9,10},{10,11},{12,13},{... | collective-permute-start | bytes 98312 | tf_op jit(solution)/shard_map/ppermute | solution.py:316
  10.0 4.9 %collective-permute-start.3 = (f32[32,256]{1,0:T(8,128)}, f32[32,256]{1,0:T(8,128)S(1)}, u32[]{:S(2)}, u32[]{:S(2)}) collective-permute-start(f32[32,256]{1,0:T(8,128)} %get-tuple-element.17), channel_id=1, source_target_pairs={{1,0},{2,1},{3,2},{5,4},{6,5},{7,6},{9,8},{10,9},{11,10},{13,12},{... | collective-permute-start | bytes 98312 | tf_op jit(solution)/shard_map/ppermute | solution.py:317
  11.9 2.9 %copy-start.1 = (f32[32,256]{1,0:T(8,128)}, f32[32,256]{1,0:T(8,128)S(1)}, u32[]{:S(2)}) copy-start(f32[32,256]{1,0:T(8,128)S(1)} %collective-permute-done.g0_ref) | copy-start | bytes 98308
  13.2 1.7 %copy-start.3 = (f32[32,256]{1,0:T(8,128)}, f32[32,256]{1,0:T(8,128)S(1)}, u32[]{:S(2)}) copy-start(f32[32,256]{1,0:T(8,128)S(1)} %collective-permute-done.1.g1_ref) | copy-start | bytes 98308
  13.2 1.6 %copy-start.5 = (f32[32,256]{1,0:T(8,128)}, f32[32,256]{1,0:T(8,128)S(1)}, u32[]{:S(2)}) copy-start(f32[32,256]{1,0:T(8,128)S(1)} %collective-permute-done.2.g2_ref) | copy-start | bytes 98308
  14.9 0.6 copy-start.7
  15.5 52.9 %copy-start.8 = (f32[4,4,4]{2,1,0:T(4,128)S(1)}, f32[4,4,4]{2,1,0:T(4,128)}, u32[]{:S(2)}) copy-start(f32[4,4,4]{2,1,0:T(4,128)} %constant.52.clone) | copy-start | bytes 772
  26.5 11.4 %collective-permute-start.4 = (f32[32,256]{1,0:T(8,128)}, f32[32,256]{1,0:T(8,128)S(1)}, u32[]{:S(2)}, u32[]{:S(2)}) collective-permute-start(f32[32,256]{1,0:T(8,128)} %get-tuple-element.19), channel_id=1, source_target_pairs={{0,4},{4,8},{8,12},{12,16},{16,20},{20,24},{24,28},{1,5},{5,9},{9,... | collective-permute-start | bytes 98312 | tf_op jit(solution)/shard_map/ppermute | solution.py:314
  31.0 6.9 %collective-permute-start.5 = (f32[32,256]{1,0:T(8,128)}, f32[32,256]{1,0:T(8,128)S(1)}, u32[]{:S(2)}, u32[]{:S(2)}) collective-permute-start(f32[32,256]{1,0:T(8,128)} %get-tuple-element.20), channel_id=1, source_target_pairs={{4,0},{8,4},{12,8},{16,12},{20,16},{24,20},{28,24},{5,1},{9,5},{13... | collective-permute-start | bytes 98312 | tf_op jit(solution)/shard_map/ppermute | solution.py:315
  32.3 5.6 %collective-permute-start.6 = (f32[32,256]{1,0:T(8,128)}, f32[32,256]{1,0:T(8,128)S(1)}, u32[]{:S(2)}, u32[]{:S(2)}) collective-permute-start(f32[32,256]{1,0:T(8,128)} %get-tuple-element.21), channel_id=1, source_target_pairs={{0,1},{1,2},{2,3},{4,5},{5,6},{6,7},{8,9},{9,10},{10,11},{12,13},{... | collective-permute-start | bytes 98312 | tf_op jit(solution)/shard_map/ppermute | solution.py:316
  36.6 3.3 %collective-permute-start.7 = (f32[32,256]{1,0:T(8,128)}, f32[32,256]{1,0:T(8,128)S(1)}, u32[]{:S(2)}, u32[]{:S(2)}) collective-permute-start(f32[32,256]{1,0:T(8,128)} %get-tuple-element.22), channel_id=1, source_target_pairs={{1,0},{2,1},{3,2},{5,4},{6,5},{7,6},{9,8},{10,9},{11,10},{13,12},{... | collective-permute-start | bytes 98312 | tf_op jit(solution)/shard_map/ppermute | solution.py:317
  37.9 2.0 %copy-start = (f32[32,256]{1,0:T(8,128)}, f32[32,256]{1,0:T(8,128)S(1)}, u32[]{:S(2)}) copy-start(f32[32,256]{1,0:T(8,128)S(1)} %collective-permute-done.4.g0_ref) | copy-start | bytes 98308
  37.9 2.0 %copy-start.2 = (f32[32,256]{1,0:T(8,128)}, f32[32,256]{1,0:T(8,128)S(1)}, u32[]{:S(2)}) copy-start(f32[32,256]{1,0:T(8,128)S(1)} %collective-permute-done.5.g1_ref) | copy-start | bytes 98308
  38.0 2.0 %copy-start.4 = (f32[32,256]{1,0:T(8,128)}, f32[32,256]{1,0:T(8,128)S(1)}, u32[]{:S(2)}) copy-start(f32[32,256]{1,0:T(8,128)S(1)} %collective-permute-done.6.g2_ref) | copy-start | bytes 98308
  39.9 0.6 copy-start.6

commit v10 on v9

--- a/solution.py
+++ b/solution.py
@@ -15,6 +15,7 @@
 LANES = 128
 SUBLANES = 8
 UNROLL = 4
+CHUNK_ROWS = 16
 ROWS_PER_STEP = 32
 
 
@@ -115,135 +116,135 @@
     )
 
 
-def coupling_kernel(with_gram, count_ref, lend_ref, jac_ref, own_ref, g0_ref, g1_ref, g2_ref, g3_ref, cols_ref, *rest):
+def coupling_kernel(with_gram, count_ref, lend_ref, jac_hbm, own_ref, g0_ref, g1_ref, g2_ref, g3_ref, cols_ref, *rest):
     if with_gram:
         anchor_ref, rest = rest[0], rest[1:]
     out_ref, l0_ref, l1_ref, l2_ref, l3_ref, kept_ref = rest[:6]
     rest = rest[6:]
     if with_gram:
         gram_ref, rest = rest[0], rest[1:]
-    source_ref, picked_ref, z_ref, parts_ref = rest
-    step = pl.program_id(0)
-    rows = jac_ref.shape[1]
+    jac_ref, sems, source_ref, picked_ref, z_ref, parts_ref = rest
     tiles = jac_ref.shape[2] // LANES
     count = own_ref.shape[0]
     width = own_ref.shape[1]
     ghost = g0_ref.shape[0]
-    row0 = pl.multiple_of(step * rows, rows)
-
-    @pl.when(step == 0)
-    def _():
-        living = lax.broadcasted_iota(jnp.int32, (count, 1), 0) < count_ref[0]
-        source_ref[0:count] = split_three(jnp.where(living, own_ref[...], jnp.float32(0.0)))
-        for q, piece in enumerate((g0_ref, g1_ref, g2_ref, g3_ref)):
-            source_ref[count + q * ghost:count + (q + 1) * ghost] = split_three(piece[...])
-        slots = lax.broadcasted_iota(jnp.int32, (source_ref.shape[0], count), 0)
-        for k in range(NB):
-            chosen = (cols_ref[k:k + 1, :] == slots).astype(jnp.bfloat16)
-            spread = lax.dot_general(
-                chosen, source_ref[...], (((0,), (0,)), ((), ())), preferred_element_type=jnp.float32
-            )
-            picked_ref[k] = spread[:, 0:width] + spread[:, width:2 * width] + spread[:, 2 * width:3 * width]
+    chunks = sems.shape[0]
+    chunk_rows = count // chunks
+
+    def chunk_copy(b):
+        rows = pl.ds(pl.multiple_of(b * chunk_rows, chunk_rows), chunk_rows)
+        return pltpu.make_async_copy(jac_hbm.at[:, rows, :], jac_ref.at[:, rows, :], sems.at[b])
+
+    for b in range(chunks):
+        chunk_copy(b).start()
+
+    living = lax.broadcasted_iota(jnp.int32, (count, 1), 0) < count_ref[0]
+    source_ref[0:count] = split_three(jnp.where(living, own_ref[...], jnp.float32(0.0)))
+    for q, piece in enumerate((g0_ref, g1_ref, g2_ref, g3_ref)):
+        source_ref[count + q * ghost:count + (q + 1) * ghost] = split_three(piece[...])
+    slots = lax.broadcasted_iota(jnp.int32, (source_ref.shape[0], count), 0)
+    for k in range(NB):
+        chosen = (cols_ref[k:k + 1, :] == slots).astype(jnp.bfloat16)
+        spread = lax.dot_general(
+            chosen, source_ref[...], (((0,), (0,)), ((), ())), preferred_element_type=jnp.float32
+        )
+        picked_ref[k] = spread[:, 0:width] + spread[:, width:2 * width] + spread[:, 2 * width:3 * width]
 
     lane = lax.broadcasted_iota(jnp.int32, (SUBLANES, LANES), 1)
-    for group in range(rows // SUBLANES):
-        top = group * SUBLANES
-        first_row = pl.multiple_of(row0 + top, SUBLANES)
-        doubled = []
-        for k in range(NB):
-            per_vector = []
-            for pair in range(VECS // 2):
-                tile = picked_ref[k, pl.ds(first_row, SUBLANES), pair * LANES:(pair + 1) * LANES]
-                swapped = pltpu.roll(tile, BLK, 1)
-                per_vector.append(jnp.where(lane < BLK, tile, swapped))
-                per_vector.append(jnp.where(lane >= BLK, tile, swapped))
-            doubled.append(per_vector)
-
-        def one_tile(t, carry):
-            off = pl.multiple_of(t * LANES, LANES)
-            blocks = [jac_ref[k, top:top + SUBLANES, pl.ds(off, LANES)] for k in range(NB)]
-            for c in range(VECS):
-                terms = [blocks[k] * doubled[k][c] for k in range(NB)]
-                while len(terms) > 1:
-                    terms = [terms[i] + terms[i + 1] for i in range(0, len(terms) - 1, 2)] + (
-                        [terms[-1]] if len(terms) % 2 else []
-                    )
-                z_ref[c, pl.ds(first_row, SUBLANES), pl.ds(off, LANES)] = terms[0]
-            return carry
-
-        lax.fori_loop(0, tiles, one_tile, 0, unroll=UNROLL)
-
-    @pl.when(step == pl.num_programs(0) - 1)
-    def _():
-        full = tiles * LANES
-        for c in range(VECS):
-            total = z_ref[c]
-            high = total.astype(jnp.bfloat16)
-            parts_ref[2 * c] = high
-            parts_ref[2 * c + 1] = (total - high.astype(jnp.float32)).astype(jnp.bfloat16)
-        flat = parts_ref[...].reshape(2 * VECS * count, full)
-        seg = (
-            lax.broadcasted_iota(jnp.int32, (full, BLK), 0) // BLK
-            == lax.broadcasted_iota(jnp.int32, (full, BLK), 1)
-        ).astype(jnp.bfloat16)
-        sums = jnp.dot(flat, seg, preferred_element_type=jnp.float32)
-        coupled = jnp.concatenate(
-            [sums[(2 * c) * count:(2 * c + 1) * count] + sums[(2 * c + 1) * count:(2 * c + 2) * count] for c in range(VECS)],
-            axis=1,
-        )
-        own = own_ref[...]
-        living = lax.broadcasted_iota(jnp.int32, (count, 1), 0) < count_ref[0]
-        image = jnp.where(living, DIAG_SHIFT * own + coupled, jnp.float32(0.0))
-        out_ref[...] = image
-        kept = jnp.where(living, own, jnp.float32(0.0))
-        kept_ref[...] = kept
-        for q, lent_ref in enumerate((l0_ref, l1_ref, l2_ref, l3_ref)):
-            for j in range(lend_ref.shape[1]):
-                lent_ref[j:j + 1, :] = out_ref[pl.ds(lend_ref[q, j], 1), :]
-        if with_gram:
-            anchor = anchor_ref[...]
-            partial = gram_columns(((kept, anchor), (kept, kept), (image, anchor), (image, kept), (image, image)))
-            for target in range(gram_ref.shape[0]):
-                gram_ref[target] = partial
+
+    def one_chunk(b, carry):
+        chunk_copy(b).wait()
+        for group in range(chunk_rows // SUBLANES):
+            first_row = pl.multiple_of(b * chunk_rows + group * SUBLANES, SUBLANES)
+            doubled = []
+            for k in range(NB):
+                per_vector = []
+                for pair in range(VECS // 2):
+                    tile = picked_ref[k, pl.ds(first_row, SUBLANES), pair * LANES:(pair + 1) * LANES]
+                    swapped = pltpu.roll(tile, BLK, 1)
+                    per_vector.append(jnp.where(lane < BLK, tile, swapped))
+                    per_vector.append(jnp.where(lane >= BLK, tile, swapped))
+                doubled.append(per_vector)
+
+            def one_tile(t, inner):
+                off = pl.multiple_of(t * LANES, LANES)
+                blocks = [jac_ref[k, pl.ds(first_row, SUBLANES), pl.ds(off, LANES)] for k in range(NB)]
+                for c in range(VECS):
+                    terms = [blocks[k] * doubled[k][c] for k in range(NB)]
+                    while len(terms) > 1:
+                        terms = [terms[i] + terms[i + 1] for i in range(0, len(terms) - 1, 2)] + (
+                            [terms[-1]] if len(terms) % 2 else []
+                        )
+                    z_ref[c, pl.ds(first_row, SUBLANES), pl.ds(off, LANES)] = terms[0]
+                return inner
+
+            lax.fori_loop(0, tiles, one_tile, 0, unroll=UNROLL)
+        return carry
+
+    lax.fori_loop(0, chunks, one_chunk, 0)
+
+    full = tiles * LANES
+    for c in range(VECS):
+        total = z_ref[c]
+        high = total.astype(jnp.bfloat16)
+        parts_ref[2 * c] = high
+        parts_ref[2 * c + 1] = (total - high.astype(jnp.float32)).astype(jnp.bfloat16)
+    flat = parts_ref[...].reshape(2 * VECS * count, full)
+    seg = (
+        lax.broadcasted_iota(jnp.int32, (full, BLK), 0) // BLK
+        == lax.broadcasted_iota(jnp.int32, (full, BLK), 1)
+    ).astype(jnp.bfloat16)
+    sums = jnp.dot(flat, seg, preferred_element_type=jnp.float32)
+    coupled = jnp.concatenate(
+        [sums[(2 * c) * count:(2 * c + 1) * count] + sums[(2 * c + 1) * count:(2 * c + 2) * count] for c in range(VECS)],
+        axis=1,
+    )
+    own = own_ref[...]
+    image = jnp.where(living, DIAG_SHIFT * own + coupled, jnp.float32(0.0))
+    out_ref[...] = image
+    kept = jnp.where(living, own, jnp.float32(0.0))
+    kept_ref[...] = kept
+    for q, lent_ref in enumerate((l0_ref, l1_ref, l2_ref, l3_ref)):
+        for j in range(lend_ref.shape[1]):
+            lent_ref[j:j + 1, :] = out_ref[pl.ds(lend_ref[q, j], 1), :]
+    if with_gram:
+        anchor = anchor_ref[...]
+        partial = gram_columns(((kept, anchor), (kept, kept), (image, anchor), (image, kept), (image, image)))
+        for target in range(gram_ref.shape[0]):
+            gram_ref[target] = partial
 
 
 def apply_operator(jac_t, own, ghost_rows, cols_t, counts, lend_rows, anchor=None, peers=1):
     blocks, count, full = jac_t.shape
     width = own.shape[1]
     ghost = ghost_rows[0].shape[0]
-    rows = min(ROWS_PER_STEP, count)
+    chunks = max(count // CHUNK_ROWS, 1)
     with_gram = anchor is not None
     smem = pl.BlockSpec(memory_space=pltpu.SMEM)
-    whole = pl.BlockSpec((count, width), lambda b: (0, 0))
-    piece = pl.BlockSpec((ghost, width), lambda b: (0, 0))
+    vmem = pl.BlockSpec(memory_space=pltpu.VMEM)
     lent = lend_rows.shape[1]
-    lent_spec = pl.BlockSpec((lent, width), lambda b: (0, 0))
-    in_specs = [smem, smem, pl.BlockSpec((blocks, rows, full), lambda b: (0, b, 0)), whole, piece, piece, piece, piece,
-                pl.BlockSpec((blocks, count), lambda b: (0, 0))]
+    in_specs = [smem, smem, pl.BlockSpec(memory_space=pl.ANY), vmem, vmem, vmem, vmem, vmem, vmem]
     out_shape = [jax.ShapeDtypeStruct((count, width), jnp.float32)]
     out_shape += [jax.ShapeDtypeStruct((lent, width), jnp.float32)] * lend_rows.shape[0]
     out_shape += [jax.ShapeDtypeStruct((count, width), jnp.float32)]
-    out_specs = [whole] + [lent_spec] * lend_rows.shape[0] + [whole]
     args = [counts, lend_rows, jac_t, own, *ghost_rows, cols_t]
     if with_gram:
-        in_specs.append(whole)
+        in_specs.append(vmem)
         args.append(anchor)
-        gram_count = 5 * VECS
-        out_shape.append(jax.ShapeDtypeStruct((peers, VECS, gram_count), jnp.float32))
-        out_specs.append(pl.BlockSpec((peers, VECS, gram_count), lambda b: (0, 0, 0)))
+        out_shape.append(jax.ShapeDtypeStruct((peers, VECS, 5 * VECS), jnp.float32))
     return pl.pallas_call(
         functools.partial(coupling_kernel, with_gram),
         out_shape=tuple(out_shape),
-        grid=(count // rows,),
         in_specs=in_specs,
-        out_specs=tuple(out_specs),
+        out_specs=tuple(vmem for _ in out_shape),
         scratch_shapes=[
+            pltpu.VMEM((blocks, count, full), jnp.float32),
+            pltpu.SemaphoreType.DMA((chunks,)),
             pltpu.VMEM((count + 4 * ghost, 3 * width), jnp.bfloat16),
             pltpu.VMEM((blocks, count, width), jnp.float32),
             pltpu.VMEM((VECS, count, full), jnp.float32),
             pltpu.VMEM((2 * VECS, count, full), jnp.bfloat16),
         ],
-        compiler_params=pltpu.CompilerParams(dimension_semantics=("arbitrary",)),
         cost_estimate=pl.CostEstimate(
             flops=2 * blocks * count * full * VECS + 2 * 2 * VECS * count * full * BLK,
             bytes_accessed=4 * (blocks * count * full + 6 * count * width),

time: 75.2 us -> 74 us (0.984)
  Pallas kernels: 25.9 us -> 24.7 us
    pallas_call x2, Pallas kernels: 22.2 us -> 21 us  [apply_operator(): pl.pallas_call(functools.partial(coupling_kernel, with_gram), out_shape=t...]
where the time goes in v10:
time: 74 us; the launch traced here: 73.5 us
  Pallas kernels  24.7 us (33%)
  starting transfers between devices  20.3 us (27%)
  blocking collectives  16.5 us (22%)
  waiting for transfers between devices  4.88 us (7%)
  other arithmetic  2.89 us (4%)
  local copies, waits for them, and re-layouts  1.98 us (3%)
  between operations  1.46 us (2%)
  matrix products  0.93 us (1%)
    pallas_call x2, Pallas kernels, apply_operator(): pl.pallas_call(functools.partial(coupling_kernel, with_gram), out_shape=t...  21 us
    all_to_all x1, blocking collectives, per_device(): everyone = lax.all_to_all(raw_gram, ('wide', 'narrow'), 0, 0, tiled=True)  16.5 us
    ppermute x2, starting transfers between devices, ghosts(): lax.ppermute(outgoing[0], 'wide', [(i, i + 1) for i in range(wide - 1)])  9.38 us
    ppermute x2, starting transfers between devices, ghosts(): lax.ppermute(outgoing[2], 'narrow', [(i, i + 1) for i in range(narrow - 1)])  5.71 us
    ppermute x2, waiting for transfers between devices, ghosts(): lax.ppermute(outgoing[3], 'narrow', [(i + 1, i) for i in range(narrow - 1)])  3.59 us
    ppermute x2, starting transfers between devices, ghosts(): lax.ppermute(outgoing[1], 'wide', [(i + 1, i) for i in range(wide - 1)])  2.58 us
    ppermute x2, starting transfers between devices, ghosts(): lax.ppermute(outgoing[3], 'narrow', [(i + 1, i) for i in range(narrow - 1)])  2.58 us
    pallas_call x1, Pallas kernels, mix_outputs(): pl.pallas_call(mixing_kernel, out_shape=(jax.ShapeDtypeStruct(anchor.shap...  1.93 us
  transfers between devices with their start and end apart: 8, of which 3 were waited for; matrix products, arithmetic and copies ran while one was open for 0% of the time, Pallas kernels for 0%

profile of v10, /device:TPU:0, one launch (start us, length us, event | category | flops | bytes accessed | tf_op | source)
XLA Modules:
  0.0 73.5 jit_solution(7809297399014916597)
XLA Ops:
  0.6 1.8 %shard_map.77 = (f32[32,256]{1,0:T(8,128)}, f32[32,256]{1,0:T(8,128)}, f32[32,256]{1,0:T(8,128)}, f32[32,256]{1,0:T(8,128)}) custom-call(s32[4,32]{1,0:T(4,128)} %bitcast.26, f32[128,256]{1,0:T(8,128)} %own_ref.1), custom_call_target="tpu_custom_call" | custom-call | tf_op jit(solution)/shard_map/pallas_call | solution.py:265
  2.4 4.8 %collective-permute-start = (f32[32,256]{1,0:T(8,128)}, f32[32,256]{1,0:T(8,128)S(1)}, u32[]{:S(2)}, u32[]{:S(2)}) collective-permute-start(f32[32,256]{1,0:T(8,128)} %get-tuple-element.14), channel_id=1, source_target_pairs={{0,4},{4,8},{8,12},{12,16},{16,20},{20,24},{24,28},{1,5},{5,9},{9,... | collective-permute-start | bytes 98312 | tf_op jit(solution)/shard_map/ppermute | solution.py:315
  7.2 1.3 %collective-permute-start.1 = (f32[32,256]{1,0:T(8,128)}, f32[32,256]{1,0:T(8,128)S(1)}, u32[]{:S(2)}, u32[]{:S(2)}) collective-permute-start(f32[32,256]{1,0:T(8,128)} %get-tuple-element.15), channel_id=1, source_target_pairs={{4,0},{8,4},{12,8},{16,12},{20,16},{24,20},{28,24},{5,1},{9,5},{13... | collective-permute-start | bytes 98312 | tf_op jit(solution)/shard_map/ppermute | solution.py:316
  8.5 1.5 %collective-permute-start.2 = (f32[32,256]{1,0:T(8,128)}, f32[32,256]{1,0:T(8,128)S(1)}, u32[]{:S(2)}, u32[]{:S(2)}) collective-permute-start(f32[32,256]{1,0:T(8,128)} %get-tuple-element.16), channel_id=1, source_target_pairs={{0,1},{1,2},{2,3},{4,5},{5,6},{6,7},{8,9},{9,10},{10,11},{12,13},{... | collective-permute-start | bytes 98312 | tf_op jit(solution)/shard_map/ppermute | solution.py:317
  10.0 1.3 %collective-permute-start.3 = (f32[32,256]{1,0:T(8,128)}, f32[32,256]{1,0:T(8,128)S(1)}, u32[]{:S(2)}, u32[]{:S(2)}) collective-permute-start(f32[32,256]{1,0:T(8,128)} %get-tuple-element.17), channel_id=1, source_target_pairs={{1,0},{2,1},{3,2},{5,4},{6,5},{7,6},{9,8},{10,9},{11,10},{13,12},{... | collective-permute-start | bytes 98312 | tf_op jit(solution)/shard_map/ppermute | solution.py:318
  11.9 0.0 collective-permute-done.g0_ref
  11.9 0.0 copy-start.1
  12.0 1.3 %collective-permute-done.1.g1_ref = f32[32,256]{1,0:T(8,128)S(1)} collective-permute-done((f32[32,256]{1,0:T(8,128)}, f32[32,256]{1,0:T(8,128)S(1)}, u32[]{:S(2)}, u32[]{:S(2)}) %collective-permute-start.1) | collective-permute-done | bytes 32800 | tf_op jit(solution)/shard_map/ppermute | solution.py:316
  13.2 0.0 collective-permute-done.2.g2_ref
  13.2 1.6 %collective-permute-done.3.g3_ref = f32[32,256]{1,0:T(8,128)S(1)} collective-permute-done((f32[32,256]{1,0:T(8,128)}, f32[32,256]{1,0:T(8,128)S(1)}, u32[]{:S(2)}, u32[]{:S(2)}) %collective-permute-start.3) | collective-permute-done | bytes 32800 | tf_op jit(solution)/shard_map/ppermute | solution.py:318
  14.9 0.0 copy-done.1
  14.9 0.0 copy-done.3
  14.9 0.0 copy-done.5
  14.9 0.6 copy-done.7
  15.5 10.4 %shard_map.78 = (f32[128,256]{1,0:T(8,128)}, f32[32,256]{1,0:T(8,128)}, f32[32,256]{1,0:T(8,128)}, f32[32,256]{1,0:T(8,128)}, f32[32,256]{1,0:T(8,128)}, /*index=5*/f32[128,256]{1,0:T(8,128)}) custom-call(s32[1]{0:T(128)S(6)} %copy.39.count_ref, s32[4,32]{1,0:T(4,128)} %bitcast.27, f32[5,128,4096]{2,1,0:T(8,128)} %bitcast.23, f32[128,256]{1,0:T(8,128)} %own_ref.1, ...), custom_call_target="tpu_custom_call" | custom-call | flops 557842432 | bytes 11272192 | tf_op jit(solution)/shard_map/pallas_call | solution.py:235
  25.9 4.5 %collective-permute-start.4 = (f32[32,256]{1,0:T(8,128)}, f32[32,256]{1,0:T(8,128)S(1)}, u32[]{:S(2)}, u32[]{:S(2)}) collective-permute-start(f32[32,256]{1,0:T(8,128)} %get-tuple-element.19), channel_id=1, source_target_pairs={{0,4},{4,8},{8,12},{12,16},{16,20},{20,24},{24,28},{1,5},{5,9},{9,... | collective-permute-start | bytes 98312 | tf_op jit(solution)/shard_map/ppermute | solution.py:315
  30.5 1.3 %collective-permute-start.5 = (f32[32,256]{1,0:T(8,128)}, f32[32,256]{1,0:T(8,128)S(1)}, u32[]{:S(2)}, u32[]{:S(2)}) collective-permute-start(f32[32,256]{1,0:T(8,128)} %get-tuple-element.20), channel_id=1, source_target_pairs={{4,0},{8,4},{12,8},{16,12},{20,16},{24,20},{28,24},{5,1},{9,5},{13... | collective-permute-start | bytes 98312 | tf_op jit(solution)/shard_map/ppermute | solution.py:316
  31.8 4.3 %collective-permute-start.6 = (f32[32,256]{1,0:T(8,128)}, f32[32,256]{1,0:T(8,128)S(1)}, u32[]{:S(2)}, u32[]{:S(2)}) collective-permute-start(f32[32,256]{1,0:T(8,128)} %get-tuple-element.21), channel_id=1, source_target_pairs={{0,1},{1,2},{2,3},{4,5},{5,6},{6,7},{8,9},{9,10},{10,11},{12,13},{... | collective-permute-start | bytes 98312 | tf_op jit(solution)/shard_map/ppermute | solution.py:317
  36.0 1.3 %collective-permute-start.7 = (f32[32,256]{1,0:T(8,128)}, f32[32,256]{1,0:T(8,128)S(1)}, u32[]{:S(2)}, u32[]{:S(2)}) collective-permute-start(f32[32,256]{1,0:T(8,128)} %get-tuple-element.22), channel_id=1, source_target_pairs={{1,0},{2,1},{3,2},{5,4},{6,5},{7,6},{9,8},{10,9},{11,10},{13,12},{... | collective-permute-start | bytes 98312 | tf_op jit(solution)/shard_map/ppermute | solution.py:318
  37.3 0.0 collective-permute-done.4.g0_ref
  37.3 0.0 copy-start
  37.3 0.0 collective-permute-done.5.g1_ref
  37.3 0.0 copy-start.2
  37.4 0.0 collective-permute-done.6.g2_ref
  37.4 0.0 copy-start.4
  37.4 1.9 %collective-permute-done.7.g3_ref = f32[32,256]{1,0:T(8,128)S(1)} collective-permute-done((f32[32,256]{1,0:T(8,128)}, f32[32,256]{1,0:T(8,128)S(1)}, u32[]{:S(2)}, u32[]{:S(2)}) %collective-permute-start.7) | collective-permute-done | bytes 32800 | tf_op jit(solution)/shard_map/ppermute | solution.py:318
  39.3 0.0 copy-done
  39.3 0.0 copy-done.2
  39.3 0.6 copy-done.6
  39.9 10.6 %shard_map.79 = (f32[128,256]{1,0:T(8,128)}, f32[32,256]{1,0:T(8,128)}, f32[32,256]{1,0:T(8,128)}, f32[32,256]{1,0:T(8,128)}, f32[32,256]{1,0:T(8,128)}, /*index=5*/f32[128,256]{1,0:T(8,128)}, f32[32,4,20]{2,1,0:T(4,128)}) custom-call(s32[1]{0:T(128)S(6)} %copy.39.count_ref, s32[4,32]{1,0:T(4,128)} %bitcast.28, f32[5,128,4096]{2,1,0:T(8,128)} %bitcast.24, ...), custom_call_target="tpu_custom_call" | custom-call | flops 557842432 | bytes 11272192 | tf_op jit(solution)/shard_map/pallas_call | solution.py:235
  50.5 16.5 %all_to_all.5 = f32[32,4,20]{2,1,0:T(4,128)S(1)} all-to-all(f32[32,4,20]{2,1,0:T(4,128)} %get-tuple-element.24), channel_id=1, replica_groups=mesh['wide'=8,'narrow'=4] {'wide','narrow'}, dimensions={0} | all-to-all | bytes 20480 | tf_op jit(solution)/shard_map/all_to_all | solution.py:327
  67.1 0.1 mul.15
  67.1 0.1 copy.29
  67.2 0.1 multiply_reduce_fusion
  67.3 0.2 fusion.10
  67.5 0.1 copy.37
  67.6 0.1 copy.38
  67.7 0.1 copy.31
  67.8 0.1 maximum_maximum_fusion
  67.9 0.1 copy.33
  68.0 0.7 cholesky.16
  68.7 0.1 select_reduce_fusion
  68.7 0.6 compare_reduce_fusion
  69.4 0.6 fusion
  70.0 0.6 custom-call.10
  70.7 0.2 fusion.1
  70.9 0.7 %fusion.6.mix_ref = f32[8,4]{1,0:T(8,128)} fusion(f32[8,4]{0,1:T(4,128)S(1)} %fusion.1, f32[1,8,8]{1,2,0:T(8,128)S(1)} %custom-call.10), kind=kOutput, calls=%fused_computation.12 | convolution fusion | flops 3072 | bytes 512 | tf_op jit(solution)/shard_map/jit(_cho_solve)/triangular_solve | solution.py:343
  71.6 1.9 %shard_map.80 = (f32[128,256]{1,0:T(8,128)}, f32[128,256]{1,0:T(8,128)}) custom-call(f32[8,4]{1,0:T(8,128)} %fusion.6.mix_ref, f32[128,256]{1,0:T(8,128)} %get-tuple-element.23.rest_0_.anchor_ref, f32[128,256]{1,0:T(8,128)} %get-tuple-element.18.own_ref.first_ref, f32[128,256]{1,0:T(8,128)} %get-tuple-element.25.second_ref), custom_call_target="tpu_custom_call" | custom-call | tf_op jit(solution)/shard_map/pallas_call | solution.py:300
  (9 shorter events, 0.1 us)
Async XLA Ops:
  2.4 9.6 %collective-permute-start = (f32[32,256]{1,0:T(8,128)}, f32[32,256]{1,0:T(8,128)S(1)}, u32[]{:S(2)}, u32[]{:S(2)}) collective-permute-start(f32[32,256]{1,0:T(8,128)} %get-tuple-element.14), channel_id=1, source_target_pairs={{0,4},{4,8},{8,12},{12,16},{16,20},{20,24},{24,28},{1,5},{5,9},{9,... | collective-permute-start | bytes 98312 | tf_op jit(solution)/shard_map/ppermute | solution.py:315
  7.2 6.0 %collective-permute-start.1 = (f32[32,256]{1,0:T(8,128)}, f32[32,256]{1,0:T(8,128)S(1)}, u32[]{:S(2)}, u32[]{:S(2)}) collective-permute-start(f32[32,256]{1,0:T(8,128)} %get-tuple-element.15), channel_id=1, source_target_pairs={{4,0},{8,4},{12,8},{16,12},{20,16},{24,20},{28,24},{5,1},{9,5},{13... | collective-permute-start | bytes 98312 | tf_op jit(solution)/shard_map/ppermute | solution.py:316
  8.5 4.7 %collective-permute-start.2 = (f32[32,256]{1,0:T(8,128)}, f32[32,256]{1,0:T(8,128)S(1)}, u32[]{:S(2)}, u32[]{:S(2)}) collective-permute-start(f32[32,256]{1,0:T(8,128)} %get-tuple-element.16), channel_id=1, source_target_pairs={{0,1},{1,2},{2,3},{4,5},{5,6},{6,7},{8,9},{9,10},{10,11},{12,13},{... | collective-permute-start | bytes 98312 | tf_op jit(solution)/shard_map/ppermute | solution.py:317
  10.0 4.9 %collective-permute-start.3 = (f32[32,256]{1,0:T(8,128)}, f32[32,256]{1,0:T(8,128)S(1)}, u32[]{:S(2)}, u32[]{:S(2)}) collective-permute-start(f32[32,256]{1,0:T(8,128)} %get-tuple-element.17), channel_id=1, source_target_pairs={{1,0},{2,1},{3,2},{5,4},{6,5},{7,6},{9,8},{10,9},{11,10},{13,12},{... | collective-permute-start | bytes 98312 | tf_op jit(solution)/shard_map/ppermute | solution.py:318
  11.9 2.9 %copy-start.1 = (f32[32,256]{1,0:T(8,128)}, f32[32,256]{1,0:T(8,128)S(1)}, u32[]{:S(2)}) copy-start(f32[32,256]{1,0:T(8,128)S(1)} %collective-permute-done.g0_ref) | copy-start | bytes 98308
  13.2 1.7 %copy-start.3 = (f32[32,256]{1,0:T(8,128)}, f32[32,256]{1,0:T(8,128)S(1)}, u32[]{:S(2)}) copy-start(f32[32,256]{1,0:T(8,128)S(1)} %collective-permute-done.1.g1_ref) | copy-start | bytes 98308
  13.2 1.6 %copy-start.5 = (f32[32,256]{1,0:T(8,128)}, f32[32,256]{1,0:T(8,128)S(1)}, u32[]{:S(2)}) copy-start(f32[32,256]{1,0:T(8,128)S(1)} %collective-permute-done.2.g2_ref) | copy-start | bytes 98308
  14.9 0.6 copy-start.7
  15.5 51.7 %copy-start.8 = (f32[4,4,4]{2,1,0:T(4,128)S(1)}, f32[4,4,4]{2,1,0:T(4,128)}, u32[]{:S(2)}) copy-start(f32[4,4,4]{2,1,0:T(4,128)} %constant.52.clone) | copy-start | bytes 772
  25.9 11.4 %collective-permute-start.4 = (f32[32,256]{1,0:T(8,128)}, f32[32,256]{1,0:T(8,128)S(1)}, u32[]{:S(2)}, u32[]{:S(2)}) collective-permute-start(f32[32,256]{1,0:T(8,128)} %get-tuple-element.19), channel_id=1, source_target_pairs={{0,4},{4,8},{8,12},{12,16},{16,20},{20,24},{24,28},{1,5},{5,9},{9,... | collective-permute-start | bytes 98312 | tf_op jit(solution)/shard_map/ppermute | solution.py:315
  30.5 6.9 %collective-permute-start.5 = (f32[32,256]{1,0:T(8,128)}, f32[32,256]{1,0:T(8,128)S(1)}, u32[]{:S(2)}, u32[]{:S(2)}) collective-permute-start(f32[32,256]{1,0:T(8,128)} %get-tuple-element.20), channel_id=1, source_target_pairs={{4,0},{8,4},{12,8},{16,12},{20,16},{24,20},{28,24},{5,1},{9,5},{13... | collective-permute-start | bytes 98312 | tf_op jit(solution)/shard_map/ppermute | solution.py:316
  31.8 5.6 %collective-permute-start.6 = (f32[32,256]{1,0:T(8,128)}, f32[32,256]{1,0:T(8,128)S(1)}, u32[]{:S(2)}, u32[]{:S(2)}) collective-permute-start(f32[32,256]{1,0:T(8,128)} %get-tuple-element.21), channel_id=1, source_target_pairs={{0,1},{1,2},{2,3},{4,5},{5,6},{6,7},{8,9},{9,10},{10,11},{12,13},{... | collective-permute-start | bytes 98312 | tf_op jit(solution)/shard_map/ppermute | solution.py:317
  36.0 3.3 %collective-permute-start.7 = (f32[32,256]{1,0:T(8,128)}, f32[32,256]{1,0:T(8,128)S(1)}, u32[]{:S(2)}, u32[]{:S(2)}) collective-permute-start(f32[32,256]{1,0:T(8,128)} %get-tuple-element.22), channel_id=1, source_target_pairs={{1,0},{2,1},{3,2},{5,4},{6,5},{7,6},{9,8},{10,9},{11,10},{13,12},{... | collective-permute-start | bytes 98312 | tf_op jit(solution)/shard_map/ppermute | solution.py:318
  37.3 2.0 %copy-start = (f32[32,256]{1,0:T(8,128)}, f32[32,256]{1,0:T(8,128)S(1)}, u32[]{:S(2)}) copy-start(f32[32,256]{1,0:T(8,128)S(1)} %collective-permute-done.4.g0_ref) | copy-start | bytes 98308
  37.3 2.0 %copy-start.2 = (f32[32,256]{1,0:T(8,128)}, f32[32,256]{1,0:T(8,128)S(1)}, u32[]{:S(2)}) copy-start(f32[32,256]{1,0:T(8,128)S(1)} %collective-permute-done.5.g1_ref) | copy-start | bytes 98308
  37.4 2.0 %copy-start.4 = (f32[32,256]{1,0:T(8,128)}, f32[32,256]{1,0:T(8,128)S(1)}, u32[]{:S(2)}) copy-start(f32[32,256]{1,0:T(8,128)S(1)} %collective-permute-done.6.g2_ref) | copy-start | bytes 98308
  39.3 0.6 copy-start.6

commit v11 on v10

--- a/solution.py
+++ b/solution.py
@@ -116,6 +116,15 @@
     )
 
 
+def gather_rows(values, index_row):
+    width = values.shape[1]
+    chosen = (index_row == lax.broadcasted_iota(jnp.int32, (values.shape[0], index_row.shape[1]), 0)).astype(jnp.bfloat16)
+    spread = lax.dot_general(
+        chosen, split_three(values), (((0,), (0,)), ((), ())), preferred_element_type=jnp.float32
+    )
+    return spread[:, 0:width] + spread[:, width:2 * width] + spread[:, 2 * width:3 * width]
+
+
 def coupling_kernel(with_gram, count_ref, lend_ref, jac_hbm, own_ref, g0_ref, g1_ref, g2_ref, g3_ref, cols_ref, *rest):
     if with_gram:
         anchor_ref, rest = rest[0], rest[1:]
@@ -204,9 +213,9 @@
     out_ref[...] = image
     kept = jnp.where(living, own, jnp.float32(0.0))
     kept_ref[...] = kept
+    lent = gather_rows(image, lend_ref[...])
     for q, lent_ref in enumerate((l0_ref, l1_ref, l2_ref, l3_ref)):
-        for j in range(lend_ref.shape[1]):
-            lent_ref[j:j + 1, :] = out_ref[pl.ds(lend_ref[q, j], 1), :]
+        lent_ref[...] = lent[q * ghost:(q + 1) * ghost]
     if with_gram:
         anchor = anchor_ref[...]
         partial = gram_columns(((kept, anchor), (kept, kept), (image, anchor), (image, kept), (image, image)))
@@ -222,10 +231,9 @@
     with_gram = anchor is not None
     smem = pl.BlockSpec(memory_space=pltpu.SMEM)
     vmem = pl.BlockSpec(memory_space=pltpu.VMEM)
-    lent = lend_rows.shape[1]
-    in_specs = [smem, smem, pl.BlockSpec(memory_space=pl.ANY), vmem, vmem, vmem, vmem, vmem, vmem]
+    in_specs = [smem, vmem, pl.BlockSpec(memory_space=pl.ANY), vmem, vmem, vmem, vmem, vmem, vmem]
     out_shape = [jax.ShapeDtypeStruct((count, width), jnp.float32)]
-    out_shape += [jax.ShapeDtypeStruct((lent, width), jnp.float32)] * lend_rows.shape[0]
+    out_shape += [jax.ShapeDtypeStruct((ghost, width), jnp.float32)] * len(ghost_rows)
     out_shape += [jax.ShapeDtypeStruct((count, width), jnp.float32)]
     args = [counts, lend_rows, jac_t, own, *ghost_rows, cols_t]
     if with_gram:
@@ -253,21 +261,23 @@
     )(*args)
 
 
-def lending_kernel(lend_ref, values_ref, *lent_refs):
+def lending_kernel(count_ref, lend_ref, values_ref, *lent_refs):
+    living = lax.broadcasted_iota(jnp.int32, (values_ref.shape[0], 1), 0) < count_ref[0]
+    lent = gather_rows(jnp.where(living, values_ref[...], jnp.float32(0.0)), lend_ref[...])
+    ghost = lent_refs[0].shape[0]
     for q, lent_ref in enumerate(lent_refs):
-        for j in range(lend_ref.shape[1]):
-            lent_ref[j:j + 1, :] = values_ref[pl.ds(lend_ref[q, j], 1), :]
-
-
-def lent_rows_of(values, lend_rows):
-    shape = jax.ShapeDtypeStruct((lend_rows.shape[1], values.shape[1]), values.dtype)
+        lent_ref[...] = lent[q * ghost:(q + 1) * ghost]
+
+
+def lent_rows_of(values, counts, lend_flat, ghost, directions):
+    shape = jax.ShapeDtypeStruct((ghost, values.shape[1]), values.dtype)
     whole = pl.BlockSpec(memory_space=pltpu.VMEM)
     return pl.pallas_call(
         lending_kernel,
-        out_shape=(shape,) * lend_rows.shape[0],
-        in_specs=[pl.BlockSpec(memory_space=pltpu.SMEM), whole],
-        out_specs=(whole,) * lend_rows.shape[0],
-    )(lend_rows, values)
+        out_shape=(shape,) * directions,
+        in_specs=[pl.BlockSpec(memory_space=pltpu.SMEM), whole, whole],
+        out_specs=(whole,) * directions,
+    )(counts, lend_flat, values)
 
 
 def mixing_kernel(mix_ref, anchor_ref, first_ref, second_ref, correction_ref, residual_ref):
@@ -306,7 +316,6 @@
 
 
 def per_device(start_block, jacobian, counts, columns, send_list):
-    lend_rows = send_list[0]
     jac_t = jnp.transpose(jacobian, (1, 0, 2))
 
     def ghosts(outgoing):
@@ -319,10 +328,13 @@
         )
 
     cols_t = jnp.transpose(columns, (1, 0))
-    first = apply_operator(jac_t, start_block, ghosts(lent_rows_of(start_block, lend_rows)), cols_t, counts, lend_rows)
-    first_image, first_lent, anchor = first[0], jnp.stack(first[1:5]), first[5]
+    directions, ghost = send_list.shape[1], send_list.shape[2]
+    lend_flat = send_list.reshape(1, directions * ghost)
+    first_lent = lent_rows_of(start_block, counts, lend_flat, ghost, directions)
+    first = apply_operator(jac_t, start_block, ghosts(first_lent), cols_t, counts, lend_flat)
+    first_image, first_lent, anchor = first[0], first[1:5], first[5]
     peers = lax.axis_size("wide") * lax.axis_size("narrow")
-    second = apply_operator(jac_t, first_image, ghosts(first_lent), cols_t, counts, lend_rows, anchor, peers)
+    second = apply_operator(jac_t, first_image, ghosts(first_lent), cols_t, counts, lend_flat, anchor, peers)
     second_image, raw_gram = second[0], second[6]
     everyone = lax.all_to_all(raw_gram, ("wide", "narrow"), 0, 0, tiled=True)
     raw_gram = jnp.transpose(jnp.sum(everyone, axis=0), (1, 0)).reshape(5, VECS, VECS)

time: 74 us -> 76.1 us (1.028)
  local copies, waits for them, and re-layouts: 1.98 us -> 3.31 us
    reshape x0 -> x1, local copies, waits for them, and re-layouts: none -> 1.33 us  [per_device(): lend_flat = send_list.reshape(1, directions * ghost)]
where the time goes in v11:
time: 76.1 us; the launch traced here: 75.7 us
  Pallas kernels  24.8 us (33%)
  starting transfers between devices  20.3 us (27%)
  blocking collectives  16.5 us (22%)
  waiting for transfers between devices  5.53 us (7%)
  local copies, waits for them, and re-layouts  3.31 us (4%)
  other arithmetic  2.89 us (4%)
  between operations  1.46 us (2%)
  matrix products  0.93 us (1%)
    pallas_call x2, Pallas kernels, apply_operator(): pl.pallas_call(functools.partial(coupling_kernel, with_gram), out_shape=t...  21.1 us
    all_to_all x1, blocking collectives, per_device(): everyone = lax.all_to_all(raw_gram, ('wide', 'narrow'), 0, 0, tiled=True)  16.5 us
    ppermute x2, starting transfers between devices, ghosts(): lax.ppermute(outgoing[0], 'wide', [(i, i + 1) for i in range(wide - 1)])  9.38 us
    ppermute x2, starting transfers between devices, ghosts(): lax.ppermute(outgoing[2], 'narrow', [(i, i + 1) for i in range(narrow - 1)])  5.71 us
    ppermute x2, waiting for transfers between devices, ghosts(): lax.ppermute(outgoing[3], 'narrow', [(i + 1, i) for i in range(narrow - 1)])  3.59 us
    ppermute x2, starting transfers between devices, ghosts(): lax.ppermute(outgoing[1], 'wide', [(i + 1, i) for i in range(wide - 1)])  2.58 us
    ppermute x2, starting transfers between devices, ghosts(): lax.ppermute(outgoing[3], 'narrow', [(i + 1, i) for i in range(narrow - 1)])  2.58 us
    pallas_call x1, Pallas kernels, mix_outputs(): pl.pallas_call(mixing_kernel, out_shape=(jax.ShapeDtypeStruct(anchor.shap...  1.93 us
  transfers between devices with their start and end apart: 8, of which 3 were waited for; matrix products, arithmetic and copies ran while one was open for 0% of the time, Pallas kernels for 0%

profile of v11, /device:TPU:0, one launch (start us, length us, event | category | flops | bytes accessed | tf_op | source)
XLA Modules:
  0.0 75.7 jit_solution(7208933219991078189)
XLA Ops:
  1.3 1.3 %reshape.22.lend_ref = s32[1,128]{1,0:T(1,128)} reshape(s32[1,4,32]{2,1,0:T(4,128)} %param.10) | data formatting | bytes 1024 | tf_op jit(solution)/shard_map/reshape | solution.py:332
  2.6 1.8 %shard_map.77 = (f32[32,256]{1,0:T(8,128)}, f32[32,256]{1,0:T(8,128)}, f32[32,256]{1,0:T(8,128)}, f32[32,256]{1,0:T(8,128)}) custom-call(s32[1]{0:T(128)S(6)} %copy.39.count_ref, s32[1,128]{1,0:T(1,128)} %reshape.22.lend_ref, f32[128,256]{1,0:T(8,128)} %own_ref.1), custom_call_target="tpu_custom_call" | custom-call | tf_op jit(solution)/shard_map/pallas_call | solution.py:275
  4.4 4.8 %collective-permute-start = (f32[32,256]{1,0:T(8,128)}, f32[32,256]{1,0:T(8,128)S(1)}, u32[]{:S(2)}, u32[]{:S(2)}) collective-permute-start(f32[32,256]{1,0:T(8,128)} %get-tuple-element.14), channel_id=1, source_target_pairs={{0,4},{4,8},{8,12},{12,16},{16,20},{20,24},{24,28},{1,5},{5,9},{9,... | collective-permute-start | bytes 98312 | tf_op jit(solution)/shard_map/ppermute | solution.py:324
  9.2 1.3 %collective-permute-start.1 = (f32[32,256]{1,0:T(8,128)}, f32[32,256]{1,0:T(8,128)S(1)}, u32[]{:S(2)}, u32[]{:S(2)}) collective-permute-start(f32[32,256]{1,0:T(8,128)} %get-tuple-element.15), channel_id=1, source_target_pairs={{4,0},{8,4},{12,8},{16,12},{20,16},{24,20},{28,24},{5,1},{9,5},{13... | collective-permute-start | bytes 98312 | tf_op jit(solution)/shard_map/ppermute | solution.py:325
  10.5 1.5 %collective-permute-start.2 = (f32[32,256]{1,0:T(8,128)}, f32[32,256]{1,0:T(8,128)S(1)}, u32[]{:S(2)}, u32[]{:S(2)}) collective-permute-start(f32[32,256]{1,0:T(8,128)} %get-tuple-element.16), channel_id=1, source_target_pairs={{0,1},{1,2},{2,3},{4,5},{5,6},{6,7},{8,9},{9,10},{10,11},{12,13},{... | collective-permute-start | bytes 98312 | tf_op jit(solution)/shard_map/ppermute | solution.py:326
  12.0 1.3 %collective-permute-start.3 = (f32[32,256]{1,0:T(8,128)}, f32[32,256]{1,0:T(8,128)S(1)}, u32[]{:S(2)}, u32[]{:S(2)}) collective-permute-start(f32[32,256]{1,0:T(8,128)} %get-tuple-element.17), channel_id=1, source_target_pairs={{1,0},{2,1},{3,2},{5,4},{6,5},{7,6},{9,8},{10,9},{11,10},{13,12},{... | collective-permute-start | bytes 98312 | tf_op jit(solution)/shard_map/ppermute | solution.py:327
  13.3 0.0 collective-permute-done.g0_ref
  13.3 0.0 copy-start.1
  13.3 1.9 %collective-permute-done.1.g1_ref = f32[32,256]{1,0:T(8,128)S(1)} collective-permute-done((f32[32,256]{1,0:T(8,128)}, f32[32,256]{1,0:T(8,128)S(1)}, u32[]{:S(2)}, u32[]{:S(2)}) %collective-permute-start.1) | collective-permute-done | bytes 32800 | tf_op jit(solution)/shard_map/ppermute | solution.py:325
  15.2 0.0 collective-permute-done.2.g2_ref
  15.2 1.6 %collective-permute-done.3.g3_ref = f32[32,256]{1,0:T(8,128)S(1)} collective-permute-done((f32[32,256]{1,0:T(8,128)}, f32[32,256]{1,0:T(8,128)S(1)}, u32[]{:S(2)}, u32[]{:S(2)}) %collective-permute-start.3) | collective-permute-done | bytes 32800 | tf_op jit(solution)/shard_map/ppermute | solution.py:327
  16.9 0.0 copy-done.1
  16.9 0.0 copy-done.3
  16.9 0.0 copy-done.5
  16.9 0.6 copy-done.7
  17.5 10.4 %shard_map.78 = (f32[128,256]{1,0:T(8,128)}, f32[32,256]{1,0:T(8,128)}, f32[32,256]{1,0:T(8,128)}, f32[32,256]{1,0:T(8,128)}, f32[32,256]{1,0:T(8,128)}, /*index=5*/f32[128,256]{1,0:T(8,128)}) custom-call(s32[1]{0:T(128)S(6)} %copy.39.count_ref, s32[1,128]{1,0:T(1,128)} %reshape.22.lend_ref, f32[5,128,4096]{2,1,0:T(8,128)} %bitcast.22, f32[128,256]{1,0:T(8,128)} %own_ref.1, ...), custom_call_target="tpu_custom_call" | custom-call | flops 557842432 | bytes 11272192 | tf_op jit(solution)/shard_map/pallas_call | solution.py:243
  27.9 4.5 %collective-permute-start.4 = (f32[32,256]{1,0:T(8,128)}, f32[32,256]{1,0:T(8,128)S(1)}, u32[]{:S(2)}, u32[]{:S(2)}) collective-permute-start(f32[32,256]{1,0:T(8,128)} %get-tuple-element.19), channel_id=1, source_target_pairs={{0,4},{4,8},{8,12},{12,16},{16,20},{20,24},{24,28},{1,5},{5,9},{9,... | collective-permute-start | bytes 98312 | tf_op jit(solution)/shard_map/ppermute | solution.py:324
  32.5 1.3 %collective-permute-start.5 = (f32[32,256]{1,0:T(8,128)}, f32[32,256]{1,0:T(8,128)S(1)}, u32[]{:S(2)}, u32[]{:S(2)}) collective-permute-start(f32[32,256]{1,0:T(8,128)} %get-tuple-element.20), channel_id=1, source_target_pairs={{4,0},{8,4},{12,8},{16,12},{20,16},{24,20},{28,24},{5,1},{9,5},{13... | collective-permute-start | bytes 98312 | tf_op jit(solution)/shard_map/ppermute | solution.py:325
  33.8 4.2 %collective-permute-start.6 = (f32[32,256]{1,0:T(8,128)}, f32[32,256]{1,0:T(8,128)S(1)}, u32[]{:S(2)}, u32[]{:S(2)}) collective-permute-start(f32[32,256]{1,0:T(8,128)} %get-tuple-element.21), channel_id=1, source_target_pairs={{0,1},{1,2},{2,3},{4,5},{5,6},{6,7},{8,9},{9,10},{10,11},{12,13},{... | collective-permute-start | bytes 98312 | tf_op jit(solution)/shard_map/ppermute | solution.py:326
  38.0 1.3 %collective-permute-start.7 = (f32[32,256]{1,0:T(8,128)}, f32[32,256]{1,0:T(8,128)S(1)}, u32[]{:S(2)}, u32[]{:S(2)}) collective-permute-start(f32[32,256]{1,0:T(8,128)} %get-tuple-element.22), channel_id=1, source_target_pairs={{1,0},{2,1},{3,2},{5,4},{6,5},{7,6},{9,8},{10,9},{11,10},{13,12},{... | collective-permute-start | bytes 98312 | tf_op jit(solution)/shard_map/ppermute | solution.py:327
  39.3 0.0 collective-permute-done.4.g0_ref
  39.4 0.0 copy-start
  39.4 0.0 collective-permute-done.5.g1_ref
  39.4 0.0 copy-start.2
  39.4 0.0 collective-permute-done.6.g2_ref
  39.4 1.9 %collective-permute-done.7.g3_ref = f32[32,256]{1,0:T(8,128)S(1)} collective-permute-done((f32[32,256]{1,0:T(8,128)}, f32[32,256]{1,0:T(8,128)S(1)}, u32[]{:S(2)}, u32[]{:S(2)}) %collective-permute-start.7) | collective-permute-done | bytes 32800 | tf_op jit(solution)/shard_map/ppermute | solution.py:327
  41.4 0.0 copy-done
  41.4 0.0 copy-done.4
  41.4 0.6 copy-done.6
  42.0 10.7 %shard_map.79 = (f32[128,256]{1,0:T(8,128)}, f32[32,256]{1,0:T(8,128)}, f32[32,256]{1,0:T(8,128)}, f32[32,256]{1,0:T(8,128)}, f32[32,256]{1,0:T(8,128)}, /*index=5*/f32[128,256]{1,0:T(8,128)}, f32[32,4,20]{2,1,0:T(4,128)}) custom-call(s32[1]{0:T(128)S(6)} %copy.39.count_ref, s32[1,128]{1,0:T(1,128)} %reshape.22.lend_ref, f32[5,128,4096]{2,1,0:T(8,128)} %bitcast.23, ...), custom_call_target="tpu_custom_call" | custom-call | flops 557842432 | bytes 11272192 | tf_op jit(solution)/shard_map/pallas_call | solution.py:243
  52.7 16.5 %all_to_all.5 = f32[32,4,20]{2,1,0:T(4,128)S(1)} all-to-all(f32[32,4,20]{2,1,0:T(4,128)} %get-tuple-element.24), channel_id=1, replica_groups=mesh['wide'=8,'narrow'=4] {'wide','narrow'}, dimensions={0} | all-to-all | bytes 20480 | tf_op jit(solution)/shard_map/all_to_all | solution.py:339
  69.2 0.1 mul.15
  69.3 0.1 copy.29
  69.4 0.1 multiply_reduce_fusion
  69.5 0.2 fusion.10
  69.7 0.1 copy.37
  69.8 0.1 copy.38
  69.9 0.1 copy.31
  70.0 0.1 maximum_maximum_fusion
  70.1 0.1 copy.33
  70.1 0.7 cholesky.16
  70.8 0.1 select_reduce_fusion
  70.9 0.6 compare_reduce_fusion
  71.5 0.6 fusion
  72.2 0.6 custom-call.10
  72.8 0.2 fusion.1
  73.0 0.7 fusion.6.mix_ref
  73.8 1.9 %shard_map.80 = (f32[128,256]{1,0:T(8,128)}, f32[128,256]{1,0:T(8,128)}) custom-call(f32[8,4]{1,0:T(8,128)} %fusion.6.mix_ref, f32[128,256]{1,0:T(8,128)} %get-tuple-element.23.rest_0_.anchor_ref, f32[128,256]{1,0:T(8,128)} %get-tuple-element.18.own_ref.first_ref, f32[128,256]{1,0:T(8,128)} %get-tuple-element.25.second_ref), custom_call_target="tpu_custom_call" | custom-call | tf_op jit(solution)/shard_map/pallas_call | solution.py:310
  (10 shorter events, 0.1 us)
Async XLA Ops:
  4.4 8.9 %collective-permute-start = (f32[32,256]{1,0:T(8,128)}, f32[32,256]{1,0:T(8,128)S(1)}, u32[]{:S(2)}, u32[]{:S(2)}) collective-permute-start(f32[32,256]{1,0:T(8,128)} %get-tuple-element.14), channel_id=1, source_target_pairs={{0,4},{4,8},{8,12},{12,16},{16,20},{20,24},{24,28},{1,5},{5,9},{9,... | collective-permute-start | bytes 98312 | tf_op jit(solution)/shard_map/ppermute | solution.py:324
  9.2 6.0 %collective-permute-start.1 = (f32[32,256]{1,0:T(8,128)}, f32[32,256]{1,0:T(8,128)S(1)}, u32[]{:S(2)}, u32[]{:S(2)}) collective-permute-start(f32[32,256]{1,0:T(8,128)} %get-tuple-element.15), channel_id=1, source_target_pairs={{4,0},{8,4},{12,8},{16,12},{20,16},{24,20},{28,24},{5,1},{9,5},{13... | collective-permute-start | bytes 98312 | tf_op jit(solution)/shard_map/ppermute | solution.py:325
  10.5 4.7 %collective-permute-start.2 = (f32[32,256]{1,0:T(8,128)}, f32[32,256]{1,0:T(8,128)S(1)}, u32[]{:S(2)}, u32[]{:S(2)}) collective-permute-start(f32[32,256]{1,0:T(8,128)} %get-tuple-element.16), channel_id=1, source_target_pairs={{0,1},{1,2},{2,3},{4,5},{5,6},{6,7},{8,9},{9,10},{10,11},{12,13},{... | collective-permute-start | bytes 98312 | tf_op jit(solution)/shard_map/ppermute | solution.py:326
  12.0 4.9 %collective-permute-start.3 = (f32[32,256]{1,0:T(8,128)}, f32[32,256]{1,0:T(8,128)S(1)}, u32[]{:S(2)}, u32[]{:S(2)}) collective-permute-start(f32[32,256]{1,0:T(8,128)} %get-tuple-element.17), channel_id=1, source_target_pairs={{1,0},{2,1},{3,2},{5,4},{6,5},{7,6},{9,8},{10,9},{11,10},{13,12},{... | collective-permute-start | bytes 98312 | tf_op jit(solution)/shard_map/ppermute | solution.py:327
  13.3 3.6 %copy-start.1 = (f32[32,256]{1,0:T(8,128)}, f32[32,256]{1,0:T(8,128)S(1)}, u32[]{:S(2)}) copy-start(f32[32,256]{1,0:T(8,128)S(1)} %collective-permute-done.g0_ref) | copy-start | bytes 98308
  15.2 1.7 %copy-start.3 = (f32[32,256]{1,0:T(8,128)}, f32[32,256]{1,0:T(8,128)S(1)}, u32[]{:S(2)}) copy-start(f32[32,256]{1,0:T(8,128)S(1)} %collective-permute-done.1.g1_ref) | copy-start | bytes 98308
  15.2 1.6 %copy-start.5 = (f32[32,256]{1,0:T(8,128)}, f32[32,256]{1,0:T(8,128)S(1)}, u32[]{:S(2)}) copy-start(f32[32,256]{1,0:T(8,128)S(1)} %collective-permute-done.2.g2_ref) | copy-start | bytes 98308
  16.9 0.6 copy-start.7
  17.5 51.9 %copy-start.8 = (f32[4,4,4]{2,1,0:T(4,128)S(1)}, f32[4,4,4]{2,1,0:T(4,128)}, u32[]{:S(2)}) copy-start(f32[4,4,4]{2,1,0:T(4,128)} %constant.52.clone) | copy-start | bytes 772
  27.9 11.4 %collective-permute-start.4 = (f32[32,256]{1,0:T(8,128)}, f32[32,256]{1,0:T(8,128)S(1)}, u32[]{:S(2)}, u32[]{:S(2)}) collective-permute-start(f32[32,256]{1,0:T(8,128)} %get-tuple-element.19), channel_id=1, source_target_pairs={{0,4},{4,8},{8,12},{12,16},{16,20},{20,24},{24,28},{1,5},{5,9},{9,... | collective-permute-start | bytes 98312 | tf_op jit(solution)/shard_map/ppermute | solution.py:324
  32.5 6.9 %collective-permute-start.5 = (f32[32,256]{1,0:T(8,128)}, f32[32,256]{1,0:T(8,128)S(1)}, u32[]{:S(2)}, u32[]{:S(2)}) collective-permute-start(f32[32,256]{1,0:T(8,128)} %get-tuple-element.20), channel_id=1, source_target_pairs={{4,0},{8,4},{12,8},{16,12},{20,16},{24,20},{28,24},{5,1},{9,5},{13... | collective-permute-start | bytes 98312 | tf_op jit(solution)/shard_map/ppermute | solution.py:325
  33.8 5.6 %collective-permute-start.6 = (f32[32,256]{1,0:T(8,128)}, f32[32,256]{1,0:T(8,128)S(1)}, u32[]{:S(2)}, u32[]{:S(2)}) collective-permute-start(f32[32,256]{1,0:T(8,128)} %get-tuple-element.21), channel_id=1, source_target_pairs={{0,1},{1,2},{2,3},{4,5},{5,6},{6,7},{8,9},{9,10},{10,11},{12,13},{... | collective-permute-start | bytes 98312 | tf_op jit(solution)/shard_map/ppermute | solution.py:326
  38.0 3.3 %collective-permute-start.7 = (f32[32,256]{1,0:T(8,128)}, f32[32,256]{1,0:T(8,128)S(1)}, u32[]{:S(2)}, u32[]{:S(2)}) collective-permute-start(f32[32,256]{1,0:T(8,128)} %get-tuple-element.22), channel_id=1, source_target_pairs={{1,0},{2,1},{3,2},{5,4},{6,5},{7,6},{9,8},{10,9},{11,10},{13,12},{... | collective-permute-start | bytes 98312 | tf_op jit(solution)/shard_map/ppermute | solution.py:327
  39.4 2.0 %copy-start = (f32[32,256]{1,0:T(8,128)}, f32[32,256]{1,0:T(8,128)S(1)}, u32[]{:S(2)}) copy-start(f32[32,256]{1,0:T(8,128)S(1)} %collective-permute-done.4.g0_ref) | copy-start | bytes 98308
  39.4 2.0 %copy-start.2 = (f32[32,256]{1,0:T(8,128)}, f32[32,256]{1,0:T(8,128)S(1)}, u32[]{:S(2)}) copy-start(f32[32,256]{1,0:T(8,128)S(1)} %collective-permute-done.5.g1_ref) | copy-start | bytes 98308
  39.4 2.0 %copy-start.4 = (f32[32,256]{1,0:T(8,128)}, f32[32,256]{1,0:T(8,128)S(1)}, u32[]{:S(2)}) copy-start(f32[32,256]{1,0:T(8,128)S(1)} %collective-permute-done.6.g2_ref) | copy-start | bytes 98308
  41.4 0.6 copy-start.6

commit v12 on v10

--- a/solution.py
+++ b/solution.py
@@ -296,12 +296,15 @@
 
 
 def mix_outputs(coefficients, anchor, first, second):
-    whole = pl.BlockSpec(memory_space=pltpu.VMEM)
+    count, width = anchor.shape
+    rows = min(ROWS_PER_STEP, count)
+    block = pl.BlockSpec((rows, width), lambda b: (b, 0))
     return pl.pallas_call(
         mixing_kernel,
         out_shape=(jax.ShapeDtypeStruct(anchor.shape, jnp.float32),) * 2,
-        in_specs=[pl.BlockSpec(memory_space=pltpu.SMEM), whole, whole, whole],
-        out_specs=(whole, whole),
+        grid=(count // rows,),
+        in_specs=[pl.BlockSpec(memory_space=pltpu.SMEM), block, block, block],
+        out_specs=(block, block),
     )(coefficients, anchor, first, second)
 
 

time: 74 us -> 75.4 us (1.019)
  Pallas kernels: 24.7 us -> 25.8 us
    pallas_call x1, Pallas kernels: 1.93 us -> 3.11 us  [mix_outputs(): pl.pallas_call(mixing_kernel, out_shape=(jax.ShapeDtypeStruct(anchor.shap...]
where the time goes in v12:
time: 75.4 us; the launch traced here: 74.7 us
  Pallas kernels  25.8 us (34%)
  starting transfers between devices  20.3 us (27%)
  blocking collectives  16.5 us (22%)
  waiting for transfers between devices  4.88 us (6%)
  other arithmetic  2.89 us (4%)
  local copies, waits for them, and re-layouts  1.98 us (3%)
  between operations  1.46 us (2%)
  matrix products  0.93 us (1%)
    pallas_call x2, Pallas kernels, apply_operator(): pl.pallas_call(functools.partial(coupling_kernel, with_gram), out_shape=t...  21 us
    all_to_all x1, blocking collectives, per_device(): everyone = lax.all_to_all(raw_gram, ('wide', 'narrow'), 0, 0, tiled=True)  16.5 us
    ppermute x2, starting transfers between devices, ghosts(): lax.ppermute(outgoing[0], 'wide', [(i, i + 1) for i in range(wide - 1)])  9.38 us
    ppermute x2, starting transfers between devices, ghosts(): lax.ppermute(outgoing[2], 'narrow', [(i, i + 1) for i in range(narrow - 1)])  5.71 us
    ppermute x2, waiting for transfers between devices, ghosts(): lax.ppermute(outgoing[3], 'narrow', [(i + 1, i) for i in range(narrow - 1)])  3.59 us
    pallas_call x1, Pallas kernels, mix_outputs(): pl.pallas_call(mixing_kernel, out_shape=(jax.ShapeDtypeStruct(anchor.shap...  3.11 us
    ppermute x2, starting transfers between devices, ghosts(): lax.ppermute(outgoing[3], 'narrow', [(i + 1, i) for i in range(narrow - 1)])  2.58 us
    ppermute x2, starting transfers between devices, ghosts(): lax.ppermute(outgoing[1], 'wide', [(i + 1, i) for i in range(wide - 1)])  2.58 us
  transfers between devices with their start and end apart: 8, of which 3 were waited for; matrix products, arithmetic and copies ran while one was open for 0% of the time, Pallas kernels for 0%

profile of v12, /device:TPU:0, one launch (start us, length us, event | category | flops | bytes accessed | tf_op | source)
XLA Modules:
  0.0 74.7 jit_solution(17541441844724571347)
XLA Ops:
  0.6 1.8 %shard_map.77 = (f32[32,256]{1,0:T(8,128)}, f32[32,256]{1,0:T(8,128)}, f32[32,256]{1,0:T(8,128)}, f32[32,256]{1,0:T(8,128)}) custom-call(s32[4,32]{1,0:T(4,128)} %bitcast.26, f32[128,256]{1,0:T(8,128)} %own_ref.1), custom_call_target="tpu_custom_call" | custom-call | tf_op jit(solution)/shard_map/pallas_call | solution.py:265
  2.4 4.8 %collective-permute-start = (f32[32,256]{1,0:T(8,128)}, f32[32,256]{1,0:T(8,128)S(1)}, u32[]{:S(2)}, u32[]{:S(2)}) collective-permute-start(f32[32,256]{1,0:T(8,128)} %get-tuple-element.14), channel_id=1, source_target_pairs={{0,4},{4,8},{8,12},{12,16},{16,20},{20,24},{24,28},{1,5},{5,9},{9,... | collective-permute-start | bytes 98312 | tf_op jit(solution)/shard_map/ppermute | solution.py:318
  7.2 1.3 %collective-permute-start.1 = (f32[32,256]{1,0:T(8,128)}, f32[32,256]{1,0:T(8,128)S(1)}, u32[]{:S(2)}, u32[]{:S(2)}) collective-permute-start(f32[32,256]{1,0:T(8,128)} %get-tuple-element.15), channel_id=1, source_target_pairs={{4,0},{8,4},{12,8},{16,12},{20,16},{24,20},{28,24},{5,1},{9,5},{13... | collective-permute-start | bytes 98312 | tf_op jit(solution)/shard_map/ppermute | solution.py:319
  8.5 1.5 %collective-permute-start.2 = (f32[32,256]{1,0:T(8,128)}, f32[32,256]{1,0:T(8,128)S(1)}, u32[]{:S(2)}, u32[]{:S(2)}) collective-permute-start(f32[32,256]{1,0:T(8,128)} %get-tuple-element.16), channel_id=1, source_target_pairs={{0,1},{1,2},{2,3},{4,5},{5,6},{6,7},{8,9},{9,10},{10,11},{12,13},{... | collective-permute-start | bytes 98312 | tf_op jit(solution)/shard_map/ppermute | solution.py:320
  10.0 1.3 %collective-permute-start.3 = (f32[32,256]{1,0:T(8,128)}, f32[32,256]{1,0:T(8,128)S(1)}, u32[]{:S(2)}, u32[]{:S(2)}) collective-permute-start(f32[32,256]{1,0:T(8,128)} %get-tuple-element.17), channel_id=1, source_target_pairs={{1,0},{2,1},{3,2},{5,4},{6,5},{7,6},{9,8},{10,9},{11,10},{13,12},{... | collective-permute-start | bytes 98312 | tf_op jit(solution)/shard_map/ppermute | solution.py:321
  11.9 0.0 collective-permute-done.g0_ref
  11.9 0.0 copy-start.1
  12.0 1.3 %collective-permute-done.1.g1_ref = f32[32,256]{1,0:T(8,128)S(1)} collective-permute-done((f32[32,256]{1,0:T(8,128)}, f32[32,256]{1,0:T(8,128)S(1)}, u32[]{:S(2)}, u32[]{:S(2)}) %collective-permute-start.1) | collective-permute-done | bytes 32800 | tf_op jit(solution)/shard_map/ppermute | solution.py:319
  13.2 0.0 collective-permute-done.2.g2_ref
  13.2 1.6 %collective-permute-done.3.g3_ref = f32[32,256]{1,0:T(8,128)S(1)} collective-permute-done((f32[32,256]{1,0:T(8,128)}, f32[32,256]{1,0:T(8,128)S(1)}, u32[]{:S(2)}, u32[]{:S(2)}) %collective-permute-start.3) | collective-permute-done | bytes 32800 | tf_op jit(solution)/shard_map/ppermute | solution.py:321
  14.9 0.0 copy-done.1
  14.9 0.0 copy-done.3
  14.9 0.0 copy-done.5
  14.9 0.6 copy-done.7
  15.5 10.4 %shard_map.78 = (f32[128,256]{1,0:T(8,128)}, f32[32,256]{1,0:T(8,128)}, f32[32,256]{1,0:T(8,128)}, f32[32,256]{1,0:T(8,128)}, f32[32,256]{1,0:T(8,128)}, /*index=5*/f32[128,256]{1,0:T(8,128)}) custom-call(s32[1]{0:T(128)S(6)} %copy.39.count_ref, s32[4,32]{1,0:T(4,128)} %bitcast.27, f32[5,128,4096]{2,1,0:T(8,128)} %bitcast.23, f32[128,256]{1,0:T(8,128)} %own_ref.1, ...), custom_call_target="tpu_custom_call" | custom-call | flops 557842432 | bytes 11272192 | tf_op jit(solution)/shard_map/pallas_call | solution.py:235
  25.9 4.5 %collective-permute-start.4 = (f32[32,256]{1,0:T(8,128)}, f32[32,256]{1,0:T(8,128)S(1)}, u32[]{:S(2)}, u32[]{:S(2)}) collective-permute-start(f32[32,256]{1,0:T(8,128)} %get-tuple-element.19), channel_id=1, source_target_pairs={{0,4},{4,8},{8,12},{12,16},{16,20},{20,24},{24,28},{1,5},{5,9},{9,... | collective-permute-start | bytes 98312 | tf_op jit(solution)/shard_map/ppermute | solution.py:318
  30.5 1.3 %collective-permute-start.5 = (f32[32,256]{1,0:T(8,128)}, f32[32,256]{1,0:T(8,128)S(1)}, u32[]{:S(2)}, u32[]{:S(2)}) collective-permute-start(f32[32,256]{1,0:T(8,128)} %get-tuple-element.20), channel_id=1, source_target_pairs={{4,0},{8,4},{12,8},{16,12},{20,16},{24,20},{28,24},{5,1},{9,5},{13... | collective-permute-start | bytes 98312 | tf_op jit(solution)/shard_map/ppermute | solution.py:319
  31.8 4.3 %collective-permute-start.6 = (f32[32,256]{1,0:T(8,128)}, f32[32,256]{1,0:T(8,128)S(1)}, u32[]{:S(2)}, u32[]{:S(2)}) collective-permute-start(f32[32,256]{1,0:T(8,128)} %get-tuple-element.21), channel_id=1, source_target_pairs={{0,1},{1,2},{2,3},{4,5},{5,6},{6,7},{8,9},{9,10},{10,11},{12,13},{... | collective-permute-start | bytes 98312 | tf_op jit(solution)/shard_map/ppermute | solution.py:320
  36.0 1.3 %collective-permute-start.7 = (f32[32,256]{1,0:T(8,128)}, f32[32,256]{1,0:T(8,128)S(1)}, u32[]{:S(2)}, u32[]{:S(2)}) collective-permute-start(f32[32,256]{1,0:T(8,128)} %get-tuple-element.22), channel_id=1, source_target_pairs={{1,0},{2,1},{3,2},{5,4},{6,5},{7,6},{9,8},{10,9},{11,10},{13,12},{... | collective-permute-start | bytes 98312 | tf_op jit(solution)/shard_map/ppermute | solution.py:321
  37.3 0.0 collective-permute-done.4.g0_ref
  37.3 0.0 copy-start
  37.3 0.0 collective-permute-done.5.g1_ref
  37.3 0.0 copy-start.2
  37.4 0.0 collective-permute-done.6.g2_ref
  37.4 0.0 copy-start.4
  37.4 1.9 %collective-permute-done.7.g3_ref = f32[32,256]{1,0:T(8,128)S(1)} collective-permute-done((f32[32,256]{1,0:T(8,128)}, f32[32,256]{1,0:T(8,128)S(1)}, u32[]{:S(2)}, u32[]{:S(2)}) %collective-permute-start.7) | collective-permute-done | bytes 32800 | tf_op jit(solution)/shard_map/ppermute | solution.py:321
  39.3 0.0 copy-done
  39.3 0.0 copy-done.4
  39.3 0.6 copy-done.6
  39.9 10.6 %shard_map.79 = (f32[128,256]{1,0:T(8,128)}, f32[32,256]{1,0:T(8,128)}, f32[32,256]{1,0:T(8,128)}, f32[32,256]{1,0:T(8,128)}, f32[32,256]{1,0:T(8,128)}, /*index=5*/f32[128,256]{1,0:T(8,128)}, f32[32,4,20]{2,1,0:T(4,128)}) custom-call(s32[1]{0:T(128)S(6)} %copy.39.count_ref, s32[4,32]{1,0:T(4,128)} %bitcast.28, f32[5,128,4096]{2,1,0:T(8,128)} %bitcast.24, ...), custom_call_target="tpu_custom_call" | custom-call | flops 557842432 | bytes 11272192 | tf_op jit(solution)/shard_map/pallas_call | solution.py:235
  50.5 16.5 %all_to_all.5 = f32[32,4,20]{2,1,0:T(4,128)S(1)} all-to-all(f32[32,4,20]{2,1,0:T(4,128)} %get-tuple-element.24), channel_id=1, replica_groups=mesh['wide'=8,'narrow'=4] {'wide','narrow'}, dimensions={0} | all-to-all | bytes 20480 | tf_op jit(solution)/shard_map/all_to_all | solution.py:330
  67.1 0.1 mul.15
  67.1 0.1 copy.29
  67.2 0.1 multiply_reduce_fusion
  67.3 0.2 fusion.10
  67.5 0.1 copy.37
  67.6 0.1 copy.38
  67.7 0.1 copy.31
  67.8 0.1 maximum_maximum_fusion
  67.9 0.1 copy.33
  68.0 0.7 cholesky.16
  68.7 0.1 select_reduce_fusion
  68.7 0.6 compare_reduce_fusion
  69.4 0.6 fusion
  70.0 0.6 custom-call.10
  70.7 0.2 fusion.1
  70.9 0.7 fusion.6.mix_ref
  71.6 3.1 %shard_map.80 = (f32[128,256]{1,0:T(8,128)}, f32[128,256]{1,0:T(8,128)}) custom-call(f32[8,4]{1,0:T(8,128)} %fusion.6.mix_ref, f32[128,256]{1,0:T(8,128)} %get-tuple-element.23.rest_0_.anchor_ref, f32[128,256]{1,0:T(8,128)} %get-tuple-element.18.own_ref.first_ref, f32[128,256]{1,0:T(8,128)} %get-tuple-element.25.second_ref), custom_call_target="tpu_custom_call" | custom-call | tf_op jit(solution)/shard_map/pallas_call | solution.py:302
  (9 shorter events, 0.1 us)
Async XLA Ops:
  2.4 9.6 %collective-permute-start = (f32[32,256]{1,0:T(8,128)}, f32[32,256]{1,0:T(8,128)S(1)}, u32[]{:S(2)}, u32[]{:S(2)}) collective-permute-start(f32[32,256]{1,0:T(8,128)} %get-tuple-element.14), channel_id=1, source_target_pairs={{0,4},{4,8},{8,12},{12,16},{16,20},{20,24},{24,28},{1,5},{5,9},{9,... | collective-permute-start | bytes 98312 | tf_op jit(solution)/shard_map/ppermute | solution.py:318
  7.2 6.0 %collective-permute-start.1 = (f32[32,256]{1,0:T(8,128)}, f32[32,256]{1,0:T(8,128)S(1)}, u32[]{:S(2)}, u32[]{:S(2)}) collective-permute-start(f32[32,256]{1,0:T(8,128)} %get-tuple-element.15), channel_id=1, source_target_pairs={{4,0},{8,4},{12,8},{16,12},{20,16},{24,20},{28,24},{5,1},{9,5},{13... | collective-permute-start | bytes 98312 | tf_op jit(solution)/shard_map/ppermute | solution.py:319
  8.5 4.7 %collective-permute-start.2 = (f32[32,256]{1,0:T(8,128)}, f32[32,256]{1,0:T(8,128)S(1)}, u32[]{:S(2)}, u32[]{:S(2)}) collective-permute-start(f32[32,256]{1,0:T(8,128)} %get-tuple-element.16), channel_id=1, source_target_pairs={{0,1},{1,2},{2,3},{4,5},{5,6},{6,7},{8,9},{9,10},{10,11},{12,13},{... | collective-permute-start | bytes 98312 | tf_op jit(solution)/shard_map/ppermute | solution.py:320
  10.0 4.9 %collective-permute-start.3 = (f32[32,256]{1,0:T(8,128)}, f32[32,256]{1,0:T(8,128)S(1)}, u32[]{:S(2)}, u32[]{:S(2)}) collective-permute-start(f32[32,256]{1,0:T(8,128)} %get-tuple-element.17), channel_id=1, source_target_pairs={{1,0},{2,1},{3,2},{5,4},{6,5},{7,6},{9,8},{10,9},{11,10},{13,12},{... | collective-permute-start | bytes 98312 | tf_op jit(solution)/shard_map/ppermute | solution.py:321
  11.9 2.9 %copy-start.1 = (f32[32,256]{1,0:T(8,128)}, f32[32,256]{1,0:T(8,128)S(1)}, u32[]{:S(2)}) copy-start(f32[32,256]{1,0:T(8,128)S(1)} %collective-permute-done.g0_ref) | copy-start | bytes 98308
  13.2 1.7 %copy-start.3 = (f32[32,256]{1,0:T(8,128)}, f32[32,256]{1,0:T(8,128)S(1)}, u32[]{:S(2)}) copy-start(f32[32,256]{1,0:T(8,128)S(1)} %collective-permute-done.1.g1_ref) | copy-start | bytes 98308
  13.2 1.6 %copy-start.5 = (f32[32,256]{1,0:T(8,128)}, f32[32,256]{1,0:T(8,128)S(1)}, u32[]{:S(2)}) copy-start(f32[32,256]{1,0:T(8,128)S(1)} %collective-permute-done.2.g2_ref) | copy-start | bytes 98308
  14.9 0.6 copy-start.7
  15.5 51.7 %copy-start.8 = (f32[4,4,4]{2,1,0:T(4,128)S(1)}, f32[4,4,4]{2,1,0:T(4,128)}, u32[]{:S(2)}) copy-start(f32[4,4,4]{2,1,0:T(4,128)} %constant.52.clone) | copy-start | bytes 772
  25.9 11.4 %collective-permute-start.4 = (f32[32,256]{1,0:T(8,128)}, f32[32,256]{1,0:T(8,128)S(1)}, u32[]{:S(2)}, u32[]{:S(2)}) collective-permute-start(f32[32,256]{1,0:T(8,128)} %get-tuple-element.19), channel_id=1, source_target_pairs={{0,4},{4,8},{8,12},{12,16},{16,20},{20,24},{24,28},{1,5},{5,9},{9,... | collective-permute-start | bytes 98312 | tf_op jit(solution)/shard_map/ppermute | solution.py:318
  30.5 6.9 %collective-permute-start.5 = (f32[32,256]{1,0:T(8,128)}, f32[32,256]{1,0:T(8,128)S(1)}, u32[]{:S(2)}, u32[]{:S(2)}) collective-permute-start(f32[32,256]{1,0:T(8,128)} %get-tuple-element.20), channel_id=1, source_target_pairs={{4,0},{8,4},{12,8},{16,12},{20,16},{24,20},{28,24},{5,1},{9,5},{13... | collective-permute-start | bytes 98312 | tf_op jit(solution)/shard_map/ppermute | solution.py:319
  31.8 5.6 %collective-permute-start.6 = (f32[32,256]{1,0:T(8,128)}, f32[32,256]{1,0:T(8,128)S(1)}, u32[]{:S(2)}, u32[]{:S(2)}) collective-permute-start(f32[32,256]{1,0:T(8,128)} %get-tuple-element.21), channel_id=1, source_target_pairs={{0,1},{1,2},{2,3},{4,5},{5,6},{6,7},{8,9},{9,10},{10,11},{12,13},{... | collective-permute-start | bytes 98312 | tf_op jit(solution)/shard_map/ppermute | solution.py:320
  36.0 3.3 %collective-permute-start.7 = (f32[32,256]{1,0:T(8,128)}, f32[32,256]{1,0:T(8,128)S(1)}, u32[]{:S(2)}, u32[]{:S(2)}) collective-permute-start(f32[32,256]{1,0:T(8,128)} %get-tuple-element.22), channel_id=1, source_target_pairs={{1,0},{2,1},{3,2},{5,4},{6,5},{7,6},{9,8},{10,9},{11,10},{13,12},{... | collective-permute-start | bytes 98312 | tf_op jit(solution)/shard_map/ppermute | solution.py:321
  37.3 2.0 %copy-start = (f32[32,256]{1,0:T(8,128)}, f32[32,256]{1,0:T(8,128)S(1)}, u32[]{:S(2)}) copy-start(f32[32,256]{1,0:T(8,128)S(1)} %collective-permute-done.4.g0_ref) | copy-start | bytes 98308
  37.3 2.0 %copy-start.2 = (f32[32,256]{1,0:T(8,128)}, f32[32,256]{1,0:T(8,128)S(1)}, u32[]{:S(2)}) copy-start(f32[32,256]{1,0:T(8,128)S(1)} %collective-permute-done.5.g1_ref) | copy-start | bytes 98308
  37.4 2.0 %copy-start.4 = (f32[32,256]{1,0:T(8,128)}, f32[32,256]{1,0:T(8,128)S(1)}, u32[]{:S(2)}) copy-start(f32[32,256]{1,0:T(8,128)S(1)} %collective-permute-done.6.g2_ref) | copy-start | bytes 98308
  39.3 0.6 copy-start.6

commit v13 on v10

--- a/solution.py
+++ b/solution.py
@@ -14,7 +14,7 @@
 E_DEV = 128
 LANES = 128
 SUBLANES = 8
-UNROLL = 4
+UNROLL = 32
 CHUNK_ROWS = 16
 ROWS_PER_STEP = 32
 

time: 74 us -> 70.7 us (0.955)
  Pallas kernels: 24.7 us -> 21.4 us
    pallas_call x2, Pallas kernels: 21 us -> 17.7 us  [apply_operator(): pl.pallas_call(functools.partial(coupling_kernel, with_gram), out_shape=t...]
where the time goes in v13:
time: 70.7 us; the launch traced here: 70.3 us
  Pallas kernels  21.4 us (30%)
  starting transfers between devices  20.3 us (29%)
  blocking collectives  16.5 us (23%)
  waiting for transfers between devices  4.88 us (7%)
  other arithmetic  2.89 us (4%)
  local copies, waits for them, and re-layouts  1.98 us (3%)
  between operations  1.46 us (2%)
  matrix products  0.93 us (1%)
    pallas_call x2, Pallas kernels, apply_operator(): pl.pallas_call(functools.partial(coupling_kernel, with_gram), out_shape=t...  17.7 us
    all_to_all x1, blocking collectives, per_device(): everyone = lax.all_to_all(raw_gram, ('wide', 'narrow'), 0, 0, tiled=True)  16.5 us
    ppermute x2, starting transfers between devices, ghosts(): lax.ppermute(outgoing[0], 'wide', [(i, i + 1) for i in range(wide - 1)])  9.38 us
    ppermute x2, starting transfers between devices, ghosts(): lax.ppermute(outgoing[2], 'narrow', [(i, i + 1) for i in range(narrow - 1)])  5.72 us
    ppermute x2, waiting for transfers between devices, ghosts(): lax.ppermute(outgoing[3], 'narrow', [(i + 1, i) for i in range(narrow - 1)])  3.59 us
    ppermute x2, starting transfers between devices, ghosts(): lax.ppermute(outgoing[1], 'wide', [(i + 1, i) for i in range(wide - 1)])  2.58 us
    ppermute x2, starting transfers between devices, ghosts(): lax.ppermute(outgoing[3], 'narrow', [(i + 1, i) for i in range(narrow - 1)])  2.58 us
    pallas_call x1, Pallas kernels, mix_outputs(): pl.pallas_call(mixing_kernel, out_shape=(jax.ShapeDtypeStruct(anchor.shap...  1.93 us
  transfers between devices with their start and end apart: 8, of which 3 were waited for; matrix products, arithmetic and copies ran while one was open for 0% of the time, Pallas kernels for 0%

profile of v13, /device:TPU:0, one launch (start us, length us, event | category | flops | bytes accessed | tf_op | source)
XLA Modules:
  0.0 70.3 jit_solution(1377780537472888565)
XLA Ops:
  0.6 1.8 %shard_map.77 = (f32[32,256]{1,0:T(8,128)}, f32[32,256]{1,0:T(8,128)}, f32[32,256]{1,0:T(8,128)}, f32[32,256]{1,0:T(8,128)}) custom-call(s32[4,32]{1,0:T(4,128)} %bitcast.26, f32[128,256]{1,0:T(8,128)} %own_ref.1), custom_call_target="tpu_custom_call" | custom-call | tf_op jit(solution)/shard_map/pallas_call | solution.py:265
  2.4 4.8 %collective-permute-start = (f32[32,256]{1,0:T(8,128)}, f32[32,256]{1,0:T(8,128)S(1)}, u32[]{:S(2)}, u32[]{:S(2)}) collective-permute-start(f32[32,256]{1,0:T(8,128)} %get-tuple-element.14), channel_id=1, source_target_pairs={{0,4},{4,8},{8,12},{12,16},{16,20},{20,24},{24,28},{1,5},{5,9},{9,... | collective-permute-start | bytes 98312 | tf_op jit(solution)/shard_map/ppermute | solution.py:315
  7.2 1.3 %collective-permute-start.1 = (f32[32,256]{1,0:T(8,128)}, f32[32,256]{1,0:T(8,128)S(1)}, u32[]{:S(2)}, u32[]{:S(2)}) collective-permute-start(f32[32,256]{1,0:T(8,128)} %get-tuple-element.15), channel_id=1, source_target_pairs={{4,0},{8,4},{12,8},{16,12},{20,16},{24,20},{28,24},{5,1},{9,5},{13... | collective-permute-start | bytes 98312 | tf_op jit(solution)/shard_map/ppermute | solution.py:316
  8.5 1.5 %collective-permute-start.2 = (f32[32,256]{1,0:T(8,128)}, f32[32,256]{1,0:T(8,128)S(1)}, u32[]{:S(2)}, u32[]{:S(2)}) collective-permute-start(f32[32,256]{1,0:T(8,128)} %get-tuple-element.16), channel_id=1, source_target_pairs={{0,1},{1,2},{2,3},{4,5},{5,6},{6,7},{8,9},{9,10},{10,11},{12,13},{... | collective-permute-start | bytes 98312 | tf_op jit(solution)/shard_map/ppermute | solution.py:317
  10.0 1.3 %collective-permute-start.3 = (f32[32,256]{1,0:T(8,128)}, f32[32,256]{1,0:T(8,128)S(1)}, u32[]{:S(2)}, u32[]{:S(2)}) collective-permute-start(f32[32,256]{1,0:T(8,128)} %get-tuple-element.17), channel_id=1, source_target_pairs={{1,0},{2,1},{3,2},{5,4},{6,5},{7,6},{9,8},{10,9},{11,10},{13,12},{... | collective-permute-start | bytes 98312 | tf_op jit(solution)/shard_map/ppermute | solution.py:318
  11.9 0.0 collective-permute-done.g0_ref
  11.9 0.0 copy-start.1
  12.0 1.3 %collective-permute-done.1.g1_ref = f32[32,256]{1,0:T(8,128)S(1)} collective-permute-done((f32[32,256]{1,0:T(8,128)}, f32[32,256]{1,0:T(8,128)S(1)}, u32[]{:S(2)}, u32[]{:S(2)}) %collective-permute-start.1) | collective-permute-done | bytes 32800 | tf_op jit(solution)/shard_map/ppermute | solution.py:316
  13.2 0.0 collective-permute-done.2.g2_ref
  13.2 1.6 %collective-permute-done.3.g3_ref = f32[32,256]{1,0:T(8,128)S(1)} collective-permute-done((f32[32,256]{1,0:T(8,128)}, f32[32,256]{1,0:T(8,128)S(1)}, u32[]{:S(2)}, u32[]{:S(2)}) %collective-permute-start.3) | collective-permute-done | bytes 32800 | tf_op jit(solution)/shard_map/ppermute | solution.py:318
  14.9 0.0 copy-done.1
  14.9 0.0 copy-done.3
  14.9 0.0 copy-done.5
  14.9 0.6 copy-done.7
  15.5 8.7 %shard_map.78 = (f32[128,256]{1,0:T(8,128)}, f32[32,256]{1,0:T(8,128)}, f32[32,256]{1,0:T(8,128)}, f32[32,256]{1,0:T(8,128)}, f32[32,256]{1,0:T(8,128)}, /*index=5*/f32[128,256]{1,0:T(8,128)}) custom-call(s32[1]{0:T(128)S(6)} %copy.39.count_ref, s32[4,32]{1,0:T(4,128)} %bitcast.27, f32[5,128,4096]{2,1,0:T(8,128)} %bitcast.23, f32[128,256]{1,0:T(8,128)} %own_ref.1, ...), custom_call_target="tpu_custom_call" | custom-call | flops 557842432 | bytes 11272192 | tf_op jit(solution)/shard_map/pallas_call | solution.py:235
  24.3 4.5 %collective-permute-start.4 = (f32[32,256]{1,0:T(8,128)}, f32[32,256]{1,0:T(8,128)S(1)}, u32[]{:S(2)}, u32[]{:S(2)}) collective-permute-start(f32[32,256]{1,0:T(8,128)} %get-tuple-element.19), channel_id=1, source_target_pairs={{0,4},{4,8},{8,12},{12,16},{16,20},{20,24},{24,28},{1,5},{5,9},{9,... | collective-permute-start | bytes 98312 | tf_op jit(solution)/shard_map/ppermute | solution.py:315
  28.8 1.3 %collective-permute-start.5 = (f32[32,256]{1,0:T(8,128)}, f32[32,256]{1,0:T(8,128)S(1)}, u32[]{:S(2)}, u32[]{:S(2)}) collective-permute-start(f32[32,256]{1,0:T(8,128)} %get-tuple-element.20), channel_id=1, source_target_pairs={{4,0},{8,4},{12,8},{16,12},{20,16},{24,20},{28,24},{5,1},{9,5},{13... | collective-permute-start | bytes 98312 | tf_op jit(solution)/shard_map/ppermute | solution.py:316
  30.1 4.3 %collective-permute-start.6 = (f32[32,256]{1,0:T(8,128)}, f32[32,256]{1,0:T(8,128)S(1)}, u32[]{:S(2)}, u32[]{:S(2)}) collective-permute-start(f32[32,256]{1,0:T(8,128)} %get-tuple-element.21), channel_id=1, source_target_pairs={{0,1},{1,2},{2,3},{4,5},{5,6},{6,7},{8,9},{9,10},{10,11},{12,13},{... | collective-permute-start | bytes 98312 | tf_op jit(solution)/shard_map/ppermute | solution.py:317
  34.4 1.3 %collective-permute-start.7 = (f32[32,256]{1,0:T(8,128)}, f32[32,256]{1,0:T(8,128)S(1)}, u32[]{:S(2)}, u32[]{:S(2)}) collective-permute-start(f32[32,256]{1,0:T(8,128)} %get-tuple-element.22), channel_id=1, source_target_pairs={{1,0},{2,1},{3,2},{5,4},{6,5},{7,6},{9,8},{10,9},{11,10},{13,12},{... | collective-permute-start | bytes 98312 | tf_op jit(solution)/shard_map/ppermute | solution.py:318
  35.7 0.0 collective-permute-done.4.g0_ref
  35.7 0.0 copy-start
  35.7 0.0 collective-permute-done.5.g1_ref
  35.7 0.0 copy-start.2
  35.7 0.0 collective-permute-done.6.g2_ref
  35.7 1.9 %collective-permute-done.7.g3_ref = f32[32,256]{1,0:T(8,128)S(1)} collective-permute-done((f32[32,256]{1,0:T(8,128)}, f32[32,256]{1,0:T(8,128)S(1)}, u32[]{:S(2)}, u32[]{:S(2)}) %collective-permute-start.7) | collective-permute-done | bytes 32800 | tf_op jit(solution)/shard_map/ppermute | solution.py:318
  37.7 0.0 copy-done
  37.7 0.0 copy-done.4
  37.7 0.6 copy-done.6
  38.3 8.9 %shard_map.79 = (f32[128,256]{1,0:T(8,128)}, f32[32,256]{1,0:T(8,128)}, f32[32,256]{1,0:T(8,128)}, f32[32,256]{1,0:T(8,128)}, f32[32,256]{1,0:T(8,128)}, /*index=5*/f32[128,256]{1,0:T(8,128)}, f32[32,4,20]{2,1,0:T(4,128)}) custom-call(s32[1]{0:T(128)S(6)} %copy.39.count_ref, s32[4,32]{1,0:T(4,128)} %bitcast.28, f32[5,128,4096]{2,1,0:T(8,128)} %bitcast.24, ...), custom_call_target="tpu_custom_call" | custom-call | flops 557842432 | bytes 11272192 | tf_op jit(solution)/shard_map/pallas_call | solution.py:235
  47.2 16.5 %all_to_all.5 = f32[32,4,20]{2,1,0:T(4,128)S(1)} all-to-all(f32[32,4,20]{2,1,0:T(4,128)} %get-tuple-element.24), channel_id=1, replica_groups=mesh['wide'=8,'narrow'=4] {'wide','narrow'}, dimensions={0} | all-to-all | bytes 20480 | tf_op jit(solution)/shard_map/all_to_all | solution.py:327
  63.8 0.1 mul.15
  63.9 0.1 copy.29
  64.0 0.0 copy-done.8
  64.0 0.1 multiply_reduce_fusion
  64.1 0.2 fusion.10
  64.2 0.1 copy.37
  64.3 0.1 copy.38
  64.5 0.1 copy.31
  64.5 0.1 maximum_maximum_fusion
  64.6 0.1 copy.33
  64.7 0.7 cholesky.16
  65.4 0.1 select_reduce_fusion
  65.5 0.6 compare_reduce_fusion
  66.1 0.6 fusion
  66.8 0.6 custom-call.10
  67.4 0.2 fusion.1
  67.6 0.7 %fusion.6.mix_ref = f32[8,4]{1,0:T(8,128)} fusion(f32[8,4]{0,1:T(4,128)S(1)} %fusion.1, f32[1,8,8]{1,2,0:T(8,128)S(1)} %custom-call.10), kind=kOutput, calls=%fused_computation.12 | convolution fusion | flops 3072 | bytes 512 | tf_op jit(solution)/shard_map/jit(_cho_solve)/triangular_solve | solution.py:343
  68.3 1.9 %shard_map.80 = (f32[128,256]{1,0:T(8,128)}, f32[128,256]{1,0:T(8,128)}) custom-call(f32[8,4]{1,0:T(8,128)} %fusion.6.mix_ref, f32[128,256]{1,0:T(8,128)} %get-tuple-element.23.rest_0_.anchor_ref, f32[128,256]{1,0:T(8,128)} %get-tuple-element.18.own_ref.first_ref, f32[128,256]{1,0:T(8,128)} %get-tuple-element.25.second_ref), custom_call_target="tpu_custom_call" | custom-call | tf_op jit(solution)/shard_map/pallas_call | solution.py:300
  (9 shorter events, 0.1 us)
Async XLA Ops:
  2.4 9.6 %collective-permute-start = (f32[32,256]{1,0:T(8,128)}, f32[32,256]{1,0:T(8,128)S(1)}, u32[]{:S(2)}, u32[]{:S(2)}) collective-permute-start(f32[32,256]{1,0:T(8,128)} %get-tuple-element.14), channel_id=1, source_target_pairs={{0,4},{4,8},{8,12},{12,16},{16,20},{20,24},{24,28},{1,5},{5,9},{9,... | collective-permute-start | bytes 98312 | tf_op jit(solution)/shard_map/ppermute | solution.py:315
  7.2 6.0 %collective-permute-start.1 = (f32[32,256]{1,0:T(8,128)}, f32[32,256]{1,0:T(8,128)S(1)}, u32[]{:S(2)}, u32[]{:S(2)}) collective-permute-start(f32[32,256]{1,0:T(8,128)} %get-tuple-element.15), channel_id=1, source_target_pairs={{4,0},{8,4},{12,8},{16,12},{20,16},{24,20},{28,24},{5,1},{9,5},{13... | collective-permute-start | bytes 98312 | tf_op jit(solution)/shard_map/ppermute | solution.py:316
  8.5 4.7 %collective-permute-start.2 = (f32[32,256]{1,0:T(8,128)}, f32[32,256]{1,0:T(8,128)S(1)}, u32[]{:S(2)}, u32[]{:S(2)}) collective-permute-start(f32[32,256]{1,0:T(8,128)} %get-tuple-element.16), channel_id=1, source_target_pairs={{0,1},{1,2},{2,3},{4,5},{5,6},{6,7},{8,9},{9,10},{10,11},{12,13},{... | collective-permute-start | bytes 98312 | tf_op jit(solution)/shard_map/ppermute | solution.py:317
  10.0 4.9 %collective-permute-start.3 = (f32[32,256]{1,0:T(8,128)}, f32[32,256]{1,0:T(8,128)S(1)}, u32[]{:S(2)}, u32[]{:S(2)}) collective-permute-start(f32[32,256]{1,0:T(8,128)} %get-tuple-element.17), channel_id=1, source_target_pairs={{1,0},{2,1},{3,2},{5,4},{6,5},{7,6},{9,8},{10,9},{11,10},{13,12},{... | collective-permute-start | bytes 98312 | tf_op jit(solution)/shard_map/ppermute | solution.py:318
  11.9 2.9 %copy-start.1 = (f32[32,256]{1,0:T(8,128)}, f32[32,256]{1,0:T(8,128)S(1)}, u32[]{:S(2)}) copy-start(f32[32,256]{1,0:T(8,128)S(1)} %collective-permute-done.g0_ref) | copy-start | bytes 98308
  13.2 1.7 %copy-start.3 = (f32[32,256]{1,0:T(8,128)}, f32[32,256]{1,0:T(8,128)S(1)}, u32[]{:S(2)}) copy-start(f32[32,256]{1,0:T(8,128)S(1)} %collective-permute-done.1.g1_ref) | copy-start | bytes 98308
  13.2 1.6 %copy-start.5 = (f32[32,256]{1,0:T(8,128)}, f32[32,256]{1,0:T(8,128)S(1)}, u32[]{:S(2)}) copy-start(f32[32,256]{1,0:T(8,128)S(1)} %collective-permute-done.2.g2_ref) | copy-start | bytes 98308
  14.9 0.6 copy-start.7
  15.5 48.5 %copy-start.8 = (f32[4,4,4]{2,1,0:T(4,128)S(1)}, f32[4,4,4]{2,1,0:T(4,128)}, u32[]{:S(2)}) copy-start(f32[4,4,4]{2,1,0:T(4,128)} %constant.52.clone) | copy-start | bytes 772
  24.3 11.4 %collective-permute-start.4 = (f32[32,256]{1,0:T(8,128)}, f32[32,256]{1,0:T(8,128)S(1)}, u32[]{:S(2)}, u32[]{:S(2)}) collective-permute-start(f32[32,256]{1,0:T(8,128)} %get-tuple-element.19), channel_id=1, source_target_pairs={{0,4},{4,8},{8,12},{12,16},{16,20},{20,24},{24,28},{1,5},{5,9},{9,... | collective-permute-start | bytes 98312 | tf_op jit(solution)/shard_map/ppermute | solution.py:315
  28.8 6.9 %collective-permute-start.5 = (f32[32,256]{1,0:T(8,128)}, f32[32,256]{1,0:T(8,128)S(1)}, u32[]{:S(2)}, u32[]{:S(2)}) collective-permute-start(f32[32,256]{1,0:T(8,128)} %get-tuple-element.20), channel_id=1, source_target_pairs={{4,0},{8,4},{12,8},{16,12},{20,16},{24,20},{28,24},{5,1},{9,5},{13... | collective-permute-start | bytes 98312 | tf_op jit(solution)/shard_map/ppermute | solution.py:316
  30.1 5.6 %collective-permute-start.6 = (f32[32,256]{1,0:T(8,128)}, f32[32,256]{1,0:T(8,128)S(1)}, u32[]{:S(2)}, u32[]{:S(2)}) collective-permute-start(f32[32,256]{1,0:T(8,128)} %get-tuple-element.21), channel_id=1, source_target_pairs={{0,1},{1,2},{2,3},{4,5},{5,6},{6,7},{8,9},{9,10},{10,11},{12,13},{... | collective-permute-start | bytes 98312 | tf_op jit(solution)/shard_map/ppermute | solution.py:317
  34.4 3.3 %collective-permute-start.7 = (f32[32,256]{1,0:T(8,128)}, f32[32,256]{1,0:T(8,128)S(1)}, u32[]{:S(2)}, u32[]{:S(2)}) collective-permute-start(f32[32,256]{1,0:T(8,128)} %get-tuple-element.22), channel_id=1, source_target_pairs={{1,0},{2,1},{3,2},{5,4},{6,5},{7,6},{9,8},{10,9},{11,10},{13,12},{... | collective-permute-start | bytes 98312 | tf_op jit(solution)/shard_map/ppermute | solution.py:318
  35.7 2.0 %copy-start = (f32[32,256]{1,0:T(8,128)}, f32[32,256]{1,0:T(8,128)S(1)}, u32[]{:S(2)}) copy-start(f32[32,256]{1,0:T(8,128)S(1)} %collective-permute-done.4.g0_ref) | copy-start | bytes 98308
  35.7 2.0 %copy-start.2 = (f32[32,256]{1,0:T(8,128)}, f32[32,256]{1,0:T(8,128)S(1)}, u32[]{:S(2)}) copy-start(f32[32,256]{1,0:T(8,128)S(1)} %collective-permute-done.5.g1_ref) | copy-start | bytes 98308
  35.7 2.0 %copy-start.4 = (f32[32,256]{1,0:T(8,128)}, f32[32,256]{1,0:T(8,128)S(1)}, u32[]{:S(2)}) copy-start(f32[32,256]{1,0:T(8,128)S(1)} %collective-permute-done.6.g2_ref) | copy-start | bytes 98308
  37.7 0.6 copy-start.6

commit v14 on v13

--- a/solution.py
+++ b/solution.py
@@ -118,11 +118,11 @@
 
 def coupling_kernel(with_gram, count_ref, lend_ref, jac_hbm, own_ref, g0_ref, g1_ref, g2_ref, g3_ref, cols_ref, *rest):
     if with_gram:
-        anchor_ref, rest = rest[0], rest[1:]
-    out_ref, l0_ref, l1_ref, l2_ref, l3_ref, kept_ref = rest[:6]
-    rest = rest[6:]
-    if with_gram:
-        gram_ref, rest = rest[0], rest[1:]
+        anchor_ref, out_ref, gram_ref = rest[:3]
+        rest = rest[3:]
+    else:
+        out_ref, l0_ref, l1_ref, l2_ref, l3_ref, kept_ref = rest[:6]
+        rest = rest[6:]
     jac_ref, sems, source_ref, picked_ref, z_ref, parts_ref = rest
     tiles = jac_ref.shape[2] // LANES
     count = own_ref.shape[0]
@@ -203,11 +203,12 @@
     image = jnp.where(living, DIAG_SHIFT * own + coupled, jnp.float32(0.0))
     out_ref[...] = image
     kept = jnp.where(living, own, jnp.float32(0.0))
-    kept_ref[...] = kept
-    for q, lent_ref in enumerate((l0_ref, l1_ref, l2_ref, l3_ref)):
-        for j in range(lend_ref.shape[1]):
-            lent_ref[j:j + 1, :] = out_ref[pl.ds(lend_ref[q, j], 1), :]
-    if with_gram:
+    if not with_gram:
+        kept_ref[...] = kept
+        for q, lent_ref in enumerate((l0_ref, l1_ref, l2_ref, l3_ref)):
+            for j in range(lend_ref.shape[1]):
+                lent_ref[j:j + 1, :] = out_ref[pl.ds(lend_ref[q, j], 1), :]
+    else:
         anchor = anchor_ref[...]
         partial = gram_columns(((kept, anchor), (kept, kept), (image, anchor), (image, kept), (image, image)))
         for target in range(gram_ref.shape[0]):
@@ -225,13 +226,14 @@
     lent = lend_rows.shape[1]
     in_specs = [smem, smem, pl.BlockSpec(memory_space=pl.ANY), vmem, vmem, vmem, vmem, vmem, vmem]
     out_shape = [jax.ShapeDtypeStruct((count, width), jnp.float32)]
-    out_shape += [jax.ShapeDtypeStruct((lent, width), jnp.float32)] * lend_rows.shape[0]
-    out_shape += [jax.ShapeDtypeStruct((count, width), jnp.float32)]
     args = [counts, lend_rows, jac_t, own, *ghost_rows, cols_t]
     if with_gram:
         in_specs.append(vmem)
         args.append(anchor)
         out_shape.append(jax.ShapeDtypeStruct((peers, VECS, 5 * VECS), jnp.float32))
+    else:
+        out_shape += [jax.ShapeDtypeStruct((lent, width), jnp.float32)] * lend_rows.shape[0]
+        out_shape += [jax.ShapeDtypeStruct((count, width), jnp.float32)]
     return pl.pallas_call(
         functools.partial(coupling_kernel, with_gram),
         out_shape=tuple(out_shape),
@@ -323,7 +325,7 @@
     first_image, first_lent, anchor = first[0], jnp.stack(first[1:5]), first[5]
     peers = lax.axis_size("wide") * lax.axis_size("narrow")
     second = apply_operator(jac_t, first_image, ghosts(first_lent), cols_t, counts, lend_rows, anchor, peers)
-    second_image, raw_gram = second[0], second[6]
+    second_image, raw_gram = second
     everyone = lax.all_to_all(raw_gram, ("wide", "narrow"), 0, 0, tiled=True)
     raw_gram = jnp.transpose(jnp.sum(everyone, axis=0), (1, 0)).reshape(5, VECS, VECS)
     shift = np.arange(VECS)[:, None, None]

time: 70.7 us -> 70.6 us (level)
  no operation moved by 1% of the time
where the time goes in v14:
time: 70.6 us; the launch traced here: 70.2 us
  Pallas kernels  21.3 us (30%)
  starting transfers between devices  20.3 us (29%)
  blocking collectives  16.5 us (23%)
  waiting for transfers between devices  4.88 us (7%)
  other arithmetic  2.89 us (4%)
  local copies, waits for them, and re-layouts  1.96 us (3%)
  between operations  1.46 us (2%)
  matrix products  0.93 us (1%)
    pallas_call x2, Pallas kernels, apply_operator(): pl.pallas_call(functools.partial(coupling_kernel, with_gram), out_shape=t...  17.6 us
    all_to_all x1, blocking collectives, per_device(): everyone = lax.all_to_all(raw_gram, ('wide', 'narrow'), 0, 0, tiled=True)  16.5 us
    ppermute x2, starting transfers between devices, ghosts(): lax.ppermute(outgoing[0], 'wide', [(i, i + 1) for i in range(wide - 1)])  9.37 us
    ppermute x2, starting transfers between devices, ghosts(): lax.ppermute(outgoing[2], 'narrow', [(i, i + 1) for i in range(narrow - 1)])  5.72 us
    ppermute x2, waiting for transfers between devices, ghosts(): lax.ppermute(outgoing[3], 'narrow', [(i + 1, i) for i in range(narrow - 1)])  3.59 us
    ppermute x2, starting transfers between devices, ghosts(): lax.ppermute(outgoing[1], 'wide', [(i + 1, i) for i in range(wide - 1)])  2.58 us
    ppermute x2, starting transfers between devices, ghosts(): lax.ppermute(outgoing[3], 'narrow', [(i + 1, i) for i in range(narrow - 1)])  2.58 us
    pallas_call x1, Pallas kernels, mix_outputs(): pl.pallas_call(mixing_kernel, out_shape=(jax.ShapeDtypeStruct(anchor.shap...  1.93 us
  transfers between devices with their start and end apart: 8, of which 3 were waited for; matrix products, arithmetic and copies ran while one was open for 0% of the time, Pallas kernels for 0%

profile of v14, /device:TPU:0, one launch (start us, length us, event | category | flops | bytes accessed | tf_op | source)
XLA Modules:
  0.0 70.2 jit_solution(14342126771020191497)
XLA Ops:
  0.6 1.8 %shard_map.77 = (f32[32,256]{1,0:T(8,128)}, f32[32,256]{1,0:T(8,128)}, f32[32,256]{1,0:T(8,128)}, f32[32,256]{1,0:T(8,128)}) custom-call(s32[4,32]{1,0:T(4,128)} %bitcast.26, f32[128,256]{1,0:T(8,128)} %own_ref.1), custom_call_target="tpu_custom_call" | custom-call | tf_op jit(solution)/shard_map/pallas_call | solution.py:267
  2.4 4.8 %collective-permute-start = (f32[32,256]{1,0:T(8,128)}, f32[32,256]{1,0:T(8,128)S(1)}, u32[]{:S(2)}, u32[]{:S(2)}) collective-permute-start(f32[32,256]{1,0:T(8,128)} %get-tuple-element.14), channel_id=1, source_target_pairs={{0,4},{4,8},{8,12},{12,16},{16,20},{20,24},{24,28},{1,5},{5,9},{9,... | collective-permute-start | bytes 98312 | tf_op jit(solution)/shard_map/ppermute | solution.py:317
  7.2 1.3 %collective-permute-start.1 = (f32[32,256]{1,0:T(8,128)}, f32[32,256]{1,0:T(8,128)S(1)}, u32[]{:S(2)}, u32[]{:S(2)}) collective-permute-start(f32[32,256]{1,0:T(8,128)} %get-tuple-element.15), channel_id=1, source_target_pairs={{4,0},{8,4},{12,8},{16,12},{20,16},{24,20},{28,24},{5,1},{9,5},{13... | collective-permute-start | bytes 98312 | tf_op jit(solution)/shard_map/ppermute | solution.py:318
  8.5 1.5 %collective-permute-start.2 = (f32[32,256]{1,0:T(8,128)}, f32[32,256]{1,0:T(8,128)S(1)}, u32[]{:S(2)}, u32[]{:S(2)}) collective-permute-start(f32[32,256]{1,0:T(8,128)} %get-tuple-element.16), channel_id=1, source_target_pairs={{0,1},{1,2},{2,3},{4,5},{5,6},{6,7},{8,9},{9,10},{10,11},{12,13},{... | collective-permute-start | bytes 98312 | tf_op jit(solution)/shard_map/ppermute | solution.py:319
  10.0 1.3 %collective-permute-start.3 = (f32[32,256]{1,0:T(8,128)}, f32[32,256]{1,0:T(8,128)S(1)}, u32[]{:S(2)}, u32[]{:S(2)}) collective-permute-start(f32[32,256]{1,0:T(8,128)} %get-tuple-element.17), channel_id=1, source_target_pairs={{1,0},{2,1},{3,2},{5,4},{6,5},{7,6},{9,8},{10,9},{11,10},{13,12},{... | collective-permute-start | bytes 98312 | tf_op jit(solution)/shard_map/ppermute | solution.py:320
  11.9 0.0 collective-permute-done.g0_ref
  11.9 0.0 copy-start
  12.0 1.3 %collective-permute-done.1.g1_ref = f32[32,256]{1,0:T(8,128)S(1)} collective-permute-done((f32[32,256]{1,0:T(8,128)}, f32[32,256]{1,0:T(8,128)S(1)}, u32[]{:S(2)}, u32[]{:S(2)}) %collective-permute-start.1) | collective-permute-done | bytes 32800 | tf_op jit(solution)/shard_map/ppermute | solution.py:318
  13.2 0.0 collective-permute-done.2.g2_ref
  13.2 1.6 %collective-permute-done.3.g3_ref = f32[32,256]{1,0:T(8,128)S(1)} collective-permute-done((f32[32,256]{1,0:T(8,128)}, f32[32,256]{1,0:T(8,128)S(1)}, u32[]{:S(2)}, u32[]{:S(2)}) %collective-permute-start.3) | collective-permute-done | bytes 32800 | tf_op jit(solution)/shard_map/ppermute | solution.py:320
  14.9 0.0 copy-done
  14.9 0.0 copy-done.1
  14.9 0.0 copy-done.3
  14.9 0.6 copy-done.5
  15.5 8.7 %shard_map.78 = (f32[128,256]{1,0:T(8,128)}, f32[32,256]{1,0:T(8,128)}, f32[32,256]{1,0:T(8,128)}, f32[32,256]{1,0:T(8,128)}, f32[32,256]{1,0:T(8,128)}, /*index=5*/f32[128,256]{1,0:T(8,128)}) custom-call(s32[1]{0:T(128)S(6)} %copy.39.count_ref, s32[4,32]{1,0:T(4,128)} %bitcast.27, f32[5,128,4096]{2,1,0:T(8,128)} %bitcast.23, f32[128,256]{1,0:T(8,128)} %own_ref.1, ...), custom_call_target="tpu_custom_call" | custom-call | flops 557842432 | bytes 11272192 | tf_op jit(solution)/shard_map/pallas_call | solution.py:237
  24.2 4.5 %collective-permute-start.4 = (f32[32,256]{1,0:T(8,128)}, f32[32,256]{1,0:T(8,128)S(1)}, u32[]{:S(2)}, u32[]{:S(2)}) collective-permute-start(f32[32,256]{1,0:T(8,128)} %get-tuple-element.19), channel_id=1, source_target_pairs={{0,4},{4,8},{8,12},{12,16},{16,20},{20,24},{24,28},{1,5},{5,9},{9,... | collective-permute-start | bytes 98312 | tf_op jit(solution)/shard_map/ppermute | solution.py:317
  28.8 1.3 %collective-permute-start.5 = (f32[32,256]{1,0:T(8,128)}, f32[32,256]{1,0:T(8,128)S(1)}, u32[]{:S(2)}, u32[]{:S(2)}) collective-permute-start(f32[32,256]{1,0:T(8,128)} %get-tuple-element.20), channel_id=1, source_target_pairs={{4,0},{8,4},{12,8},{16,12},{20,16},{24,20},{28,24},{5,1},{9,5},{13... | collective-permute-start | bytes 98312 | tf_op jit(solution)/shard_map/ppermute | solution.py:318
  30.1 4.3 %collective-permute-start.6 = (f32[32,256]{1,0:T(8,128)}, f32[32,256]{1,0:T(8,128)S(1)}, u32[]{:S(2)}, u32[]{:S(2)}) collective-permute-start(f32[32,256]{1,0:T(8,128)} %get-tuple-element.21), channel_id=1, source_target_pairs={{0,1},{1,2},{2,3},{4,5},{5,6},{6,7},{8,9},{9,10},{10,11},{12,13},{... | collective-permute-start | bytes 98312 | tf_op jit(solution)/shard_map/ppermute | solution.py:319
  34.4 1.3 %collective-permute-start.7 = (f32[32,256]{1,0:T(8,128)}, f32[32,256]{1,0:T(8,128)S(1)}, u32[]{:S(2)}, u32[]{:S(2)}) collective-permute-start(f32[32,256]{1,0:T(8,128)} %get-tuple-element.22), channel_id=1, source_target_pairs={{1,0},{2,1},{3,2},{5,4},{6,5},{7,6},{9,8},{10,9},{11,10},{13,12},{... | collective-permute-start | bytes 98312 | tf_op jit(solution)/shard_map/ppermute | solution.py:320
  35.7 0.0 collective-permute-done.4.g0_ref
  35.7 0.0 copy-start.2
  35.7 0.0 collective-permute-done.5.g1_ref
  35.7 0.0 copy-start.4
  35.7 0.0 collective-permute-done.6.g2_ref
  35.7 0.0 copy-start.6
  35.7 1.9 %collective-permute-done.7.g3_ref = f32[32,256]{1,0:T(8,128)S(1)} collective-permute-done((f32[32,256]{1,0:T(8,128)}, f32[32,256]{1,0:T(8,128)S(1)}, u32[]{:S(2)}, u32[]{:S(2)}) %collective-permute-start.7) | collective-permute-done | bytes 32800 | tf_op jit(solution)/shard_map/ppermute | solution.py:320
  37.7 0.0 copy-done.4
  37.7 0.6 copy-done.7
  38.3 8.9 %shard_map.79 = (f32[128,256]{1,0:T(8,128)}, f32[32,4,20]{2,1,0:T(4,128)}) custom-call(s32[1]{0:T(128)S(6)} %copy.39.count_ref, s32[4,32]{1,0:T(4,128)} %bitcast.28, f32[5,128,4096]{2,1,0:T(8,128)} %bitcast.24, f32[128,256]{1,0:T(8,128)} %get-tuple-element.18.own_ref.first_ref, f32[32,256]{1,0:T(8,128)} %copy-done.2, f32[32,256]{1,0:T(8,128)} %copy-done.4, ...), custom_call_target="tpu_custom_call" | custom-call | flops 557842432 | bytes 11272192 | tf_op jit(solution)/shard_map/pallas_call | solution.py:237
  47.2 16.5 %all_to_all.5 = f32[32,4,20]{2,1,0:T(4,128)S(1)} all-to-all(f32[32,4,20]{2,1,0:T(4,128)} %get-tuple-element.24), channel_id=1, replica_groups=mesh['wide'=8,'narrow'=4] {'wide','narrow'}, dimensions={0} | all-to-all | bytes 20480 | tf_op jit(solution)/shard_map/all_to_all | solution.py:329
  63.7 0.1 mul.15
  63.8 0.1 copy.29
  63.9 0.0 copy-done.8
  63.9 0.1 multiply_reduce_fusion
  64.0 0.2 fusion.10
  64.2 0.1 copy.37
  64.3 0.1 copy.38
  64.4 0.1 copy.31
  64.5 0.1 maximum_maximum_fusion
  64.5 0.1 copy.33
  64.6 0.7 cholesky.16
  65.3 0.1 select_reduce_fusion
  65.4 0.6 compare_reduce_fusion
  66.0 0.6 fusion
  66.7 0.6 custom-call.10
  67.3 0.2 fusion.1
  67.5 0.7 %fusion.6.mix_ref = f32[8,4]{1,0:T(8,128)} fusion(f32[8,4]{0,1:T(4,128)S(1)} %fusion.1, f32[1,8,8]{1,2,0:T(8,128)S(1)} %custom-call.10), kind=kOutput, calls=%fused_computation.12 | convolution fusion | flops 3072 | bytes 512 | tf_op jit(solution)/shard_map/jit(_cho_solve)/triangular_solve | solution.py:345
  68.2 1.9 %shard_map.80 = (f32[128,256]{1,0:T(8,128)}, f32[128,256]{1,0:T(8,128)}) custom-call(f32[8,4]{1,0:T(8,128)} %fusion.6.mix_ref, f32[128,256]{1,0:T(8,128)} %get-tuple-element.23.rest_0_.anchor_ref, f32[128,256]{1,0:T(8,128)} %get-tuple-element.18.own_ref.first_ref, f32[128,256]{1,0:T(8,128)} %get-tuple-element.25.second_ref), custom_call_target="tpu_custom_call" | custom-call | tf_op jit(solution)/shard_map/pallas_call | solution.py:302
  (9 shorter events, 0.1 us)
Async XLA Ops:
  2.4 9.6 %collective-permute-start = (f32[32,256]{1,0:T(8,128)}, f32[32,256]{1,0:T(8,128)S(1)}, u32[]{:S(2)}, u32[]{:S(2)}) collective-permute-start(f32[32,256]{1,0:T(8,128)} %get-tuple-element.14), channel_id=1, source_target_pairs={{0,4},{4,8},{8,12},{12,16},{16,20},{20,24},{24,28},{1,5},{5,9},{9,... | collective-permute-start | bytes 98312 | tf_op jit(solution)/shard_map/ppermute | solution.py:317
  7.2 6.0 %collective-permute-start.1 = (f32[32,256]{1,0:T(8,128)}, f32[32,256]{1,0:T(8,128)S(1)}, u32[]{:S(2)}, u32[]{:S(2)}) collective-permute-start(f32[32,256]{1,0:T(8,128)} %get-tuple-element.15), channel_id=1, source_target_pairs={{4,0},{8,4},{12,8},{16,12},{20,16},{24,20},{28,24},{5,1},{9,5},{13... | collective-permute-start | bytes 98312 | tf_op jit(solution)/shard_map/ppermute | solution.py:318
  8.5 4.7 %collective-permute-start.2 = (f32[32,256]{1,0:T(8,128)}, f32[32,256]{1,0:T(8,128)S(1)}, u32[]{:S(2)}, u32[]{:S(2)}) collective-permute-start(f32[32,256]{1,0:T(8,128)} %get-tuple-element.16), channel_id=1, source_target_pairs={{0,1},{1,2},{2,3},{4,5},{5,6},{6,7},{8,9},{9,10},{10,11},{12,13},{... | collective-permute-start | bytes 98312 | tf_op jit(solution)/shard_map/ppermute | solution.py:319
  10.0 4.9 %collective-permute-start.3 = (f32[32,256]{1,0:T(8,128)}, f32[32,256]{1,0:T(8,128)S(1)}, u32[]{:S(2)}, u32[]{:S(2)}) collective-permute-start(f32[32,256]{1,0:T(8,128)} %get-tuple-element.17), channel_id=1, source_target_pairs={{1,0},{2,1},{3,2},{5,4},{6,5},{7,6},{9,8},{10,9},{11,10},{13,12},{... | collective-permute-start | bytes 98312 | tf_op jit(solution)/shard_map/ppermute | solution.py:320
  11.9 2.9 %copy-start = (f32[32,256]{1,0:T(8,128)}, f32[32,256]{1,0:T(8,128)S(1)}, u32[]{:S(2)}) copy-start(f32[32,256]{1,0:T(8,128)S(1)} %collective-permute-done.g0_ref) | copy-start | bytes 98308
  13.2 1.7 %copy-start.1 = (f32[32,256]{1,0:T(8,128)}, f32[32,256]{1,0:T(8,128)S(1)}, u32[]{:S(2)}) copy-start(f32[32,256]{1,0:T(8,128)S(1)} %collective-permute-done.1.g1_ref) | copy-start | bytes 98308
  13.2 1.6 %copy-start.3 = (f32[32,256]{1,0:T(8,128)}, f32[32,256]{1,0:T(8,128)S(1)}, u32[]{:S(2)}) copy-start(f32[32,256]{1,0:T(8,128)S(1)} %collective-permute-done.2.g2_ref) | copy-start | bytes 98308
  14.9 0.6 copy-start.5
  15.5 48.4 %copy-start.8 = (f32[4,4,4]{2,1,0:T(4,128)S(1)}, f32[4,4,4]{2,1,0:T(4,128)}, u32[]{:S(2)}) copy-start(f32[4,4,4]{2,1,0:T(4,128)} %constant.52.clone) | copy-start | bytes 772
  24.2 11.4 %collective-permute-start.4 = (f32[32,256]{1,0:T(8,128)}, f32[32,256]{1,0:T(8,128)S(1)}, u32[]{:S(2)}, u32[]{:S(2)}) collective-permute-start(f32[32,256]{1,0:T(8,128)} %get-tuple-element.19), channel_id=1, source_target_pairs={{0,4},{4,8},{8,12},{12,16},{16,20},{20,24},{24,28},{1,5},{5,9},{9,... | collective-permute-start | bytes 98312 | tf_op jit(solution)/shard_map/ppermute | solution.py:317
  28.8 6.9 %collective-permute-start.5 = (f32[32,256]{1,0:T(8,128)}, f32[32,256]{1,0:T(8,128)S(1)}, u32[]{:S(2)}, u32[]{:S(2)}) collective-permute-start(f32[32,256]{1,0:T(8,128)} %get-tuple-element.20), channel_id=1, source_target_pairs={{4,0},{8,4},{12,8},{16,12},{20,16},{24,20},{28,24},{5,1},{9,5},{13... | collective-permute-start | bytes 98312 | tf_op jit(solution)/shard_map/ppermute | solution.py:318
  30.1 5.6 %collective-permute-start.6 = (f32[32,256]{1,0:T(8,128)}, f32[32,256]{1,0:T(8,128)S(1)}, u32[]{:S(2)}, u32[]{:S(2)}) collective-permute-start(f32[32,256]{1,0:T(8,128)} %get-tuple-element.21), channel_id=1, source_target_pairs={{0,1},{1,2},{2,3},{4,5},{5,6},{6,7},{8,9},{9,10},{10,11},{12,13},{... | collective-permute-start | bytes 98312 | tf_op jit(solution)/shard_map/ppermute | solution.py:319
  34.4 3.3 %collective-permute-start.7 = (f32[32,256]{1,0:T(8,128)}, f32[32,256]{1,0:T(8,128)S(1)}, u32[]{:S(2)}, u32[]{:S(2)}) collective-permute-start(f32[32,256]{1,0:T(8,128)} %get-tuple-element.22), channel_id=1, source_target_pairs={{1,0},{2,1},{3,2},{5,4},{6,5},{7,6},{9,8},{10,9},{11,10},{13,12},{... | collective-permute-start | bytes 98312 | tf_op jit(solution)/shard_map/ppermute | solution.py:320
  35.7 2.0 %copy-start.2 = (f32[32,256]{1,0:T(8,128)}, f32[32,256]{1,0:T(8,128)S(1)}, u32[]{:S(2)}) copy-start(f32[32,256]{1,0:T(8,128)S(1)} %collective-permute-done.4.g0_ref) | copy-start | bytes 98308
  35.7 2.0 %copy-start.4 = (f32[32,256]{1,0:T(8,128)}, f32[32,256]{1,0:T(8,128)S(1)}, u32[]{:S(2)}) copy-start(f32[32,256]{1,0:T(8,128)S(1)} %collective-permute-done.5.g1_ref) | copy-start | bytes 98308
  35.7 2.0 %copy-start.6 = (f32[32,256]{1,0:T(8,128)}, f32[32,256]{1,0:T(8,128)S(1)}, u32[]{:S(2)}) copy-start(f32[32,256]{1,0:T(8,128)S(1)} %collective-permute-done.6.g2_ref) | copy-start | bytes 98308
  37.7 0.6 copy-start.7

commit v15 on v14

--- a/solution.py
+++ b/solution.py
@@ -341,7 +341,7 @@
         0,
     )
     right_terms = jnp.concatenate([gram_parts[0], gram_parts[2]], 0)
-    factor = jnp.linalg.cholesky(normal_matrix)
+    factor = lax.linalg.cholesky(normal_matrix, symmetrize_input=False)
     coefficients = jax.scipy.linalg.cho_solve((factor, True), right_terms)
     return mix_outputs(coefficients, anchor, first_image, second_image)
 

time: 70.6 us -> 70.3 us (level)
  no operation moved by 1% of the time
where the time goes in v15:
time: 70.3 us; the launch traced here: 69.9 us
  Pallas kernels  21.3 us (30%)
  starting transfers between devices  20.3 us (29%)
  blocking collectives  16.5 us (23%)
  waiting for transfers between devices  4.88 us (7%)
  other arithmetic  2.89 us (4%)
  local copies, waits for them, and re-layouts  1.68 us (2%)
  between operations  1.46 us (2%)
  matrix products  0.93 us (1%)
    pallas_call x2, Pallas kernels, apply_operator(): pl.pallas_call(functools.partial(coupling_kernel, with_gram), out_shape=t...  17.6 us
    all_to_all x1, blocking collectives, per_device(): everyone = lax.all_to_all(raw_gram, ('wide', 'narrow'), 0, 0, tiled=True)  16.5 us
    ppermute x2, starting transfers between devices, ghosts(): lax.ppermute(outgoing[0], 'wide', [(i, i + 1) for i in range(wide - 1)])  9.37 us
    ppermute x2, starting transfers between devices, ghosts(): lax.ppermute(outgoing[2], 'narrow', [(i, i + 1) for i in range(narrow - 1)])  5.72 us
    ppermute x2, waiting for transfers between devices, ghosts(): lax.ppermute(outgoing[3], 'narrow', [(i + 1, i) for i in range(narrow - 1)])  3.59 us
    ppermute x2, starting transfers between devices, ghosts(): lax.ppermute(outgoing[1], 'wide', [(i + 1, i) for i in range(wide - 1)])  2.58 us
    ppermute x2, starting transfers between devices, ghosts(): lax.ppermute(outgoing[3], 'narrow', [(i + 1, i) for i in range(narrow - 1)])  2.58 us
    pallas_call x1, Pallas kernels, mix_outputs(): pl.pallas_call(mixing_kernel, out_shape=(jax.ShapeDtypeStruct(anchor.shap...  1.93 us
  transfers between devices with their start and end apart: 8, of which 3 were waited for; matrix products, arithmetic and copies ran while one was open for 0% of the time, Pallas kernels for 0%

profile of v15, /device:TPU:0, one launch (start us, length us, event | category | flops | bytes accessed | tf_op | source)
XLA Modules:
  0.0 69.9 jit_solution(4786441501039900560)
XLA Ops:
  0.6 1.7 %shard_map.77 = (f32[32,256]{1,0:T(8,128)}, f32[32,256]{1,0:T(8,128)}, f32[32,256]{1,0:T(8,128)}, f32[32,256]{1,0:T(8,128)}) custom-call(s32[4,32]{1,0:T(4,128)} %bitcast.19, f32[128,256]{1,0:T(8,128)} %own_ref.1), custom_call_target="tpu_custom_call" | custom-call | tf_op jit(solution)/shard_map/pallas_call | solution.py:267
  2.4 4.8 %collective-permute-start = (f32[32,256]{1,0:T(8,128)}, f32[32,256]{1,0:T(8,128)S(1)}, u32[]{:S(2)}, u32[]{:S(2)}) collective-permute-start(f32[32,256]{1,0:T(8,128)} %get-tuple-element.14), channel_id=1, source_target_pairs={{0,4},{4,8},{8,12},{12,16},{16,20},{20,24},{24,28},{1,5},{5,9},{9,... | collective-permute-start | bytes 98312 | tf_op jit(solution)/shard_map/ppermute | solution.py:317
  7.2 1.3 %collective-permute-start.1 = (f32[32,256]{1,0:T(8,128)}, f32[32,256]{1,0:T(8,128)S(1)}, u32[]{:S(2)}, u32[]{:S(2)}) collective-permute-start(f32[32,256]{1,0:T(8,128)} %get-tuple-element.15), channel_id=1, source_target_pairs={{4,0},{8,4},{12,8},{16,12},{20,16},{24,20},{28,24},{5,1},{9,5},{13... | collective-permute-start | bytes 98312 | tf_op jit(solution)/shard_map/ppermute | solution.py:318
  8.5 1.5 %collective-permute-start.2 = (f32[32,256]{1,0:T(8,128)}, f32[32,256]{1,0:T(8,128)S(1)}, u32[]{:S(2)}, u32[]{:S(2)}) collective-permute-start(f32[32,256]{1,0:T(8,128)} %get-tuple-element.16), channel_id=1, source_target_pairs={{0,1},{1,2},{2,3},{4,5},{5,6},{6,7},{8,9},{9,10},{10,11},{12,13},{... | collective-permute-start | bytes 98312 | tf_op jit(solution)/shard_map/ppermute | solution.py:319
  10.0 1.3 %collective-permute-start.3 = (f32[32,256]{1,0:T(8,128)}, f32[32,256]{1,0:T(8,128)S(1)}, u32[]{:S(2)}, u32[]{:S(2)}) collective-permute-start(f32[32,256]{1,0:T(8,128)} %get-tuple-element.17), channel_id=1, source_target_pairs={{1,0},{2,1},{3,2},{5,4},{6,5},{7,6},{9,8},{10,9},{11,10},{13,12},{... | collective-permute-start | bytes 98312 | tf_op jit(solution)/shard_map/ppermute | solution.py:320
  11.9 0.0 collective-permute-done.g0_ref
  11.9 0.0 copy-start
  11.9 1.3 %collective-permute-done.1.g1_ref = f32[32,256]{1,0:T(8,128)S(1)} collective-permute-done((f32[32,256]{1,0:T(8,128)}, f32[32,256]{1,0:T(8,128)S(1)}, u32[]{:S(2)}, u32[]{:S(2)}) %collective-permute-start.1) | collective-permute-done | bytes 32800 | tf_op jit(solution)/shard_map/ppermute | solution.py:318
  13.2 0.0 copy-start.1
  13.2 0.0 collective-permute-done.2.g2_ref
  13.2 1.6 %collective-permute-done.3.g3_ref = f32[32,256]{1,0:T(8,128)S(1)} collective-permute-done((f32[32,256]{1,0:T(8,128)}, f32[32,256]{1,0:T(8,128)S(1)}, u32[]{:S(2)}, u32[]{:S(2)}) %collective-permute-start.3) | collective-permute-done | bytes 32800 | tf_op jit(solution)/shard_map/ppermute | solution.py:320
  14.9 0.0 copy-done
  14.9 0.0 copy-done.1
  14.9 0.0 copy-done.3
  14.9 0.6 copy-done.5
  15.5 8.7 %shard_map.78 = (f32[128,256]{1,0:T(8,128)}, f32[32,256]{1,0:T(8,128)}, f32[32,256]{1,0:T(8,128)}, f32[32,256]{1,0:T(8,128)}, f32[32,256]{1,0:T(8,128)}, /*index=5*/f32[128,256]{1,0:T(8,128)}) custom-call(s32[1]{0:T(128)S(6)} %copy.25.count_ref, s32[4,32]{1,0:T(4,128)} %bitcast.20, f32[5,128,4096]{2,1,0:T(8,128)} %bitcast.17, f32[128,256]{1,0:T(8,128)} %own_ref.1, ...), custom_call_target="tpu_custom_call" | custom-call | flops 557842432 | bytes 11272192 | tf_op jit(solution)/shard_map/pallas_call | solution.py:237
  24.2 4.5 %collective-permute-start.4 = (f32[32,256]{1,0:T(8,128)}, f32[32,256]{1,0:T(8,128)S(1)}, u32[]{:S(2)}, u32[]{:S(2)}) collective-permute-start(f32[32,256]{1,0:T(8,128)} %get-tuple-element.19), channel_id=1, source_target_pairs={{0,4},{4,8},{8,12},{12,16},{16,20},{20,24},{24,28},{1,5},{5,9},{9,... | collective-permute-start | bytes 98312 | tf_op jit(solution)/shard_map/ppermute | solution.py:317
  28.8 1.3 %collective-permute-start.5 = (f32[32,256]{1,0:T(8,128)}, f32[32,256]{1,0:T(8,128)S(1)}, u32[]{:S(2)}, u32[]{:S(2)}) collective-permute-start(f32[32,256]{1,0:T(8,128)} %get-tuple-element.20), channel_id=1, source_target_pairs={{4,0},{8,4},{12,8},{16,12},{20,16},{24,20},{28,24},{5,1},{9,5},{13... | collective-permute-start | bytes 98312 | tf_op jit(solution)/shard_map/ppermute | solution.py:318
  30.1 4.3 %collective-permute-start.6 = (f32[32,256]{1,0:T(8,128)}, f32[32,256]{1,0:T(8,128)S(1)}, u32[]{:S(2)}, u32[]{:S(2)}) collective-permute-start(f32[32,256]{1,0:T(8,128)} %get-tuple-element.21), channel_id=1, source_target_pairs={{0,1},{1,2},{2,3},{4,5},{5,6},{6,7},{8,9},{9,10},{10,11},{12,13},{... | collective-permute-start | bytes 98312 | tf_op jit(solution)/shard_map/ppermute | solution.py:319
  34.3 1.3 %collective-permute-start.7 = (f32[32,256]{1,0:T(8,128)}, f32[32,256]{1,0:T(8,128)S(1)}, u32[]{:S(2)}, u32[]{:S(2)}) collective-permute-start(f32[32,256]{1,0:T(8,128)} %get-tuple-element.22), channel_id=1, source_target_pairs={{1,0},{2,1},{3,2},{5,4},{6,5},{7,6},{9,8},{10,9},{11,10},{13,12},{... | collective-permute-start | bytes 98312 | tf_op jit(solution)/shard_map/ppermute | solution.py:320
  35.6 0.0 collective-permute-done.4.g0_ref
  35.7 0.0 copy-start.2
  35.7 0.0 collective-permute-done.5.g1_ref
  35.7 0.0 copy-start.4
  35.7 0.0 collective-permute-done.6.g2_ref
  35.7 0.0 copy-start.6
  35.7 1.9 %collective-permute-done.7.g3_ref = f32[32,256]{1,0:T(8,128)S(1)} collective-permute-done((f32[32,256]{1,0:T(8,128)}, f32[32,256]{1,0:T(8,128)S(1)}, u32[]{:S(2)}, u32[]{:S(2)}) %collective-permute-start.7) | collective-permute-done | bytes 32800 | tf_op jit(solution)/shard_map/ppermute | solution.py:320
  37.7 0.0 copy-done.2
  37.7 0.0 copy-done.4
  37.7 0.0 copy-done.6
  37.7 0.6 copy-done.7
  38.3 8.9 %shard_map.79 = (f32[128,256]{1,0:T(8,128)}, f32[32,4,20]{2,1,0:T(4,128)}) custom-call(s32[1]{0:T(128)S(6)} %copy.25.count_ref, s32[4,32]{1,0:T(4,128)} %bitcast.21, f32[5,128,4096]{2,1,0:T(8,128)} %bitcast.18, f32[128,256]{1,0:T(8,128)} %get-tuple-element.18.own_ref.first_ref, f32[32,256]{1,0:T(8,128)} %copy-done.2, f32[32,256]{1,0:T(8,128)} %copy-done.4, ...), custom_call_target="tpu_custom_call" | custom-call | flops 557842432 | bytes 11272192 | tf_op jit(solution)/shard_map/pallas_call | solution.py:237
  47.1 16.5 %all_to_all.5 = f32[32,4,20]{2,1,0:T(4,128)S(1)} all-to-all(f32[32,4,20]{2,1,0:T(4,128)} %get-tuple-element.24), channel_id=1, replica_groups=mesh['wide'=8,'narrow'=4] {'wide','narrow'}, dimensions={0} | all-to-all | bytes 20480 | tf_op jit(solution)/shard_map/all_to_all | solution.py:329
  63.7 0.1 mul.15
  63.7 0.1 copy.20
  63.9 0.0 copy-done.8
  63.9 0.1 multiply_reduce_fusion
  64.0 0.2 slice_reduce_fusion.4
  64.1 0.1 copy.21
  64.2 0.1 maximum_maximum_fusion
  64.3 0.7 cholesky.16
  65.0 0.1 select_reduce_fusion
  65.1 0.6 compare_reduce_fusion
  65.7 0.6 fusion
  66.4 0.6 custom-call.9
  67.0 0.2 fusion.1
  67.2 0.7 %fusion.6.mix_ref = f32[8,4]{1,0:T(8,128)} fusion(f32[8,4]{0,1:T(4,128)S(1)} %fusion.1, f32[1,8,8]{1,2,0:T(8,128)S(1)} %custom-call.9), kind=kOutput, calls=%fused_computation.14 | convolution fusion | flops 3072 | bytes 512 | tf_op jit(solution)/shard_map/jit(_cho_solve)/triangular_solve | solution.py:345
  67.9 1.9 %shard_map.80 = (f32[128,256]{1,0:T(8,128)}, f32[128,256]{1,0:T(8,128)}) custom-call(f32[8,4]{1,0:T(8,128)} %fusion.6.mix_ref, f32[128,256]{1,0:T(8,128)} %get-tuple-element.23.rest_0_.anchor_ref, f32[128,256]{1,0:T(8,128)} %get-tuple-element.18.own_ref.first_ref, f32[128,256]{1,0:T(8,128)} %get-tuple-element.25.second_ref), custom_call_target="tpu_custom_call" | custom-call | tf_op jit(solution)/shard_map/pallas_call | solution.py:302
  (5 shorter events, 0.1 us)
Async XLA Ops:
  2.4 9.6 %collective-permute-start = (f32[32,256]{1,0:T(8,128)}, f32[32,256]{1,0:T(8,128)S(1)}, u32[]{:S(2)}, u32[]{:S(2)}) collective-permute-start(f32[32,256]{1,0:T(8,128)} %get-tuple-element.14), channel_id=1, source_target_pairs={{0,4},{4,8},{8,12},{12,16},{16,20},{20,24},{24,28},{1,5},{5,9},{9,... | collective-permute-start | bytes 98312 | tf_op jit(solution)/shard_map/ppermute | solution.py:317
  7.2 6.0 %collective-permute-start.1 = (f32[32,256]{1,0:T(8,128)}, f32[32,256]{1,0:T(8,128)S(1)}, u32[]{:S(2)}, u32[]{:S(2)}) collective-permute-start(f32[32,256]{1,0:T(8,128)} %get-tuple-element.15), channel_id=1, source_target_pairs={{4,0},{8,4},{12,8},{16,12},{20,16},{24,20},{28,24},{5,1},{9,5},{13... | collective-permute-start | bytes 98312 | tf_op jit(solution)/shard_map/ppermute | solution.py:318
  8.5 4.7 %collective-permute-start.2 = (f32[32,256]{1,0:T(8,128)}, f32[32,256]{1,0:T(8,128)S(1)}, u32[]{:S(2)}, u32[]{:S(2)}) collective-permute-start(f32[32,256]{1,0:T(8,128)} %get-tuple-element.16), channel_id=1, source_target_pairs={{0,1},{1,2},{2,3},{4,5},{5,6},{6,7},{8,9},{9,10},{10,11},{12,13},{... | collective-permute-start | bytes 98312 | tf_op jit(solution)/shard_map/ppermute | solution.py:319
  10.0 4.9 %collective-permute-start.3 = (f32[32,256]{1,0:T(8,128)}, f32[32,256]{1,0:T(8,128)S(1)}, u32[]{:S(2)}, u32[]{:S(2)}) collective-permute-start(f32[32,256]{1,0:T(8,128)} %get-tuple-element.17), channel_id=1, source_target_pairs={{1,0},{2,1},{3,2},{5,4},{6,5},{7,6},{9,8},{10,9},{11,10},{13,12},{... | collective-permute-start | bytes 98312 | tf_op jit(solution)/shard_map/ppermute | solution.py:320
  11.9 2.9 %copy-start = (f32[32,256]{1,0:T(8,128)}, f32[32,256]{1,0:T(8,128)S(1)}, u32[]{:S(2)}) copy-start(f32[32,256]{1,0:T(8,128)S(1)} %collective-permute-done.g0_ref) | copy-start | bytes 98308
  13.2 1.7 %copy-start.1 = (f32[32,256]{1,0:T(8,128)}, f32[32,256]{1,0:T(8,128)S(1)}, u32[]{:S(2)}) copy-start(f32[32,256]{1,0:T(8,128)S(1)} %collective-permute-done.1.g1_ref) | copy-start | bytes 98308
  13.2 1.6 %copy-start.3 = (f32[32,256]{1,0:T(8,128)}, f32[32,256]{1,0:T(8,128)S(1)}, u32[]{:S(2)}) copy-start(f32[32,256]{1,0:T(8,128)S(1)} %collective-permute-done.2.g2_ref) | copy-start | bytes 98308
  14.9 0.6 copy-start.5
  15.5 48.4 %copy-start.8 = (f32[4,4,4]{2,1,0:T(4,128)S(1)}, f32[4,4,4]{2,1,0:T(4,128)}, u32[]{:S(2)}) copy-start(f32[4,4,4]{2,1,0:T(4,128)} %constant.38.clone) | copy-start | bytes 772
  24.2 11.4 %collective-permute-start.4 = (f32[32,256]{1,0:T(8,128)}, f32[32,256]{1,0:T(8,128)S(1)}, u32[]{:S(2)}, u32[]{:S(2)}) collective-permute-start(f32[32,256]{1,0:T(8,128)} %get-tuple-element.19), channel_id=1, source_target_pairs={{0,4},{4,8},{8,12},{12,16},{16,20},{20,24},{24,28},{1,5},{5,9},{9,... | collective-permute-start | bytes 98312 | tf_op jit(solution)/shard_map/ppermute | solution.py:317
  28.8 6.9 %collective-permute-start.5 = (f32[32,256]{1,0:T(8,128)}, f32[32,256]{1,0:T(8,128)S(1)}, u32[]{:S(2)}, u32[]{:S(2)}) collective-permute-start(f32[32,256]{1,0:T(8,128)} %get-tuple-element.20), channel_id=1, source_target_pairs={{4,0},{8,4},{12,8},{16,12},{20,16},{24,20},{28,24},{5,1},{9,5},{13... | collective-permute-start | bytes 98312 | tf_op jit(solution)/shard_map/ppermute | solution.py:318
  30.1 5.6 %collective-permute-start.6 = (f32[32,256]{1,0:T(8,128)}, f32[32,256]{1,0:T(8,128)S(1)}, u32[]{:S(2)}, u32[]{:S(2)}) collective-permute-start(f32[32,256]{1,0:T(8,128)} %get-tuple-element.21), channel_id=1, source_target_pairs={{0,1},{1,2},{2,3},{4,5},{5,6},{6,7},{8,9},{9,10},{10,11},{12,13},{... | collective-permute-start | bytes 98312 | tf_op jit(solution)/shard_map/ppermute | solution.py:319
  34.3 3.3 %collective-permute-start.7 = (f32[32,256]{1,0:T(8,128)}, f32[32,256]{1,0:T(8,128)S(1)}, u32[]{:S(2)}, u32[]{:S(2)}) collective-permute-start(f32[32,256]{1,0:T(8,128)} %get-tuple-element.22), channel_id=1, source_target_pairs={{1,0},{2,1},{3,2},{5,4},{6,5},{7,6},{9,8},{10,9},{11,10},{13,12},{... | collective-permute-start | bytes 98312 | tf_op jit(solution)/shard_map/ppermute | solution.py:320
  35.7 2.0 %copy-start.2 = (f32[32,256]{1,0:T(8,128)}, f32[32,256]{1,0:T(8,128)S(1)}, u32[]{:S(2)}) copy-start(f32[32,256]{1,0:T(8,128)S(1)} %collective-permute-done.4.g0_ref) | copy-start | bytes 98308
  35.7 2.0 %copy-start.4 = (f32[32,256]{1,0:T(8,128)}, f32[32,256]{1,0:T(8,128)S(1)}, u32[]{:S(2)}) copy-start(f32[32,256]{1,0:T(8,128)S(1)} %collective-permute-done.5.g1_ref) | copy-start | bytes 98308
  35.7 2.0 %copy-start.6 = (f32[32,256]{1,0:T(8,128)}, f32[32,256]{1,0:T(8,128)S(1)}, u32[]{:S(2)}) copy-start(f32[32,256]{1,0:T(8,128)S(1)} %collective-permute-done.6.g2_ref) | copy-start | bytes 98308
  37.7 0.6 copy-start.7

commit v16 on v14

--- a/solution.py
+++ b/solution.py
@@ -181,7 +181,7 @@
             lax.fori_loop(0, tiles, one_tile, 0, unroll=UNROLL)
         return carry
 
-    lax.fori_loop(0, chunks, one_chunk, 0)
+    lax.fori_loop(0, chunks, one_chunk, 0, unroll=True)
 
     full = tiles * LANES
     for c in range(VECS):

time: 70.6 us -> 70 us (level)
  no operation moved by 1% of the time
where the time goes in v16:
time: 70 us; the launch traced here: 69.5 us
  Pallas kernels  20.7 us (30%)
  starting transfers between devices  20.3 us (29%)
  blocking collectives  16.5 us (24%)
  waiting for transfers between devices  4.88 us (7%)
  other arithmetic  2.89 us (4%)
  local copies, waits for them, and re-layouts  1.96 us (3%)
  between operations  1.46 us (2%)
  matrix products  0.93 us (1%)
    pallas_call x2, Pallas kernels, apply_operator(): pl.pallas_call(functools.partial(coupling_kernel, with_gram), out_shape=t...  17 us
    all_to_all x1, blocking collectives, per_device(): everyone = lax.all_to_all(raw_gram, ('wide', 'narrow'), 0, 0, tiled=True)  16.5 us
    ppermute x2, starting transfers between devices, ghosts(): lax.ppermute(outgoing[0], 'wide', [(i, i + 1) for i in range(wide - 1)])  9.37 us
    ppermute x2, starting transfers between devices, ghosts(): lax.ppermute(outgoing[2], 'narrow', [(i, i + 1) for i in range(narrow - 1)])  5.71 us
    ppermute x2, waiting for transfers between devices, ghosts(): lax.ppermute(outgoing[3], 'narrow', [(i + 1, i) for i in range(narrow - 1)])  3.59 us
    ppermute x2, starting transfers between devices, ghosts(): lax.ppermute(outgoing[1], 'wide', [(i + 1, i) for i in range(wide - 1)])  2.58 us
    ppermute x2, starting transfers between devices, ghosts(): lax.ppermute(outgoing[3], 'narrow', [(i + 1, i) for i in range(narrow - 1)])  2.58 us
    pallas_call x1, Pallas kernels, mix_outputs(): pl.pallas_call(mixing_kernel, out_shape=(jax.ShapeDtypeStruct(anchor.shap...  1.93 us
  transfers between devices with their start and end apart: 8, of which 3 were waited for; matrix products, arithmetic and copies ran while one was open for 0% of the time, Pallas kernels for 0%

profile of v16, /device:TPU:0, one launch (start us, length us, event | category | flops | bytes accessed | tf_op | source)
XLA Modules:
  0.0 69.5 jit_solution(9185809417245522524)
XLA Ops:
  0.6 1.8 %shard_map.77 = (f32[32,256]{1,0:T(8,128)}, f32[32,256]{1,0:T(8,128)}, f32[32,256]{1,0:T(8,128)}, f32[32,256]{1,0:T(8,128)}) custom-call(s32[4,32]{1,0:T(4,128)} %bitcast.26, f32[128,256]{1,0:T(8,128)} %own_ref.1), custom_call_target="tpu_custom_call" | custom-call | tf_op jit(solution)/shard_map/pallas_call | solution.py:267
  2.4 4.8 %collective-permute-start = (f32[32,256]{1,0:T(8,128)}, f32[32,256]{1,0:T(8,128)S(1)}, u32[]{:S(2)}, u32[]{:S(2)}) collective-permute-start(f32[32,256]{1,0:T(8,128)} %get-tuple-element.14), channel_id=1, source_target_pairs={{0,4},{4,8},{8,12},{12,16},{16,20},{20,24},{24,28},{1,5},{5,9},{9,... | collective-permute-start | bytes 98312 | tf_op jit(solution)/shard_map/ppermute | solution.py:317
  7.2 1.3 %collective-permute-start.1 = (f32[32,256]{1,0:T(8,128)}, f32[32,256]{1,0:T(8,128)S(1)}, u32[]{:S(2)}, u32[]{:S(2)}) collective-permute-start(f32[32,256]{1,0:T(8,128)} %get-tuple-element.15), channel_id=1, source_target_pairs={{4,0},{8,4},{12,8},{16,12},{20,16},{24,20},{28,24},{5,1},{9,5},{13... | collective-permute-start | bytes 98312 | tf_op jit(solution)/shard_map/ppermute | solution.py:318
  8.5 1.5 %collective-permute-start.2 = (f32[32,256]{1,0:T(8,128)}, f32[32,256]{1,0:T(8,128)S(1)}, u32[]{:S(2)}, u32[]{:S(2)}) collective-permute-start(f32[32,256]{1,0:T(8,128)} %get-tuple-element.16), channel_id=1, source_target_pairs={{0,1},{1,2},{2,3},{4,5},{5,6},{6,7},{8,9},{9,10},{10,11},{12,13},{... | collective-permute-start | bytes 98312 | tf_op jit(solution)/shard_map/ppermute | solution.py:319
  10.0 1.3 %collective-permute-start.3 = (f32[32,256]{1,0:T(8,128)}, f32[32,256]{1,0:T(8,128)S(1)}, u32[]{:S(2)}, u32[]{:S(2)}) collective-permute-start(f32[32,256]{1,0:T(8,128)} %get-tuple-element.17), channel_id=1, source_target_pairs={{1,0},{2,1},{3,2},{5,4},{6,5},{7,6},{9,8},{10,9},{11,10},{13,12},{... | collective-permute-start | bytes 98312 | tf_op jit(solution)/shard_map/ppermute | solution.py:320
  11.9 0.0 collective-permute-done.g0_ref
  11.9 0.0 copy-start
  12.0 1.3 %collective-permute-done.1.g1_ref = f32[32,256]{1,0:T(8,128)S(1)} collective-permute-done((f32[32,256]{1,0:T(8,128)}, f32[32,256]{1,0:T(8,128)S(1)}, u32[]{:S(2)}, u32[]{:S(2)}) %collective-permute-start.1) | collective-permute-done | bytes 32800 | tf_op jit(solution)/shard_map/ppermute | solution.py:318
  13.2 0.0 collective-permute-done.2.g2_ref
  13.2 1.6 %collective-permute-done.3.g3_ref = f32[32,256]{1,0:T(8,128)S(1)} collective-permute-done((f32[32,256]{1,0:T(8,128)}, f32[32,256]{1,0:T(8,128)S(1)}, u32[]{:S(2)}, u32[]{:S(2)}) %collective-permute-start.3) | collective-permute-done | bytes 32800 | tf_op jit(solution)/shard_map/ppermute | solution.py:320
  14.9 0.0 copy-done
  14.9 0.0 copy-done.1
  14.9 0.0 copy-done.3
  14.9 0.6 copy-done.5
  15.5 8.4 %shard_map.78 = (f32[128,256]{1,0:T(8,128)}, f32[32,256]{1,0:T(8,128)}, f32[32,256]{1,0:T(8,128)}, f32[32,256]{1,0:T(8,128)}, f32[32,256]{1,0:T(8,128)}, /*index=5*/f32[128,256]{1,0:T(8,128)}) custom-call(s32[1]{0:T(128)S(6)} %copy.39.count_ref, s32[4,32]{1,0:T(4,128)} %bitcast.27, f32[5,128,4096]{2,1,0:T(8,128)} %bitcast.23, f32[128,256]{1,0:T(8,128)} %own_ref.1, ...), custom_call_target="tpu_custom_call" | custom-call | flops 557842432 | bytes 11272192 | tf_op jit(solution)/shard_map/pallas_call | solution.py:237
  23.9 4.5 %collective-permute-start.4 = (f32[32,256]{1,0:T(8,128)}, f32[32,256]{1,0:T(8,128)S(1)}, u32[]{:S(2)}, u32[]{:S(2)}) collective-permute-start(f32[32,256]{1,0:T(8,128)} %get-tuple-element.19), channel_id=1, source_target_pairs={{0,4},{4,8},{8,12},{12,16},{16,20},{20,24},{24,28},{1,5},{5,9},{9,... | collective-permute-start | bytes 98312 | tf_op jit(solution)/shard_map/ppermute | solution.py:317
  28.5 1.3 %collective-permute-start.5 = (f32[32,256]{1,0:T(8,128)}, f32[32,256]{1,0:T(8,128)S(1)}, u32[]{:S(2)}, u32[]{:S(2)}) collective-permute-start(f32[32,256]{1,0:T(8,128)} %get-tuple-element.20), channel_id=1, source_target_pairs={{4,0},{8,4},{12,8},{16,12},{20,16},{24,20},{28,24},{5,1},{9,5},{13... | collective-permute-start | bytes 98312 | tf_op jit(solution)/shard_map/ppermute | solution.py:318
  29.8 4.3 %collective-permute-start.6 = (f32[32,256]{1,0:T(8,128)}, f32[32,256]{1,0:T(8,128)S(1)}, u32[]{:S(2)}, u32[]{:S(2)}) collective-permute-start(f32[32,256]{1,0:T(8,128)} %get-tuple-element.21), channel_id=1, source_target_pairs={{0,1},{1,2},{2,3},{4,5},{5,6},{6,7},{8,9},{9,10},{10,11},{12,13},{... | collective-permute-start | bytes 98312 | tf_op jit(solution)/shard_map/ppermute | solution.py:319
  34.0 1.3 %collective-permute-start.7 = (f32[32,256]{1,0:T(8,128)}, f32[32,256]{1,0:T(8,128)S(1)}, u32[]{:S(2)}, u32[]{:S(2)}) collective-permute-start(f32[32,256]{1,0:T(8,128)} %get-tuple-element.22), channel_id=1, source_target_pairs={{1,0},{2,1},{3,2},{5,4},{6,5},{7,6},{9,8},{10,9},{11,10},{13,12},{... | collective-permute-start | bytes 98312 | tf_op jit(solution)/shard_map/ppermute | solution.py:320
  35.3 0.0 collective-permute-done.4.g0_ref
  35.3 0.0 copy-start.2
  35.3 0.0 collective-permute-done.5.g1_ref
  35.4 0.0 copy-start.4
  35.4 0.0 collective-permute-done.6.g2_ref
  35.4 0.0 copy-start.6
  35.4 1.9 %collective-permute-done.7.g3_ref = f32[32,256]{1,0:T(8,128)S(1)} collective-permute-done((f32[32,256]{1,0:T(8,128)}, f32[32,256]{1,0:T(8,128)S(1)}, u32[]{:S(2)}, u32[]{:S(2)}) %collective-permute-start.7) | collective-permute-done | bytes 32800 | tf_op jit(solution)/shard_map/ppermute | solution.py:320
  37.3 0.0 copy-done.2
  37.3 0.0 copy-done.4
  37.3 0.6 copy-done.7
  37.9 8.6 %shard_map.79 = (f32[128,256]{1,0:T(8,128)}, f32[32,4,20]{2,1,0:T(4,128)}) custom-call(s32[1]{0:T(128)S(6)} %copy.39.count_ref, s32[4,32]{1,0:T(4,128)} %bitcast.28, f32[5,128,4096]{2,1,0:T(8,128)} %bitcast.24, f32[128,256]{1,0:T(8,128)} %get-tuple-element.18.own_ref.first_ref, f32[32,256]{1,0:T(8,128)} %copy-done.2, f32[32,256]{1,0:T(8,128)} %copy-done.4, ...), custom_call_target="tpu_custom_call" | custom-call | flops 557842432 | bytes 11272192 | tf_op jit(solution)/shard_map/pallas_call | solution.py:237
  46.5 16.5 %all_to_all.5 = f32[32,4,20]{2,1,0:T(4,128)S(1)} all-to-all(f32[32,4,20]{2,1,0:T(4,128)} %get-tuple-element.24), channel_id=1, replica_groups=mesh['wide'=8,'narrow'=4] {'wide','narrow'}, dimensions={0} | all-to-all | bytes 20480 | tf_op jit(solution)/shard_map/all_to_all | solution.py:329
  63.0 0.1 mul.15
  63.1 0.1 copy.29
  63.2 0.1 multiply_reduce_fusion
  63.3 0.2 fusion.10
  63.5 0.1 copy.37
  63.6 0.1 copy.38
  63.7 0.1 copy.31
  63.8 0.1 maximum_maximum_fusion
  63.9 0.1 copy.33
  64.0 0.7 %cholesky.16 = f32[8,8]{1,0:T(8,128)S(1)} custom-call(f32[8,8]{1,0:T(8,128)S(1)} %fusion.8), custom_call_target="Cholesky" | custom-call | tf_op jit(solution)/shard_map/jit(cholesky)/cholesky | solution.py:344
  64.7 0.1 select_reduce_fusion
  64.7 0.6 compare_reduce_fusion
  65.4 0.6 fusion
  66.0 0.6 custom-call.10
  66.7 0.2 fusion.1
  66.9 0.7 %fusion.6.mix_ref = f32[8,4]{1,0:T(8,128)} fusion(f32[8,4]{0,1:T(4,128)S(1)} %fusion.1, f32[1,8,8]{1,2,0:T(8,128)S(1)} %custom-call.10), kind=kOutput, calls=%fused_computation.12 | convolution fusion | flops 3072 | bytes 512 | tf_op jit(solution)/shard_map/jit(_cho_solve)/triangular_solve | solution.py:345
  67.6 1.9 %shard_map.80 = (f32[128,256]{1,0:T(8,128)}, f32[128,256]{1,0:T(8,128)}) custom-call(f32[8,4]{1,0:T(8,128)} %fusion.6.mix_ref, f32[128,256]{1,0:T(8,128)} %get-tuple-element.23.rest_0_.anchor_ref, f32[128,256]{1,0:T(8,128)} %get-tuple-element.18.own_ref.first_ref, f32[128,256]{1,0:T(8,128)} %get-tuple-element.25.second_ref), custom_call_target="tpu_custom_call" | custom-call | tf_op jit(solution)/shard_map/pallas_call | solution.py:302
  (9 shorter events, 0.1 us)
Async XLA Ops:
  2.4 9.6 %collective-permute-start = (f32[32,256]{1,0:T(8,128)}, f32[32,256]{1,0:T(8,128)S(1)}, u32[]{:S(2)}, u32[]{:S(2)}) collective-permute-start(f32[32,256]{1,0:T(8,128)} %get-tuple-element.14), channel_id=1, source_target_pairs={{0,4},{4,8},{8,12},{12,16},{16,20},{20,24},{24,28},{1,5},{5,9},{9,... | collective-permute-start | bytes 98312 | tf_op jit(solution)/shard_map/ppermute | solution.py:317
  7.2 6.0 %collective-permute-start.1 = (f32[32,256]{1,0:T(8,128)}, f32[32,256]{1,0:T(8,128)S(1)}, u32[]{:S(2)}, u32[]{:S(2)}) collective-permute-start(f32[32,256]{1,0:T(8,128)} %get-tuple-element.15), channel_id=1, source_target_pairs={{4,0},{8,4},{12,8},{16,12},{20,16},{24,20},{28,24},{5,1},{9,5},{13... | collective-permute-start | bytes 98312 | tf_op jit(solution)/shard_map/ppermute | solution.py:318
  8.5 4.7 %collective-permute-start.2 = (f32[32,256]{1,0:T(8,128)}, f32[32,256]{1,0:T(8,128)S(1)}, u32[]{:S(2)}, u32[]{:S(2)}) collective-permute-start(f32[32,256]{1,0:T(8,128)} %get-tuple-element.16), channel_id=1, source_target_pairs={{0,1},{1,2},{2,3},{4,5},{5,6},{6,7},{8,9},{9,10},{10,11},{12,13},{... | collective-permute-start | bytes 98312 | tf_op jit(solution)/shard_map/ppermute | solution.py:319
  10.0 4.9 %collective-permute-start.3 = (f32[32,256]{1,0:T(8,128)}, f32[32,256]{1,0:T(8,128)S(1)}, u32[]{:S(2)}, u32[]{:S(2)}) collective-permute-start(f32[32,256]{1,0:T(8,128)} %get-tuple-element.17), channel_id=1, source_target_pairs={{1,0},{2,1},{3,2},{5,4},{6,5},{7,6},{9,8},{10,9},{11,10},{13,12},{... | collective-permute-start | bytes 98312 | tf_op jit(solution)/shard_map/ppermute | solution.py:320
  11.9 2.9 %copy-start = (f32[32,256]{1,0:T(8,128)}, f32[32,256]{1,0:T(8,128)S(1)}, u32[]{:S(2)}) copy-start(f32[32,256]{1,0:T(8,128)S(1)} %collective-permute-done.g0_ref) | copy-start | bytes 98308
  13.2 1.7 %copy-start.1 = (f32[32,256]{1,0:T(8,128)}, f32[32,256]{1,0:T(8,128)S(1)}, u32[]{:S(2)}) copy-start(f32[32,256]{1,0:T(8,128)S(1)} %collective-permute-done.1.g1_ref) | copy-start | bytes 98308
  13.2 1.6 %copy-start.3 = (f32[32,256]{1,0:T(8,128)}, f32[32,256]{1,0:T(8,128)S(1)}, u32[]{:S(2)}) copy-start(f32[32,256]{1,0:T(8,128)S(1)} %collective-permute-done.2.g2_ref) | copy-start | bytes 98308
  14.9 0.6 copy-start.5
  15.5 47.7 %copy-start.8 = (f32[4,4,4]{2,1,0:T(4,128)S(1)}, f32[4,4,4]{2,1,0:T(4,128)}, u32[]{:S(2)}) copy-start(f32[4,4,4]{2,1,0:T(4,128)} %constant.52.clone) | copy-start | bytes 772
  23.9 11.4 %collective-permute-start.4 = (f32[32,256]{1,0:T(8,128)}, f32[32,256]{1,0:T(8,128)S(1)}, u32[]{:S(2)}, u32[]{:S(2)}) collective-permute-start(f32[32,256]{1,0:T(8,128)} %get-tuple-element.19), channel_id=1, source_target_pairs={{0,4},{4,8},{8,12},{12,16},{16,20},{20,24},{24,28},{1,5},{5,9},{9,... | collective-permute-start | bytes 98312 | tf_op jit(solution)/shard_map/ppermute | solution.py:317
  28.5 6.9 %collective-permute-start.5 = (f32[32,256]{1,0:T(8,128)}, f32[32,256]{1,0:T(8,128)S(1)}, u32[]{:S(2)}, u32[]{:S(2)}) collective-permute-start(f32[32,256]{1,0:T(8,128)} %get-tuple-element.20), channel_id=1, source_target_pairs={{4,0},{8,4},{12,8},{16,12},{20,16},{24,20},{28,24},{5,1},{9,5},{13... | collective-permute-start | bytes 98312 | tf_op jit(solution)/shard_map/ppermute | solution.py:318
  29.8 5.6 %collective-permute-start.6 = (f32[32,256]{1,0:T(8,128)}, f32[32,256]{1,0:T(8,128)S(1)}, u32[]{:S(2)}, u32[]{:S(2)}) collective-permute-start(f32[32,256]{1,0:T(8,128)} %get-tuple-element.21), channel_id=1, source_target_pairs={{0,1},{1,2},{2,3},{4,5},{5,6},{6,7},{8,9},{9,10},{10,11},{12,13},{... | collective-permute-start | bytes 98312 | tf_op jit(solution)/shard_map/ppermute | solution.py:319
  34.0 3.3 %collective-permute-start.7 = (f32[32,256]{1,0:T(8,128)}, f32[32,256]{1,0:T(8,128)S(1)}, u32[]{:S(2)}, u32[]{:S(2)}) collective-permute-start(f32[32,256]{1,0:T(8,128)} %get-tuple-element.22), channel_id=1, source_target_pairs={{1,0},{2,1},{3,2},{5,4},{6,5},{7,6},{9,8},{10,9},{11,10},{13,12},{... | collective-permute-start | bytes 98312 | tf_op jit(solution)/shard_map/ppermute | solution.py:320
  35.3 2.0 %copy-start.2 = (f32[32,256]{1,0:T(8,128)}, f32[32,256]{1,0:T(8,128)S(1)}, u32[]{:S(2)}) copy-start(f32[32,256]{1,0:T(8,128)S(1)} %collective-permute-done.4.g0_ref) | copy-start | bytes 98308
  35.4 2.0 %copy-start.4 = (f32[32,256]{1,0:T(8,128)}, f32[32,256]{1,0:T(8,128)S(1)}, u32[]{:S(2)}) copy-start(f32[32,256]{1,0:T(8,128)S(1)} %collective-permute-done.5.g1_ref) | copy-start | bytes 98308
  35.4 2.0 %copy-start.6 = (f32[32,256]{1,0:T(8,128)}, f32[32,256]{1,0:T(8,128)S(1)}, u32[]{:S(2)}) copy-start(f32[32,256]{1,0:T(8,128)S(1)} %collective-permute-done.6.g2_ref) | copy-start | bytes 98308
  37.3 0.6 copy-start.7

commit v17 on v16

--- a/solution.py
+++ b/solution.py
@@ -15,7 +15,7 @@
 LANES = 128
 SUBLANES = 8
 UNROLL = 32
-CHUNK_ROWS = 16
+CHUNK_ROWS = 8
 ROWS_PER_STEP = 32
 
 

time: 70 us -> 71 us (1.014)
  Pallas kernels: 20.7 us -> 21.7 us
    pallas_call x2, Pallas kernels: 17 us -> 18 us  [apply_operator(): pl.pallas_call(functools.partial(coupling_kernel, with_gram), out_shape=t...]
where the time goes in v17:
time: 71 us; the launch traced here: 70.5 us
  Pallas kernels  21.7 us (31%)
  starting transfers between devices  20.4 us (29%)
  blocking collectives  16.5 us (23%)
  waiting for transfers between devices  4.7 us (7%)
  other arithmetic  2.89 us (4%)
  local copies, waits for them, and re-layouts  1.96 us (3%)
  between operations  1.46 us (2%)
  matrix products  0.93 us (1%)
    pallas_call x2, Pallas kernels, apply_operator(): pl.pallas_call(functools.partial(coupling_kernel, with_gram), out_shape=t...  18 us
    all_to_all x1, blocking collectives, per_device(): everyone = lax.all_to_all(raw_gram, ('wide', 'narrow'), 0, 0, tiled=True)  16.5 us
    ppermute x2, starting transfers between devices, ghosts(): lax.ppermute(outgoing[0], 'wide', [(i, i + 1) for i in range(wide - 1)])  9.38 us
    ppermute x2, starting transfers between devices, ghosts(): lax.ppermute(outgoing[2], 'narrow', [(i, i + 1) for i in range(narrow - 1)])  5.72 us
    ppermute x2, waiting for transfers between devices, ghosts(): lax.ppermute(outgoing[3], 'narrow', [(i + 1, i) for i in range(narrow - 1)])  3.41 us
    ppermute x2, starting transfers between devices, ghosts(): lax.ppermute(outgoing[3], 'narrow', [(i + 1, i) for i in range(narrow - 1)])  2.76 us
    ppermute x2, starting transfers between devices, ghosts(): lax.ppermute(outgoing[1], 'wide', [(i + 1, i) for i in range(wide - 1)])  2.58 us
    pallas_call x1, Pallas kernels, mix_outputs(): pl.pallas_call(mixing_kernel, out_shape=(jax.ShapeDtypeStruct(anchor.shap...  1.93 us
  transfers between devices with their start and end apart: 8, of which 3 were waited for; matrix products, arithmetic and copies ran while one was open for 0% of the time, Pallas kernels for 0%

profile of v17, /device:TPU:0, one launch (start us, length us, event | category | flops | bytes accessed | tf_op | source)
XLA Modules:
  0.0 70.5 jit_solution(11003740686881229934)
XLA Ops:
  0.6 1.8 %shard_map.77 = (f32[32,256]{1,0:T(8,128)}, f32[32,256]{1,0:T(8,128)}, f32[32,256]{1,0:T(8,128)}, f32[32,256]{1,0:T(8,128)}) custom-call(s32[4,32]{1,0:T(4,128)} %bitcast.26, f32[128,256]{1,0:T(8,128)} %own_ref.1), custom_call_target="tpu_custom_call" | custom-call | tf_op jit(solution)/shard_map/pallas_call | solution.py:267
  2.4 4.8 %collective-permute-start = (f32[32,256]{1,0:T(8,128)}, f32[32,256]{1,0:T(8,128)S(1)}, u32[]{:S(2)}, u32[]{:S(2)}) collective-permute-start(f32[32,256]{1,0:T(8,128)} %get-tuple-element.14), channel_id=1, source_target_pairs={{0,4},{4,8},{8,12},{12,16},{16,20},{20,24},{24,28},{1,5},{5,9},{9,... | collective-permute-start | bytes 98312 | tf_op jit(solution)/shard_map/ppermute | solution.py:317
  7.2 1.3 %collective-permute-start.1 = (f32[32,256]{1,0:T(8,128)}, f32[32,256]{1,0:T(8,128)S(1)}, u32[]{:S(2)}, u32[]{:S(2)}) collective-permute-start(f32[32,256]{1,0:T(8,128)} %get-tuple-element.15), channel_id=1, source_target_pairs={{4,0},{8,4},{12,8},{16,12},{20,16},{24,20},{28,24},{5,1},{9,5},{13... | collective-permute-start | bytes 98312 | tf_op jit(solution)/shard_map/ppermute | solution.py:318
  8.5 1.5 %collective-permute-start.2 = (f32[32,256]{1,0:T(8,128)}, f32[32,256]{1,0:T(8,128)S(1)}, u32[]{:S(2)}, u32[]{:S(2)}) collective-permute-start(f32[32,256]{1,0:T(8,128)} %get-tuple-element.16), channel_id=1, source_target_pairs={{0,1},{1,2},{2,3},{4,5},{5,6},{6,7},{8,9},{9,10},{10,11},{12,13},{... | collective-permute-start | bytes 98312 | tf_op jit(solution)/shard_map/ppermute | solution.py:319
  10.0 1.3 %collective-permute-start.3 = (f32[32,256]{1,0:T(8,128)}, f32[32,256]{1,0:T(8,128)S(1)}, u32[]{:S(2)}, u32[]{:S(2)}) collective-permute-start(f32[32,256]{1,0:T(8,128)} %get-tuple-element.17), channel_id=1, source_target_pairs={{1,0},{2,1},{3,2},{5,4},{6,5},{7,6},{9,8},{10,9},{11,10},{13,12},{... | collective-permute-start | bytes 98312 | tf_op jit(solution)/shard_map/ppermute | solution.py:320
  11.9 0.0 collective-permute-done.g0_ref
  11.9 0.0 copy-start
  12.0 1.3 %collective-permute-done.1.g1_ref = f32[32,256]{1,0:T(8,128)S(1)} collective-permute-done((f32[32,256]{1,0:T(8,128)}, f32[32,256]{1,0:T(8,128)S(1)}, u32[]{:S(2)}, u32[]{:S(2)}) %collective-permute-start.1) | collective-permute-done | bytes 32800 | tf_op jit(solution)/shard_map/ppermute | solution.py:318
  13.2 0.0 collective-permute-done.2.g2_ref
  13.2 1.6 %collective-permute-done.3.g3_ref = f32[32,256]{1,0:T(8,128)S(1)} collective-permute-done((f32[32,256]{1,0:T(8,128)}, f32[32,256]{1,0:T(8,128)S(1)}, u32[]{:S(2)}, u32[]{:S(2)}) %collective-permute-start.3) | collective-permute-done | bytes 32800 | tf_op jit(solution)/shard_map/ppermute | solution.py:320
  14.9 0.0 copy-done
  14.9 0.0 copy-done.1
  14.9 0.0 copy-done.3
  14.9 0.6 copy-done.5
  15.5 8.9 %shard_map.78 = (f32[128,256]{1,0:T(8,128)}, f32[32,256]{1,0:T(8,128)}, f32[32,256]{1,0:T(8,128)}, f32[32,256]{1,0:T(8,128)}, f32[32,256]{1,0:T(8,128)}, /*index=5*/f32[128,256]{1,0:T(8,128)}) custom-call(s32[1]{0:T(128)S(6)} %copy.39.count_ref, s32[4,32]{1,0:T(4,128)} %bitcast.27, f32[5,128,4096]{2,1,0:T(8,128)} %bitcast.23, f32[128,256]{1,0:T(8,128)} %own_ref.1, ...), custom_call_target="tpu_custom_call" | custom-call | flops 557842432 | bytes 11272192 | tf_op jit(solution)/shard_map/pallas_call | solution.py:237
  24.4 4.5 %collective-permute-start.4 = (f32[32,256]{1,0:T(8,128)}, f32[32,256]{1,0:T(8,128)S(1)}, u32[]{:S(2)}, u32[]{:S(2)}) collective-permute-start(f32[32,256]{1,0:T(8,128)} %get-tuple-element.19), channel_id=1, source_target_pairs={{0,4},{4,8},{8,12},{12,16},{16,20},{20,24},{24,28},{1,5},{5,9},{9,... | collective-permute-start | bytes 98312 | tf_op jit(solution)/shard_map/ppermute | solution.py:317
  29.0 1.3 %collective-permute-start.5 = (f32[32,256]{1,0:T(8,128)}, f32[32,256]{1,0:T(8,128)S(1)}, u32[]{:S(2)}, u32[]{:S(2)}) collective-permute-start(f32[32,256]{1,0:T(8,128)} %get-tuple-element.20), channel_id=1, source_target_pairs={{4,0},{8,4},{12,8},{16,12},{20,16},{24,20},{28,24},{5,1},{9,5},{13... | collective-permute-start | bytes 98312 | tf_op jit(solution)/shard_map/ppermute | solution.py:318
  30.3 4.3 %collective-permute-start.6 = (f32[32,256]{1,0:T(8,128)}, f32[32,256]{1,0:T(8,128)S(1)}, u32[]{:S(2)}, u32[]{:S(2)}) collective-permute-start(f32[32,256]{1,0:T(8,128)} %get-tuple-element.21), channel_id=1, source_target_pairs={{0,1},{1,2},{2,3},{4,5},{5,6},{6,7},{8,9},{9,10},{10,11},{12,13},{... | collective-permute-start | bytes 98312 | tf_op jit(solution)/shard_map/ppermute | solution.py:319
  34.5 1.5 %collective-permute-start.7 = (f32[32,256]{1,0:T(8,128)}, f32[32,256]{1,0:T(8,128)S(1)}, u32[]{:S(2)}, u32[]{:S(2)}) collective-permute-start(f32[32,256]{1,0:T(8,128)} %get-tuple-element.22), channel_id=1, source_target_pairs={{1,0},{2,1},{3,2},{5,4},{6,5},{7,6},{9,8},{10,9},{11,10},{13,12},{... | collective-permute-start | bytes 98312 | tf_op jit(solution)/shard_map/ppermute | solution.py:320
  36.0 0.0 collective-permute-done.4.g0_ref
  36.0 0.0 copy-start.2
  36.0 0.0 collective-permute-done.5.g1_ref
  36.0 0.0 copy-start.4
  36.0 0.0 collective-permute-done.6.g2_ref
  36.1 0.0 copy-start.6
  36.1 1.8 %collective-permute-done.7.g3_ref = f32[32,256]{1,0:T(8,128)S(1)} collective-permute-done((f32[32,256]{1,0:T(8,128)}, f32[32,256]{1,0:T(8,128)S(1)}, u32[]{:S(2)}, u32[]{:S(2)}) %collective-permute-start.7) | collective-permute-done | bytes 32800 | tf_op jit(solution)/shard_map/ppermute | solution.py:320
  37.8 0.0 copy-done.2
  37.8 0.0 copy-done.4
  37.8 0.6 copy-done.7
  38.4 9.1 %shard_map.79 = (f32[128,256]{1,0:T(8,128)}, f32[32,4,20]{2,1,0:T(4,128)}) custom-call(s32[1]{0:T(128)S(6)} %copy.39.count_ref, s32[4,32]{1,0:T(4,128)} %bitcast.28, f32[5,128,4096]{2,1,0:T(8,128)} %bitcast.24, f32[128,256]{1,0:T(8,128)} %get-tuple-element.18.own_ref.first_ref, f32[32,256]{1,0:T(8,128)} %copy-done.2, f32[32,256]{1,0:T(8,128)} %copy-done.4, ...), custom_call_target="tpu_custom_call" | custom-call | flops 557842432 | bytes 11272192 | tf_op jit(solution)/shard_map/pallas_call | solution.py:237
  47.5 16.5 %all_to_all.5 = f32[32,4,20]{2,1,0:T(4,128)S(1)} all-to-all(f32[32,4,20]{2,1,0:T(4,128)} %get-tuple-element.24), channel_id=1, replica_groups=mesh['wide'=8,'narrow'=4] {'wide','narrow'}, dimensions={0} | all-to-all | bytes 20480 | tf_op jit(solution)/shard_map/all_to_all | solution.py:329
  64.0 0.1 mul.15
  64.1 0.1 copy.29
  64.2 0.1 multiply_reduce_fusion
  64.3 0.2 fusion.10
  64.5 0.1 copy.37
  64.6 0.1 copy.38
  64.7 0.1 copy.31
  64.8 0.1 maximum_maximum_fusion
  64.9 0.1 copy.33
  65.0 0.7 cholesky.16
  65.7 0.1 select_reduce_fusion
  65.7 0.6 compare_reduce_fusion
  66.4 0.6 fusion
  67.0 0.6 custom-call.10
  67.7 0.2 fusion.1
  67.9 0.7 %fusion.6.mix_ref = f32[8,4]{1,0:T(8,128)} fusion(f32[8,4]{0,1:T(4,128)S(1)} %fusion.1, f32[1,8,8]{1,2,0:T(8,128)S(1)} %custom-call.10), kind=kOutput, calls=%fused_computation.12 | convolution fusion | flops 3072 | bytes 512 | tf_op jit(solution)/shard_map/jit(_cho_solve)/triangular_solve | solution.py:345
  68.6 1.9 %shard_map.80 = (f32[128,256]{1,0:T(8,128)}, f32[128,256]{1,0:T(8,128)}) custom-call(f32[8,4]{1,0:T(8,128)} %fusion.6.mix_ref, f32[128,256]{1,0:T(8,128)} %get-tuple-element.23.rest_0_.anchor_ref, f32[128,256]{1,0:T(8,128)} %get-tuple-element.18.own_ref.first_ref, f32[128,256]{1,0:T(8,128)} %get-tuple-element.25.second_ref), custom_call_target="tpu_custom_call" | custom-call | tf_op jit(solution)/shard_map/pallas_call | solution.py:302
  (9 shorter events, 0.1 us)
Async XLA Ops:
  2.4 9.6 %collective-permute-start = (f32[32,256]{1,0:T(8,128)}, f32[32,256]{1,0:T(8,128)S(1)}, u32[]{:S(2)}, u32[]{:S(2)}) collective-permute-start(f32[32,256]{1,0:T(8,128)} %get-tuple-element.14), channel_id=1, source_target_pairs={{0,4},{4,8},{8,12},{12,16},{16,20},{20,24},{24,28},{1,5},{5,9},{9,... | collective-permute-start | bytes 98312 | tf_op jit(solution)/shard_map/ppermute | solution.py:317
  7.2 6.0 %collective-permute-start.1 = (f32[32,256]{1,0:T(8,128)}, f32[32,256]{1,0:T(8,128)S(1)}, u32[]{:S(2)}, u32[]{:S(2)}) collective-permute-start(f32[32,256]{1,0:T(8,128)} %get-tuple-element.15), channel_id=1, source_target_pairs={{4,0},{8,4},{12,8},{16,12},{20,16},{24,20},{28,24},{5,1},{9,5},{13... | collective-permute-start | bytes 98312 | tf_op jit(solution)/shard_map/ppermute | solution.py:318
  8.5 4.7 %collective-permute-start.2 = (f32[32,256]{1,0:T(8,128)}, f32[32,256]{1,0:T(8,128)S(1)}, u32[]{:S(2)}, u32[]{:S(2)}) collective-permute-start(f32[32,256]{1,0:T(8,128)} %get-tuple-element.16), channel_id=1, source_target_pairs={{0,1},{1,2},{2,3},{4,5},{5,6},{6,7},{8,9},{9,10},{10,11},{12,13},{... | collective-permute-start | bytes 98312 | tf_op jit(solution)/shard_map/ppermute | solution.py:319
  10.0 4.9 %collective-permute-start.3 = (f32[32,256]{1,0:T(8,128)}, f32[32,256]{1,0:T(8,128)S(1)}, u32[]{:S(2)}, u32[]{:S(2)}) collective-permute-start(f32[32,256]{1,0:T(8,128)} %get-tuple-element.17), channel_id=1, source_target_pairs={{1,0},{2,1},{3,2},{5,4},{6,5},{7,6},{9,8},{10,9},{11,10},{13,12},{... | collective-permute-start | bytes 98312 | tf_op jit(solution)/shard_map/ppermute | solution.py:320
  11.9 2.9 %copy-start = (f32[32,256]{1,0:T(8,128)}, f32[32,256]{1,0:T(8,128)S(1)}, u32[]{:S(2)}) copy-start(f32[32,256]{1,0:T(8,128)S(1)} %collective-permute-done.g0_ref) | copy-start | bytes 98308
  13.2 1.7 %copy-start.1 = (f32[32,256]{1,0:T(8,128)}, f32[32,256]{1,0:T(8,128)S(1)}, u32[]{:S(2)}) copy-start(f32[32,256]{1,0:T(8,128)S(1)} %collective-permute-done.1.g1_ref) | copy-start | bytes 98308
  13.2 1.6 %copy-start.3 = (f32[32,256]{1,0:T(8,128)}, f32[32,256]{1,0:T(8,128)S(1)}, u32[]{:S(2)}) copy-start(f32[32,256]{1,0:T(8,128)S(1)} %collective-permute-done.2.g2_ref) | copy-start | bytes 98308
  14.9 0.6 copy-start.5
  15.5 48.7 %copy-start.8 = (f32[4,4,4]{2,1,0:T(4,128)S(1)}, f32[4,4,4]{2,1,0:T(4,128)}, u32[]{:S(2)}) copy-start(f32[4,4,4]{2,1,0:T(4,128)} %constant.52.clone) | copy-start | bytes 772
  24.4 11.6 %collective-permute-start.4 = (f32[32,256]{1,0:T(8,128)}, f32[32,256]{1,0:T(8,128)S(1)}, u32[]{:S(2)}, u32[]{:S(2)}) collective-permute-start(f32[32,256]{1,0:T(8,128)} %get-tuple-element.19), channel_id=1, source_target_pairs={{0,4},{4,8},{8,12},{12,16},{16,20},{20,24},{24,28},{1,5},{5,9},{9,... | collective-permute-start | bytes 98312 | tf_op jit(solution)/shard_map/ppermute | solution.py:317
  29.0 7.1 %collective-permute-start.5 = (f32[32,256]{1,0:T(8,128)}, f32[32,256]{1,0:T(8,128)S(1)}, u32[]{:S(2)}, u32[]{:S(2)}) collective-permute-start(f32[32,256]{1,0:T(8,128)} %get-tuple-element.20), channel_id=1, source_target_pairs={{4,0},{8,4},{12,8},{16,12},{20,16},{24,20},{28,24},{5,1},{9,5},{13... | collective-permute-start | bytes 98312 | tf_op jit(solution)/shard_map/ppermute | solution.py:318
  30.3 5.8 %collective-permute-start.6 = (f32[32,256]{1,0:T(8,128)}, f32[32,256]{1,0:T(8,128)S(1)}, u32[]{:S(2)}, u32[]{:S(2)}) collective-permute-start(f32[32,256]{1,0:T(8,128)} %get-tuple-element.21), channel_id=1, source_target_pairs={{0,1},{1,2},{2,3},{4,5},{5,6},{6,7},{8,9},{9,10},{10,11},{12,13},{... | collective-permute-start | bytes 98312 | tf_op jit(solution)/shard_map/ppermute | solution.py:319
  34.5 3.3 %collective-permute-start.7 = (f32[32,256]{1,0:T(8,128)}, f32[32,256]{1,0:T(8,128)S(1)}, u32[]{:S(2)}, u32[]{:S(2)}) collective-permute-start(f32[32,256]{1,0:T(8,128)} %get-tuple-element.22), channel_id=1, source_target_pairs={{1,0},{2,1},{3,2},{5,4},{6,5},{7,6},{9,8},{10,9},{11,10},{13,12},{... | collective-permute-start | bytes 98312 | tf_op jit(solution)/shard_map/ppermute | solution.py:320
  36.0 1.8 %copy-start.2 = (f32[32,256]{1,0:T(8,128)}, f32[32,256]{1,0:T(8,128)S(1)}, u32[]{:S(2)}) copy-start(f32[32,256]{1,0:T(8,128)S(1)} %collective-permute-done.4.g0_ref) | copy-start | bytes 98308
  36.0 1.8 %copy-start.4 = (f32[32,256]{1,0:T(8,128)}, f32[32,256]{1,0:T(8,128)S(1)}, u32[]{:S(2)}) copy-start(f32[32,256]{1,0:T(8,128)S(1)} %collective-permute-done.5.g1_ref) | copy-start | bytes 98308
  36.1 1.8 %copy-start.6 = (f32[32,256]{1,0:T(8,128)}, f32[32,256]{1,0:T(8,128)S(1)}, u32[]{:S(2)}) copy-start(f32[32,256]{1,0:T(8,128)S(1)} %collective-permute-done.6.g2_ref) | copy-start | bytes 98308
  37.8 0.6 copy-start.7

commit v18 on v16

--- a/solution.py
+++ b/solution.py
@@ -179,16 +179,17 @@
                 return inner
 
             lax.fori_loop(0, tiles, one_tile, 0, unroll=UNROLL)
+        rows = pl.ds(pl.multiple_of(b * chunk_rows, chunk_rows), chunk_rows)
+        for c in range(VECS):
+            total = z_ref[c, rows, :]
+            high = total.astype(jnp.bfloat16)
+            parts_ref[2 * c, rows, :] = high
+            parts_ref[2 * c + 1, rows, :] = (total - high.astype(jnp.float32)).astype(jnp.bfloat16)
         return carry
 
     lax.fori_loop(0, chunks, one_chunk, 0, unroll=True)
 
     full = tiles * LANES
-    for c in range(VECS):
-        total = z_ref[c]
-        high = total.astype(jnp.bfloat16)
-        parts_ref[2 * c] = high
-        parts_ref[2 * c + 1] = (total - high.astype(jnp.float32)).astype(jnp.bfloat16)
     flat = parts_ref[...].reshape(2 * VECS * count, full)
     seg = (
         lax.broadcasted_iota(jnp.int32, (full, BLK), 0) // BLK

time: 70 us -> 71.8 us (1.026)
  Pallas kernels: 20.7 us -> 22.5 us
    pallas_call x2, Pallas kernels: 17 us -> 18.8 us  [apply_operator(): pl.pallas_call(functools.partial(coupling_kernel, with_gram), out_shape=t...]
where the time goes in v18:
time: 71.8 us; the launch traced here: 71.4 us
  Pallas kernels  22.5 us (31%)
  starting transfers between devices  20.4 us (28%)
  blocking collectives  16.5 us (23%)
  waiting for transfers between devices  4.7 us (7%)
  other arithmetic  2.89 us (4%)
  local copies, waits for them, and re-layouts  1.96 us (3%)
  between operations  1.46 us (2%)
  matrix products  0.93 us (1%)
    pallas_call x2, Pallas kernels, apply_operator(): pl.pallas_call(functools.partial(coupling_kernel, with_gram), out_shape=t...  18.8 us
    all_to_all x1, blocking collectives, per_device(): everyone = lax.all_to_all(raw_gram, ('wide', 'narrow'), 0, 0, tiled=True)  16.5 us
    ppermute x2, starting transfers between devices, ghosts(): lax.ppermute(outgoing[0], 'wide', [(i, i + 1) for i in range(wide - 1)])  9.38 us
    ppermute x2, starting transfers between devices, ghosts(): lax.ppermute(outgoing[2], 'narrow', [(i, i + 1) for i in range(narrow - 1)])  5.71 us
    ppermute x2, waiting for transfers between devices, ghosts(): lax.ppermute(outgoing[3], 'narrow', [(i + 1, i) for i in range(narrow - 1)])  3.41 us
    ppermute x2, starting transfers between devices, ghosts(): lax.ppermute(outgoing[3], 'narrow', [(i + 1, i) for i in range(narrow - 1)])  2.76 us
    ppermute x2, starting transfers between devices, ghosts(): lax.ppermute(outgoing[1], 'wide', [(i + 1, i) for i in range(wide - 1)])  2.58 us
    pallas_call x1, Pallas kernels, mix_outputs(): pl.pallas_call(mixing_kernel, out_shape=(jax.ShapeDtypeStruct(anchor.shap...  1.93 us
  transfers between devices with their start and end apart: 8, of which 3 were waited for; matrix products, arithmetic and copies ran while one was open for 0% of the time, Pallas kernels for 0%

profile of v18, /device:TPU:0, one launch (start us, length us, event | category | flops | bytes accessed | tf_op | source)
XLA Modules:
  0.0 71.4 jit_solution(7318076608904669781)
XLA Ops:
  0.6 1.8 %shard_map.77 = (f32[32,256]{1,0:T(8,128)}, f32[32,256]{1,0:T(8,128)}, f32[32,256]{1,0:T(8,128)}, f32[32,256]{1,0:T(8,128)}) custom-call(s32[4,32]{1,0:T(4,128)} %bitcast.26, f32[128,256]{1,0:T(8,128)} %own_ref.1), custom_call_target="tpu_custom_call" | custom-call | tf_op jit(solution)/shard_map/pallas_call | solution.py:268
  2.4 4.8 %collective-permute-start = (f32[32,256]{1,0:T(8,128)}, f32[32,256]{1,0:T(8,128)S(1)}, u32[]{:S(2)}, u32[]{:S(2)}) collective-permute-start(f32[32,256]{1,0:T(8,128)} %get-tuple-element.14), channel_id=1, source_target_pairs={{0,4},{4,8},{8,12},{12,16},{16,20},{20,24},{24,28},{1,5},{5,9},{9,... | collective-permute-start | bytes 98312 | tf_op jit(solution)/shard_map/ppermute | solution.py:318
  7.2 1.3 %collective-permute-start.1 = (f32[32,256]{1,0:T(8,128)}, f32[32,256]{1,0:T(8,128)S(1)}, u32[]{:S(2)}, u32[]{:S(2)}) collective-permute-start(f32[32,256]{1,0:T(8,128)} %get-tuple-element.15), channel_id=1, source_target_pairs={{4,0},{8,4},{12,8},{16,12},{20,16},{24,20},{28,24},{5,1},{9,5},{13... | collective-permute-start | bytes 98312 | tf_op jit(solution)/shard_map/ppermute | solution.py:319
  8.5 1.5 %collective-permute-start.2 = (f32[32,256]{1,0:T(8,128)}, f32[32,256]{1,0:T(8,128)S(1)}, u32[]{:S(2)}, u32[]{:S(2)}) collective-permute-start(f32[32,256]{1,0:T(8,128)} %get-tuple-element.16), channel_id=1, source_target_pairs={{0,1},{1,2},{2,3},{4,5},{5,6},{6,7},{8,9},{9,10},{10,11},{12,13},{... | collective-permute-start | bytes 98312 | tf_op jit(solution)/shard_map/ppermute | solution.py:320
  10.0 1.3 %collective-permute-start.3 = (f32[32,256]{1,0:T(8,128)}, f32[32,256]{1,0:T(8,128)S(1)}, u32[]{:S(2)}, u32[]{:S(2)}) collective-permute-start(f32[32,256]{1,0:T(8,128)} %get-tuple-element.17), channel_id=1, source_target_pairs={{1,0},{2,1},{3,2},{5,4},{6,5},{7,6},{9,8},{10,9},{11,10},{13,12},{... | collective-permute-start | bytes 98312 | tf_op jit(solution)/shard_map/ppermute | solution.py:321
  11.9 0.0 collective-permute-done.g0_ref
  11.9 0.0 copy-start
  12.0 1.3 %collective-permute-done.1.g1_ref = f32[32,256]{1,0:T(8,128)S(1)} collective-permute-done((f32[32,256]{1,0:T(8,128)}, f32[32,256]{1,0:T(8,128)S(1)}, u32[]{:S(2)}, u32[]{:S(2)}) %collective-permute-start.1) | collective-permute-done | bytes 32800 | tf_op jit(solution)/shard_map/ppermute | solution.py:319
  13.2 0.0 collective-permute-done.2.g2_ref
  13.2 1.6 %collective-permute-done.3.g3_ref = f32[32,256]{1,0:T(8,128)S(1)} collective-permute-done((f32[32,256]{1,0:T(8,128)}, f32[32,256]{1,0:T(8,128)S(1)}, u32[]{:S(2)}, u32[]{:S(2)}) %collective-permute-start.3) | collective-permute-done | bytes 32800 | tf_op jit(solution)/shard_map/ppermute | solution.py:321
  14.9 0.0 copy-done
  14.9 0.0 copy-done.1
  14.9 0.0 copy-done.3
  14.9 0.6 copy-done.5
  15.5 9.3 %shard_map.78 = (f32[128,256]{1,0:T(8,128)}, f32[32,256]{1,0:T(8,128)}, f32[32,256]{1,0:T(8,128)}, f32[32,256]{1,0:T(8,128)}, f32[32,256]{1,0:T(8,128)}, /*index=5*/f32[128,256]{1,0:T(8,128)}) custom-call(s32[1]{0:T(128)S(6)} %copy.39.count_ref, s32[4,32]{1,0:T(4,128)} %bitcast.27, f32[5,128,4096]{2,1,0:T(8,128)} %bitcast.23, f32[128,256]{1,0:T(8,128)} %own_ref.1, ...), custom_call_target="tpu_custom_call" | custom-call | flops 557842432 | bytes 11272192 | tf_op jit(solution)/shard_map/pallas_call | solution.py:238
  24.8 4.5 %collective-permute-start.4 = (f32[32,256]{1,0:T(8,128)}, f32[32,256]{1,0:T(8,128)S(1)}, u32[]{:S(2)}, u32[]{:S(2)}) collective-permute-start(f32[32,256]{1,0:T(8,128)} %get-tuple-element.19), channel_id=1, source_target_pairs={{0,4},{4,8},{8,12},{12,16},{16,20},{20,24},{24,28},{1,5},{5,9},{9,... | collective-permute-start | bytes 98312 | tf_op jit(solution)/shard_map/ppermute | solution.py:318
  29.4 1.3 %collective-permute-start.5 = (f32[32,256]{1,0:T(8,128)}, f32[32,256]{1,0:T(8,128)S(1)}, u32[]{:S(2)}, u32[]{:S(2)}) collective-permute-start(f32[32,256]{1,0:T(8,128)} %get-tuple-element.20), channel_id=1, source_target_pairs={{4,0},{8,4},{12,8},{16,12},{20,16},{24,20},{28,24},{5,1},{9,5},{13... | collective-permute-start | bytes 98312 | tf_op jit(solution)/shard_map/ppermute | solution.py:319
  30.7 4.3 %collective-permute-start.6 = (f32[32,256]{1,0:T(8,128)}, f32[32,256]{1,0:T(8,128)S(1)}, u32[]{:S(2)}, u32[]{:S(2)}) collective-permute-start(f32[32,256]{1,0:T(8,128)} %get-tuple-element.21), channel_id=1, source_target_pairs={{0,1},{1,2},{2,3},{4,5},{5,6},{6,7},{8,9},{9,10},{10,11},{12,13},{... | collective-permute-start | bytes 98312 | tf_op jit(solution)/shard_map/ppermute | solution.py:320
  35.0 1.5 %collective-permute-start.7 = (f32[32,256]{1,0:T(8,128)}, f32[32,256]{1,0:T(8,128)S(1)}, u32[]{:S(2)}, u32[]{:S(2)}) collective-permute-start(f32[32,256]{1,0:T(8,128)} %get-tuple-element.22), channel_id=1, source_target_pairs={{1,0},{2,1},{3,2},{5,4},{6,5},{7,6},{9,8},{10,9},{11,10},{13,12},{... | collective-permute-start | bytes 98312 | tf_op jit(solution)/shard_map/ppermute | solution.py:321
  36.4 0.0 collective-permute-done.4.g0_ref
  36.4 0.0 copy-start.2
  36.5 0.0 collective-permute-done.5.g1_ref
  36.5 0.0 copy-start.4
  36.5 0.0 collective-permute-done.6.g2_ref
  36.5 0.0 copy-start.6
  36.5 1.8 %collective-permute-done.7.g3_ref = f32[32,256]{1,0:T(8,128)S(1)} collective-permute-done((f32[32,256]{1,0:T(8,128)}, f32[32,256]{1,0:T(8,128)S(1)}, u32[]{:S(2)}, u32[]{:S(2)}) %collective-permute-start.7) | collective-permute-done | bytes 32800 | tf_op jit(solution)/shard_map/ppermute | solution.py:321
  38.3 0.0 copy-done.2
  38.3 0.0 copy-done.4
  38.3 0.6 copy-done.7
  38.9 9.5 %shard_map.79 = (f32[128,256]{1,0:T(8,128)}, f32[32,4,20]{2,1,0:T(4,128)}) custom-call(s32[1]{0:T(128)S(6)} %copy.39.count_ref, s32[4,32]{1,0:T(4,128)} %bitcast.28, f32[5,128,4096]{2,1,0:T(8,128)} %bitcast.24, f32[128,256]{1,0:T(8,128)} %get-tuple-element.18.own_ref.first_ref, f32[32,256]{1,0:T(8,128)} %copy-done.2, f32[32,256]{1,0:T(8,128)} %copy-done.4, ...), custom_call_target="tpu_custom_call" | custom-call | flops 557842432 | bytes 11272192 | tf_op jit(solution)/shard_map/pallas_call | solution.py:238
  48.4 16.5 %all_to_all.5 = f32[32,4,20]{2,1,0:T(4,128)S(1)} all-to-all(f32[32,4,20]{2,1,0:T(4,128)} %get-tuple-element.24), channel_id=1, replica_groups=mesh['wide'=8,'narrow'=4] {'wide','narrow'}, dimensions={0} | all-to-all | bytes 20480 | tf_op jit(solution)/shard_map/all_to_all | solution.py:330
  64.9 0.1 mul.15
  65.0 0.1 copy.29
  65.1 0.1 multiply_reduce_fusion
  65.2 0.2 fusion.10
  65.4 0.1 copy.37
  65.5 0.1 copy.38
  65.6 0.1 copy.31
  65.7 0.1 maximum_maximum_fusion
  65.8 0.1 copy.33
  65.8 0.7 cholesky.16
  66.5 0.1 select_reduce_fusion
  66.6 0.6 compare_reduce_fusion
  67.2 0.6 fusion
  67.9 0.6 custom-call.10
  68.5 0.2 fusion.1
  68.7 0.7 %fusion.6.mix_ref = f32[8,4]{1,0:T(8,128)} fusion(f32[8,4]{0,1:T(4,128)S(1)} %fusion.1, f32[1,8,8]{1,2,0:T(8,128)S(1)} %custom-call.10), kind=kOutput, calls=%fused_computation.12 | convolution fusion | flops 3072 | bytes 512 | tf_op jit(solution)/shard_map/jit(_cho_solve)/triangular_solve | solution.py:346
  69.5 1.9 %shard_map.80 = (f32[128,256]{1,0:T(8,128)}, f32[128,256]{1,0:T(8,128)}) custom-call(f32[8,4]{1,0:T(8,128)} %fusion.6.mix_ref, f32[128,256]{1,0:T(8,128)} %get-tuple-element.23.rest_0_.anchor_ref, f32[128,256]{1,0:T(8,128)} %get-tuple-element.18.own_ref.first_ref, f32[128,256]{1,0:T(8,128)} %get-tuple-element.25.second_ref), custom_call_target="tpu_custom_call" | custom-call | tf_op jit(solution)/shard_map/pallas_call | solution.py:303
  (9 shorter events, 0.1 us)
Async XLA Ops:
  2.4 9.6 %collective-permute-start = (f32[32,256]{1,0:T(8,128)}, f32[32,256]{1,0:T(8,128)S(1)}, u32[]{:S(2)}, u32[]{:S(2)}) collective-permute-start(f32[32,256]{1,0:T(8,128)} %get-tuple-element.14), channel_id=1, source_target_pairs={{0,4},{4,8},{8,12},{12,16},{16,20},{20,24},{24,28},{1,5},{5,9},{9,... | collective-permute-start | bytes 98312 | tf_op jit(solution)/shard_map/ppermute | solution.py:318
  7.2 6.0 %collective-permute-start.1 = (f32[32,256]{1,0:T(8,128)}, f32[32,256]{1,0:T(8,128)S(1)}, u32[]{:S(2)}, u32[]{:S(2)}) collective-permute-start(f32[32,256]{1,0:T(8,128)} %get-tuple-element.15), channel_id=1, source_target_pairs={{4,0},{8,4},{12,8},{16,12},{20,16},{24,20},{28,24},{5,1},{9,5},{13... | collective-permute-start | bytes 98312 | tf_op jit(solution)/shard_map/ppermute | solution.py:319
  8.5 4.7 %collective-permute-start.2 = (f32[32,256]{1,0:T(8,128)}, f32[32,256]{1,0:T(8,128)S(1)}, u32[]{:S(2)}, u32[]{:S(2)}) collective-permute-start(f32[32,256]{1,0:T(8,128)} %get-tuple-element.16), channel_id=1, source_target_pairs={{0,1},{1,2},{2,3},{4,5},{5,6},{6,7},{8,9},{9,10},{10,11},{12,13},{... | collective-permute-start | bytes 98312 | tf_op jit(solution)/shard_map/ppermute | solution.py:320
  10.0 4.9 %collective-permute-start.3 = (f32[32,256]{1,0:T(8,128)}, f32[32,256]{1,0:T(8,128)S(1)}, u32[]{:S(2)}, u32[]{:S(2)}) collective-permute-start(f32[32,256]{1,0:T(8,128)} %get-tuple-element.17), channel_id=1, source_target_pairs={{1,0},{2,1},{3,2},{5,4},{6,5},{7,6},{9,8},{10,9},{11,10},{13,12},{... | collective-permute-start | bytes 98312 | tf_op jit(solution)/shard_map/ppermute | solution.py:321
  11.9 2.9 %copy-start = (f32[32,256]{1,0:T(8,128)}, f32[32,256]{1,0:T(8,128)S(1)}, u32[]{:S(2)}) copy-start(f32[32,256]{1,0:T(8,128)S(1)} %collective-permute-done.g0_ref) | copy-start | bytes 98308
  13.2 1.7 %copy-start.1 = (f32[32,256]{1,0:T(8,128)}, f32[32,256]{1,0:T(8,128)S(1)}, u32[]{:S(2)}) copy-start(f32[32,256]{1,0:T(8,128)S(1)} %collective-permute-done.1.g1_ref) | copy-start | bytes 98308
  13.2 1.6 %copy-start.3 = (f32[32,256]{1,0:T(8,128)}, f32[32,256]{1,0:T(8,128)S(1)}, u32[]{:S(2)}) copy-start(f32[32,256]{1,0:T(8,128)S(1)} %collective-permute-done.2.g2_ref) | copy-start | bytes 98308
  14.9 0.6 copy-start.5
  15.5 49.6 %copy-start.8 = (f32[4,4,4]{2,1,0:T(4,128)S(1)}, f32[4,4,4]{2,1,0:T(4,128)}, u32[]{:S(2)}) copy-start(f32[4,4,4]{2,1,0:T(4,128)} %constant.52.clone) | copy-start | bytes 772
  24.8 11.6 %collective-permute-start.4 = (f32[32,256]{1,0:T(8,128)}, f32[32,256]{1,0:T(8,128)S(1)}, u32[]{:S(2)}, u32[]{:S(2)}) collective-permute-start(f32[32,256]{1,0:T(8,128)} %get-tuple-element.19), channel_id=1, source_target_pairs={{0,4},{4,8},{8,12},{12,16},{16,20},{20,24},{24,28},{1,5},{5,9},{9,... | collective-permute-start | bytes 98312 | tf_op jit(solution)/shard_map/ppermute | solution.py:318
  29.4 7.1 %collective-permute-start.5 = (f32[32,256]{1,0:T(8,128)}, f32[32,256]{1,0:T(8,128)S(1)}, u32[]{:S(2)}, u32[]{:S(2)}) collective-permute-start(f32[32,256]{1,0:T(8,128)} %get-tuple-element.20), channel_id=1, source_target_pairs={{4,0},{8,4},{12,8},{16,12},{20,16},{24,20},{28,24},{5,1},{9,5},{13... | collective-permute-start | bytes 98312 | tf_op jit(solution)/shard_map/ppermute | solution.py:319
  30.7 5.8 %collective-permute-start.6 = (f32[32,256]{1,0:T(8,128)}, f32[32,256]{1,0:T(8,128)S(1)}, u32[]{:S(2)}, u32[]{:S(2)}) collective-permute-start(f32[32,256]{1,0:T(8,128)} %get-tuple-element.21), channel_id=1, source_target_pairs={{0,1},{1,2},{2,3},{4,5},{5,6},{6,7},{8,9},{9,10},{10,11},{12,13},{... | collective-permute-start | bytes 98312 | tf_op jit(solution)/shard_map/ppermute | solution.py:320
  35.0 3.3 %collective-permute-start.7 = (f32[32,256]{1,0:T(8,128)}, f32[32,256]{1,0:T(8,128)S(1)}, u32[]{:S(2)}, u32[]{:S(2)}) collective-permute-start(f32[32,256]{1,0:T(8,128)} %get-tuple-element.22), channel_id=1, source_target_pairs={{1,0},{2,1},{3,2},{5,4},{6,5},{7,6},{9,8},{10,9},{11,10},{13,12},{... | collective-permute-start | bytes 98312 | tf_op jit(solution)/shard_map/ppermute | solution.py:321
  36.4 1.8 %copy-start.2 = (f32[32,256]{1,0:T(8,128)}, f32[32,256]{1,0:T(8,128)S(1)}, u32[]{:S(2)}) copy-start(f32[32,256]{1,0:T(8,128)S(1)} %collective-permute-done.4.g0_ref) | copy-start | bytes 98308
  36.5 1.8 %copy-start.4 = (f32[32,256]{1,0:T(8,128)}, f32[32,256]{1,0:T(8,128)S(1)}, u32[]{:S(2)}) copy-start(f32[32,256]{1,0:T(8,128)S(1)} %collective-permute-done.5.g1_ref) | copy-start | bytes 98308
  36.5 1.8 %copy-start.6 = (f32[32,256]{1,0:T(8,128)}, f32[32,256]{1,0:T(8,128)S(1)}, u32[]{:S(2)}) copy-start(f32[32,256]{1,0:T(8,128)S(1)} %collective-permute-done.6.g2_ref) | copy-start | bytes 98308
  38.3 0.6 copy-start.7

commit v19 on v16

--- a/solution.py
+++ b/solution.py
@@ -142,6 +142,9 @@
     source_ref[0:count] = split_three(jnp.where(living, own_ref[...], jnp.float32(0.0)))
     for q, piece in enumerate((g0_ref, g1_ref, g2_ref, g3_ref)):
         source_ref[count + q * ghost:count + (q + 1) * ghost] = split_three(piece[...])
+    if with_gram:
+        kept_early = jnp.where(living, own_ref[...], jnp.float32(0.0))
+        early = gram_columns(((kept_early, anchor_ref[...]), (kept_early, kept_early)))
     slots = lax.broadcasted_iota(jnp.int32, (source_ref.shape[0], count), 0)
     for k in range(NB):
         chosen = (cols_ref[k:k + 1, :] == slots).astype(jnp.bfloat16)
@@ -210,7 +213,8 @@
                 lent_ref[j:j + 1, :] = out_ref[pl.ds(lend_ref[q, j], 1), :]
     else:
         anchor = anchor_ref[...]
-        partial = gram_columns(((kept, anchor), (kept, kept), (image, anchor), (image, kept), (image, image)))
+        late = gram_columns(((image, anchor), (image, kept), (image, image)))
+        partial = jnp.concatenate([early, late], axis=1)
         for target in range(gram_ref.shape[0]):
             gram_ref[target] = partial
 

time: 70 us -> 70 us (level)
  no operation moved by 1% of the time
where the time goes in v19:
time: 70 us; the launch traced here: 69.5 us
  Pallas kernels  20.7 us (30%)
  starting transfers between devices  20.3 us (29%)
  blocking collectives  16.5 us (24%)
  waiting for transfers between devices  4.88 us (7%)
  other arithmetic  2.89 us (4%)
  local copies, waits for them, and re-layouts  1.96 us (3%)
  between operations  1.46 us (2%)
  matrix products  0.93 us (1%)
    pallas_call x2, Pallas kernels, apply_operator(): pl.pallas_call(functools.partial(coupling_kernel, with_gram), out_shape=t...  17 us
    all_to_all x1, blocking collectives, per_device(): everyone = lax.all_to_all(raw_gram, ('wide', 'narrow'), 0, 0, tiled=True)  16.5 us
    ppermute x2, starting transfers between devices, ghosts(): lax.ppermute(outgoing[0], 'wide', [(i, i + 1) for i in range(wide - 1)])  9.37 us
    ppermute x2, starting transfers between devices, ghosts(): lax.ppermute(outgoing[2], 'narrow', [(i, i + 1) for i in range(narrow - 1)])  5.71 us
    ppermute x2, waiting for transfers between devices, ghosts(): lax.ppermute(outgoing[3], 'narrow', [(i + 1, i) for i in range(narrow - 1)])  3.59 us
    ppermute x2, starting transfers between devices, ghosts(): lax.ppermute(outgoing[1], 'wide', [(i + 1, i) for i in range(wide - 1)])  2.58 us
    ppermute x2, starting transfers between devices, ghosts(): lax.ppermute(outgoing[3], 'narrow', [(i + 1, i) for i in range(narrow - 1)])  2.58 us
    pallas_call x1, Pallas kernels, mix_outputs(): pl.pallas_call(mixing_kernel, out_shape=(jax.ShapeDtypeStruct(anchor.shap...  1.93 us
  transfers between devices with their start and end apart: 8, of which 3 were waited for; matrix products, arithmetic and copies ran while one was open for 0% of the time, Pallas kernels for 0%

profile of v19, /device:TPU:0, one launch (start us, length us, event | category | flops | bytes accessed | tf_op | source)
XLA Modules:
  0.0 69.5 jit_solution(3063904662656938537)
XLA Ops:
  0.6 1.8 %shard_map.77 = (f32[32,256]{1,0:T(8,128)}, f32[32,256]{1,0:T(8,128)}, f32[32,256]{1,0:T(8,128)}, f32[32,256]{1,0:T(8,128)}) custom-call(s32[4,32]{1,0:T(4,128)} %bitcast.26, f32[128,256]{1,0:T(8,128)} %own_ref.1), custom_call_target="tpu_custom_call" | custom-call | tf_op jit(solution)/shard_map/pallas_call | solution.py:271
  2.4 4.8 %collective-permute-start = (f32[32,256]{1,0:T(8,128)}, f32[32,256]{1,0:T(8,128)S(1)}, u32[]{:S(2)}, u32[]{:S(2)}) collective-permute-start(f32[32,256]{1,0:T(8,128)} %get-tuple-element.14), channel_id=1, source_target_pairs={{0,4},{4,8},{8,12},{12,16},{16,20},{20,24},{24,28},{1,5},{5,9},{9,... | collective-permute-start | bytes 98312 | tf_op jit(solution)/shard_map/ppermute | solution.py:321
  7.2 1.3 %collective-permute-start.1 = (f32[32,256]{1,0:T(8,128)}, f32[32,256]{1,0:T(8,128)S(1)}, u32[]{:S(2)}, u32[]{:S(2)}) collective-permute-start(f32[32,256]{1,0:T(8,128)} %get-tuple-element.15), channel_id=1, source_target_pairs={{4,0},{8,4},{12,8},{16,12},{20,16},{24,20},{28,24},{5,1},{9,5},{13... | collective-permute-start | bytes 98312 | tf_op jit(solution)/shard_map/ppermute | solution.py:322
  8.5 1.5 %collective-permute-start.2 = (f32[32,256]{1,0:T(8,128)}, f32[32,256]{1,0:T(8,128)S(1)}, u32[]{:S(2)}, u32[]{:S(2)}) collective-permute-start(f32[32,256]{1,0:T(8,128)} %get-tuple-element.16), channel_id=1, source_target_pairs={{0,1},{1,2},{2,3},{4,5},{5,6},{6,7},{8,9},{9,10},{10,11},{12,13},{... | collective-permute-start | bytes 98312 | tf_op jit(solution)/shard_map/ppermute | solution.py:323
  10.0 1.3 %collective-permute-start.3 = (f32[32,256]{1,0:T(8,128)}, f32[32,256]{1,0:T(8,128)S(1)}, u32[]{:S(2)}, u32[]{:S(2)}) collective-permute-start(f32[32,256]{1,0:T(8,128)} %get-tuple-element.17), channel_id=1, source_target_pairs={{1,0},{2,1},{3,2},{5,4},{6,5},{7,6},{9,8},{10,9},{11,10},{13,12},{... | collective-permute-start | bytes 98312 | tf_op jit(solution)/shard_map/ppermute | solution.py:324
  11.9 0.0 collective-permute-done.g0_ref
  11.9 0.0 copy-start
  12.0 1.3 %collective-permute-done.1.g1_ref = f32[32,256]{1,0:T(8,128)S(1)} collective-permute-done((f32[32,256]{1,0:T(8,128)}, f32[32,256]{1,0:T(8,128)S(1)}, u32[]{:S(2)}, u32[]{:S(2)}) %collective-permute-start.1) | collective-permute-done | bytes 32800 | tf_op jit(solution)/shard_map/ppermute | solution.py:322
  13.2 0.0 collective-permute-done.2.g2_ref
  13.2 1.6 %collective-permute-done.3.g3_ref = f32[32,256]{1,0:T(8,128)S(1)} collective-permute-done((f32[32,256]{1,0:T(8,128)}, f32[32,256]{1,0:T(8,128)S(1)}, u32[]{:S(2)}, u32[]{:S(2)}) %collective-permute-start.3) | collective-permute-done | bytes 32800 | tf_op jit(solution)/shard_map/ppermute | solution.py:324
  14.9 0.0 copy-done
  14.9 0.0 copy-done.1
  14.9 0.0 copy-done.3
  14.9 0.6 copy-done.5
  15.5 8.4 %shard_map.78 = (f32[128,256]{1,0:T(8,128)}, f32[32,256]{1,0:T(8,128)}, f32[32,256]{1,0:T(8,128)}, f32[32,256]{1,0:T(8,128)}, f32[32,256]{1,0:T(8,128)}, /*index=5*/f32[128,256]{1,0:T(8,128)}) custom-call(s32[1]{0:T(128)S(6)} %copy.39.count_ref, s32[4,32]{1,0:T(4,128)} %bitcast.27, f32[5,128,4096]{2,1,0:T(8,128)} %bitcast.23, f32[128,256]{1,0:T(8,128)} %own_ref.1, ...), custom_call_target="tpu_custom_call" | custom-call | flops 557842432 | bytes 11272192 | tf_op jit(solution)/shard_map/pallas_call | solution.py:241
  23.9 4.5 %collective-permute-start.4 = (f32[32,256]{1,0:T(8,128)}, f32[32,256]{1,0:T(8,128)S(1)}, u32[]{:S(2)}, u32[]{:S(2)}) collective-permute-start(f32[32,256]{1,0:T(8,128)} %get-tuple-element.19), channel_id=1, source_target_pairs={{0,4},{4,8},{8,12},{12,16},{16,20},{20,24},{24,28},{1,5},{5,9},{9,... | collective-permute-start | bytes 98312 | tf_op jit(solution)/shard_map/ppermute | solution.py:321
  28.5 1.3 %collective-permute-start.5 = (f32[32,256]{1,0:T(8,128)}, f32[32,256]{1,0:T(8,128)S(1)}, u32[]{:S(2)}, u32[]{:S(2)}) collective-permute-start(f32[32,256]{1,0:T(8,128)} %get-tuple-element.20), channel_id=1, source_target_pairs={{4,0},{8,4},{12,8},{16,12},{20,16},{24,20},{28,24},{5,1},{9,5},{13... | collective-permute-start | bytes 98312 | tf_op jit(solution)/shard_map/ppermute | solution.py:322
  29.8 4.3 %collective-permute-start.6 = (f32[32,256]{1,0:T(8,128)}, f32[32,256]{1,0:T(8,128)S(1)}, u32[]{:S(2)}, u32[]{:S(2)}) collective-permute-start(f32[32,256]{1,0:T(8,128)} %get-tuple-element.21), channel_id=1, source_target_pairs={{0,1},{1,2},{2,3},{4,5},{5,6},{6,7},{8,9},{9,10},{10,11},{12,13},{... | collective-permute-start | bytes 98312 | tf_op jit(solution)/shard_map/ppermute | solution.py:323
  34.0 1.3 %collective-permute-start.7 = (f32[32,256]{1,0:T(8,128)}, f32[32,256]{1,0:T(8,128)S(1)}, u32[]{:S(2)}, u32[]{:S(2)}) collective-permute-start(f32[32,256]{1,0:T(8,128)} %get-tuple-element.22), channel_id=1, source_target_pairs={{1,0},{2,1},{3,2},{5,4},{6,5},{7,6},{9,8},{10,9},{11,10},{13,12},{... | collective-permute-start | bytes 98312 | tf_op jit(solution)/shard_map/ppermute | solution.py:324
  35.3 0.0 collective-permute-done.4.g0_ref
  35.3 0.0 copy-start.2
  35.3 0.0 collective-permute-done.5.g1_ref
  35.4 0.0 copy-start.4
  35.4 0.0 collective-permute-done.6.g2_ref
  35.4 0.0 copy-start.6
  35.4 1.9 %collective-permute-done.7.g3_ref = f32[32,256]{1,0:T(8,128)S(1)} collective-permute-done((f32[32,256]{1,0:T(8,128)}, f32[32,256]{1,0:T(8,128)S(1)}, u32[]{:S(2)}, u32[]{:S(2)}) %collective-permute-start.7) | collective-permute-done | bytes 32800 | tf_op jit(solution)/shard_map/ppermute | solution.py:324
  37.3 0.0 copy-done.2
  37.3 0.0 copy-done.4
  37.3 0.6 copy-done.7
  37.9 8.6 %shard_map.79 = (f32[128,256]{1,0:T(8,128)}, f32[32,4,20]{2,1,0:T(4,128)}) custom-call(s32[1]{0:T(128)S(6)} %copy.39.count_ref, s32[4,32]{1,0:T(4,128)} %bitcast.28, f32[5,128,4096]{2,1,0:T(8,128)} %bitcast.24, f32[128,256]{1,0:T(8,128)} %get-tuple-element.18.own_ref.first_ref, f32[32,256]{1,0:T(8,128)} %copy-done.2, f32[32,256]{1,0:T(8,128)} %copy-done.4, ...), custom_call_target="tpu_custom_call" | custom-call | flops 557842432 | bytes 11272192 | tf_op jit(solution)/shard_map/pallas_call | solution.py:241
  46.5 16.5 %all_to_all.5 = f32[32,4,20]{2,1,0:T(4,128)S(1)} all-to-all(f32[32,4,20]{2,1,0:T(4,128)} %get-tuple-element.24), channel_id=1, replica_groups=mesh['wide'=8,'narrow'=4] {'wide','narrow'}, dimensions={0} | all-to-all | bytes 20480 | tf_op jit(solution)/shard_map/all_to_all | solution.py:333
  63.1 0.1 mul.15
  63.1 0.1 copy.29
  63.3 0.1 multiply_reduce_fusion
  63.3 0.2 fusion.10
  63.5 0.1 copy.37
  63.6 0.1 copy.38
  63.7 0.1 copy.31
  63.8 0.1 maximum_maximum_fusion
  63.9 0.1 copy.33
  64.0 0.7 %cholesky.16 = f32[8,8]{1,0:T(8,128)S(1)} custom-call(f32[8,8]{1,0:T(8,128)S(1)} %fusion.8), custom_call_target="Cholesky" | custom-call | tf_op jit(solution)/shard_map/jit(cholesky)/cholesky | solution.py:348
  64.7 0.1 select_reduce_fusion
  64.7 0.6 compare_reduce_fusion
  65.4 0.6 fusion
  66.0 0.6 custom-call.10
  66.7 0.2 fusion.1
  66.9 0.7 %fusion.6.mix_ref = f32[8,4]{1,0:T(8,128)} fusion(f32[8,4]{0,1:T(4,128)S(1)} %fusion.1, f32[1,8,8]{1,2,0:T(8,128)S(1)} %custom-call.10), kind=kOutput, calls=%fused_computation.12 | convolution fusion | flops 3072 | bytes 512 | tf_op jit(solution)/shard_map/jit(_cho_solve)/triangular_solve | solution.py:349
  67.6 1.9 %shard_map.80 = (f32[128,256]{1,0:T(8,128)}, f32[128,256]{1,0:T(8,128)}) custom-call(f32[8,4]{1,0:T(8,128)} %fusion.6.mix_ref, f32[128,256]{1,0:T(8,128)} %get-tuple-element.23.rest_0_.anchor_ref, f32[128,256]{1,0:T(8,128)} %get-tuple-element.18.own_ref.first_ref, f32[128,256]{1,0:T(8,128)} %get-tuple-element.25.second_ref), custom_call_target="tpu_custom_call" | custom-call | tf_op jit(solution)/shard_map/pallas_call | solution.py:306
  (9 shorter events, 0.1 us)
Async XLA Ops:
  2.4 9.6 %collective-permute-start = (f32[32,256]{1,0:T(8,128)}, f32[32,256]{1,0:T(8,128)S(1)}, u32[]{:S(2)}, u32[]{:S(2)}) collective-permute-start(f32[32,256]{1,0:T(8,128)} %get-tuple-element.14), channel_id=1, source_target_pairs={{0,4},{4,8},{8,12},{12,16},{16,20},{20,24},{24,28},{1,5},{5,9},{9,... | collective-permute-start | bytes 98312 | tf_op jit(solution)/shard_map/ppermute | solution.py:321
  7.2 6.0 %collective-permute-start.1 = (f32[32,256]{1,0:T(8,128)}, f32[32,256]{1,0:T(8,128)S(1)}, u32[]{:S(2)}, u32[]{:S(2)}) collective-permute-start(f32[32,256]{1,0:T(8,128)} %get-tuple-element.15), channel_id=1, source_target_pairs={{4,0},{8,4},{12,8},{16,12},{20,16},{24,20},{28,24},{5,1},{9,5},{13... | collective-permute-start | bytes 98312 | tf_op jit(solution)/shard_map/ppermute | solution.py:322
  8.5 4.7 %collective-permute-start.2 = (f32[32,256]{1,0:T(8,128)}, f32[32,256]{1,0:T(8,128)S(1)}, u32[]{:S(2)}, u32[]{:S(2)}) collective-permute-start(f32[32,256]{1,0:T(8,128)} %get-tuple-element.16), channel_id=1, source_target_pairs={{0,1},{1,2},{2,3},{4,5},{5,6},{6,7},{8,9},{9,10},{10,11},{12,13},{... | collective-permute-start | bytes 98312 | tf_op jit(solution)/shard_map/ppermute | solution.py:323
  10.0 4.9 %collective-permute-start.3 = (f32[32,256]{1,0:T(8,128)}, f32[32,256]{1,0:T(8,128)S(1)}, u32[]{:S(2)}, u32[]{:S(2)}) collective-permute-start(f32[32,256]{1,0:T(8,128)} %get-tuple-element.17), channel_id=1, source_target_pairs={{1,0},{2,1},{3,2},{5,4},{6,5},{7,6},{9,8},{10,9},{11,10},{13,12},{... | collective-permute-start | bytes 98312 | tf_op jit(solution)/shard_map/ppermute | solution.py:324
  11.9 2.9 %copy-start = (f32[32,256]{1,0:T(8,128)}, f32[32,256]{1,0:T(8,128)S(1)}, u32[]{:S(2)}) copy-start(f32[32,256]{1,0:T(8,128)S(1)} %collective-permute-done.g0_ref) | copy-start | bytes 98308
  13.2 1.7 %copy-start.1 = (f32[32,256]{1,0:T(8,128)}, f32[32,256]{1,0:T(8,128)S(1)}, u32[]{:S(2)}) copy-start(f32[32,256]{1,0:T(8,128)S(1)} %collective-permute-done.1.g1_ref) | copy-start | bytes 98308
  13.2 1.6 %copy-start.3 = (f32[32,256]{1,0:T(8,128)}, f32[32,256]{1,0:T(8,128)S(1)}, u32[]{:S(2)}) copy-start(f32[32,256]{1,0:T(8,128)S(1)} %collective-permute-done.2.g2_ref) | copy-start | bytes 98308
  14.9 0.6 copy-start.5
  15.5 47.8 %copy-start.8 = (f32[4,4,4]{2,1,0:T(4,128)S(1)}, f32[4,4,4]{2,1,0:T(4,128)}, u32[]{:S(2)}) copy-start(f32[4,4,4]{2,1,0:T(4,128)} %constant.52.clone) | copy-start | bytes 772
  23.9 11.4 %collective-permute-start.4 = (f32[32,256]{1,0:T(8,128)}, f32[32,256]{1,0:T(8,128)S(1)}, u32[]{:S(2)}, u32[]{:S(2)}) collective-permute-start(f32[32,256]{1,0:T(8,128)} %get-tuple-element.19), channel_id=1, source_target_pairs={{0,4},{4,8},{8,12},{12,16},{16,20},{20,24},{24,28},{1,5},{5,9},{9,... | collective-permute-start | bytes 98312 | tf_op jit(solution)/shard_map/ppermute | solution.py:321
  28.5 6.9 %collective-permute-start.5 = (f32[32,256]{1,0:T(8,128)}, f32[32,256]{1,0:T(8,128)S(1)}, u32[]{:S(2)}, u32[]{:S(2)}) collective-permute-start(f32[32,256]{1,0:T(8,128)} %get-tuple-element.20), channel_id=1, source_target_pairs={{4,0},{8,4},{12,8},{16,12},{20,16},{24,20},{28,24},{5,1},{9,5},{13... | collective-permute-start | bytes 98312 | tf_op jit(solution)/shard_map/ppermute | solution.py:322
  29.8 5.6 %collective-permute-start.6 = (f32[32,256]{1,0:T(8,128)}, f32[32,256]{1,0:T(8,128)S(1)}, u32[]{:S(2)}, u32[]{:S(2)}) collective-permute-start(f32[32,256]{1,0:T(8,128)} %get-tuple-element.21), channel_id=1, source_target_pairs={{0,1},{1,2},{2,3},{4,5},{5,6},{6,7},{8,9},{9,10},{10,11},{12,13},{... | collective-permute-start | bytes 98312 | tf_op jit(solution)/shard_map/ppermute | solution.py:323
  34.0 3.3 %collective-permute-start.7 = (f32[32,256]{1,0:T(8,128)}, f32[32,256]{1,0:T(8,128)S(1)}, u32[]{:S(2)}, u32[]{:S(2)}) collective-permute-start(f32[32,256]{1,0:T(8,128)} %get-tuple-element.22), channel_id=1, source_target_pairs={{1,0},{2,1},{3,2},{5,4},{6,5},{7,6},{9,8},{10,9},{11,10},{13,12},{... | collective-permute-start | bytes 98312 | tf_op jit(solution)/shard_map/ppermute | solution.py:324
  35.3 2.0 %copy-start.2 = (f32[32,256]{1,0:T(8,128)}, f32[32,256]{1,0:T(8,128)S(1)}, u32[]{:S(2)}) copy-start(f32[32,256]{1,0:T(8,128)S(1)} %collective-permute-done.4.g0_ref) | copy-start | bytes 98308
  35.4 2.0 %copy-start.4 = (f32[32,256]{1,0:T(8,128)}, f32[32,256]{1,0:T(8,128)S(1)}, u32[]{:S(2)}) copy-start(f32[32,256]{1,0:T(8,128)S(1)} %collective-permute-done.5.g1_ref) | copy-start | bytes 98308
  35.4 2.0 %copy-start.6 = (f32[32,256]{1,0:T(8,128)}, f32[32,256]{1,0:T(8,128)S(1)}, u32[]{:S(2)}) copy-start(f32[32,256]{1,0:T(8,128)S(1)} %collective-permute-done.6.g2_ref) | copy-start | bytes 98308
  37.3 0.6 copy-start.7

commit v20 on v17

--- a/solution.py
+++ b/solution.py
@@ -15,7 +15,7 @@
 LANES = 128
 SUBLANES = 8
 UNROLL = 32
-CHUNK_ROWS = 8
+CHUNK_ROWS = 32
 ROWS_PER_STEP = 32
 
 

time: 71 us -> 69.9 us (0.985)
  Pallas kernels: 21.7 us -> 20.6 us
    pallas_call x2, Pallas kernels: 18 us -> 16.9 us  [apply_operator(): pl.pallas_call(functools.partial(coupling_kernel, with_gram), out_shape=t...]
where the time goes in v20:
time: 69.9 us; the launch traced here: 69.5 us
  Pallas kernels  20.6 us (29%)
  starting transfers between devices  20.3 us (29%)
  blocking collectives  16.5 us (24%)
  waiting for transfers between devices  4.88 us (7%)
  other arithmetic  2.89 us (4%)
  local copies, waits for them, and re-layouts  1.96 us (3%)
  between operations  1.46 us (2%)
  matrix products  0.93 us (1%)
    pallas_call x2, Pallas kernels, apply_operator(): pl.pallas_call(functools.partial(coupling_kernel, with_gram), out_shape=t...  16.9 us
    all_to_all x1, blocking collectives, per_device(): everyone = lax.all_to_all(raw_gram, ('wide', 'narrow'), 0, 0, tiled=True)  16.5 us
    ppermute x2, starting transfers between devices, ghosts(): lax.ppermute(outgoing[0], 'wide', [(i, i + 1) for i in range(wide - 1)])  9.38 us
    ppermute x2, starting transfers between devices, ghosts(): lax.ppermute(outgoing[2], 'narrow', [(i, i + 1) for i in range(narrow - 1)])  5.72 us
    ppermute x2, waiting for transfers between devices, ghosts(): lax.ppermute(outgoing[3], 'narrow', [(i + 1, i) for i in range(narrow - 1)])  3.59 us
    ppermute x2, starting transfers between devices, ghosts(): lax.ppermute(outgoing[1], 'wide', [(i + 1, i) for i in range(wide - 1)])  2.58 us
    ppermute x2, starting transfers between devices, ghosts(): lax.ppermute(outgoing[3], 'narrow', [(i + 1, i) for i in range(narrow - 1)])  2.58 us
    pallas_call x1, Pallas kernels, mix_outputs(): pl.pallas_call(mixing_kernel, out_shape=(jax.ShapeDtypeStruct(anchor.shap...  1.93 us
  transfers between devices with their start and end apart: 8, of which 3 were waited for; matrix products, arithmetic and copies ran while one was open for 0% of the time, Pallas kernels for 0%

profile of v20, /device:TPU:0, one launch (start us, length us, event | category | flops | bytes accessed | tf_op | source)
XLA Modules:
  0.0 69.5 jit_solution(18027732335185102038)
XLA Ops:
  0.6 1.8 %shard_map.77 = (f32[32,256]{1,0:T(8,128)}, f32[32,256]{1,0:T(8,128)}, f32[32,256]{1,0:T(8,128)}, f32[32,256]{1,0:T(8,128)}) custom-call(s32[4,32]{1,0:T(4,128)} %bitcast.26, f32[128,256]{1,0:T(8,128)} %own_ref.1), custom_call_target="tpu_custom_call" | custom-call | tf_op jit(solution)/shard_map/pallas_call | solution.py:267
  2.4 4.8 %collective-permute-start = (f32[32,256]{1,0:T(8,128)}, f32[32,256]{1,0:T(8,128)S(1)}, u32[]{:S(2)}, u32[]{:S(2)}) collective-permute-start(f32[32,256]{1,0:T(8,128)} %get-tuple-element.14), channel_id=1, source_target_pairs={{0,4},{4,8},{8,12},{12,16},{16,20},{20,24},{24,28},{1,5},{5,9},{9,... | collective-permute-start | bytes 98312 | tf_op jit(solution)/shard_map/ppermute | solution.py:317
  7.2 1.3 %collective-permute-start.1 = (f32[32,256]{1,0:T(8,128)}, f32[32,256]{1,0:T(8,128)S(1)}, u32[]{:S(2)}, u32[]{:S(2)}) collective-permute-start(f32[32,256]{1,0:T(8,128)} %get-tuple-element.15), channel_id=1, source_target_pairs={{4,0},{8,4},{12,8},{16,12},{20,16},{24,20},{28,24},{5,1},{9,5},{13... | collective-permute-start | bytes 98312 | tf_op jit(solution)/shard_map/ppermute | solution.py:318
  8.5 1.5 %collective-permute-start.2 = (f32[32,256]{1,0:T(8,128)}, f32[32,256]{1,0:T(8,128)S(1)}, u32[]{:S(2)}, u32[]{:S(2)}) collective-permute-start(f32[32,256]{1,0:T(8,128)} %get-tuple-element.16), channel_id=1, source_target_pairs={{0,1},{1,2},{2,3},{4,5},{5,6},{6,7},{8,9},{9,10},{10,11},{12,13},{... | collective-permute-start | bytes 98312 | tf_op jit(solution)/shard_map/ppermute | solution.py:319
  10.0 1.3 %collective-permute-start.3 = (f32[32,256]{1,0:T(8,128)}, f32[32,256]{1,0:T(8,128)S(1)}, u32[]{:S(2)}, u32[]{:S(2)}) collective-permute-start(f32[32,256]{1,0:T(8,128)} %get-tuple-element.17), channel_id=1, source_target_pairs={{1,0},{2,1},{3,2},{5,4},{6,5},{7,6},{9,8},{10,9},{11,10},{13,12},{... | collective-permute-start | bytes 98312 | tf_op jit(solution)/shard_map/ppermute | solution.py:320
  11.9 0.0 collective-permute-done.g0_ref
  11.9 0.0 copy-start
  12.0 1.3 %collective-permute-done.1.g1_ref = f32[32,256]{1,0:T(8,128)S(1)} collective-permute-done((f32[32,256]{1,0:T(8,128)}, f32[32,256]{1,0:T(8,128)S(1)}, u32[]{:S(2)}, u32[]{:S(2)}) %collective-permute-start.1) | collective-permute-done | bytes 32800 | tf_op jit(solution)/shard_map/ppermute | solution.py:318
  13.2 0.0 collective-permute-done.2.g2_ref
  13.2 1.6 %collective-permute-done.3.g3_ref = f32[32,256]{1,0:T(8,128)S(1)} collective-permute-done((f32[32,256]{1,0:T(8,128)}, f32[32,256]{1,0:T(8,128)S(1)}, u32[]{:S(2)}, u32[]{:S(2)}) %collective-permute-start.3) | collective-permute-done | bytes 32800 | tf_op jit(solution)/shard_map/ppermute | solution.py:320
  14.9 0.0 copy-done
  14.9 0.0 copy-done.1
  14.9 0.0 copy-done.3
  14.9 0.6 copy-done.5
  15.5 8.4 %shard_map.78 = (f32[128,256]{1,0:T(8,128)}, f32[32,256]{1,0:T(8,128)}, f32[32,256]{1,0:T(8,128)}, f32[32,256]{1,0:T(8,128)}, f32[32,256]{1,0:T(8,128)}, /*index=5*/f32[128,256]{1,0:T(8,128)}) custom-call(s32[1]{0:T(128)S(6)} %copy.39.count_ref, s32[4,32]{1,0:T(4,128)} %bitcast.27, f32[5,128,4096]{2,1,0:T(8,128)} %bitcast.23, f32[128,256]{1,0:T(8,128)} %own_ref.1, ...), custom_call_target="tpu_custom_call" | custom-call | flops 557842432 | bytes 11272192 | tf_op jit(solution)/shard_map/pallas_call | solution.py:237
  23.9 4.5 %collective-permute-start.4 = (f32[32,256]{1,0:T(8,128)}, f32[32,256]{1,0:T(8,128)S(1)}, u32[]{:S(2)}, u32[]{:S(2)}) collective-permute-start(f32[32,256]{1,0:T(8,128)} %get-tuple-element.19), channel_id=1, source_target_pairs={{0,4},{4,8},{8,12},{12,16},{16,20},{20,24},{24,28},{1,5},{5,9},{9,... | collective-permute-start | bytes 98312 | tf_op jit(solution)/shard_map/ppermute | solution.py:317
  28.4 1.3 %collective-permute-start.5 = (f32[32,256]{1,0:T(8,128)}, f32[32,256]{1,0:T(8,128)S(1)}, u32[]{:S(2)}, u32[]{:S(2)}) collective-permute-start(f32[32,256]{1,0:T(8,128)} %get-tuple-element.20), channel_id=1, source_target_pairs={{4,0},{8,4},{12,8},{16,12},{20,16},{24,20},{28,24},{5,1},{9,5},{13... | collective-permute-start | bytes 98312 | tf_op jit(solution)/shard_map/ppermute | solution.py:318
  29.7 4.3 %collective-permute-start.6 = (f32[32,256]{1,0:T(8,128)}, f32[32,256]{1,0:T(8,128)S(1)}, u32[]{:S(2)}, u32[]{:S(2)}) collective-permute-start(f32[32,256]{1,0:T(8,128)} %get-tuple-element.21), channel_id=1, source_target_pairs={{0,1},{1,2},{2,3},{4,5},{5,6},{6,7},{8,9},{9,10},{10,11},{12,13},{... | collective-permute-start | bytes 98312 | tf_op jit(solution)/shard_map/ppermute | solution.py:319
  34.0 1.3 %collective-permute-start.7 = (f32[32,256]{1,0:T(8,128)}, f32[32,256]{1,0:T(8,128)S(1)}, u32[]{:S(2)}, u32[]{:S(2)}) collective-permute-start(f32[32,256]{1,0:T(8,128)} %get-tuple-element.22), channel_id=1, source_target_pairs={{1,0},{2,1},{3,2},{5,4},{6,5},{7,6},{9,8},{10,9},{11,10},{13,12},{... | collective-permute-start | bytes 98312 | tf_op jit(solution)/shard_map/ppermute | solution.py:320
  35.3 0.0 collective-permute-done.4.g0_ref
  35.3 0.0 copy-start.2
  35.3 0.0 collective-permute-done.5.g1_ref
  35.3 0.0 copy-start.4
  35.3 0.0 collective-permute-done.6.g2_ref
  35.4 0.0 copy-start.6
  35.4 1.9 %collective-permute-done.7.g3_ref = f32[32,256]{1,0:T(8,128)S(1)} collective-permute-done((f32[32,256]{1,0:T(8,128)}, f32[32,256]{1,0:T(8,128)S(1)}, u32[]{:S(2)}, u32[]{:S(2)}) %collective-permute-start.7) | collective-permute-done | bytes 32800 | tf_op jit(solution)/shard_map/ppermute | solution.py:320
  37.3 0.0 copy-done.2
  37.3 0.0 copy-done.4
  37.3 0.6 copy-done.7
  37.9 8.6 %shard_map.79 = (f32[128,256]{1,0:T(8,128)}, f32[32,4,20]{2,1,0:T(4,128)}) custom-call(s32[1]{0:T(128)S(6)} %copy.39.count_ref, s32[4,32]{1,0:T(4,128)} %bitcast.28, f32[5,128,4096]{2,1,0:T(8,128)} %bitcast.24, f32[128,256]{1,0:T(8,128)} %get-tuple-element.18.own_ref.first_ref, f32[32,256]{1,0:T(8,128)} %copy-done.2, f32[32,256]{1,0:T(8,128)} %copy-done.4, ...), custom_call_target="tpu_custom_call" | custom-call | flops 557842432 | bytes 11272192 | tf_op jit(solution)/shard_map/pallas_call | solution.py:237
  46.5 16.5 %all_to_all.5 = f32[32,4,20]{2,1,0:T(4,128)S(1)} all-to-all(f32[32,4,20]{2,1,0:T(4,128)} %get-tuple-element.24), channel_id=1, replica_groups=mesh['wide'=8,'narrow'=4] {'wide','narrow'}, dimensions={0} | all-to-all | bytes 20480 | tf_op jit(solution)/shard_map/all_to_all | solution.py:329
  63.0 0.1 mul.15
  63.1 0.1 copy.29
  63.2 0.1 multiply_reduce_fusion
  63.3 0.2 fusion.10
  63.5 0.1 copy.37
  63.6 0.1 copy.38
  63.7 0.1 copy.31
  63.8 0.1 maximum_maximum_fusion
  63.9 0.1 copy.33
  64.0 0.7 %cholesky.16 = f32[8,8]{1,0:T(8,128)S(1)} custom-call(f32[8,8]{1,0:T(8,128)S(1)} %fusion.8), custom_call_target="Cholesky" | custom-call | tf_op jit(solution)/shard_map/jit(cholesky)/cholesky | solution.py:344
  64.6 0.1 select_reduce_fusion
  64.7 0.6 compare_reduce_fusion
  65.4 0.6 fusion
  66.0 0.6 custom-call.10
  66.6 0.2 fusion.1
  66.8 0.7 %fusion.6.mix_ref = f32[8,4]{1,0:T(8,128)} fusion(f32[8,4]{0,1:T(4,128)S(1)} %fusion.1, f32[1,8,8]{1,2,0:T(8,128)S(1)} %custom-call.10), kind=kOutput, calls=%fused_computation.12 | convolution fusion | flops 3072 | bytes 512 | tf_op jit(solution)/shard_map/jit(_cho_solve)/triangular_solve | solution.py:345
  67.6 1.9 %shard_map.80 = (f32[128,256]{1,0:T(8,128)}, f32[128,256]{1,0:T(8,128)}) custom-call(f32[8,4]{1,0:T(8,128)} %fusion.6.mix_ref, f32[128,256]{1,0:T(8,128)} %get-tuple-element.23.rest_0_.anchor_ref, f32[128,256]{1,0:T(8,128)} %get-tuple-element.18.own_ref.first_ref, f32[128,256]{1,0:T(8,128)} %get-tuple-element.25.second_ref), custom_call_target="tpu_custom_call" | custom-call | tf_op jit(solution)/shard_map/pallas_call | solution.py:302
  (9 shorter events, 0.1 us)
Async XLA Ops:
  2.4 9.6 %collective-permute-start = (f32[32,256]{1,0:T(8,128)}, f32[32,256]{1,0:T(8,128)S(1)}, u32[]{:S(2)}, u32[]{:S(2)}) collective-permute-start(f32[32,256]{1,0:T(8,128)} %get-tuple-element.14), channel_id=1, source_target_pairs={{0,4},{4,8},{8,12},{12,16},{16,20},{20,24},{24,28},{1,5},{5,9},{9,... | collective-permute-start | bytes 98312 | tf_op jit(solution)/shard_map/ppermute | solution.py:317
  7.2 6.0 %collective-permute-start.1 = (f32[32,256]{1,0:T(8,128)}, f32[32,256]{1,0:T(8,128)S(1)}, u32[]{:S(2)}, u32[]{:S(2)}) collective-permute-start(f32[32,256]{1,0:T(8,128)} %get-tuple-element.15), channel_id=1, source_target_pairs={{4,0},{8,4},{12,8},{16,12},{20,16},{24,20},{28,24},{5,1},{9,5},{13... | collective-permute-start | bytes 98312 | tf_op jit(solution)/shard_map/ppermute | solution.py:318
  8.5 4.7 %collective-permute-start.2 = (f32[32,256]{1,0:T(8,128)}, f32[32,256]{1,0:T(8,128)S(1)}, u32[]{:S(2)}, u32[]{:S(2)}) collective-permute-start(f32[32,256]{1,0:T(8,128)} %get-tuple-element.16), channel_id=1, source_target_pairs={{0,1},{1,2},{2,3},{4,5},{5,6},{6,7},{8,9},{9,10},{10,11},{12,13},{... | collective-permute-start | bytes 98312 | tf_op jit(solution)/shard_map/ppermute | solution.py:319
  10.0 4.9 %collective-permute-start.3 = (f32[32,256]{1,0:T(8,128)}, f32[32,256]{1,0:T(8,128)S(1)}, u32[]{:S(2)}, u32[]{:S(2)}) collective-permute-start(f32[32,256]{1,0:T(8,128)} %get-tuple-element.17), channel_id=1, source_target_pairs={{1,0},{2,1},{3,2},{5,4},{6,5},{7,6},{9,8},{10,9},{11,10},{13,12},{... | collective-permute-start | bytes 98312 | tf_op jit(solution)/shard_map/ppermute | solution.py:320
  11.9 2.9 %copy-start = (f32[32,256]{1,0:T(8,128)}, f32[32,256]{1,0:T(8,128)S(1)}, u32[]{:S(2)}) copy-start(f32[32,256]{1,0:T(8,128)S(1)} %collective-permute-done.g0_ref) | copy-start | bytes 98308
  13.2 1.7 %copy-start.1 = (f32[32,256]{1,0:T(8,128)}, f32[32,256]{1,0:T(8,128)S(1)}, u32[]{:S(2)}) copy-start(f32[32,256]{1,0:T(8,128)S(1)} %collective-permute-done.1.g1_ref) | copy-start | bytes 98308
  13.2 1.6 %copy-start.3 = (f32[32,256]{1,0:T(8,128)}, f32[32,256]{1,0:T(8,128)S(1)}, u32[]{:S(2)}) copy-start(f32[32,256]{1,0:T(8,128)S(1)} %collective-permute-done.2.g2_ref) | copy-start | bytes 98308
  14.9 0.6 copy-start.5
  15.5 47.7 %copy-start.8 = (f32[4,4,4]{2,1,0:T(4,128)S(1)}, f32[4,4,4]{2,1,0:T(4,128)}, u32[]{:S(2)}) copy-start(f32[4,4,4]{2,1,0:T(4,128)} %constant.52.clone) | copy-start | bytes 772
  23.9 11.4 %collective-permute-start.4 = (f32[32,256]{1,0:T(8,128)}, f32[32,256]{1,0:T(8,128)S(1)}, u32[]{:S(2)}, u32[]{:S(2)}) collective-permute-start(f32[32,256]{1,0:T(8,128)} %get-tuple-element.19), channel_id=1, source_target_pairs={{0,4},{4,8},{8,12},{12,16},{16,20},{20,24},{24,28},{1,5},{5,9},{9,... | collective-permute-start | bytes 98312 | tf_op jit(solution)/shard_map/ppermute | solution.py:317
  28.4 6.9 %collective-permute-start.5 = (f32[32,256]{1,0:T(8,128)}, f32[32,256]{1,0:T(8,128)S(1)}, u32[]{:S(2)}, u32[]{:S(2)}) collective-permute-start(f32[32,256]{1,0:T(8,128)} %get-tuple-element.20), channel_id=1, source_target_pairs={{4,0},{8,4},{12,8},{16,12},{20,16},{24,20},{28,24},{5,1},{9,5},{13... | collective-permute-start | bytes 98312 | tf_op jit(solution)/shard_map/ppermute | solution.py:318
  29.7 5.6 %collective-permute-start.6 = (f32[32,256]{1,0:T(8,128)}, f32[32,256]{1,0:T(8,128)S(1)}, u32[]{:S(2)}, u32[]{:S(2)}) collective-permute-start(f32[32,256]{1,0:T(8,128)} %get-tuple-element.21), channel_id=1, source_target_pairs={{0,1},{1,2},{2,3},{4,5},{5,6},{6,7},{8,9},{9,10},{10,11},{12,13},{... | collective-permute-start | bytes 98312 | tf_op jit(solution)/shard_map/ppermute | solution.py:319
  34.0 3.3 %collective-permute-start.7 = (f32[32,256]{1,0:T(8,128)}, f32[32,256]{1,0:T(8,128)S(1)}, u32[]{:S(2)}, u32[]{:S(2)}) collective-permute-start(f32[32,256]{1,0:T(8,128)} %get-tuple-element.22), channel_id=1, source_target_pairs={{1,0},{2,1},{3,2},{5,4},{6,5},{7,6},{9,8},{10,9},{11,10},{13,12},{... | collective-permute-start | bytes 98312 | tf_op jit(solution)/shard_map/ppermute | solution.py:320
  35.3 2.0 %copy-start.2 = (f32[32,256]{1,0:T(8,128)}, f32[32,256]{1,0:T(8,128)S(1)}, u32[]{:S(2)}) copy-start(f32[32,256]{1,0:T(8,128)S(1)} %collective-permute-done.4.g0_ref) | copy-start | bytes 98308
  35.3 2.0 %copy-start.4 = (f32[32,256]{1,0:T(8,128)}, f32[32,256]{1,0:T(8,128)S(1)}, u32[]{:S(2)}) copy-start(f32[32,256]{1,0:T(8,128)S(1)} %collective-permute-done.5.g1_ref) | copy-start | bytes 98308
  35.4 2.0 %copy-start.6 = (f32[32,256]{1,0:T(8,128)}, f32[32,256]{1,0:T(8,128)S(1)}, u32[]{:S(2)}) copy-start(f32[32,256]{1,0:T(8,128)S(1)} %collective-permute-done.6.g2_ref) | copy-start | bytes 98308
  37.3 0.6 copy-start.7
